TPU v7x, 32 devices: a whole 2x2x4 slice. The times are simulated.
32 devices in a mesh: ang: 8 (over z, core), row: 4 (over y, x).
Axes of the slice: x: 2, y: 2, z: 4, core: 2. Of those that a mesh axis runs over, the one named last changes fastest.
Arguments:
- panels: bfloat16 [4, 32, 64, 2, 128], P('row', None, 'ang'), may hold values from -6 to 6
- panel_slot: int32 [4, 32], P('row'), may hold values from 0 to 15
- panel_cell: int32 [4, 32, 2], P('row'), may hold values from 0 to 15
- bloch_k: float32 [8, 2], replicated, may hold values from -3.140625 to 3.140625
- leaf_inverse: bfloat16 [8, 2, 8192, 256], P('ang', None, 'row'), may hold values from -0.25 to 0.25
- level_left: bfloat16 [8, 3, 2, 32, 8192], P('ang', None, None, None, 'row'), may hold values from -0.75 to 0.75
- level_right: bfloat16 [8, 3, 2, 32, 8192], P('ang', None, None, None, 'row'), may hold values from -0.125 to 0.125
- block_left: bfloat16 [8, 2, 32, 8192], P('ang', None, None, 'row'), may hold values from -0.75 to 0.75
- block_right: bfloat16 [8, 2, 32, 8192], P('ang', None, None, 'row'), may hold values from -0.09375 to 0.09375
- block_coupling: bfloat16 [8, 4, 2, 32, 128], P('ang', 'row'), may hold values from -0.375 to 0.375
- rank_count: int32 [8, 4], P('ang', 'row'), may hold values from 16 to 32
- quad_weight: float32 [8, 2], P('ang'), may hold values from -2 to 2
Outputs:
- response: float32 [64, 2, 8192], P('ang', None, 'row')
All inputs are finite; a program needn't handle non-finite values.
Results may differ from a plain program's by a relative error of at most 0.0045.
Values may be sent and summed in bfloat16 or wider, within the bound.
No kernel may reach another device: no remote copies, remote signals or barrier semaphores. Data moves between devices by JAX's collectives and lax.ppermute only.
A program may use at most 64 MiB of HBM per device.

v0:
```python
import jax
import jax.numpy as jnp
from jax import lax
from jax.sharding import PartitionSpec as P


def complex_product(form, left_real, left_imag, right_real, right_imag):

    def single(first, second):
        return jnp.einsum(form, first, second, preferred_element_type=jnp.float32)

    return (
        single(left_real, right_real) - single(left_imag, right_imag),
        single(left_real, right_imag) + single(left_imag, right_real),
    )


def assemble(phase_cosine, phase_sin, onehot, panel_group):
    coef_cos = phase_cosine[:, :, None] * onehot[None]
    coef_sin = phase_sin[:, :, None] * onehot[None]
    panel_real = panel_group[:, :, 0]
    panel_imag = panel_group[:, :, 1]

    def single(coefficient, entry_values):
        return jnp.einsum(
            "aqk,qsw->askw", coefficient, entry_values, preferred_element_type=jnp.float32
        )

    real_part = single(coef_cos, panel_real) + single(coef_sin, panel_imag)
    imag_part = single(coef_cos, panel_imag) - single(coef_sin, panel_real)
    stacked = jnp.stack([real_part, imag_part], 2)
    dims = stacked.shape
    return stacked.reshape(dims[0], dims[1], 2, dims[3] * dims[4]).astype(jnp.bfloat16)


def near_field(excite, leaf_block, right_factors, left_factors):
    source_count = excite.shape[0]
    row_count = excite.shape[2]
    leaf_width = leaf_block.shape[2]
    leaf_count = row_count // leaf_width
    rank_width = right_factors.shape[2]
    gathered_groups = excite.reshape(source_count, 2, leaf_count, leaf_width)
    real_part, imag_part = complex_product(
        "lwv,slv->slw",
        leaf_block[0].reshape(leaf_count, leaf_width, leaf_width),
        leaf_block[1].reshape(leaf_count, leaf_width, leaf_width),
        gathered_groups[:, 0],
        gathered_groups[:, 1],
    )
    real_part = real_part.reshape(source_count, row_count)
    imag_part = imag_part.reshape(source_count, row_count)
    for tree_level_index in range(right_factors.shape[0]):
        node_size = row_count // 2 ** (tree_level_index + 1)
        groups = row_count // node_size
        node_view = excite.reshape(source_count, 2, groups, node_size)
        right_real = right_factors[tree_level_index, 0].reshape(rank_width, groups, node_size)
        right_imag = right_factors[tree_level_index, 1].reshape(rank_width, groups, node_size)
        proj_real, proj_imag = complex_product(
            "rgm,sgm->sgr", right_real, right_imag, node_view[:, 0], node_view[:, 1]
        )
        projected = jnp.stack([proj_real, proj_imag], 1).astype(jnp.bfloat16)
        swapped = projected.reshape(source_count, 2, groups // 2, 2, rank_width)[
            :, :, :, ::-1
        ].reshape(source_count, 2, groups, rank_width)
        left_real = left_factors[tree_level_index, 0].reshape(rank_width, groups, node_size)
        left_imag = left_factors[tree_level_index, 1].reshape(rank_width, groups, node_size)
        add_real, add_imag = complex_product(
            "rgm,sgr->sgm", left_real, left_imag, swapped[:, 0], swapped[:, 1]
        )
        real_part = real_part + add_real.reshape(source_count, row_count)
        imag_part = imag_part + add_imag.reshape(source_count, row_count)
    return (real_part, imag_part)


def shards(
    panels,
    panel_slot,
    panel_cell,
    bloch_k,
    leaf_inverse,
    level_left,
    level_right,
    block_left,
    block_right,
    block_coupling,
    rank_count,
    quad_weight,
):
    local_angles = leaf_inverse.shape[0]
    row_count = leaf_inverse.shape[2]
    panel_width = panels.shape[4]
    slot_count = row_count // panel_width
    onehot = (panel_slot[0][:, None] == jnp.arange(slot_count, dtype=jnp.int32)[None, :]).astype(
        jnp.bfloat16
    )
    cell_float = panel_cell[0].astype(jnp.float32)
    own_wave = lax.dynamic_slice_in_dim(
        bloch_k, lax.axis_index("ang") * local_angles, local_angles, 0
    )
    theta = own_wave[:, 0:1] * cell_float[None, :, 0] + own_wave[:, 1:2] * cell_float[None, :, 1]
    own_cos = jnp.cos(theta).astype(jnp.bfloat16)
    own_sin = jnp.sin(theta).astype(jnp.bfloat16)
    excitation = assemble(
        own_cos, own_sin, onehot, lax.all_gather(panels, "ang", axis=2, tiled=True)[0]
    )
    rank_width = block_right.shape[2]
    rank_iota = jnp.arange(rank_width, dtype=jnp.int32)
    rank_masks = (rank_iota[None, :] < rank_count).astype(jnp.bfloat16)
    right_masked = block_right * rank_masks[:, None, :, None]
    left_masked = block_left * rank_masks[:, None, :, None]
    proj_real, proj_imag = complex_product(
        "arm,asm->asr",
        right_masked[:, 0],
        right_masked[:, 1],
        excitation[:, :, 0],
        excitation[:, :, 1],
    )
    projected = jnp.stack([proj_real, proj_imag], 2).astype(jnp.bfloat16)
    gathered = lax.all_gather(projected[:, None], "row", axis=1, tiled=True)
    number_of_blocks = gathered.shape[1]
    keep_other = (jnp.arange(number_of_blocks, dtype=jnp.int32) != lax.axis_index("row")).astype(
        jnp.bfloat16
    )
    gathered = gathered * keep_other[None, :, None, None, None]
    coupling = block_coupling[:, 0].reshape(
        local_angles, 2, rank_width, number_of_blocks, rank_width
    )
    coup_real, coup_imag = complex_product(
        "arjq,ajsq->asr", coupling[:, 0], coupling[:, 1], gathered[:, :, :, 0], gathered[:, :, :, 1]
    )
    coupled = jnp.stack([coup_real, coup_imag], 2).astype(jnp.bfloat16)
    excite_part = excitation[0]
    coupled_part = coupled[0]
    near_real, near_imag = near_field(excite_part, leaf_inverse[0], level_right[0], level_left[0])
    far_real, far_imag = complex_product(
        "rm,sr->sm", left_masked[0, 0], left_masked[0, 1], coupled_part[:, 0], coupled_part[:, 1]
    )
    field_real = near_real + far_real
    field_imag = near_imag + far_imag
    weight_real = quad_weight[0, 0]
    weight_imag = quad_weight[0, 1]
    summed = jnp.stack(
        [
            weight_real * field_real - weight_imag * field_imag,
            weight_real * field_imag + weight_imag * field_real,
        ],
        1,
    )
    return lax.psum_scatter(summed, "ang", scatter_dimension=0, tiled=True)


def solution(mesh):
    placed = (
        P("row", None, "ang", None, None),
        P("row", None),
        P("row", None, None),
        P(),
        P("ang", None, "row", None),
        P("ang", None, None, None, "row"),
        P("ang", None, None, None, "row"),
        P("ang", None, None, "row"),
        P("ang", None, None, "row"),
        P("ang", "row", None, None, None),
        P("ang", "row"),
        P("ang", None),
    )
    return jax.shard_map(
        shards, mesh=mesh, in_specs=placed, out_specs=P("ang", None, "row"), check_vma=False
    )
```

profile of v0, /device:TPU:0, one launch (start us, length us, event | category | flops | bytes accessed | tf_op | source)
XLA Modules:
  0.0 121.3 jit_solution(7901270127954322322)
XLA Ops:
  6.5 1.7 %copy.87 = bf16[1,32,8,2,128]{4,1,2,3,0:T(8,128)(2,1)} copy(bf16[1,32,8,2,128]{4,3,2,1,0:T(2,128)(2,1)} %param.12) | data formatting | bytes 262144 | tf_op args[0]
  8.3 0.7 convert_bitcast_fusion
  9.0 1.3 %fusion.122 = (bf16[1,1,32,2048]{3,2,1,0:T(8,128)(2,1)S(1)}, bf16[1,1,32,2048]{3,2,1,0:T(8,128)(2,1)S(1)}, bf16[1,1,32,2048]{3,2,1,0:T(8,128)(2,1)S(1)}, bf16[1,...) fusion(bf16[3,2,32,2048]{3,2,1,0:T(8,128)(2,1)} %bitcast.282), kind=kLoop, calls=%fused_computation.173 | loop fusion | bytes 1572864 | tf_op jit(solution)/shard_map/slice | solution.py:57
  11.1 0.7 fusion.125
  11.8 0.7 reshape_squeeze.55
  12.6 0.7 reshape_squeeze.56
  13.3 0.7 reshape_squeeze.57
  14.0 0.7 reshape_squeeze.58
  14.7 0.7 reshape_squeeze.51
  15.5 0.7 reshape_squeeze.52
  16.2 0.7 reshape_squeeze.53
  17.0 0.7 copy.151
  17.7 0.7 copy.152
  18.3 0.7 copy.153
  19.0 0.7 copy.154
  20.3 1.3 %convert_bitcast_fusion.1 = (bf16[32]{0:T(256)(128)(2,1)S(1)}, f32[32,1]{0,1:T(1,128)S(1)}) fusion(f32[32,2]{0,1:T(2,128)S(1)} %convert_bitcast_fusion, f32[]{:T(128)} %bitcast.4, f32[]{:T(128)} %bitcast.2), kind=kLoop, calls=%fused_computation.163 | loop fusion | flops 128 | bytes 456 | tf_op jit(solution)/shard_map/convert_element_type | solution.py:102
  21.7 0.7 fusion.123
  22.3 0.9 broadcast_multiply_fusion
  23.2 1.7 %fusion.120 = (bf16[1,1,2048,256]{3,2,1,0:T(8,128)(2,1)S(1)}, bf16[1,1,2048,256]{3,2,1,0:T(8,128)(2,1)S(1)}) fusion(bf16[1,2,2048,256]{3,2,1,0:T(8,128)(2,1)} %param.16), kind=kLoop, calls=%fused_computation.171 | loop fusion | bytes 4194304 | tf_op jit(solution)/shard_map/slice | solution.py:46
  24.9 8.9 %all-gather.2.cloned.1.call-done = bf16[1,32,64,2,128]{4,1,2,3,0:T(8,128)(2,1)} async-done(((bf16[1,32,8,2,128]{4,1,2,3,0:T(8,128)(2,1)}), bf16[1,32,64,2,128]{4,1,2,3,0:T(8,128)(2,1)}) %all-gather.2.cloned.1.call-update) | async-done | bytes 1048592 | tf_op jit(solution)/shard_map/all_gather | solution.py:104
  33.9 1.3 %fusion.28 = f32[16,64,128]{2,0,1:T(8,128)S(1)} fusion(bf16[32,64,2,128]{3,0,1,2:T(8,128)(2,1)} %bitcast.250, s32[32]{0:T(128)S(1)} %bitcast.298, bf16[32]{0:T(256)(128)(2,1)S(1)} %convert_bitcast_fusion.2), kind=kOutput, calls=%fused_computation.57 | convolution fusion | flops 8389632 | bytes 1048768 | tf_op jit(solution)/shard_map/aqk,qsw->askw/dot_general | solution.py:25
  35.2 2.1 %fusion.29 = f32[16,64,128]{2,0,1:T(8,128)} fusion(bf16[32,64,2,128]{3,0,1,2:T(8,128)(2,1)} %bitcast.251, s32[32]{0:T(128)S(1)} %bitcast.299, bf16[32]{0:T(256)(128)(2,1)S(1)} %convert_bitcast_fusion.2), kind=kOutput, calls=%fused_computation.58 | convolution fusion | flops 8389632 | bytes 1048768 | tf_op jit(solution)/shard_map/aqk,qsw->askw/dot_general | solution.py:25
  37.5 0.8 squeeze.94
  38.3 0.8 squeeze.88
  39.0 2.0 %fusion.11 = bf16[16,64,128]{2,0,1:T(8,128)(2,1)} fusion(f32[16,64,128]{2,0,1:T(8,128)} %fusion.29, bf16[32,64,2,128]{3,0,1,2:T(8,128)(2,1)S(1)} %bitcast.253, s32[32]{0:T(128)S(1)} %bitcast.301, bf16[32]{0:T(256)(128)(2,1)S(1)} %get-tuple-element.5), kind=kOutput, calls=%fused_computation.23 | convolution fusion | flops 8651776 | bytes 1311744 | tf_op jit(solution)/shard_map/aqk,qsw->askw/dot_general | solution.py:25
  41.0 1.1 squeeze.95
  42.1 1.7 %squeeze.90 = bf16[64,2,1024]{2,1,0:T(2,128)(2,1)} reshape(bf16[1,64,16,128]{3,2,1,0:T(8,128)(2,1)} %bitcast.260) | data formatting | bytes 524288 | tf_op jit(solution)/shard_map/squeeze | solution.py:59
  43.9 1.2 fusion.44
  45.1 1.1 fusion.40
  46.7 1.1 fusion.78
  47.8 1.1 fusion.80
  49.1 1.1 fusion.34
  50.2 1.1 fusion.30
  51.3 1.1 fusion.27
  52.4 1.1 fusion.26
  53.6 8.2 %all_gather.7 = bf16[1,4,64,2,32]{2,4,3,0,1:T(8,128)(2,1)S(1)} all-gather(bf16[1,1,64,2,32]{2,4,3,0,1:T(8,128)(2,1)S(1)} %maximum_bitcast_fusion), channel_id=1, replica_groups=mesh['ang'=8,'row'=4] {'row'}, dimensions={1}, use_global_device_ids=true | all-gather | bytes 40960 | tf_op jit(solution)/shard_map/all_gather | solution.py:119
  61.8 1.5 %convolution_bitcast_fusion = f32[64,32]{0,1:T(8,128)} fusion(bf16[1,1,32,4,32]{4,3,2,1,0:T(4,128)(2,1)} %get-tuple-element.24, bf16[1,4,64,2,32]{2,4,1,3,0:T(8,128)(2,1)S(1)} %copy_multiply_fusion), kind=kOutput, calls=%fused_computation.36 | convolution fusion | flops 524288 | bytes 49152 | tf_op jit(solution)/shard_map/arjq,ajsq->asr/dot_general | solution.py:10
  63.3 1.5 %convolution_bitcast_fusion.2 = f32[64,32]{0,1:T(8,128)} fusion(bf16[1,1,32,4,32]{4,3,2,1,0:T(4,128)(2,1)} %get-tuple-element.24, bf16[1,4,64,2,32]{2,4,1,3,0:T(8,128)(2,1)S(1)} %copy_multiply_fusion), kind=kOutput, calls=%fused_computation.38 | convolution fusion | flops 524288 | bytes 49152 | tf_op jit(solution)/shard_map/arjq,ajsq->asr/dot_general | solution.py:10
  64.9 1.1 fusion.60
  66.0 1.1 fusion.54
  67.6 1.1 fusion.70
  68.7 1.1 fusion.68
  69.8 1.2 %fusion.62 = f32[8,64,256]{2,1,0:T(8,128)} fusion(bf16[8,256,256]{2,1,0:T(8,128)(2,1)S(1)} %bitcast.246, bf16[64,8,256]{2,1,0:T(8,128)(2,1)S(1)} %squeeze.86), kind=kOutput, calls=%fused_computation.91 | convolution fusion | flops 67108864 | bytes 1835008 | tf_op jit(solution)/shard_map/lwv,slv->slw/dot_general | solution.py:10
  71.0 1.2 %fusion.52 = f32[8,64,256]{2,1,0:T(8,128)} fusion(bf16[8,256,256]{2,1,0:T(8,128)(2,1)S(1)} %bitcast.247, bf16[64,8,256]{2,1,0:T(8,128)(2,1)S(1)} %squeeze.87), kind=kOutput, calls=%fused_computation.81 | convolution fusion | flops 67108864 | bytes 1835008 | tf_op jit(solution)/shard_map/lwv,slv->slw/dot_general | solution.py:10
  78.9 1.7 %subtract_bitcast_fusion = (f32[64,1,2048]{2,0,1:T(8,128)S(1)}, f32[64,1,2048]{2,0,1:T(8,128)S(1)}) fusion(f32[64,2048]{1,0:T(8,128)S(1)} %fusion, f32[]{:T(128)} %bitcast.66, f32[]{:T(128)} %bitcast, f32[64,2048]{1,0:T(8,128)S(1)} %fusion.64, bf16[64,32]{0,1:T(8,128)(2,1)S(1)} %fusion.23, bf16[1,2,32,2048]{3,2,1,0:T(8,128)(2,1)S(1)} %copy-done.3, ...), kind=kOutput, calls=%fused_computation.56 | convolution fusion | flops 9830400 | bytes 4333576 | tf_op jit(solution)/shard_map/rm,sr->sm/dot_general | solution.py:10
  80.6 1.1 pad_maximum_fusion
  81.7 31.1 %reduce-scatter.2.cloned.1.call-done = f32[8,2,2048]{2,0,1:T(8,128)} async-done(((f32[64,2,2048]{2,0,1:T(8,128)}), f32[8,2,2048]{2,0,1:T(8,128)}) %reduce-scatter.2.cloned.1.call-update) | async-done | bytes 131088 | tf_op jit(solution)/shard_map/reduce_scatter | solution.py:149
  112.8 1.7 %copy.140 = f32[8,2,2048]{2,1,0:T(2,128)} copy(f32[8,2,2048]{2,0,1:T(8,128)} %reduce-scatter.2.cloned.1.call-done) | data formatting | bytes 262144 | tf_op jit(solution)/shard_map/reduce_scatter | solution.py:149
  (136 shorter events, 8.8 us)
Async XLA Ops:
  6.5 5.2 %copy-start = (f32[8,2]{0,1:T(2,128)S(1)}, f32[8,2]{0,1:T(2,128)}, u32[]{:S(2)}) copy-start(f32[8,2]{0,1:T(2,128)} %param.15) | copy-start | bytes 196
  6.5 3.7 %copy-start.18 = (bf16[1,3,2,32,2048]{4,3,2,1,0:T(8,128)(2,1)S(1)}, bf16[1,3,2,32,2048]{4,3,2,1,0:T(8,128)(2,1)}, u32[]{:S(2)}) copy-start(bf16[1,3,2,32,2048]{4,3,2,1,0:T(8,128)(2,1)} %param.17) | copy-start | bytes 2359300
  6.5 4.5 %copy-start.40 = (f32[1,2]{1,0:T(1,128)S(1)}, f32[1,2]{1,0:T(1,128)}, u32[]{:S(2)}) copy-start(f32[1,2]{1,0:T(1,128)} %param.23) | copy-start | bytes 28
  6.5 27.3 %all-gather.2.cloned.1.call-start = ((), (), s32[]{:S(2)}) async-start(), calls=%async_computation.1 | async-start | bytes 1179648 | tf_op jit(solution)/shard_map/all_gather | solution.py:104
  8.2 104.6 %reduce-scatter.2.cloned.1.call-start = ((), (), s32[]{:S(2)}) async-start(), calls=%async_computation.2 | async-start | bytes 1179648 | tf_op jit(solution)/shard_map/reduce_scatter | solution.py:149
  10.2 9.4 %copy-start.38 = (bf16[1,1,2,32,128]{4,3,2,1,0:T(8,128)(2,1)S(1)}, bf16[1,1,2,32,128]{4,3,2,1,0:T(8,128)(2,1)}, u32[]{:S(2)}) copy-start(bf16[1,1,2,32,128]{4,3,2,1,0:T(8,128)(2,1)} %param.21) | copy-start | bytes 49156
  10.3 12.0 %copy-start.29 = (bf16[1,2,32,2048]{3,2,1,0:T(8,128)(2,1)S(1)}, bf16[1,2,32,2048]{3,2,1,0:T(8,128)(2,1)}, u32[]{:S(2)}) copy-start(bf16[1,2,32,2048]{3,2,1,0:T(8,128)(2,1)} %param.19) | copy-start | bytes 786436
  10.3 12.0 %copy-start.30 = (bf16[1,2,32,2048]{3,2,1,0:T(8,128)(2,1)S(1)}, bf16[1,2,32,2048]{3,2,1,0:T(8,128)(2,1)}, u32[]{:S(2)}) copy-start(bf16[1,2,32,2048]{3,2,1,0:T(8,128)(2,1)} %param.20) | copy-start | bytes 786436
  23.2 10.6 %copy-start.39 = (s32[1,32]{1,0:T(1,128)S(1)}, s32[1,32]{1,0:T(1,128)}, u32[]{:S(2)}) copy-start(s32[1,32]{1,0:T(1,128)} %param.13) | copy-start | bytes 388
  33.8 3.4 %copy-start.1 = (bf16[1,32,64,2,128]{4,1,2,3,0:T(8,128)(2,1)S(1)}, bf16[1,32,64,2,128]{4,1,2,3,0:T(8,128)(2,1)}, u32[]{:S(2)}) copy-start(bf16[1,32,64,2,128]{4,1,2,3,0:T(8,128)(2,1)} %all-gather.2.cloned.1.call-done) | copy-start | bytes 3145732
  41.0 5.2 %copy-start.35 = (bf16[32,4,512]{2,1,0:T(4,128)(2,1)S(1)}, bf16[32,4,512]{2,1,0:T(4,128)(2,1)}, u32[]{:S(2)}) copy-start(bf16[32,4,512]{2,1,0:T(4,128)(2,1)} %reshape_squeeze.56) | copy-start | bytes 393220
  41.0 5.4 %copy-start.28 = (bf16[64,4,512]{2,1,0:T(4,128)(2,1)S(1)}, bf16[64,4,512]{2,1,0:T(4,128)(2,1)}, u32[]{:S(2)}) copy-start(bf16[64,4,512]{2,1,0:T(4,128)(2,1)} %squeeze.94) | copy-start | bytes 786436
  41.0 5.7 %copy-start.15 = (bf16[32,4,512]{2,1,0:T(4,128)(2,1)S(1)}, bf16[32,4,512]{2,1,0:T(4,128)(2,1)}, u32[]{:S(2)}) copy-start(bf16[32,4,512]{2,1,0:T(4,128)(2,1)} %reshape_squeeze.57) | copy-start | bytes 393220
  43.9 5.1 %copy-start.2 = (bf16[16,64,128]{2,0,1:T(8,128)(2,1)S(1)}, bf16[16,64,128]{2,0,1:T(8,128)(2,1)}, u32[]{:S(2)}) copy-start(bf16[16,64,128]{2,0,1:T(8,128)(2,1)} %fusion.11) | copy-start | bytes 786436
  46.7 2.2 %copy-start.21 = (bf16[64,2,2,2,32]{0,4,3,2,1:T(8,128)(2,1)}, bf16[64,2,2,2,32]{0,4,3,2,1:T(8,128)(2,1)S(1)}, u32[]{:S(2)}) copy-start(bf16[64,2,2,2,32]{0,4,3,2,1:T(8,128)(2,1)S(1)} %rev.7) | copy-start | bytes 98308
  48.9 18.2 %copy-start.14 = (bf16[4,8,8,256]{3,2,1,0:T(8,128)(2,1)S(1)}, bf16[4,8,8,256]{3,2,1,0:T(8,128)(2,1)}, u32[]{:S(2)}) copy-start(bf16[4,8,8,256]{3,2,1,0:T(8,128)(2,1)} %copy.152) | copy-start | bytes 393220
  51.3 16.4 %copy-start.13 = (bf16[4,8,8,256]{3,2,1,0:T(8,128)(2,1)S(1)}, bf16[4,8,8,256]{3,2,1,0:T(8,128)(2,1)}, u32[]{:S(2)}) copy-start(bf16[4,8,8,256]{3,2,1,0:T(8,128)(2,1)} %copy.153) | copy-start | bytes 393220
  61.8 8.0 %copy-start.19 = (bf16[1,4,64,2,32]{2,4,1,3,0:T(8,128)(2,1)}, bf16[1,4,64,2,32]{2,4,1,3,0:T(8,128)(2,1)S(1)}, u32[]{:S(2)}) copy-start(bf16[1,4,64,2,32]{2,4,1,3,0:T(8,128)(2,1)S(1)} %copy_multiply_fusion) | copy-start | bytes 98308
  67.6 4.7 %copy-start.16 = (bf16[64,2,4,2,32]{0,4,3,2,1:T(8,128)(2,1)}, bf16[64,2,4,2,32]{0,4,3,2,1:T(8,128)(2,1)S(1)}, u32[]{:S(2)}) copy-start(bf16[64,2,4,2,32]{0,4,3,2,1:T(8,128)(2,1)S(1)} %rev.8) | copy-start | bytes 196612
  68.7 3.6 %copy-start.5 = (f32[4,64,512]{2,1,0:T(8,128)S(1)}, f32[4,64,512]{2,1,0:T(8,128)}, u32[]{:S(2)}) copy-start(f32[4,64,512]{2,1,0:T(8,128)} %fusion.78) | copy-start | bytes 1572868
  68.7 3.6 %copy-start.11 = (bf16[32,4,512]{2,1,0:T(4,128)(2,1)S(1)}, bf16[32,4,512]{2,1,0:T(4,128)(2,1)}, u32[]{:S(2)}) copy-start(bf16[32,4,512]{2,1,0:T(4,128)(2,1)} %reshape_squeeze.58) | copy-start | bytes 393220
  68.7 3.6 %copy-start.22 = (bf16[64,2,2,2,32]{0,4,3,2,1:T(8,128)(2,1)S(1)}, bf16[64,2,2,2,32]{0,4,3,2,1:T(8,128)(2,1)}, u32[]{:S(2)}) copy-start(bf16[64,2,2,2,32]{0,4,3,2,1:T(8,128)(2,1)} %copy-done.21) | copy-start | bytes 98308
  71.0 1.6 %copy-start.25 = (bf16[64,2,1024]{2,1,0:T(2,128)(2,1)S(1)}, bf16[64,2,1024]{2,1,0:T(2,128)(2,1)}, u32[]{:S(2)}) copy-start(bf16[64,2,1024]{2,1,0:T(2,128)(2,1)} %squeeze.88) | copy-start | bytes 786436
  71.0 1.6 %copy-start.34 = (bf16[32,2,1024]{2,1,0:T(2,128)(2,1)S(1)}, bf16[32,2,1024]{2,1,0:T(2,128)(2,1)}, u32[]{:S(2)}) copy-start(bf16[32,2,1024]{2,1,0:T(2,128)(2,1)} %reshape_squeeze.51) | copy-start | bytes 393220
  71.0 1.8 %copy-start.27 = (bf16[64,2,1024]{2,1,0:T(2,128)(2,1)S(1)}, bf16[64,2,1024]{2,1,0:T(2,128)(2,1)}, u32[]{:S(2)}) copy-start(bf16[64,2,1024]{2,1,0:T(2,128)(2,1)} %squeeze.90) | copy-start | bytes 786436
  72.3 0.9 copy-start.33
  72.3 1.1 copy-start.26
  72.3 1.4 %copy-start.12 = (bf16[32,2,1024]{2,1,0:T(2,128)(2,1)S(1)}, bf16[32,2,1024]{2,1,0:T(2,128)(2,1)}, u32[]{:S(2)}) copy-start(bf16[32,2,1024]{2,1,0:T(2,128)(2,1)} %reshape_squeeze.53) | copy-start | bytes 393220
  73.4 1.2 copy-start.4
  73.4 1.2 copy-start.23
  73.4 1.5 %copy-start.31 = (bf16[64,2,32]{0,2,1:T(8,128)(2,1)}, bf16[64,2,32]{0,2,1:T(8,128)(2,1)S(1)}, u32[]{:S(2)}) copy-start(bf16[64,2,32]{0,2,1:T(8,128)(2,1)S(1)} %squeeze.91) | copy-start | bytes 24580
  74.2 1.1 copy-start.9
  74.2 1.1 copy-start.10
  74.2 1.1 copy-start.17
  74.6 1.1 copy-start.20
  74.6 1.1 copy-start.24
  74.6 1.1 copy-start.37
  74.6 1.3 %copy-start.36 = (f32[64,32]{0,1:T(8,128)S(1)}, f32[64,32]{0,1:T(8,128)}, u32[]{:S(2)}) copy-start(f32[64,32]{0,1:T(8,128)} %convolution_bitcast_fusion.2) | copy-start | bytes 24580
  74.6 1.5 %copy-start.8 = (f32[8,64,256]{2,1,0:T(8,128)S(1)}, f32[8,64,256]{2,1,0:T(8,128)}, u32[]{:S(2)}) copy-start(f32[8,64,256]{2,1,0:T(8,128)} %fusion.62) | copy-start | bytes 1572868
  75.6 1.1 copy-start.7
  76.6 0.8 copy-start.32
  76.7 1.0 copy-start.3
  77.0 1.2 copy-start.6
Sparse Core Ops, SparseCore 0:
  9.0 24.8 all-gather.1
  81.8 30.9 reduce-scatter.1
where the time goes:
time: 122 us; the launch traced here: 121 us
  waiting for transfers between devices  40.1 us (33%)
  matrix products  31.9 us (26%)
  local copies, waits for them, and re-layouts  22.2 us (18%)
  between operations  14.7 us (12%)
  blocking collectives  8.16 us (7%)
  other arithmetic  4.16 us (3%)
    reduce_scatter x1, waiting for transfers between devices, shards(): return lax.psum_scatter(summed, 'ang', scatter_dimension=0, tiled=True)  31.1 us
    dot_general x40, matrix products, single(): return jnp.einsum(form, first, second, preferred_element_type=jnp.float32)  26.3 us
    all_gather x1, waiting for transfers between devices, shards(): lax.all_gather(panels, 'ang', axis=2, tiled=True)[0]  8.91 us
    all_gather x1, blocking collectives, shards(): gathered = lax.all_gather(projected[:, None], 'row', axis=1, tiled=True)  8.16 us
    dot_general x4, matrix products, single(): jnp.einsum('aqk,qsw->askw', coefficient, entry_values, preferred_element_...  5.57 us
    unnamed x87, local copies, waits for them, and re-layouts  5.45 us
    squeeze x2, local copies, waits for them, and re-layouts, near_field(): node_view[:, 1]  2.85 us
  transfers between devices with their start and end apart: 2, of which 2 were waited for; matrix products, arithmetic and copies ran while one was open for 13% of the time, Pallas kernels for 0%

commit v1 on v0

v1 whole, which is shorter than its diff:
```python
import jax
import jax.numpy as jnp
from jax import lax
from jax.experimental import pallas as pl
from jax.experimental.pallas import tpu as pltpu
from jax.sharding import PartitionSpec as P

LEAF = 256

_SMEM = pl.BlockSpec(memory_space=pltpu.MemorySpace.SMEM)
_VMEM = pl.BlockSpec(memory_space=pltpu.MemorySpace.VMEM)


def _nt(a, b):
    return lax.dot_general(a, b, (((1,), (1,)), ((), ())), preferred_element_type=jnp.float32)


def _nn(a, b):
    return lax.dot_general(a, b, (((1,), (0,)), ((), ())), preferred_element_type=jnp.float32)


def _rank_mask(rank_ref, shape):
    return lax.broadcasted_iota(jnp.int32, shape, 0) < rank_ref[0]


def _excite_kernel(slot_ref, cos_ref, sin_ref, rank_ref, g_ref, br_ref, e_ref, bp_ref, acc_re, acc_im):
    panel_count, _, width2 = g_ref.shape
    width = width2 // 2
    slots = acc_re.shape[0]
    acc_re[...] = jnp.zeros(acc_re.shape, jnp.float32)
    acc_im[...] = jnp.zeros(acc_im.shape, jnp.float32)

    def body(q, carry):
        k = slot_ref[q]
        c = cos_ref[q]
        s = sin_ref[q]
        p_re = g_ref[q, :, :width].astype(jnp.float32)
        p_im = g_ref[q, :, width:].astype(jnp.float32)
        acc_re[k] = acc_re[k] + (c * p_re + s * p_im)
        acc_im[k] = acc_im[k] + (c * p_im - s * p_re)
        return carry

    lax.fori_loop(0, panel_count, body, 0)
    for k in range(slots):
        e_ref[0, :, k * width:(k + 1) * width] = acc_re[k].astype(jnp.bfloat16)
        e_ref[1, :, k * width:(k + 1) * width] = acc_im[k].astype(jnp.bfloat16)
    e_re = e_ref[0]
    e_im = e_ref[1]
    keep = _rank_mask(rank_ref, br_ref.shape[1:])
    zero = jnp.zeros(br_ref.shape[1:], jnp.bfloat16)
    r_re = jnp.where(keep, br_ref[0], zero)
    r_im = jnp.where(keep, br_ref[1], zero)
    bp_ref[0] = (_nt(e_re, r_re) - _nt(e_im, r_im)).astype(jnp.bfloat16)
    bp_ref[1] = (_nt(e_re, r_im) + _nt(e_im, r_re)).astype(jnp.bfloat16)


def _field_kernel(qw_ref, rank_ref, me_ref, e_ref, leaf_ref, lr_ref, ll_ref, bl_ref, cp_ref, bpa_ref, out_ref):
    _, source_count, row_count = e_ref.shape
    levels = lr_ref.shape[0]
    rank_width = lr_ref.shape[2]
    blocks = bpa_ref.shape[0]
    coupling_rank = bpa_ref.shape[3]
    e_re = e_ref[0]
    e_im = e_ref[1]

    projections = []
    for j in range(levels):
        node = row_count // 2 ** (j + 1)
        level_proj = []
        for g in range(2 ** (j + 1)):
            cols = slice(g * node, (g + 1) * node)
            a = e_re[:, cols]
            b = e_im[:, cols]
            r_re = lr_ref[j, 0, :, cols]
            r_im = lr_ref[j, 1, :, cols]
            p_re = (_nt(a, r_re) - _nt(b, r_im)).astype(jnp.bfloat16)
            p_im = (_nt(a, r_im) + _nt(b, r_re)).astype(jnp.bfloat16)
            level_proj.append((p_re, p_im))
        projections.append(level_proj)

    me = me_ref[0]
    c_re = jnp.zeros((source_count, rank_width), jnp.float32)
    c_im = jnp.zeros((source_count, rank_width), jnp.float32)
    for u in range(blocks):
        own = me == u
        zero = jnp.zeros((source_count, coupling_rank), jnp.bfloat16)
        b_re = jnp.where(own, zero, bpa_ref[u, 0])
        b_im = jnp.where(own, zero, bpa_ref[u, 1])
        k_re = cp_ref[0, :, u * coupling_rank:(u + 1) * coupling_rank]
        k_im = cp_ref[1, :, u * coupling_rank:(u + 1) * coupling_rank]
        c_re = c_re + (_nt(b_re, k_re) - _nt(b_im, k_im))
        c_im = c_im + (_nt(b_re, k_im) + _nt(b_im, k_re))
    coupled_re = c_re.astype(jnp.bfloat16)
    coupled_im = c_im.astype(jnp.bfloat16)

    w_re = qw_ref[0]
    w_im = qw_ref[1]
    for l in range(row_count // LEAF):
        cols = slice(l * LEAF, (l + 1) * LEAF)
        a = e_re[:, cols]
        b = e_im[:, cols]
        lf_re = leaf_ref[0, cols, :]
        lf_im = leaf_ref[1, cols, :]
        f_re = _nt(a, lf_re) - _nt(b, lf_im)
        f_im = _nt(a, lf_im) + _nt(b, lf_re)
        for j in range(levels):
            node = row_count // 2 ** (j + 1)
            g = (l * LEAF) // node
            p_re, p_im = projections[j][g ^ 1]
            m_re = ll_ref[j, 0, :, cols]
            m_im = ll_ref[j, 1, :, cols]
            f_re = f_re + (_nn(p_re, m_re) - _nn(p_im, m_im))
            f_im = f_im + (_nn(p_re, m_im) + _nn(p_im, m_re))
        keep = _rank_mask(rank_ref, (bl_ref.shape[1], LEAF))
        zero = jnp.zeros((bl_ref.shape[1], LEAF), jnp.bfloat16)
        q_re = jnp.where(keep, bl_ref[0, :, cols], zero)
        q_im = jnp.where(keep, bl_ref[1, :, cols], zero)
        f_re = f_re + (_nn(coupled_re, q_re) - _nn(coupled_im, q_im))
        f_im = f_im + (_nn(coupled_re, q_im) + _nn(coupled_im, q_re))
        out_ref[0, :, cols] = w_re * f_re - w_im * f_im
        out_ref[1, :, cols] = w_re * f_im + w_im * f_re


def shards(
    panels,
    panel_slot,
    panel_cell,
    bloch_k,
    leaf_inverse,
    level_left,
    level_right,
    block_left,
    block_right,
    block_coupling,
    rank_count,
    quad_weight,
):
    local_angles = leaf_inverse.shape[0]
    assert local_angles == 1
    row_count = leaf_inverse.shape[2]
    panel_count = panels.shape[1]
    local_sources = panels.shape[2]
    panel_width = panels.shape[4]
    slot_count = row_count // panel_width
    source_count = local_sources * lax.axis_size("ang")
    rank_width = block_right.shape[2]

    cell_float = panel_cell[0].astype(jnp.float32)
    own_wave = lax.dynamic_slice_in_dim(bloch_k, lax.axis_index("ang") * local_angles, local_angles, 0)
    theta = own_wave[0, 0] * cell_float[:, 0] + own_wave[0, 1] * cell_float[:, 1]
    own_cos = jnp.cos(theta).astype(jnp.bfloat16).astype(jnp.float32)
    own_sin = jnp.sin(theta).astype(jnp.bfloat16).astype(jnp.float32)

    local_panels = panels[0].reshape(panel_count, local_sources, 2 * panel_width)
    gathered = lax.all_gather(local_panels, "ang", axis=1, tiled=True)
    rank = rank_count[0].reshape(1)

    excitation, projected = pl.pallas_call(
        _excite_kernel,
        out_shape=(
            jax.ShapeDtypeStruct((2, source_count, row_count), jnp.bfloat16),
            jax.ShapeDtypeStruct((2, source_count, rank_width), jnp.bfloat16),
        ),
        in_specs=[_SMEM, _SMEM, _SMEM, _SMEM, _VMEM, _VMEM],
        out_specs=(_VMEM, _VMEM),
        scratch_shapes=[
            pltpu.VMEM((slot_count, source_count, panel_width), jnp.float32),
            pltpu.VMEM((slot_count, source_count, panel_width), jnp.float32),
        ],
    )(panel_slot[0], own_cos, own_sin, rank, gathered, block_right[0])

    all_projected = lax.all_gather(projected, "row", axis=0, tiled=False)
    me = lax.axis_index("row").astype(jnp.int32).reshape(1)

    field = pl.pallas_call(
        _field_kernel,
        out_shape=jax.ShapeDtypeStruct((2, source_count, row_count), jnp.float32),
        in_specs=[_SMEM, _SMEM, _SMEM] + [_VMEM] * 7,
        out_specs=_VMEM,
    )(
        quad_weight[0],
        rank,
        me,
        excitation,
        leaf_inverse[0],
        level_right[0],
        level_left[0],
        block_left[0],
        block_coupling[0, 0],
        all_projected,
    )
    summed = lax.psum_scatter(field, "ang", scatter_dimension=1, tiled=True)
    return jnp.transpose(summed, (1, 0, 2))


def solution(mesh):
    placed = (
        P("row", None, "ang", None, None),
        P("row", None),
        P("row", None, None),
        P(),
        P("ang", None, "row", None),
        P("ang", None, None, None, "row"),
        P("ang", None, None, None, "row"),
        P("ang", None, None, "row"),
        P("ang", None, None, "row"),
        P("ang", "row", None, None, None),
        P("ang", "row"),
        P("ang", None),
    )
    return jax.shard_map(
        shards, mesh=mesh, in_specs=placed, out_specs=P("ang", None, "row"), check_vma=False
    )
```

time: 122 us -> 94.7 us (0.78)
  matrix products: 31.9 us -> 0 us
  local copies, waits for them, and re-layouts: 22.2 us -> 5.58 us
  waiting for transfers between devices: 40.1 us -> 54.7 us
  Pallas kernels: 0 us -> 9.62 us
    dot_general x44 -> x0, matrix products: 31.9 us -> none  [the longest x40 26.3 us: single(): return jnp.einsum(form, first, second, preferred_element_type=jnp.float32)]
    all_gather x1, waiting for transfers between devices: 8.91 us -> 23 us  [shards(): gathered = lax.all_gather(local_panels, 'ang', axis=1, tiled=True)]
    pallas_call x0 -> x2, Pallas kernels: none -> 9.62 us  [the longest x1 6.7 us: shards(): pl.pallas_call(_field_kernel, out_shape=jax.ShapeDtypeStruct((2, source_c...]
    unnamed x87 -> x2, local copies, waits for them, and re-layouts: 5.45 us -> 0.01 us
    squeeze x8 -> x0, local copies, waits for them, and re-layouts: 4.6 us -> none  [the longest x2 2.85 us: near_field(): node_view[:, 1]]
    slice x6 -> x1, local copies, waits for them, and re-layouts: 4.87 us -> 0.58 us  [shards(): own_wave[0, 0] * cell_float[:, 0] + own_wave[0, 1] * cell_float[:, 1]]
    another operation x9 -> x1, local copies, waits for them, and re-layouts: 5.26 us -> 1.66 us  [shards(): panels[0].reshape(panel_count, local_sources, 2 * panel_width)]
    reduce_scatter x1 -> x0, local copies, waits for them, and re-layouts: 1.66 us -> none  [shards(): return lax.psum_scatter(summed, 'ang', scatter_dimension=0, tiled=True)]
  transfers between devices with their start and end apart: 2 -> 2, of which waited for: 2 -> 2; matrix products, arithmetic and copies ran while one was open for 13% -> 4% of each run, Pallas kernels for 0% -> 0%
where the time goes in v1:
time: 94.7 us; the launch traced here: 94.4 us
  waiting for transfers between devices  54.7 us (58%)
  between operations  14.1 us (15%)
  Pallas kernels  9.62 us (10%)
  blocking collectives  7.33 us (8%)
  local copies, waits for them, and re-layouts  5.58 us (6%)
  other arithmetic  3.06 us (3%)
    reduce_scatter x1, waiting for transfers between devices, shards(): summed = lax.psum_scatter(field, 'ang', scatter_dimension=1, tiled=True)  31.7 us
    all_gather x1, waiting for transfers between devices, shards(): gathered = lax.all_gather(local_panels, 'ang', axis=1, tiled=True)  23 us
    all_gather x1, blocking collectives, shards(): all_projected = lax.all_gather(projected, 'row', axis=0, tiled=False)  7.33 us
    pallas_call x1, Pallas kernels, shards(): pl.pallas_call(_field_kernel, out_shape=jax.ShapeDtypeStruct((2, source_c...  6.7 us
    pallas_call x1, Pallas kernels, shards(): pl.pallas_call(_excite_kernel, out_shape=(jax.ShapeDtypeStruct((2, source...  2.92 us
  transfers between devices with their start and end apart: 2, of which 2 were waited for; matrix products, arithmetic and copies ran while one was open for 4% of the time, Pallas kernels for 0%

profile of v1, /device:TPU:0, one launch (start us, length us, event | category | flops | bytes accessed | tf_op | source)
XLA Modules:
  0.0 94.4 jit_solution(8418014895963058556)
XLA Ops:
  6.5 0.0 copy-start
  6.5 0.0 all-gather.3.cloned.1.call-start
  6.5 1.7 %reshape_squeeze.3 = bf16[32,8,256]{2,1,0:T(8,128)(2,1)} reshape(bf16[1,32,8,2,128]{4,3,2,1,0:T(2,128)(2,1)} %param.12) | data formatting | bytes 262144 | tf_op jit(solution)/shard_map/reshape;squeeze | solution.py:154
  8.2 0.0 all-gather.3.cloned.1.call-update
  8.2 0.0 reduce-scatter.2.cloned.1.call-start
  8.9 0.0 copy-done
  8.9 0.1 constant_dynamic-slice_fusion
  9.0 0.6 fusion
  9.6 0.7 convert_bitcast_fusion
  10.3 1.9 %bitcast_convert_fusion = (f32[32]{0:T(128)}, f32[32,1]{0,1:T(1,128)S(1)}) fusion(f32[32,2]{0,1:T(2,128)S(1)} %convert_bitcast_fusion, f32[]{:T(128)} %bitcast.6, f32[]{:T(128)} %bitcast.4), kind=kLoop, calls=%fused_computation.1 | loop fusion | flops 160 | bytes 520 | tf_op jit(solution)/shard_map/convert_element_type | solution.py:152
  12.1 0.5 bitcast_convert_fusion.1.cos_ref
  12.7 23.0 %all-gather.3.cloned.1.call-done.g_ref = bf16[32,64,256]{2,1,0:T(8,128)(2,1)} async-done(((bf16[32,8,256]{2,1,0:T(8,128)(2,1)}), bf16[32,64,256]{2,1,0:T(8,128)(2,1)}) %all-gather.3.cloned.1.call-update) | async-done | bytes 1048592 | tf_op jit(solution)/shard_map/all_gather | solution.py:155
  35.7 2.9 %shard_map.118 = (bf16[2,64,2048]{2,1,0:T(8,128)(2,1)}, bf16[2,64,32]{2,1,0:T(8,128)(2,1)}) custom-call(s32[32]{0:T(128)} %bitcast.32, f32[32]{0:T(128)} %bitcast_convert_fusion.1.cos_ref, f32[32]{0:T(128)} %get-tuple-element.9.sin_ref, s32[1]{0:T(128)} %bitcast.22.rank_ref, bf16[32,64,256]{2,1,0:T(8,128)(2,1)} %all-gather.3.cloned.1.call-done.g_ref, ...), custom_call_target="tpu_custom_call" | custom-call | tf_op jit(solution)/shard_map/pallas_call | solution.py:158
  38.6 0.8 copy.14
  39.4 7.3 %all-gather = bf16[8,64,32]{1,2,0:T(8,128)(2,1)S(1)} all-gather(bf16[2,64,32]{1,2,0:T(8,128)(2,1)S(1)} %copy.14), channel_id=2, replica_groups=mesh['ang'=8,'row'=4] {'row'}, dimensions={0}, use_global_device_ids=true | all-gather | bytes 40960 | tf_op jit(solution)/shard_map/all_gather | solution.py:172
  46.7 0.8 copy.15
  47.5 6.7 %shard_map.119 = f32[2,64,2048]{2,1,0:T(8,128)} custom-call(f32[2]{0:T(128)} %bitcast.33, s32[1]{0:T(128)} %bitcast.23.rank_ref, s32[1]{0:T(128)} %bitcast.2.me_ref, bf16[2,64,2048]{2,1,0:T(8,128)(2,1)} %get-tuple-element.7.e_ref, bf16[2,2048,256]{2,1,0:T(8,128)(2,1)} %bitcast.24, bf16[3,2,32,2048]{3,2,1,0:T(8,128)(2,1)} %bitcast.25, ...), custom_call_target="tpu_custom_call" | custom-call | tf_op jit(solution)/shard_map/pallas_call | solution.py:175
  54.2 0.0 reduce-scatter.2.cloned.1.call-update
  54.2 31.7 %reduce-scatter.2.cloned.1.call-done = f32[2,8,2048]{2,1,0:T(8,128)} async-done(((f32[2,64,2048]{2,1,0:T(8,128)}), f32[2,8,2048]{2,1,0:T(8,128)}) %reduce-scatter.2.cloned.1.call-update) | async-done | bytes 131088 | tf_op jit(solution)/shard_map/reduce_scatter | solution.py:192
  85.9 1.7 %copy.16 = f32[8,2,2048]{2,1,0:T(2,128)} copy(f32[8,2,2048]{2,0,1:T(8,128)} %bitcast.30) | data formatting | bytes 262144 | tf_op jit(solution)/shard_map/transpose | solution.py:193
Async XLA Ops:
  6.5 2.4 %copy-start = (f32[8,2]{0,1:T(2,128)S(1)}, f32[8,2]{0,1:T(2,128)}, u32[]{:S(2)}) copy-start(f32[8,2]{0,1:T(2,128)} %param.15) | copy-start | bytes 196
  6.5 29.1 %all-gather.3.cloned.1.call-start = ((), (), s32[]{:S(2)}) async-start(), calls=%async_computation.1 | async-start | bytes 1179648 | tf_op jit(solution)/shard_map/all_gather | solution.py:155
  8.2 77.7 %reduce-scatter.2.cloned.1.call-start = ((), (), s32[]{:S(2)}) async-start(), calls=%async_computation.2 | async-start | bytes 1179648 | tf_op jit(solution)/shard_map/reduce_scatter | solution.py:192
Sparse Core Ops, SparseCore 0:
  8.9 26.6 all-gather.2
  54.4 31.4 reduce-scatter.1

commit v2 on v1

--- a/solution.py
+++ b/solution.py
@@ -54,7 +54,7 @@
     bp_ref[1] = (_nt(e_re, r_im) + _nt(e_im, r_re)).astype(jnp.bfloat16)
 
 
-def _field_kernel(qw_ref, rank_ref, me_ref, e_ref, leaf_ref, lr_ref, ll_ref, bl_ref, cp_ref, bpa_ref, out_ref):
+def _field_kernel(qw_ref, rank_ref, me_ref, e_ref, leaf_ref, lr_ref, ll_ref, bl_ref, cp_ref, bpa_ref, out_ref, pj_ref, cu_ref):
     _, source_count, row_count = e_ref.shape
     levels = lr_ref.shape[0]
     rank_width = lr_ref.shape[2]
@@ -63,20 +63,20 @@
     e_re = e_ref[0]
     e_im = e_ref[1]
 
-    projections = []
+    first_group = []
+    slot = 0
     for j in range(levels):
         node = row_count // 2 ** (j + 1)
-        level_proj = []
+        first_group.append(slot)
         for g in range(2 ** (j + 1)):
             cols = slice(g * node, (g + 1) * node)
             a = e_re[:, cols]
             b = e_im[:, cols]
             r_re = lr_ref[j, 0, :, cols]
             r_im = lr_ref[j, 1, :, cols]
-            p_re = (_nt(a, r_re) - _nt(b, r_im)).astype(jnp.bfloat16)
-            p_im = (_nt(a, r_im) + _nt(b, r_re)).astype(jnp.bfloat16)
-            level_proj.append((p_re, p_im))
-        projections.append(level_proj)
+            pj_ref[slot, 0] = (_nt(a, r_re) - _nt(b, r_im)).astype(jnp.bfloat16)
+            pj_ref[slot, 1] = (_nt(a, r_im) + _nt(b, r_re)).astype(jnp.bfloat16)
+            slot += 1
 
     me = me_ref[0]
     c_re = jnp.zeros((source_count, rank_width), jnp.float32)
@@ -90,8 +90,10 @@
         k_im = cp_ref[1, :, u * coupling_rank:(u + 1) * coupling_rank]
         c_re = c_re + (_nt(b_re, k_re) - _nt(b_im, k_im))
         c_im = c_im + (_nt(b_re, k_im) + _nt(b_im, k_re))
-    coupled_re = c_re.astype(jnp.bfloat16)
-    coupled_im = c_im.astype(jnp.bfloat16)
+    cu_ref[0] = c_re.astype(jnp.bfloat16)
+    cu_ref[1] = c_im.astype(jnp.bfloat16)
+    coupled_re = cu_ref[0]
+    coupled_im = cu_ref[1]
 
     w_re = qw_ref[0]
     w_im = qw_ref[1]
@@ -106,7 +108,8 @@
         for j in range(levels):
             node = row_count // 2 ** (j + 1)
             g = (l * LEAF) // node
-            p_re, p_im = projections[j][g ^ 1]
+            p_re = pj_ref[first_group[j] + (g ^ 1), 0]
+            p_im = pj_ref[first_group[j] + (g ^ 1), 1]
             m_re = ll_ref[j, 0, :, cols]
             m_im = ll_ref[j, 1, :, cols]
             f_re = f_re + (_nn(p_re, m_re) - _nn(p_im, m_im))
@@ -144,6 +147,7 @@
     slot_count = row_count // panel_width
     source_count = local_sources * lax.axis_size("ang")
     rank_width = block_right.shape[2]
+    levels = level_right.shape[1]
 
     cell_float = panel_cell[0].astype(jnp.float32)
     own_wave = lax.dynamic_slice_in_dim(bloch_k, lax.axis_index("ang") * local_angles, local_angles, 0)
@@ -177,6 +181,10 @@
         out_shape=jax.ShapeDtypeStruct((2, source_count, row_count), jnp.float32),
         in_specs=[_SMEM, _SMEM, _SMEM] + [_VMEM] * 7,
         out_specs=_VMEM,
+        scratch_shapes=[
+            pltpu.VMEM((2 ** (levels + 1) - 2, 2, source_count, rank_width), jnp.bfloat16),
+            pltpu.VMEM((2, source_count, rank_width), jnp.bfloat16),
+        ],
     )(
         quad_weight[0],
         rank,

time: 94.7 us -> 94.7 us (level)
  no operation moved by 1% of the time
where the time goes in v2:
time: 94.7 us; the launch traced here: 94.4 us
  waiting for transfers between devices  54.7 us (58%)
  between operations  14.1 us (15%)
  Pallas kernels  9.62 us (10%)
  blocking collectives  7.33 us (8%)
  local copies, waits for them, and re-layouts  5.58 us (6%)
  other arithmetic  3.06 us (3%)
    reduce_scatter x1, waiting for transfers between devices, shards(): summed = lax.psum_scatter(field, 'ang', scatter_dimension=1, tiled=True)  31.7 us
    all_gather x1, waiting for transfers between devices, shards(): gathered = lax.all_gather(local_panels, 'ang', axis=1, tiled=True)  23 us
    all_gather x1, blocking collectives, shards(): all_projected = lax.all_gather(projected, 'row', axis=0, tiled=False)  7.33 us
    pallas_call x1, Pallas kernels, shards(): pl.pallas_call(_field_kernel, out_shape=jax.ShapeDtypeStruct((2, source_c...  6.7 us
    pallas_call x1, Pallas kernels, shards(): pl.pallas_call(_excite_kernel, out_shape=(jax.ShapeDtypeStruct((2, source...  2.92 us
  transfers between devices with their start and end apart: 2, of which 2 were waited for; matrix products, arithmetic and copies ran while one was open for 4% of the time, Pallas kernels for 0%

profile of v2, /device:TPU:0, one launch (start us, length us, event | category | flops | bytes accessed | tf_op | source)
XLA Modules:
  0.0 94.4 jit_solution(3623355649568981244)
XLA Ops:
  6.5 0.0 copy-start
  6.5 0.0 all-gather.3.cloned.1.call-start
  6.5 1.7 %reshape_squeeze.3 = bf16[32,8,256]{2,1,0:T(8,128)(2,1)} reshape(bf16[1,32,8,2,128]{4,3,2,1,0:T(2,128)(2,1)} %param.12) | data formatting | bytes 262144 | tf_op jit(solution)/shard_map/reshape;squeeze | solution.py:158
  8.2 0.0 all-gather.3.cloned.1.call-update
  8.2 0.0 reduce-scatter.2.cloned.1.call-start
  8.9 0.0 copy-done
  8.9 0.1 constant_dynamic-slice_fusion
  9.0 0.6 fusion
  9.6 0.7 convert_bitcast_fusion
  10.3 1.9 %bitcast_convert_fusion = (f32[32]{0:T(128)}, f32[32,1]{0,1:T(1,128)S(1)}) fusion(f32[32,2]{0,1:T(2,128)S(1)} %convert_bitcast_fusion, f32[]{:T(128)} %bitcast.6, f32[]{:T(128)} %bitcast.4), kind=kLoop, calls=%fused_computation.1 | loop fusion | flops 160 | bytes 520 | tf_op jit(solution)/shard_map/convert_element_type | solution.py:156
  12.1 0.5 bitcast_convert_fusion.1.cos_ref
  12.7 23.0 %all-gather.3.cloned.1.call-done.g_ref = bf16[32,64,256]{2,1,0:T(8,128)(2,1)} async-done(((bf16[32,8,256]{2,1,0:T(8,128)(2,1)}), bf16[32,64,256]{2,1,0:T(8,128)(2,1)}) %all-gather.3.cloned.1.call-update) | async-done | bytes 1048592 | tf_op jit(solution)/shard_map/all_gather | solution.py:159
  35.7 2.9 %shard_map.118 = (bf16[2,64,2048]{2,1,0:T(8,128)(2,1)}, bf16[2,64,32]{2,1,0:T(8,128)(2,1)}) custom-call(s32[32]{0:T(128)} %bitcast.32, f32[32]{0:T(128)} %bitcast_convert_fusion.1.cos_ref, f32[32]{0:T(128)} %get-tuple-element.9.sin_ref, s32[1]{0:T(128)} %bitcast.22.rank_ref, bf16[32,64,256]{2,1,0:T(8,128)(2,1)} %all-gather.3.cloned.1.call-done.g_ref, ...), custom_call_target="tpu_custom_call" | custom-call | tf_op jit(solution)/shard_map/pallas_call | solution.py:162
  38.6 0.8 copy.14
  39.4 7.3 %all-gather = bf16[8,64,32]{1,2,0:T(8,128)(2,1)S(1)} all-gather(bf16[2,64,32]{1,2,0:T(8,128)(2,1)S(1)} %copy.14), channel_id=2, replica_groups=mesh['ang'=8,'row'=4] {'row'}, dimensions={0}, use_global_device_ids=true | all-gather | bytes 40960 | tf_op jit(solution)/shard_map/all_gather | solution.py:176
  46.7 0.8 copy.15
  47.5 6.7 %shard_map.119 = f32[2,64,2048]{2,1,0:T(8,128)} custom-call(f32[2]{0:T(128)} %bitcast.33, s32[1]{0:T(128)} %bitcast.23.rank_ref, s32[1]{0:T(128)} %bitcast.2.me_ref, bf16[2,64,2048]{2,1,0:T(8,128)(2,1)} %get-tuple-element.7.e_ref, bf16[2,2048,256]{2,1,0:T(8,128)(2,1)} %bitcast.24, bf16[3,2,32,2048]{3,2,1,0:T(8,128)(2,1)} %bitcast.25, ...), custom_call_target="tpu_custom_call" | custom-call | tf_op jit(solution)/shard_map/pallas_call | solution.py:179
  54.2 0.0 reduce-scatter.2.cloned.1.call-update
  54.2 31.7 %reduce-scatter.2.cloned.1.call-done = f32[2,8,2048]{2,1,0:T(8,128)} async-done(((f32[2,64,2048]{2,1,0:T(8,128)}), f32[2,8,2048]{2,1,0:T(8,128)}) %reduce-scatter.2.cloned.1.call-update) | async-done | bytes 131088 | tf_op jit(solution)/shard_map/reduce_scatter | solution.py:200
  85.9 1.7 %copy.16 = f32[8,2,2048]{2,1,0:T(2,128)} copy(f32[8,2,2048]{2,0,1:T(8,128)} %bitcast.30) | data formatting | bytes 262144 | tf_op jit(solution)/shard_map/transpose | solution.py:201
Async XLA Ops:
  6.5 2.4 %copy-start = (f32[8,2]{0,1:T(2,128)S(1)}, f32[8,2]{0,1:T(2,128)}, u32[]{:S(2)}) copy-start(f32[8,2]{0,1:T(2,128)} %param.15) | copy-start | bytes 196
  6.5 29.1 %all-gather.3.cloned.1.call-start = ((), (), s32[]{:S(2)}) async-start(), calls=%async_computation.1 | async-start | bytes 1179648 | tf_op jit(solution)/shard_map/all_gather | solution.py:159
  8.2 77.7 %reduce-scatter.2.cloned.1.call-start = ((), (), s32[]{:S(2)}) async-start(), calls=%async_computation.2 | async-start | bytes 1179648 | tf_op jit(solution)/shard_map/reduce_scatter | solution.py:200
Sparse Core Ops, SparseCore 0:
  8.9 26.6 all-gather.2
  54.4 31.4 reduce-scatter.1

commit v3 on v2

--- a/solution.py
+++ b/solution.py
@@ -152,8 +152,8 @@
     cell_float = panel_cell[0].astype(jnp.float32)
     own_wave = lax.dynamic_slice_in_dim(bloch_k, lax.axis_index("ang") * local_angles, local_angles, 0)
     theta = own_wave[0, 0] * cell_float[:, 0] + own_wave[0, 1] * cell_float[:, 1]
-    own_cos = jnp.cos(theta).astype(jnp.bfloat16).astype(jnp.float32)
-    own_sin = jnp.sin(theta).astype(jnp.bfloat16).astype(jnp.float32)
+    own_cos = lax.reduce_precision(jnp.cos(theta), exponent_bits=8, mantissa_bits=7)
+    own_sin = lax.reduce_precision(jnp.sin(theta), exponent_bits=8, mantissa_bits=7)
 
     local_panels = panels[0].reshape(panel_count, local_sources, 2 * panel_width)
     gathered = lax.all_gather(local_panels, "ang", axis=1, tiled=True)

time: 94.7 us -> 94.7 us (level)
    reduce_precision x0 -> x2, other arithmetic: none -> 2.38 us  [the longest x1 1.86 us: shards(): lax.reduce_precision(jnp.sin(theta), exponent_bits=8, mantissa_bits=7)]
    convert_element_type x2 -> x0, other arithmetic: 2.38 us -> none  [the longest x1 1.86 us: shards(): own_sin = jnp.sin(theta).astype(jnp.bfloat16).astype(jnp.float32)]
where the time goes in v3:
time: 94.7 us; the launch traced here: 94.4 us
  waiting for transfers between devices  54.7 us (58%)
  between operations  14.1 us (15%)
  Pallas kernels  9.62 us (10%)
  blocking collectives  7.33 us (8%)
  local copies, waits for them, and re-layouts  5.58 us (6%)
  other arithmetic  3.07 us (3%)
    reduce_scatter x1, waiting for transfers between devices, shards(): summed = lax.psum_scatter(field, 'ang', scatter_dimension=1, tiled=True)  31.7 us
    all_gather x1, waiting for transfers between devices, shards(): gathered = lax.all_gather(local_panels, 'ang', axis=1, tiled=True)  23 us
    all_gather x1, blocking collectives, shards(): all_projected = lax.all_gather(projected, 'row', axis=0, tiled=False)  7.33 us
    pallas_call x1, Pallas kernels, shards(): pl.pallas_call(_field_kernel, out_shape=jax.ShapeDtypeStruct((2, source_c...  6.7 us
    pallas_call x1, Pallas kernels, shards(): pl.pallas_call(_excite_kernel, out_shape=(jax.ShapeDtypeStruct((2, source...  2.92 us
  transfers between devices with their start and end apart: 2, of which 2 were waited for; matrix products, arithmetic and copies ran while one was open for 4% of the time, Pallas kernels for 0%

profile of v3, /device:TPU:0, one launch (start us, length us, event | category | flops | bytes accessed | tf_op | source)
XLA Modules:
  0.0 94.4 jit_solution(8890927701505169720)
XLA Ops:
  6.5 0.0 copy-start
  6.5 0.0 all-gather.3.cloned.1.call-start
  6.5 1.7 %reshape_squeeze.3 = bf16[32,8,256]{2,1,0:T(8,128)(2,1)} reshape(bf16[1,32,8,2,128]{4,3,2,1,0:T(2,128)(2,1)} %param.12) | data formatting | bytes 262144 | tf_op jit(solution)/shard_map/reshape;squeeze | solution.py:158
  8.2 0.0 all-gather.3.cloned.1.call-update
  8.2 0.0 reduce-scatter.2.cloned.1.call-start
  8.9 0.0 copy-done
  8.9 0.1 constant_dynamic-slice_fusion
  9.0 0.6 fusion
  9.6 0.7 convert_bitcast_fusion
  10.3 1.9 %reduce-precision_bitcast_fusion = (f32[32]{0:T(128)}, f32[32,1]{0,1:T(1,128)S(1)}) fusion(f32[32,2]{0,1:T(2,128)S(1)} %convert_bitcast_fusion, f32[]{:T(128)} %bitcast.6, f32[]{:T(128)} %bitcast.4), kind=kLoop, calls=%fused_computation.1 | loop fusion | flops 128 | bytes 520 | tf_op jit(solution)/shard_map/reduce_precision | solution.py:156
  12.1 0.5 reduce-precision_bitcast_fusion.1.cos_ref
  12.7 23.0 %all-gather.3.cloned.1.call-done.g_ref = bf16[32,64,256]{2,1,0:T(8,128)(2,1)} async-done(((bf16[32,8,256]{2,1,0:T(8,128)(2,1)}), bf16[32,64,256]{2,1,0:T(8,128)(2,1)}) %all-gather.3.cloned.1.call-update) | async-done | bytes 1048592 | tf_op jit(solution)/shard_map/all_gather | solution.py:159
  35.7 2.9 %shard_map.118 = (bf16[2,64,2048]{2,1,0:T(8,128)(2,1)}, bf16[2,64,32]{2,1,0:T(8,128)(2,1)}) custom-call(s32[32]{0:T(128)} %bitcast.30, f32[32]{0:T(128)} %reduce-precision_bitcast_fusion.1.cos_ref, f32[32]{0:T(128)} %get-tuple-element.9.sin_ref, s32[1]{0:T(128)} %bitcast.20.rank_ref, bf16[32,64,256]{2,1,0:T(8,128)(2,1)} %all-gather.3.cloned.1.call-done.g_ref, ...), custom_call_target="tpu_custom_call" | custom-call | tf_op jit(solution)/shard_map/pallas_call | solution.py:162
  38.6 0.8 copy.14
  39.4 7.3 %all-gather = bf16[8,64,32]{1,2,0:T(8,128)(2,1)S(1)} all-gather(bf16[2,64,32]{1,2,0:T(8,128)(2,1)S(1)} %copy.14), channel_id=2, replica_groups=mesh['ang'=8,'row'=4] {'row'}, dimensions={0}, use_global_device_ids=true | all-gather | bytes 40960 | tf_op jit(solution)/shard_map/all_gather | solution.py:176
  46.7 0.8 copy.15
  47.5 6.7 %shard_map.119 = f32[2,64,2048]{2,1,0:T(8,128)} custom-call(f32[2]{0:T(128)} %bitcast.31, s32[1]{0:T(128)} %bitcast.21.rank_ref, s32[1]{0:T(128)} %bitcast.2.me_ref, bf16[2,64,2048]{2,1,0:T(8,128)(2,1)} %get-tuple-element.7.e_ref, bf16[2,2048,256]{2,1,0:T(8,128)(2,1)} %bitcast.22, bf16[3,2,32,2048]{3,2,1,0:T(8,128)(2,1)} %bitcast.23, ...), custom_call_target="tpu_custom_call" | custom-call | tf_op jit(solution)/shard_map/pallas_call | solution.py:179
  54.2 0.0 reduce-scatter.2.cloned.1.call-update
  54.2 31.7 %reduce-scatter.2.cloned.1.call-done = f32[2,8,2048]{2,1,0:T(8,128)} async-done(((f32[2,64,2048]{2,1,0:T(8,128)}), f32[2,8,2048]{2,1,0:T(8,128)}) %reduce-scatter.2.cloned.1.call-update) | async-done | bytes 131088 | tf_op jit(solution)/shard_map/reduce_scatter | solution.py:200
  85.9 1.7 %copy.16 = f32[8,2,2048]{2,1,0:T(2,128)} copy(f32[8,2,2048]{2,0,1:T(8,128)} %bitcast.28) | data formatting | bytes 262144 | tf_op jit(solution)/shard_map/transpose | solution.py:201
Async XLA Ops:
  6.5 2.4 %copy-start = (f32[8,2]{0,1:T(2,128)S(1)}, f32[8,2]{0,1:T(2,128)}, u32[]{:S(2)}) copy-start(f32[8,2]{0,1:T(2,128)} %param.15) | copy-start | bytes 196
  6.5 29.1 %all-gather.3.cloned.1.call-start = ((), (), s32[]{:S(2)}) async-start(), calls=%async_computation.1 | async-start | bytes 1179648 | tf_op jit(solution)/shard_map/all_gather | solution.py:159
  8.2 77.7 %reduce-scatter.2.cloned.1.call-start = ((), (), s32[]{:S(2)}) async-start(), calls=%async_computation.2 | async-start | bytes 1179648 | tf_op jit(solution)/shard_map/reduce_scatter | solution.py:200
Sparse Core Ops, SparseCore 0:
  8.9 26.6 all-gather.2
  54.4 31.4 reduce-scatter.1

commit v4 on v3

--- a/solution.py
+++ b/solution.py
@@ -120,8 +120,37 @@
         q_im = jnp.where(keep, bl_ref[1, :, cols], zero)
         f_re = f_re + (_nn(coupled_re, q_re) - _nn(coupled_im, q_im))
         f_im = f_im + (_nn(coupled_re, q_im) + _nn(coupled_im, q_re))
-        out_ref[0, :, cols] = w_re * f_re - w_im * f_im
-        out_ref[1, :, cols] = w_re * f_im + w_im * f_re
+        out_ref[:, cols] = w_re * f_re - w_im * f_im
+        out_ref[:, row_count + l * LEAF:row_count + (l + 1) * LEAF] = w_re * f_im + w_im * f_re
+
+
+def _pair_perm(count, bit):
+    return [(i, i ^ (1 << bit)) for i in range(count)]
+
+
+def _reduce_scatter(x, axis_name):
+    count = lax.axis_size(axis_name)
+    index = lax.axis_index(axis_name)
+    chunk = x.shape[0] // count
+    current = x.reshape(count, chunk, *x.shape[1:])
+    for bit in range(count.bit_length() - 1):
+        current = current.reshape(current.shape[0] // 2, 2, *current.shape[1:])
+        mine = (index >> bit) & 1
+        keep = lax.dynamic_index_in_dim(current, mine, axis=1, keepdims=False)
+        give = lax.dynamic_index_in_dim(current, 1 - mine, axis=1, keepdims=False)
+        current = keep + lax.ppermute(give, axis_name, _pair_perm(count, bit))
+    return current.reshape(chunk, *x.shape[1:])
+
+
+def _all_gather(x, axis_name):
+    count = lax.axis_size(axis_name)
+    index = lax.axis_index(axis_name)
+    current = x[None]
+    for bit in range(count.bit_length() - 1):
+        other = lax.ppermute(current, axis_name, _pair_perm(count, bit))
+        low = ((index >> bit) & 1) == 0
+        current = jnp.concatenate([jnp.where(low, current, other), jnp.where(low, other, current)], axis=0)
+    return current
 
 
 def shards(
@@ -173,12 +202,12 @@
         ],
     )(panel_slot[0], own_cos, own_sin, rank, gathered, block_right[0])
 
-    all_projected = lax.all_gather(projected, "row", axis=0, tiled=False)
+    all_projected = _all_gather(projected, "row")
     me = lax.axis_index("row").astype(jnp.int32).reshape(1)
 
     field = pl.pallas_call(
         _field_kernel,
-        out_shape=jax.ShapeDtypeStruct((2, source_count, row_count), jnp.float32),
+        out_shape=jax.ShapeDtypeStruct((source_count, 2 * row_count), jnp.float32),
         in_specs=[_SMEM, _SMEM, _SMEM] + [_VMEM] * 7,
         out_specs=_VMEM,
         scratch_shapes=[
@@ -197,8 +226,8 @@
         block_coupling[0, 0],
         all_projected,
     )
-    summed = lax.psum_scatter(field, "ang", scatter_dimension=1, tiled=True)
-    return jnp.transpose(summed, (1, 0, 2))
+    summed = _reduce_scatter(field, "ang")
+    return summed.reshape(summed.shape[0], 2, row_count)
 
 
 def solution(mesh):

time: 94.7 us -> 85.5 us (0.903)
  waiting for transfers between devices: 54.7 us -> 47.2 us
  blocking collectives: 7.33 us -> 0 us
  starting transfers between devices: 0.04 us -> 4.24 us
  other arithmetic: 3.07 us -> 5.72 us
  local copies, waits for them, and re-layouts: 5.58 us -> 4.24 us
    reduce_scatter x1 -> x0, waiting for transfers between devices: 31.7 us -> none  [shards(): summed = lax.psum_scatter(field, 'ang', scatter_dimension=1, tiled=True)]
    ppermute x0 -> x5, waiting for transfers between devices: none -> 24.1 us  [the longest x3 16.9 us: _reduce_scatter(): current = keep + lax.ppermute(give, axis_name, _pair_perm(count, bit))]
    all_gather x1 -> x0, blocking collectives: 7.33 us -> none  [shards(): all_projected = lax.all_gather(projected, 'row', axis=0, tiled=False)]
    ppermute x0 -> x5, starting transfers between devices: none -> 4.24 us  [the longest x3 2.96 us: _reduce_scatter(): current = keep + lax.ppermute(give, axis_name, _pair_perm(count, bit))]
    transpose x1 -> x0, local copies, waits for them, and re-layouts: 1.66 us -> none  [shards(): return jnp.transpose(summed, (1, 0, 2))]
    add x0 -> x3, other arithmetic: none -> 1.17 us  [_reduce_scatter(): current = keep + lax.ppermute(give, axis_name, _pair_perm(count, bit))]
    squeeze x0 -> x3, local copies, waits for them, and re-layouts: none -> 1.12 us  [_reduce_scatter(): give = lax.dynamic_index_in_dim(current, 1 - mine, axis=1, keepdims=False)]
  transfers between devices with their start and end apart: 2 -> 6, of which waited for: 2 -> 6; matrix products, arithmetic and copies ran while one was open for 4% -> 4% of each run, Pallas kernels for 0% -> 0%
where the time goes in v4:
time: 85.5 us; the launch traced here: 85.1 us
  waiting for transfers between devices  47.2 us (55%)
  between operations  14.1 us (16%)
  Pallas kernels  9.62 us (11%)
  other arithmetic  5.72 us (7%)
  local copies, waits for them, and re-layouts  4.24 us (5%)
  starting transfers between devices  4.24 us (5%)
    all_gather x1, waiting for transfers between devices, shards(): gathered = lax.all_gather(local_panels, 'ang', axis=1, tiled=True)  23 us
    ppermute x3, waiting for transfers between devices, _reduce_scatter(): current = keep + lax.ppermute(give, axis_name, _pair_perm(count, bit))  16.9 us
    ppermute x2, waiting for transfers between devices, _all_gather(): other = lax.ppermute(current, axis_name, _pair_perm(count, bit))  7.18 us
    pallas_call x1, Pallas kernels, shards(): pl.pallas_call(_field_kernel, out_shape=jax.ShapeDtypeStruct((source_coun...  6.71 us
    ppermute x3, starting transfers between devices, _reduce_scatter(): current = keep + lax.ppermute(give, axis_name, _pair_perm(count, bit))  2.96 us
    pallas_call x1, Pallas kernels, shards(): pl.pallas_call(_excite_kernel, out_shape=(jax.ShapeDtypeStruct((2, source...  2.92 us
    reduce_precision x1, other arithmetic, shards(): lax.reduce_precision(jnp.sin(theta), exponent_bits=8, mantissa_bits=7)  1.82 us
  transfers between devices with their start and end apart: 6, of which 6 were waited for; matrix products, arithmetic and copies ran while one was open for 4% of the time, Pallas kernels for 0%

profile of v4, /device:TPU:0, one launch (start us, length us, event | category | flops | bytes accessed | tf_op | source)
XLA Modules:
  0.0 85.1 jit_solution(18200564562675958622)
XLA Ops:
  6.5 0.0 copy-start
  6.5 0.0 all-gather.2.cloned.1.call-start
  6.5 1.7 %reshape_squeeze.3 = bf16[32,8,256]{2,1,0:T(8,128)(2,1)} reshape(bf16[1,32,8,2,128]{4,3,2,1,0:T(2,128)(2,1)} %param.12) | data formatting | bytes 262144 | tf_op jit(solution)/shard_map/reshape;squeeze | solution.py:187
  8.2 0.0 all-gather.2.cloned.1.call-update
  8.9 0.0 copy-done
  8.9 0.1 constant_dynamic-slice_fusion.1
  9.0 0.6 fusion
  9.6 0.7 convert_bitcast_fusion
  10.2 1.8 %reduce-precision_bitcast_fusion = (f32[32]{0:T(128)}, f32[32,1]{0,1:T(1,128)S(1)}) fusion(f32[32,2]{0,1:T(2,128)S(1)} %convert_bitcast_fusion, f32[]{:T(128)} %bitcast.6, f32[]{:T(128)} %bitcast.4), kind=kLoop, calls=%fused_computation.14 | loop fusion | flops 128 | bytes 520 | tf_op jit(solution)/shard_map/reduce_precision | solution.py:185
  12.1 0.6 reduce-precision_bitcast_fusion.1.cos_ref
  12.6 23.0 %all-gather.2.cloned.1.call-done.g_ref = bf16[32,64,256]{2,1,0:T(8,128)(2,1)} async-done(((bf16[32,8,256]{2,1,0:T(8,128)(2,1)}), bf16[32,64,256]{2,1,0:T(8,128)(2,1)}) %all-gather.2.cloned.1.call-update) | async-done | bytes 1048592 | tf_op jit(solution)/shard_map/all_gather | solution.py:188
  35.7 2.9 %shard_map.118 = (bf16[2,64,2048]{2,1,0:T(8,128)(2,1)}, bf16[2,64,32]{2,1,0:T(8,128)(2,1)}) custom-call(s32[32]{0:T(128)} %bitcast.44, f32[32]{0:T(128)} %reduce-precision_bitcast_fusion.1.cos_ref, f32[32]{0:T(128)} %get-tuple-element.9.sin_ref, s32[1]{0:T(128)} %bitcast.31.rank_ref, bf16[32,64,256]{2,1,0:T(8,128)(2,1)} %all-gather.2.cloned.1.call-done.g_ref, ...), custom_call_target="tpu_custom_call" | custom-call | tf_op jit(solution)/shard_map/pallas_call | solution.py:191
  38.6 0.6 collective-permute-start
  39.2 3.5 %collective-permute-done = bf16[1,2,64,32]{3,2,1,0:T(8,128)(2,1)S(1)} collective-permute-done((bf16[1,2,64,32]{3,2,1,0:T(8,128)(2,1)}, bf16[1,2,64,32]{3,2,1,0:T(8,128)(2,1)S(1)}, u32[]{:S(2)}, u32[]{:S(2)}) %collective-permute-start) | collective-permute-done | bytes 8224 | tf_op jit(solution)/shard_map/ppermute | solution.py:150
  42.7 0.8 broadcast_select_fusion.3
  43.5 0.7 collective-permute-start.1
  44.2 3.7 %collective-permute-done.1 = bf16[2,2,64,32]{3,2,1,0:T(8,128)(2,1)S(1)} collective-permute-done((bf16[2,2,64,32]{3,2,1,0:T(8,128)(2,1)S(1)}, bf16[2,2,64,32]{3,2,1,0:T(8,128)(2,1)S(1)}, u32[]{:S(2)}, u32[]{:S(2)}) %collective-permute-start.1) | collective-permute-done | bytes 16416 | tf_op jit(solution)/shard_map/ppermute | solution.py:150
  47.8 0.7 pad_maximum_fusion.bpa_ref
  48.5 6.7 %shard_map.119 = f32[64,4096]{1,0:T(8,128)} custom-call(f32[2]{0:T(128)} %bitcast.45, s32[1]{0:T(128)} %bitcast.32.rank_ref, s32[1]{0:T(128)} %bitcast.2.me_ref, bf16[2,64,2048]{2,1,0:T(8,128)(2,1)} %get-tuple-element.7.e_ref, bf16[2,2048,256]{2,1,0:T(8,128)(2,1)} %bitcast.35, bf16[3,2,32,2048]{3,2,1,0:T(8,128)(2,1)} %bitcast.38, ...), custom_call_target="tpu_custom_call" | custom-call | tf_op jit(solution)/shard_map/pallas_call | solution.py:208
  55.2 1.1 %dynamic-slice_bitcast_fusion = f32[4,8,4096]{2,1,0:T(8,128)S(1)} fusion(f32[4,2,8,4096]{3,2,1,0:T(8,128)} %bitcast.33, s32[]{:T(128)S(6)} %select_n.56), kind=kLoop, calls=%fused_computation.1 | loop fusion | bytes 1048580 | tf_op jit(solution)/shard_map/jit(dynamic_index_in_dim)/squeeze | solution.py:140
  56.3 0.1 collective-permute-start.2
  56.4 1.9 %collective-permute-done.2 = f32[4,8,4096]{2,1,0:T(8,128)S(1)} collective-permute-done((f32[4,8,4096]{2,1,0:T(8,128)S(1)}, f32[4,8,4096]{2,1,0:T(8,128)S(1)}, u32[]{:S(2)}, u32[]{:S(2)}) %collective-permute-start.2) | collective-permute-done | bytes 524320 | tf_op jit(solution)/shard_map/ppermute | solution.py:141
  58.3 1.1 %bitcast_add_fusion = f32[4,8,4096]{2,1,0:T(8,128)S(1)} fusion(f32[4,8,4096]{2,1,0:T(8,128)S(1)} %collective-permute-done.2, f32[4,2,8,4096]{3,2,1,0:T(8,128)} %bitcast.34, s32[]{:T(128)S(6)} %select_n.55), kind=kLoop, calls=%fused_computation | loop fusion | flops 131072 | bytes 1572868 | tf_op jit(solution)/shard_map/add | solution.py:141
  59.5 2.5 %collective-permute-start.3 = (f32[2,8,4096]{2,1,0:T(8,128)S(1)}, f32[2,8,4096]{2,1,0:T(8,128)S(1)}, u32[]{:S(2)}, u32[]{:S(2)}) collective-permute-start(f32[2,8,4096]{2,1,0:T(8,128)S(1)} %dynamic-slice_bitcast_fusion.1), channel_id=1, source_target_pairs={{0,8},{4,12},{8,0},{12,4},{16,24},{20,28},{24,16},{28,20},{1,9},{5... | collective-permute-start | bytes 786440 | tf_op jit(solution)/shard_map/ppermute | solution.py:141
  62.0 6.6 %collective-permute-done.3 = f32[2,8,4096]{2,1,0:T(8,128)S(1)} collective-permute-done((f32[2,8,4096]{2,1,0:T(8,128)S(1)}, f32[2,8,4096]{2,1,0:T(8,128)S(1)}, u32[]{:S(2)}, u32[]{:S(2)}) %collective-permute-start.3) | collective-permute-done | bytes 262176 | tf_op jit(solution)/shard_map/ppermute | solution.py:141
  68.7 0.4 collective-permute-start.4
  69.0 8.4 %collective-permute-done.4 = f32[1,8,4096]{2,1,0:T(8,128)S(1)} collective-permute-done((f32[1,8,4096]{2,1,0:T(8,128)S(1)}, f32[1,8,4096]{2,1,0:T(8,128)S(1)}, u32[]{:S(2)}, u32[]{:S(2)}) %collective-permute-start.4) | collective-permute-done | bytes 131104 | tf_op jit(solution)/shard_map/ppermute | solution.py:141
  77.5 0.8 reshape_reshape.7
  (6 shorter events, 0.1 us)
Async XLA Ops:
  6.5 2.3 %copy-start = (f32[8,2]{0,1:T(2,128)S(1)}, f32[8,2]{0,1:T(2,128)}, u32[]{:S(2)}) copy-start(f32[8,2]{0,1:T(2,128)} %param.15) | copy-start | bytes 196
  6.5 29.1 %all-gather.2.cloned.1.call-start = ((), (), s32[]{:S(2)}) async-start(), calls=%async_computation | async-start | bytes 1179648 | tf_op jit(solution)/shard_map/all_gather | solution.py:188
  38.6 4.1 %collective-permute-start = (bf16[1,2,64,32]{3,2,1,0:T(8,128)(2,1)}, bf16[1,2,64,32]{3,2,1,0:T(8,128)(2,1)S(1)}, u32[]{:S(2)}, u32[]{:S(2)}) collective-permute-start(bf16[1,2,64,32]{3,2,1,0:T(8,128)(2,1)} %bitcast.42), channel_id=1, source_target_pairs={{0,1},{1,0},{2,3},{3,2},{4,5},{5,4},{6,7},{7,6},{8,9},{9,8},{10,11... | collective-permute-start | bytes 24584 | tf_op jit(solution)/shard_map/ppermute | solution.py:150
  43.5 4.3 %collective-permute-start.1 = (bf16[2,2,64,32]{3,2,1,0:T(8,128)(2,1)S(1)}, bf16[2,2,64,32]{3,2,1,0:T(8,128)(2,1)S(1)}, u32[]{:S(2)}, u32[]{:S(2)}) collective-permute-start(bf16[2,2,64,32]{3,2,1,0:T(8,128)(2,1)S(1)} %pad_maximum_fusion.1), channel_id=1, source_target_pairs={{0,2},{1,3},{2,0},{3,1},{4,6},{5,7},{6,4},{7,5},{8,10},{9,11},{10,... | collective-permute-start | bytes 49160 | tf_op jit(solution)/shard_map/ppermute | solution.py:150
  56.3 2.0 %collective-permute-start.2 = (f32[4,8,4096]{2,1,0:T(8,128)S(1)}, f32[4,8,4096]{2,1,0:T(8,128)S(1)}, u32[]{:S(2)}, u32[]{:S(2)}) collective-permute-start(f32[4,8,4096]{2,1,0:T(8,128)S(1)} %dynamic-slice_bitcast_fusion), channel_id=1, source_target_pairs={{0,4},{4,0},{8,12},{12,8},{16,20},{20,16},{24,28},{28,24},{1,5},{5... | collective-permute-start | bytes 1572872 | tf_op jit(solution)/shard_map/ppermute | solution.py:141
  59.5 9.1 %collective-permute-start.3 = (f32[2,8,4096]{2,1,0:T(8,128)S(1)}, f32[2,8,4096]{2,1,0:T(8,128)S(1)}, u32[]{:S(2)}, u32[]{:S(2)}) collective-permute-start(f32[2,8,4096]{2,1,0:T(8,128)S(1)} %dynamic-slice_bitcast_fusion.1), channel_id=1, source_target_pairs={{0,8},{4,12},{8,0},{12,4},{16,24},{20,28},{24,16},{28,20},{1,9},{5... | collective-permute-start | bytes 786440 | tf_op jit(solution)/shard_map/ppermute | solution.py:141
  68.7 8.8 %collective-permute-start.4 = (f32[1,8,4096]{2,1,0:T(8,128)S(1)}, f32[1,8,4096]{2,1,0:T(8,128)S(1)}, u32[]{:S(2)}, u32[]{:S(2)}) collective-permute-start(f32[1,8,4096]{2,1,0:T(8,128)S(1)} %constant_dynamic-slice_fusion), channel_id=1, source_target_pairs={{0,16},{4,20},{8,24},{12,28},{16,0},{20,4},{24,8},{28,12},{1,17},{... | collective-permute-start | bytes 393224 | tf_op jit(solution)/shard_map/ppermute | solution.py:141
Sparse Core Ops, SparseCore 0:
  8.9 26.6 all-gather.1

commit v5 on v4

--- a/solution.py
+++ b/solution.py
@@ -54,7 +54,7 @@
     bp_ref[1] = (_nt(e_re, r_im) + _nt(e_im, r_re)).astype(jnp.bfloat16)
 
 
-def _field_kernel(qw_ref, rank_ref, me_ref, e_ref, leaf_ref, lr_ref, ll_ref, bl_ref, cp_ref, bpa_ref, out_ref, pj_ref, cu_ref):
+def _field_kernel(qw_ref, rank_ref, e_ref, leaf_ref, lr_ref, ll_ref, bl_ref, cp_ref, bpa_ref, out_ref, pj_ref, cu_ref):
     _, source_count, row_count = e_ref.shape
     levels = lr_ref.shape[0]
     rank_width = lr_ref.shape[2]
@@ -78,14 +78,11 @@
             pj_ref[slot, 1] = (_nt(a, r_im) + _nt(b, r_re)).astype(jnp.bfloat16)
             slot += 1
 
-    me = me_ref[0]
     c_re = jnp.zeros((source_count, rank_width), jnp.float32)
     c_im = jnp.zeros((source_count, rank_width), jnp.float32)
-    for u in range(blocks):
-        own = me == u
-        zero = jnp.zeros((source_count, coupling_rank), jnp.bfloat16)
-        b_re = jnp.where(own, zero, bpa_ref[u, 0])
-        b_im = jnp.where(own, zero, bpa_ref[u, 1])
+    for u in range(1, blocks):
+        b_re = bpa_ref[u, 0]
+        b_im = bpa_ref[u, 1]
         k_re = cp_ref[0, :, u * coupling_rank:(u + 1) * coupling_rank]
         k_im = cp_ref[1, :, u * coupling_rank:(u + 1) * coupling_rank]
         c_re = c_re + (_nt(b_re, k_re) - _nt(b_im, k_im))
@@ -130,26 +127,19 @@
 
 def _reduce_scatter(x, axis_name):
     count = lax.axis_size(axis_name)
-    index = lax.axis_index(axis_name)
-    chunk = x.shape[0] // count
-    current = x.reshape(count, chunk, *x.shape[1:])
+    current = x
     for bit in range(count.bit_length() - 1):
-        current = current.reshape(current.shape[0] // 2, 2, *current.shape[1:])
-        mine = (index >> bit) & 1
-        keep = lax.dynamic_index_in_dim(current, mine, axis=1, keepdims=False)
-        give = lax.dynamic_index_in_dim(current, 1 - mine, axis=1, keepdims=False)
-        current = keep + lax.ppermute(give, axis_name, _pair_perm(count, bit))
-    return current.reshape(chunk, *x.shape[1:])
-
-
-def _all_gather(x, axis_name):
+        half = current.shape[0] // 2
+        current = current[:half] + lax.ppermute(current[half:], axis_name, _pair_perm(count, bit))
+    return current
+
+
+def _all_gather(x, axis_name, axis, bits):
     count = lax.axis_size(axis_name)
-    index = lax.axis_index(axis_name)
-    current = x[None]
-    for bit in range(count.bit_length() - 1):
+    current = x
+    for bit in bits:
         other = lax.ppermute(current, axis_name, _pair_perm(count, bit))
-        low = ((index >> bit) & 1) == 0
-        current = jnp.concatenate([jnp.where(low, current, other), jnp.where(low, other, current)], axis=0)
+        current = jnp.concatenate([current, other], axis=axis)
     return current
 
 
@@ -185,7 +175,8 @@
     own_sin = lax.reduce_precision(jnp.sin(theta), exponent_bits=8, mantissa_bits=7)
 
     local_panels = panels[0].reshape(panel_count, local_sources, 2 * panel_width)
-    gathered = lax.all_gather(local_panels, "ang", axis=1, tiled=True)
+    ang_bits = lax.axis_size("ang").bit_length() - 1
+    gathered = _all_gather(local_panels, "ang", 1, list(range(ang_bits))[::-1])
     rank = rank_count[0].reshape(1)
 
     excitation, projected = pl.pallas_call(
@@ -202,13 +193,17 @@
         ],
     )(panel_slot[0], own_cos, own_sin, rank, gathered, block_right[0])
 
-    all_projected = _all_gather(projected, "row")
-    me = lax.axis_index("row").astype(jnp.int32).reshape(1)
+    row_blocks = lax.axis_size("row")
+    all_projected = _all_gather(projected[None], "row", 0, list(range(row_blocks.bit_length() - 1)))
+    me = lax.axis_index("row")
+    coupling = block_coupling[0, 0]
+    coupling = coupling.reshape(2, rank_width, row_blocks, coupling.shape[2] // row_blocks)
+    coupling = jnp.take(coupling, me ^ jnp.arange(row_blocks), axis=2).reshape(block_coupling.shape[2:])
 
     field = pl.pallas_call(
         _field_kernel,
         out_shape=jax.ShapeDtypeStruct((source_count, 2 * row_count), jnp.float32),
-        in_specs=[_SMEM, _SMEM, _SMEM] + [_VMEM] * 7,
+        in_specs=[_SMEM, _SMEM] + [_VMEM] * 7,
         out_specs=_VMEM,
         scratch_shapes=[
             pltpu.VMEM((2 ** (levels + 1) - 2, 2, source_count, rank_width), jnp.bfloat16),
@@ -217,13 +212,12 @@
     )(
         quad_weight[0],
         rank,
-        me,
         excitation,
         leaf_inverse[0],
         level_right[0],
         level_left[0],
         block_left[0],
-        block_coupling[0, 0],
+        coupling,
         all_projected,
     )
     summed = _reduce_scatter(field, "ang")

time: 85.5 us -> 65.8 us (0.77)
  waiting for transfers between devices: 47.2 us -> 29.9 us
  between operations: 14.1 us -> 0.77 us
  starting transfers between devices: 4.24 us -> 12.3 us
  other arithmetic: 5.72 us -> 8.25 us
    all_gather x1 -> x0, waiting for transfers between devices: 23 us -> none  [shards(): gathered = lax.all_gather(local_panels, 'ang', axis=1, tiled=True)]
    ppermute x2 -> x5, waiting for transfers between devices: 7.18 us -> 15.4 us  [_all_gather(): other = lax.ppermute(current, axis_name, _pair_perm(count, bit))]
    ppermute x2 -> x5, starting transfers between devices: 1.27 us -> 7.54 us  [_all_gather(): other = lax.ppermute(current, axis_name, _pair_perm(count, bit))]
    concatenate x2 -> x5, other arithmetic: 0.7 us -> 3.38 us  [_all_gather(): current = jnp.concatenate([current, other], axis=axis)]
    ppermute x3, waiting for transfers between devices: 16.9 us -> 14.6 us  [_reduce_scatter(): lax.ppermute(current[half:], axis_name, _pair_perm(count, bit))]
    ppermute x3, starting transfers between devices: 2.96 us -> 4.75 us  [_reduce_scatter(): lax.ppermute(current[half:], axis_name, _pair_perm(count, bit))]
    squeeze x3 -> x0, local copies, waits for them, and re-layouts: 1.12 us -> none  [_reduce_scatter(): give = lax.dynamic_index_in_dim(current, 1 - mine, axis=1, keepdims=False)]
    slice x0 -> x3, local copies, waits for them, and re-layouts: none -> 1.1 us  [_reduce_scatter(): current[half:]]
  transfers between devices with their start and end apart: 6 -> 8, of which waited for: 6 -> 7; matrix products, arithmetic and copies ran while one was open for 4% -> 8% of each run, Pallas kernels for 0% -> 0%
where the time goes in v5:
time: 65.8 us; the launch traced here: 65.3 us
  waiting for transfers between devices  29.9 us (45%)
  starting transfers between devices  12.3 us (19%)
  Pallas kernels  9.61 us (15%)
  other arithmetic  8.25 us (13%)
  local copies, waits for them, and re-layouts  4.47 us (7%)
  between operations  0.77 us (1%)
    ppermute x5, waiting for transfers between devices, _all_gather(): other = lax.ppermute(current, axis_name, _pair_perm(count, bit))  15.4 us
    ppermute x3, waiting for transfers between devices, _reduce_scatter(): lax.ppermute(current[half:], axis_name, _pair_perm(count, bit))  14.6 us
    ppermute x5, starting transfers between devices, _all_gather(): other = lax.ppermute(current, axis_name, _pair_perm(count, bit))  7.54 us
    pallas_call x1, Pallas kernels, shards(): pl.pallas_call(_field_kernel, out_shape=jax.ShapeDtypeStruct((source_coun...  6.7 us
    ppermute x3, starting transfers between devices, _reduce_scatter(): lax.ppermute(current[half:], axis_name, _pair_perm(count, bit))  4.75 us
    concatenate x5, other arithmetic, _all_gather(): current = jnp.concatenate([current, other], axis=axis)  3.38 us
    pallas_call x1, Pallas kernels, shards(): pl.pallas_call(_excite_kernel, out_shape=(jax.ShapeDtypeStruct((2, source...  2.92 us
    reduce_precision x1, other arithmetic, shards(): lax.reduce_precision(jnp.sin(theta), exponent_bits=8, mantissa_bits=7)  1.84 us
  transfers between devices with their start and end apart: 8, of which 7 were waited for; matrix products, arithmetic and copies ran while one was open for 8% of the time, Pallas kernels for 0%

profile of v5, /device:TPU:0, one launch (start us, length us, event | category | flops | bytes accessed | tf_op | source)
XLA Modules:
  0.0 65.3 jit_solution(3153239379530137836)
XLA Ops:
  0.0 0.0 copy-start
  0.0 1.0 %reshape_squeeze.6 = bf16[32,8,256]{2,1,0:T(8,128)(2,1)S(1)} reshape(bf16[1,32,8,2,128]{4,3,2,1,0:T(2,128)(2,1)} %param.12) | data formatting | bytes 262144 | tf_op jit(solution)/shard_map/reshape;squeeze | solution.py:177
  1.0 4.1 %collective-permute-start = (bf16[32,8,256]{2,1,0:T(8,128)(2,1)S(1)}, bf16[32,8,256]{2,1,0:T(8,128)(2,1)S(1)}, u32[]{:S(2)}, u32[]{:S(2)}) collective-permute-start(bf16[32,8,256]{2,1,0:T(8,128)(2,1)S(1)} %reshape_squeeze.6), channel_id=1, source_target_pairs={{0,16},{4,20},{8,24},{12,28},{16,0},{20,4},{24,8},{28,12},{1,17},{... | collective-permute-start | bytes 393224 | tf_op jit(solution)/shard_map/ppermute | solution.py:141
  5.1 0.0 copy-done
  5.1 0.1 constant_dynamic-slice_fusion
  5.2 0.5 fusion.1
  5.7 5.7 %collective-permute-done = bf16[32,8,256]{2,1,0:T(8,128)(2,1)S(1)} collective-permute-done((bf16[32,8,256]{2,1,0:T(8,128)(2,1)S(1)}, bf16[32,8,256]{2,1,0:T(8,128)(2,1)S(1)}, u32[]{:S(2)}, u32[]{:S(2)}) %collective-permute-start) | collective-permute-done | bytes 131104 | tf_op jit(solution)/shard_map/ppermute | solution.py:141
  11.4 0.8 %collective-permute-start.1 = (bf16[32,16,256]{2,1,0:T(8,128)(2,1)S(1)}, bf16[32,16,256]{2,1,0:T(8,128)(2,1)S(1)}, u32[]{:S(2)}, u32[]{:S(2)}) collective-permute-start(bf16[32,16,256]{2,1,0:T(8,128)(2,1)S(1)} %pad_maximum_fusion.2), channel_id=1, source_target_pairs={{0,8},{4,12},{8,0},{12,4},{16,24},{20,28},{24,16},{28,20},{1,9},{5... | collective-permute-start | bytes 786440 | tf_op jit(solution)/shard_map/ppermute | solution.py:141
  12.9 0.7 %convert_bitcast_fusion = f32[32,2]{0,1:T(2,128)S(1)} fusion(s32[1,32,2]{1,2,0:T(2,128)} %param.14), kind=kLoop, calls=%fused_computation.14 | loop fusion | flops 64 | bytes 512 | tf_op jit(solution)/shard_map/convert_element_type | solution.py:171
  13.6 0.0 copy-start.1
  13.6 5.4 %collective-permute-done.1 = bf16[32,16,256]{2,1,0:T(8,128)(2,1)S(1)} collective-permute-done((bf16[32,16,256]{2,1,0:T(8,128)(2,1)S(1)}, bf16[32,16,256]{2,1,0:T(8,128)(2,1)S(1)}, u32[]{:S(2)}, u32[]{:S(2)}) %collective-permute-start.1) | collective-permute-done | bytes 262176 | tf_op jit(solution)/shard_map/ppermute | solution.py:141
  19.0 0.1 pad_maximum_fusion.1
  19.1 0.1 collective-permute-start.2
  19.2 1.8 %reduce-precision_bitcast_fusion = (f32[32]{0:T(128)}, f32[32,1]{0,1:T(1,128)S(1)}) fusion(f32[32,2]{0,1:T(2,128)S(1)} %convert_bitcast_fusion, f32[]{:T(128)} %bitcast.5, f32[]{:T(128)} %bitcast.3), kind=kLoop, calls=%fused_computation.16 | loop fusion | flops 128 | bytes 520 | tf_op jit(solution)/shard_map/reduce_precision | solution.py:175
  21.0 0.6 reduce-precision_bitcast_fusion.1.cos_ref
  21.6 0.0 collective-permute-done.2
  21.6 1.1 %pad_maximum_fusion.g_ref = bf16[32,64,256]{2,1,0:T(8,128)(2,1)} fusion(bf16[32,32,256]{2,1,0:T(8,128)(2,1)S(1)} %collective-permute-done.2, bf16[32,16,256]{2,1,0:T(8,128)(2,1)S(1)} %collective-permute-done.1, bf16[32,8,256]{2,1,0:T(8,128)(2,1)S(1)} %collective-permute-done, bf16[32,8,256]{2,1,0:T(8,128)(2,1)S(1)} %reshape_squeeze.6), kind=kLoop, calls=%fused_computation.1 | loop fusion | flops 4194304 | bytes 2097152 | tf_op jit(solution)/shard_map/concatenate | solution.py:142
  22.6 2.9 %shard_map.118 = (bf16[2,64,2048]{2,1,0:T(8,128)(2,1)}, bf16[2,64,32]{2,1,0:T(8,128)(2,1)}) custom-call(s32[32]{0:T(128)} %bitcast.35, f32[32]{0:T(128)} %reduce-precision_bitcast_fusion.1.cos_ref, f32[32]{0:T(128)} %get-tuple-element.9.sin_ref, s32[1]{0:T(128)} %bitcast.23.rank_ref, bf16[32,64,256]{2,1,0:T(8,128)(2,1)} %pad_maximum_fusion.g_ref, ...), custom_call_target="tpu_custom_call" | custom-call | tf_op jit(solution)/shard_map/pallas_call | solution.py:182
  25.6 1.2 %collective-permute-start.3 = (bf16[1,2,64,32]{3,2,1,0:T(8,128)(2,1)}, bf16[1,2,64,32]{3,2,1,0:T(8,128)(2,1)S(1)}, u32[]{:S(2)}, u32[]{:S(2)}) collective-permute-start(bf16[1,2,64,32]{3,2,1,0:T(8,128)(2,1)} %bitcast.32), channel_id=1, source_target_pairs={{0,1},{1,0},{2,3},{3,2},{4,5},{5,4},{6,7},{7,6},{8,9},{9,8},{10,11... | collective-permute-start | bytes 24584 | tf_op jit(solution)/shard_map/ppermute | solution.py:141
  26.8 0.0 copy-done.1
  26.8 0.1 reshape_squeeze.7
  26.9 0.6 gather_fusion
  27.5 0.1 copy.17
  27.6 0.1 gather.7
  27.7 0.1 broadcast_in_dim.17
  27.7 0.1 broadcast_in_dim.18
  27.8 1.9 %collective-permute-done.3 = bf16[1,2,64,32]{3,2,1,0:T(8,128)(2,1)S(1)} collective-permute-done((bf16[1,2,64,32]{3,2,1,0:T(8,128)(2,1)}, bf16[1,2,64,32]{3,2,1,0:T(8,128)(2,1)S(1)}, u32[]{:S(2)}, u32[]{:S(2)}) %collective-permute-start.3) | collective-permute-done | bytes 8224 | tf_op jit(solution)/shard_map/ppermute | solution.py:141
  29.7 0.8 %pad_maximum_fusion.4 = bf16[2,2,64,32]{3,2,1,0:T(8,128)(2,1)S(1)} fusion(bf16[1,2,64,32]{3,2,1,0:T(8,128)(2,1)S(1)} %collective-permute-done.3, bf16[1,2,64,32]{3,2,1,0:T(8,128)(2,1)} %bitcast.33), kind=kLoop, calls=%fused_computation.8 | loop fusion | flops 8192 | bytes 32768 | tf_op jit(solution)/shard_map/concatenate | solution.py:142
  30.5 1.3 %collective-permute-start.4 = (bf16[2,2,64,32]{3,2,1,0:T(8,128)(2,1)S(1)}, bf16[2,2,64,32]{3,2,1,0:T(8,128)(2,1)S(1)}, u32[]{:S(2)}, u32[]{:S(2)}) collective-permute-start(bf16[2,2,64,32]{3,2,1,0:T(8,128)(2,1)S(1)} %pad_maximum_fusion.4), channel_id=1, source_target_pairs={{0,2},{1,3},{2,0},{3,1},{4,6},{5,7},{6,4},{7,5},{8,10},{9,11},{10,... | collective-permute-start | bytes 49160 | tf_op jit(solution)/shard_map/ppermute | solution.py:141
  31.8 0.6 broadcast_select_fusion.cp_ref
  32.4 2.4 %collective-permute-done.4 = bf16[2,2,64,32]{3,2,1,0:T(8,128)(2,1)S(1)} collective-permute-done((bf16[2,2,64,32]{3,2,1,0:T(8,128)(2,1)S(1)}, bf16[2,2,64,32]{3,2,1,0:T(8,128)(2,1)S(1)}, u32[]{:S(2)}, u32[]{:S(2)}) %collective-permute-start.4) | collective-permute-done | bytes 16416 | tf_op jit(solution)/shard_map/ppermute | solution.py:141
  34.8 1.4 %pad_maximum_fusion.3.bpa_ref = bf16[4,2,64,32]{3,2,1,0:T(8,128)(2,1)} fusion(bf16[2,2,64,32]{3,2,1,0:T(8,128)(2,1)S(1)} %collective-permute-done.4, bf16[1,2,64,32]{3,2,1,0:T(8,128)(2,1)S(1)} %collective-permute-done.3, bf16[1,2,64,32]{3,2,1,0:T(8,128)(2,1)} %bitcast.34), kind=kLoop, calls=%fused_computation.7 | loop fusion | flops 32768 | bytes 65536 | tf_op jit(solution)/shard_map/concatenate | solution.py:142
  36.2 6.7 %shard_map.119 = f32[64,4096]{1,0:T(8,128)} custom-call(f32[2]{0:T(128)} %bitcast.36, s32[1]{0:T(128)} %bitcast.24.rank_ref, bf16[2,64,2048]{2,1,0:T(8,128)(2,1)} %get-tuple-element.7.e_ref, bf16[2,2048,256]{2,1,0:T(8,128)(2,1)} %bitcast.25, bf16[3,2,32,2048]{3,2,1,0:T(8,128)(2,1)} %bitcast.26, bf16[3,2,32,2048]{3,2,1,0:T(8,128)(2,1)} %bitcast.27, ...), custom_call_target="tpu_custom_call" | custom-call | tf_op jit(solution)/shard_map/pallas_call | solution.py:203
  42.9 1.1 %slice.43 = f32[32,4096]{1,0:T(8,128)S(1)} slice(f32[64,4096]{1,0:T(8,128)} %shard_map.119), slice={[32:64], [0:4096]} | slice | bytes 1048576 | tf_op jit(solution)/shard_map/slice | solution.py:133
  44.0 0.1 collective-permute-start.5
  44.1 1.9 %collective-permute-done.5 = f32[32,4096]{1,0:T(8,128)S(1)} collective-permute-done((f32[32,4096]{1,0:T(8,128)S(1)}, f32[32,4096]{1,0:T(8,128)S(1)}, u32[]{:S(2)}, u32[]{:S(2)}) %collective-permute-start.5) | collective-permute-done | bytes 524320 | tf_op jit(solution)/shard_map/ppermute | solution.py:133
  46.0 1.1 %slice_add_fusion = f32[32,4096]{1,0:T(8,128)S(1)} fusion(f32[32,4096]{1,0:T(8,128)S(1)} %collective-permute-done.5, f32[64,4096]{1,0:T(8,128)} %shard_map.119), kind=kLoop, calls=%fused_computation.2 | loop fusion | flops 131072 | bytes 1572864 | tf_op jit(solution)/shard_map/add | solution.py:133
  47.1 1.5 %collective-permute-start.6 = (f32[16,4096]{1,0:T(8,128)S(1)}, f32[16,4096]{1,0:T(8,128)S(1)}, u32[]{:S(2)}, u32[]{:S(2)}) collective-permute-start(f32[16,4096]{1,0:T(8,128)S(1)} %slice.45), channel_id=1, source_target_pairs={{0,8},{4,12},{8,0},{12,4},{16,24},{20,28},{24,16},{28,20},{1,9},{5... | collective-permute-start | bytes 786440 | tf_op jit(solution)/shard_map/ppermute | solution.py:133
  48.7 6.9 %collective-permute-done.6 = f32[16,4096]{1,0:T(8,128)S(1)} collective-permute-done((f32[16,4096]{1,0:T(8,128)S(1)}, f32[16,4096]{1,0:T(8,128)S(1)}, u32[]{:S(2)}, u32[]{:S(2)}) %collective-permute-start.6) | collective-permute-done | bytes 262176 | tf_op jit(solution)/shard_map/ppermute | solution.py:133
  55.6 3.2 %collective-permute-start.7 = (f32[8,4096]{1,0:T(8,128)S(1)}, f32[8,4096]{1,0:T(8,128)S(1)}, u32[]{:S(2)}, u32[]{:S(2)}) collective-permute-start(f32[8,4096]{1,0:T(8,128)S(1)} %slice.47), channel_id=1, source_target_pairs={{0,16},{4,20},{8,24},{12,28},{16,0},{20,4},{24,8},{28,12},{1,17},{... | collective-permute-start | bytes 393224 | tf_op jit(solution)/shard_map/ppermute | solution.py:133
  58.8 5.8 %collective-permute-done.7 = f32[8,4096]{1,0:T(8,128)S(1)} collective-permute-done((f32[8,4096]{1,0:T(8,128)S(1)}, f32[8,4096]{1,0:T(8,128)S(1)}, u32[]{:S(2)}, u32[]{:S(2)}) %collective-permute-start.7) | collective-permute-done | bytes 131104 | tf_op jit(solution)/shard_map/ppermute | solution.py:133
  64.6 0.8 %copy.18 = f32[8,2,2048]{2,1,0:T(2,128)} copy(f32[8,2,2048]{2,0,1:T(8,128)S(1)} %bitcast.28) | data formatting | bytes 262144 | tf_op jit(solution)/shard_map/reshape | solution.py:224
  (9 shorter events, 0.1 us)
Async XLA Ops:
  0.0 5.1 %copy-start = (f32[8,2]{0,1:T(2,128)S(1)}, f32[8,2]{0,1:T(2,128)}, u32[]{:S(2)}) copy-start(f32[8,2]{0,1:T(2,128)} %param.15) | copy-start | bytes 196
  1.0 10.4 %collective-permute-start = (bf16[32,8,256]{2,1,0:T(8,128)(2,1)S(1)}, bf16[32,8,256]{2,1,0:T(8,128)(2,1)S(1)}, u32[]{:S(2)}, u32[]{:S(2)}) collective-permute-start(bf16[32,8,256]{2,1,0:T(8,128)(2,1)S(1)} %reshape_squeeze.6), channel_id=1, source_target_pairs={{0,16},{4,20},{8,24},{12,28},{16,0},{20,4},{24,8},{28,12},{1,17},{... | collective-permute-start | bytes 393224 | tf_op jit(solution)/shard_map/ppermute | solution.py:141
  11.4 7.6 %collective-permute-start.1 = (bf16[32,16,256]{2,1,0:T(8,128)(2,1)S(1)}, bf16[32,16,256]{2,1,0:T(8,128)(2,1)S(1)}, u32[]{:S(2)}, u32[]{:S(2)}) collective-permute-start(bf16[32,16,256]{2,1,0:T(8,128)(2,1)S(1)} %pad_maximum_fusion.2), channel_id=1, source_target_pairs={{0,8},{4,12},{8,0},{12,4},{16,24},{20,28},{24,16},{28,20},{1,9},{5... | collective-permute-start | bytes 786440 | tf_op jit(solution)/shard_map/ppermute | solution.py:141
  13.6 13.2 %copy-start.1 = (bf16[1,1,2,32,128]{4,3,2,1,0:T(8,128)(2,1)S(1)}, bf16[1,1,2,32,128]{4,3,2,1,0:T(8,128)(2,1)}, u32[]{:S(2)}) copy-start(bf16[1,1,2,32,128]{4,3,2,1,0:T(8,128)(2,1)} %param.21) | copy-start | bytes 49156
  19.1 2.5 %collective-permute-start.2 = (bf16[32,32,256]{2,1,0:T(8,128)(2,1)S(1)}, bf16[32,32,256]{2,1,0:T(8,128)(2,1)S(1)}, u32[]{:S(2)}, u32[]{:S(2)}) collective-permute-start(bf16[32,32,256]{2,1,0:T(8,128)(2,1)S(1)} %pad_maximum_fusion.1), channel_id=1, source_target_pairs={{0,4},{4,0},{8,12},{12,8},{16,20},{20,16},{24,28},{28,24},{1,5},{5... | collective-permute-start | bytes 1572872 | tf_op jit(solution)/shard_map/ppermute | solution.py:141
  25.6 4.1 %collective-permute-start.3 = (bf16[1,2,64,32]{3,2,1,0:T(8,128)(2,1)}, bf16[1,2,64,32]{3,2,1,0:T(8,128)(2,1)S(1)}, u32[]{:S(2)}, u32[]{:S(2)}) collective-permute-start(bf16[1,2,64,32]{3,2,1,0:T(8,128)(2,1)} %bitcast.32), channel_id=1, source_target_pairs={{0,1},{1,0},{2,3},{3,2},{4,5},{5,4},{6,7},{7,6},{8,9},{9,8},{10,11... | collective-permute-start | bytes 24584 | tf_op jit(solution)/shard_map/ppermute | solution.py:141
  30.5 4.3 %collective-permute-start.4 = (bf16[2,2,64,32]{3,2,1,0:T(8,128)(2,1)S(1)}, bf16[2,2,64,32]{3,2,1,0:T(8,128)(2,1)S(1)}, u32[]{:S(2)}, u32[]{:S(2)}) collective-permute-start(bf16[2,2,64,32]{3,2,1,0:T(8,128)(2,1)S(1)} %pad_maximum_fusion.4), channel_id=1, source_target_pairs={{0,2},{1,3},{2,0},{3,1},{4,6},{5,7},{6,4},{7,5},{8,10},{9,11},{10,... | collective-permute-start | bytes 49160 | tf_op jit(solution)/shard_map/ppermute | solution.py:141
  44.0 2.0 %collective-permute-start.5 = (f32[32,4096]{1,0:T(8,128)S(1)}, f32[32,4096]{1,0:T(8,128)S(1)}, u32[]{:S(2)}, u32[]{:S(2)}) collective-permute-start(f32[32,4096]{1,0:T(8,128)S(1)} %slice.43), channel_id=1, source_target_pairs={{0,4},{4,0},{8,12},{12,8},{16,20},{20,16},{24,28},{28,24},{1,5},{5... | collective-permute-start | bytes 1572872 | tf_op jit(solution)/shard_map/ppermute | solution.py:133
  47.1 8.4 %collective-permute-start.6 = (f32[16,4096]{1,0:T(8,128)S(1)}, f32[16,4096]{1,0:T(8,128)S(1)}, u32[]{:S(2)}, u32[]{:S(2)}) collective-permute-start(f32[16,4096]{1,0:T(8,128)S(1)} %slice.45), channel_id=1, source_target_pairs={{0,8},{4,12},{8,0},{12,4},{16,24},{20,28},{24,16},{28,20},{1,9},{5... | collective-permute-start | bytes 786440 | tf_op jit(solution)/shard_map/ppermute | solution.py:133
  55.6 8.9 %collective-permute-start.7 = (f32[8,4096]{1,0:T(8,128)S(1)}, f32[8,4096]{1,0:T(8,128)S(1)}, u32[]{:S(2)}, u32[]{:S(2)}) collective-permute-start(f32[8,4096]{1,0:T(8,128)S(1)} %slice.47), channel_id=1, source_target_pairs={{0,16},{4,20},{8,24},{12,28},{16,0},{20,4},{24,8},{28,12},{1,17},{... | collective-permute-start | bytes 393224 | tf_op jit(solution)/shard_map/ppermute | solution.py:133

commit v6 on v5

--- a/solution.py
+++ b/solution.py
@@ -54,12 +54,9 @@
     bp_ref[1] = (_nt(e_re, r_im) + _nt(e_im, r_re)).astype(jnp.bfloat16)
 
 
-def _field_kernel(qw_ref, rank_ref, e_ref, leaf_ref, lr_ref, ll_ref, bl_ref, cp_ref, bpa_ref, out_ref, pj_ref, cu_ref):
+def _near_kernel(e_ref, leaf_ref, lr_ref, ll_ref, out_ref, pj_ref):
     _, source_count, row_count = e_ref.shape
     levels = lr_ref.shape[0]
-    rank_width = lr_ref.shape[2]
-    blocks = bpa_ref.shape[0]
-    coupling_rank = bpa_ref.shape[3]
     e_re = e_ref[0]
     e_im = e_ref[1]
 
@@ -78,22 +75,6 @@
             pj_ref[slot, 1] = (_nt(a, r_im) + _nt(b, r_re)).astype(jnp.bfloat16)
             slot += 1
 
-    c_re = jnp.zeros((source_count, rank_width), jnp.float32)
-    c_im = jnp.zeros((source_count, rank_width), jnp.float32)
-    for u in range(1, blocks):
-        b_re = bpa_ref[u, 0]
-        b_im = bpa_ref[u, 1]
-        k_re = cp_ref[0, :, u * coupling_rank:(u + 1) * coupling_rank]
-        k_im = cp_ref[1, :, u * coupling_rank:(u + 1) * coupling_rank]
-        c_re = c_re + (_nt(b_re, k_re) - _nt(b_im, k_im))
-        c_im = c_im + (_nt(b_re, k_im) + _nt(b_im, k_re))
-    cu_ref[0] = c_re.astype(jnp.bfloat16)
-    cu_ref[1] = c_im.astype(jnp.bfloat16)
-    coupled_re = cu_ref[0]
-    coupled_im = cu_ref[1]
-
-    w_re = qw_ref[0]
-    w_im = qw_ref[1]
     for l in range(row_count // LEAF):
         cols = slice(l * LEAF, (l + 1) * LEAF)
         a = e_re[:, cols]
@@ -111,14 +92,44 @@
             m_im = ll_ref[j, 1, :, cols]
             f_re = f_re + (_nn(p_re, m_re) - _nn(p_im, m_im))
             f_im = f_im + (_nn(p_re, m_im) + _nn(p_im, m_re))
-        keep = _rank_mask(rank_ref, (bl_ref.shape[1], LEAF))
-        zero = jnp.zeros((bl_ref.shape[1], LEAF), jnp.bfloat16)
+        out_ref[:, cols] = f_re
+        out_ref[:, row_count + l * LEAF:row_count + (l + 1) * LEAF] = f_im
+
+
+def _far_kernel(qw_ref, rank_ref, near_ref, bl_ref, cp_ref, bpa_ref, out_ref, cu_ref):
+    source_count = near_ref.shape[0]
+    row_count = bl_ref.shape[2]
+    rank_width = bl_ref.shape[1]
+    blocks = bpa_ref.shape[0]
+    coupling_rank = bpa_ref.shape[3]
+
+    c_re = jnp.zeros((source_count, rank_width), jnp.float32)
+    c_im = jnp.zeros((source_count, rank_width), jnp.float32)
+    for u in range(1, blocks):
+        b_re = bpa_ref[u, 0]
+        b_im = bpa_ref[u, 1]
+        k_re = cp_ref[0, :, u * coupling_rank:(u + 1) * coupling_rank]
+        k_im = cp_ref[1, :, u * coupling_rank:(u + 1) * coupling_rank]
+        c_re = c_re + (_nt(b_re, k_re) - _nt(b_im, k_im))
+        c_im = c_im + (_nt(b_re, k_im) + _nt(b_im, k_re))
+    cu_ref[0] = c_re.astype(jnp.bfloat16)
+    cu_ref[1] = c_im.astype(jnp.bfloat16)
+    coupled_re = cu_ref[0]
+    coupled_im = cu_ref[1]
+
+    w_re = qw_ref[0]
+    w_im = qw_ref[1]
+    for l in range(row_count // LEAF):
+        cols = slice(l * LEAF, (l + 1) * LEAF)
+        imag_cols = slice(row_count + l * LEAF, row_count + (l + 1) * LEAF)
+        keep = _rank_mask(rank_ref, (rank_width, LEAF))
+        zero = jnp.zeros((rank_width, LEAF), jnp.bfloat16)
         q_re = jnp.where(keep, bl_ref[0, :, cols], zero)
         q_im = jnp.where(keep, bl_ref[1, :, cols], zero)
-        f_re = f_re + (_nn(coupled_re, q_re) - _nn(coupled_im, q_im))
-        f_im = f_im + (_nn(coupled_re, q_im) + _nn(coupled_im, q_re))
+        f_re = near_ref[:, cols] + (_nn(coupled_re, q_re) - _nn(coupled_im, q_im))
+        f_im = near_ref[:, imag_cols] + (_nn(coupled_re, q_im) + _nn(coupled_im, q_re))
         out_ref[:, cols] = w_re * f_re - w_im * f_im
-        out_ref[:, row_count + l * LEAF:row_count + (l + 1) * LEAF] = w_re * f_im + w_im * f_re
+        out_ref[:, imag_cols] = w_re * f_im + w_im * f_re
 
 
 def _pair_perm(count, bit):
@@ -141,6 +152,14 @@
         other = lax.ppermute(current, axis_name, _pair_perm(count, bit))
         current = jnp.concatenate([current, other], axis=axis)
     return current
+
+
+def _exchange(x, axis_name):
+    count = lax.axis_size(axis_name)
+    if count > 4:
+        return _all_gather(x[None], axis_name, 0, list(range(count.bit_length() - 1)))
+    parts = [x] + [lax.ppermute(x, axis_name, [(i, i ^ p) for i in range(count)]) for p in range(1, count)]
+    return jnp.stack(parts, axis=0)
 
 
 def shards(
@@ -194,32 +213,28 @@
     )(panel_slot[0], own_cos, own_sin, rank, gathered, block_right[0])
 
     row_blocks = lax.axis_size("row")
-    all_projected = _all_gather(projected[None], "row", 0, list(range(row_blocks.bit_length() - 1)))
+    all_projected = _exchange(projected, "row")
     me = lax.axis_index("row")
     coupling = block_coupling[0, 0]
     coupling = coupling.reshape(2, rank_width, row_blocks, coupling.shape[2] // row_blocks)
     coupling = jnp.take(coupling, me ^ jnp.arange(row_blocks), axis=2).reshape(block_coupling.shape[2:])
 
+    near = pl.pallas_call(
+        _near_kernel,
+        out_shape=jax.ShapeDtypeStruct((source_count, 2 * row_count), jnp.float32),
+        in_specs=[_VMEM] * 4,
+        out_specs=_VMEM,
+        scratch_shapes=[pltpu.VMEM((2 ** (levels + 1) - 2, 2, source_count, rank_width), jnp.bfloat16)],
+    )(excitation, leaf_inverse[0], level_right[0], level_left[0])
+
     field = pl.pallas_call(
-        _field_kernel,
+        _far_kernel,
         out_shape=jax.ShapeDtypeStruct((source_count, 2 * row_count), jnp.float32),
-        in_specs=[_SMEM, _SMEM] + [_VMEM] * 7,
+        in_specs=[_SMEM, _SMEM] + [_VMEM] * 4,
         out_specs=_VMEM,
-        scratch_shapes=[
-            pltpu.VMEM((2 ** (levels + 1) - 2, 2, source_count, rank_width), jnp.bfloat16),
-            pltpu.VMEM((2, source_count, rank_width), jnp.bfloat16),
-        ],
-    )(
-        quad_weight[0],
-        rank,
-        excitation,
-        leaf_inverse[0],
-        level_right[0],
-        level_left[0],
-        block_left[0],
-        coupling,
-        all_projected,
-    )
+        scratch_shapes=[pltpu.VMEM((2, source_count, rank_width), jnp.bfloat16)],
+        input_output_aliases={2: 0},
+    )(quad_weight[0], rank, near, block_left[0], coupling, all_projected)
     summed = _reduce_scatter(field, "ang")
     return summed.reshape(summed.shape[0], 2, row_count)
 

time: 65.8 us -> 62.9 us (0.956)
  waiting for transfers between devices: 29.9 us -> 24.5 us
  Pallas kernels: 9.61 us -> 12.1 us
  other arithmetic: 8.25 us -> 6.75 us
  starting transfers between devices: 12.3 us -> 13.2 us
  local copies, waits for them, and re-layouts: 4.47 us -> 5.16 us
    ppermute x5 -> x3, waiting for transfers between devices: 15.4 us -> 9.92 us  [_all_gather(): other = lax.ppermute(current, axis_name, _pair_perm(count, bit))]
    ppermute x0 -> x3, starting transfers between devices: none -> 3.49 us  [_exchange(): lax.ppermute(x, axis_name, [(i, i ^ p) for i in range(count)])]
    ppermute x5 -> x3, starting transfers between devices: 7.54 us -> 4.96 us  [_all_gather(): other = lax.ppermute(current, axis_name, _pair_perm(count, bit))]
    pallas_call x1 -> x2, Pallas kernels: 6.7 us -> 9.23 us  [the longest x1 6.25 us: shards(): pl.pallas_call(_near_kernel, out_shape=jax.ShapeDtypeStruct((source_count...]
    concatenate x5 -> x3, other arithmetic: 3.38 us -> 1.16 us  [_all_gather(): current = jnp.concatenate([current, other], axis=axis)]
    another operation x2, local copies, waits for them, and re-layouts: 0.1 us -> 0.82 us  [shards(): coupling.reshape(2, rank_width, row_blocks, coupling.shape[2] // row_blocks)]
    another operation x0 -> x1, other arithmetic: none -> 0.69 us  [_exchange(): return jnp.stack(parts, axis=0)]
  transfers between devices with their start and end apart: 8 -> 9, of which waited for: 7 -> 5; matrix products, arithmetic and copies ran while one was open for 8% -> 10% of each run, Pallas kernels for 0% -> 10%
where the time goes in v6:
time: 62.9 us; the launch traced here: 62.5 us
  waiting for transfers between devices  24.5 us (39%)
  starting transfers between devices  13.2 us (21%)
  Pallas kernels  12.1 us (19%)
  other arithmetic  6.75 us (11%)
  local copies, waits for them, and re-layouts  5.16 us (8%)
  between operations  0.77 us (1%)
    ppermute x3, waiting for transfers between devices, _reduce_scatter(): lax.ppermute(current[half:], axis_name, _pair_perm(count, bit))  14.6 us
    ppermute x3, waiting for transfers between devices, _all_gather(): other = lax.ppermute(current, axis_name, _pair_perm(count, bit))  9.92 us
    pallas_call x1, Pallas kernels, shards(): pl.pallas_call(_near_kernel, out_shape=jax.ShapeDtypeStruct((source_count...  6.25 us
    ppermute x3, starting transfers between devices, _all_gather(): other = lax.ppermute(current, axis_name, _pair_perm(count, bit))  4.96 us
    ppermute x3, starting transfers between devices, _reduce_scatter(): lax.ppermute(current[half:], axis_name, _pair_perm(count, bit))  4.74 us
    ppermute x3, starting transfers between devices, _exchange(): lax.ppermute(x, axis_name, [(i, i ^ p) for i in range(count)])  3.49 us
    pallas_call x1, Pallas kernels, shards(): pl.pallas_call(_far_kernel, out_shape=jax.ShapeDtypeStruct((source_count,...  2.97 us
    pallas_call x1, Pallas kernels, shards(): pl.pallas_call(_excite_kernel, out_shape=(jax.ShapeDtypeStruct((2, source...  2.92 us
  transfers between devices with their start and end apart: 9, of which 5 were waited for; matrix products, arithmetic and copies ran while one was open for 10% of the time, Pallas kernels for 10%

profile of v6, /device:TPU:0, one launch (start us, length us, event | category | flops | bytes accessed | tf_op | source)
XLA Modules:
  0.0 62.5 jit_solution(246554744601503194)
XLA Ops:
  0.0 0.0 copy-start
  0.0 1.0 %reshape_squeeze.6 = bf16[32,8,256]{2,1,0:T(8,128)(2,1)S(1)} reshape(bf16[1,32,8,2,128]{4,3,2,1,0:T(2,128)(2,1)} %param.12) | data formatting | bytes 262144 | tf_op jit(solution)/shard_map/reshape;squeeze | solution.py:196
  1.0 4.1 %collective-permute-start = (bf16[32,8,256]{2,1,0:T(8,128)(2,1)S(1)}, bf16[32,8,256]{2,1,0:T(8,128)(2,1)S(1)}, u32[]{:S(2)}, u32[]{:S(2)}) collective-permute-start(bf16[32,8,256]{2,1,0:T(8,128)(2,1)S(1)} %reshape_squeeze.6), channel_id=1, source_target_pairs={{0,16},{4,20},{8,24},{12,28},{16,0},{20,4},{24,8},{28,12},{1,17},{... | collective-permute-start | bytes 393224 | tf_op jit(solution)/shard_map/ppermute | solution.py:152
  5.1 0.0 copy-done
  5.1 0.1 constant_dynamic-slice_fusion
  5.2 6.2 %collective-permute-done = bf16[32,8,256]{2,1,0:T(8,128)(2,1)S(1)} collective-permute-done((bf16[32,8,256]{2,1,0:T(8,128)(2,1)S(1)}, bf16[32,8,256]{2,1,0:T(8,128)(2,1)S(1)}, u32[]{:S(2)}, u32[]{:S(2)}) %collective-permute-start) | collective-permute-done | bytes 131104 | tf_op jit(solution)/shard_map/ppermute | solution.py:152
  11.4 0.8 %collective-permute-start.1 = (bf16[32,16,256]{2,1,0:T(8,128)(2,1)S(1)}, bf16[32,16,256]{2,1,0:T(8,128)(2,1)S(1)}, u32[]{:S(2)}, u32[]{:S(2)}) collective-permute-start(bf16[32,16,256]{2,1,0:T(8,128)(2,1)S(1)} %pad_maximum_fusion.2), channel_id=1, source_target_pairs={{0,8},{4,12},{8,0},{12,4},{16,24},{20,28},{24,16},{28,20},{1,9},{5... | collective-permute-start | bytes 786440 | tf_op jit(solution)/shard_map/ppermute | solution.py:152
  12.9 0.1 broadcast_in_dim.14
  13.0 0.1 broadcast_in_dim.15
  13.1 0.8 %reshape_squeeze.7 = bf16[2,32,4,32]{3,2,1,0:T(4,128)(2,1)S(1)} reshape(bf16[1,1,2,32,128]{4,3,2,1,0:T(8,128)(2,1)} %param.21) | data formatting | bytes 32768 | tf_op jit(solution)/shard_map/reshape;squeeze | solution.py:219
  13.9 0.6 gather_fusion
  14.5 0.1 copy.18
  14.5 0.1 gather.7
  14.6 0.7 %convert_bitcast_fusion = f32[32,2]{0,1:T(2,128)S(1)} fusion(s32[1,32,2]{1,2,0:T(2,128)} %param.14), kind=kLoop, calls=%fused_computation.13 | loop fusion | flops 64 | bytes 512 | tf_op jit(solution)/shard_map/convert_element_type | solution.py:190
  15.3 3.7 %collective-permute-done.1 = bf16[32,16,256]{2,1,0:T(8,128)(2,1)S(1)} collective-permute-done((bf16[32,16,256]{2,1,0:T(8,128)(2,1)S(1)}, bf16[32,16,256]{2,1,0:T(8,128)(2,1)S(1)}, u32[]{:S(2)}, u32[]{:S(2)}) %collective-permute-start.1) | collective-permute-done | bytes 262176 | tf_op jit(solution)/shard_map/ppermute | solution.py:152
  19.0 0.1 pad_maximum_fusion.1
  19.1 0.1 collective-permute-start.2
  19.1 0.5 fusion.1
  19.7 1.8 %reduce-precision_bitcast_fusion = (f32[32]{0:T(128)}, f32[32,1]{0,1:T(1,128)S(1)}) fusion(f32[32,2]{0,1:T(2,128)S(1)} %convert_bitcast_fusion, f32[]{:T(128)} %bitcast.5, f32[]{:T(128)} %bitcast.3), kind=kLoop, calls=%fused_computation.15 | loop fusion | flops 128 | bytes 520 | tf_op jit(solution)/shard_map/reduce_precision | solution.py:194
  21.5 0.6 reduce-precision_bitcast_fusion.1.cos_ref
  22.1 0.0 collective-permute-done.2
  22.1 1.1 %pad_maximum_fusion.g_ref = bf16[32,64,256]{2,1,0:T(8,128)(2,1)} fusion(bf16[32,32,256]{2,1,0:T(8,128)(2,1)S(1)} %collective-permute-done.2, bf16[32,16,256]{2,1,0:T(8,128)(2,1)S(1)} %collective-permute-done.1, bf16[32,8,256]{2,1,0:T(8,128)(2,1)S(1)} %collective-permute-done, bf16[32,8,256]{2,1,0:T(8,128)(2,1)S(1)} %reshape_squeeze.6), kind=kLoop, calls=%fused_computation.1 | loop fusion | flops 4194304 | bytes 2097152 | tf_op jit(solution)/shard_map/concatenate | solution.py:153
  23.2 2.9 %shard_map.118 = (bf16[2,64,2048]{2,1,0:T(8,128)(2,1)}, bf16[2,64,32]{2,1,0:T(8,128)(2,1)}) custom-call(s32[32]{0:T(128)} %bitcast.39, f32[32]{0:T(128)} %reduce-precision_bitcast_fusion.1.cos_ref, f32[32]{0:T(128)} %get-tuple-element.9.sin_ref, s32[1]{0:T(128)} %bitcast.26.rank_ref, bf16[32,64,256]{2,1,0:T(8,128)(2,1)} %pad_maximum_fusion.g_ref, ...), custom_call_target="tpu_custom_call" | custom-call | tf_op jit(solution)/shard_map/pallas_call | solution.py:201
  26.1 2.2 %collective-permute-start.5 = (bf16[2,64,32]{2,1,0:T(8,128)(2,1)}, bf16[2,64,32]{2,1,0:T(8,128)(2,1)S(1)}, u32[]{:S(2)}, u32[]{:S(2)}) collective-permute-start(bf16[2,64,32]{2,1,0:T(8,128)(2,1)} %get-tuple-element.8), channel_id=1, source_target_pairs={{0,3},{1,2},{2,1},{3,0},{4,7},{5,6},{6,5},{7,4},{8,11},{9,10},{10,... | collective-permute-start | bytes 24584 | tf_op jit(solution)/shard_map/ppermute | solution.py:161
  28.3 0.5 collective-permute-start.4
  28.8 0.8 %collective-permute-start.3 = (bf16[2,64,32]{2,1,0:T(8,128)(2,1)}, bf16[2,64,32]{2,1,0:T(8,128)(2,1)S(1)}, u32[]{:S(2)}, u32[]{:S(2)}) collective-permute-start(bf16[2,64,32]{2,1,0:T(8,128)(2,1)} %get-tuple-element.8), channel_id=1, source_target_pairs={{0,1},{1,0},{2,3},{3,2},{4,5},{5,4},{6,7},{7,6},{8,9},{9,8},{10,11... | collective-permute-start | bytes 24584 | tf_op jit(solution)/shard_map/ppermute | solution.py:161
  29.6 0.6 broadcast_select_fusion.cp_ref
  30.2 0.0 copy-start.1
  30.2 6.3 %shard_map.119.near_ref = f32[64,4096]{1,0:T(8,128)} custom-call(bf16[2,64,2048]{2,1,0:T(8,128)(2,1)} %get-tuple-element.7.e_ref, bf16[2,2048,256]{2,1,0:T(8,128)(2,1)} %bitcast.28, bf16[3,2,32,2048]{3,2,1,0:T(8,128)(2,1)} %bitcast.29, bf16[3,2,32,2048]{3,2,1,0:T(8,128)(2,1)} %bitcast.30), custom_call_target="tpu_custom_call" | custom-call | tf_op jit(solution)/shard_map/pallas_call | solution.py:222
  36.4 0.0 collective-permute-done.5
  36.4 0.0 collective-permute-done.4
  36.4 0.0 collective-permute-done.3
  36.4 0.0 copy-done.1
  36.5 0.7 %pad_maximum_fusion.3.bpa_ref = bf16[4,2,64,32]{3,2,1,0:T(8,128)(2,1)} fusion(bf16[1,2,64,32]{3,2,1,0:T(8,128)(2,1)S(1)} %bitcast.36, bf16[1,2,64,32]{3,2,1,0:T(8,128)(2,1)S(1)} %bitcast.37, bf16[1,2,64,32]{3,2,1,0:T(8,128)(2,1)S(1)} %bitcast.38, bf16[1,2,64,32]{3,2,1,0:T(8,128)(2,1)S(1)} %bitcast.35), kind=kLoop, calls=%fused_computation.7 | loop fusion | flops 49152 | bytes 65536 | tf_op jit(solution)/shard_map/stack | solution.py:162
  37.1 3.0 %shard_map.120 = f32[64,4096]{1,0:T(8,128)} custom-call(f32[2]{0:T(128)} %bitcast.40, s32[1]{0:T(128)} %bitcast.27.rank_ref, f32[64,4096]{1,0:T(8,128)} %shard_map.119.near_ref, bf16[2,32,2048]{2,1,0:T(8,128)(2,1)} %bitcast.33, bf16[2,32,128]{2,1,0:T(8,128)(2,1)} %broadcast_select_fusion.cp_ref, ...), custom_call_target="tpu_custom_call", output_to_operand_aliasing={{}: (2, {})} | custom-call | tf_op jit(solution)/shard_map/pallas_call | solution.py:230
  40.1 1.1 %slice.43 = f32[32,4096]{1,0:T(8,128)S(1)} slice(f32[64,4096]{1,0:T(8,128)} %shard_map.120), slice={[32:64], [0:4096]} | slice | bytes 1048576 | tf_op jit(solution)/shard_map/slice | solution.py:144
  41.2 0.1 collective-permute-start.6
  41.3 1.9 %collective-permute-done.6 = f32[32,4096]{1,0:T(8,128)S(1)} collective-permute-done((f32[32,4096]{1,0:T(8,128)S(1)}, f32[32,4096]{1,0:T(8,128)S(1)}, u32[]{:S(2)}, u32[]{:S(2)}) %collective-permute-start.6) | collective-permute-done | bytes 524320 | tf_op jit(solution)/shard_map/ppermute | solution.py:144
  43.2 1.1 %slice_add_fusion = f32[32,4096]{1,0:T(8,128)S(1)} fusion(f32[32,4096]{1,0:T(8,128)S(1)} %collective-permute-done.6, f32[64,4096]{1,0:T(8,128)} %shard_map.120), kind=kLoop, calls=%fused_computation.2 | loop fusion | flops 131072 | bytes 1572864 | tf_op jit(solution)/shard_map/add | solution.py:144
  44.3 1.5 %collective-permute-start.7 = (f32[16,4096]{1,0:T(8,128)S(1)}, f32[16,4096]{1,0:T(8,128)S(1)}, u32[]{:S(2)}, u32[]{:S(2)}) collective-permute-start(f32[16,4096]{1,0:T(8,128)S(1)} %slice.45), channel_id=1, source_target_pairs={{0,8},{4,12},{8,0},{12,4},{16,24},{20,28},{24,16},{28,20},{1,9},{5... | collective-permute-start | bytes 786440 | tf_op jit(solution)/shard_map/ppermute | solution.py:144
  45.8 6.9 %collective-permute-done.7 = f32[16,4096]{1,0:T(8,128)S(1)} collective-permute-done((f32[16,4096]{1,0:T(8,128)S(1)}, f32[16,4096]{1,0:T(8,128)S(1)}, u32[]{:S(2)}, u32[]{:S(2)}) %collective-permute-start.7) | collective-permute-done | bytes 262176 | tf_op jit(solution)/shard_map/ppermute | solution.py:144
  52.8 3.2 %collective-permute-start.8 = (f32[8,4096]{1,0:T(8,128)S(1)}, f32[8,4096]{1,0:T(8,128)S(1)}, u32[]{:S(2)}, u32[]{:S(2)}) collective-permute-start(f32[8,4096]{1,0:T(8,128)S(1)} %slice.47), channel_id=1, source_target_pairs={{0,16},{4,20},{8,24},{12,28},{16,0},{20,4},{24,8},{28,12},{1,17},{... | collective-permute-start | bytes 393224 | tf_op jit(solution)/shard_map/ppermute | solution.py:144
  56.0 5.8 %collective-permute-done.8 = f32[8,4096]{1,0:T(8,128)S(1)} collective-permute-done((f32[8,4096]{1,0:T(8,128)S(1)}, f32[8,4096]{1,0:T(8,128)S(1)}, u32[]{:S(2)}, u32[]{:S(2)}) %collective-permute-start.8) | collective-permute-done | bytes 131104 | tf_op jit(solution)/shard_map/ppermute | solution.py:144
  61.8 0.8 %copy.19 = f32[8,2,2048]{2,1,0:T(2,128)} copy(f32[8,2,2048]{2,0,1:T(8,128)S(1)} %bitcast.31) | data formatting | bytes 262144 | tf_op jit(solution)/shard_map/reshape | solution.py:239
  (9 shorter events, 0.1 us)
Async XLA Ops:
  0.0 5.1 %copy-start = (f32[8,2]{0,1:T(2,128)S(1)}, f32[8,2]{0,1:T(2,128)}, u32[]{:S(2)}) copy-start(f32[8,2]{0,1:T(2,128)} %param.15) | copy-start | bytes 196
  1.0 10.4 %collective-permute-start = (bf16[32,8,256]{2,1,0:T(8,128)(2,1)S(1)}, bf16[32,8,256]{2,1,0:T(8,128)(2,1)S(1)}, u32[]{:S(2)}, u32[]{:S(2)}) collective-permute-start(bf16[32,8,256]{2,1,0:T(8,128)(2,1)S(1)} %reshape_squeeze.6), channel_id=1, source_target_pairs={{0,16},{4,20},{8,24},{12,28},{16,0},{20,4},{24,8},{28,12},{1,17},{... | collective-permute-start | bytes 393224 | tf_op jit(solution)/shard_map/ppermute | solution.py:152
  11.4 7.6 %collective-permute-start.1 = (bf16[32,16,256]{2,1,0:T(8,128)(2,1)S(1)}, bf16[32,16,256]{2,1,0:T(8,128)(2,1)S(1)}, u32[]{:S(2)}, u32[]{:S(2)}) collective-permute-start(bf16[32,16,256]{2,1,0:T(8,128)(2,1)S(1)} %pad_maximum_fusion.2), channel_id=1, source_target_pairs={{0,8},{4,12},{8,0},{12,4},{16,24},{20,28},{24,16},{28,20},{1,9},{5... | collective-permute-start | bytes 786440 | tf_op jit(solution)/shard_map/ppermute | solution.py:152
  19.1 3.0 %collective-permute-start.2 = (bf16[32,32,256]{2,1,0:T(8,128)(2,1)S(1)}, bf16[32,32,256]{2,1,0:T(8,128)(2,1)S(1)}, u32[]{:S(2)}, u32[]{:S(2)}) collective-permute-start(bf16[32,32,256]{2,1,0:T(8,128)(2,1)S(1)} %pad_maximum_fusion.1), channel_id=1, source_target_pairs={{0,4},{4,0},{8,12},{12,8},{16,20},{20,16},{24,28},{28,24},{1,5},{5... | collective-permute-start | bytes 1572872 | tf_op jit(solution)/shard_map/ppermute | solution.py:152
  26.1 10.4 %collective-permute-start.5 = (bf16[2,64,32]{2,1,0:T(8,128)(2,1)}, bf16[2,64,32]{2,1,0:T(8,128)(2,1)S(1)}, u32[]{:S(2)}, u32[]{:S(2)}) collective-permute-start(bf16[2,64,32]{2,1,0:T(8,128)(2,1)} %get-tuple-element.8), channel_id=1, source_target_pairs={{0,3},{1,2},{2,1},{3,0},{4,7},{5,6},{6,5},{7,4},{8,11},{9,10},{10,... | collective-permute-start | bytes 24584 | tf_op jit(solution)/shard_map/ppermute | solution.py:161
  28.3 8.2 %collective-permute-start.4 = (bf16[2,64,32]{2,1,0:T(8,128)(2,1)}, bf16[2,64,32]{2,1,0:T(8,128)(2,1)S(1)}, u32[]{:S(2)}, u32[]{:S(2)}) collective-permute-start(bf16[2,64,32]{2,1,0:T(8,128)(2,1)} %get-tuple-element.8), channel_id=1, source_target_pairs={{0,2},{1,3},{2,0},{3,1},{4,6},{5,7},{6,4},{7,5},{8,10},{9,11},{10,... | collective-permute-start | bytes 24584 | tf_op jit(solution)/shard_map/ppermute | solution.py:161
  28.8 7.7 %collective-permute-start.3 = (bf16[2,64,32]{2,1,0:T(8,128)(2,1)}, bf16[2,64,32]{2,1,0:T(8,128)(2,1)S(1)}, u32[]{:S(2)}, u32[]{:S(2)}) collective-permute-start(bf16[2,64,32]{2,1,0:T(8,128)(2,1)} %get-tuple-element.8), channel_id=1, source_target_pairs={{0,1},{1,0},{2,3},{3,2},{4,5},{5,4},{6,7},{7,6},{8,9},{9,8},{10,11... | collective-permute-start | bytes 24584 | tf_op jit(solution)/shard_map/ppermute | solution.py:161
  30.2 6.3 %copy-start.1 = (bf16[2,64,32]{2,1,0:T(8,128)(2,1)S(1)}, bf16[2,64,32]{2,1,0:T(8,128)(2,1)}, u32[]{:S(2)}) copy-start(bf16[2,64,32]{2,1,0:T(8,128)(2,1)} %get-tuple-element.8) | copy-start | bytes 24580
  41.2 2.0 %collective-permute-start.6 = (f32[32,4096]{1,0:T(8,128)S(1)}, f32[32,4096]{1,0:T(8,128)S(1)}, u32[]{:S(2)}, u32[]{:S(2)}) collective-permute-start(f32[32,4096]{1,0:T(8,128)S(1)} %slice.43), channel_id=1, source_target_pairs={{0,4},{4,0},{8,12},{12,8},{16,20},{20,16},{24,28},{28,24},{1,5},{5... | collective-permute-start | bytes 1572872 | tf_op jit(solution)/shard_map/ppermute | solution.py:144
  44.3 8.4 %collective-permute-start.7 = (f32[16,4096]{1,0:T(8,128)S(1)}, f32[16,4096]{1,0:T(8,128)S(1)}, u32[]{:S(2)}, u32[]{:S(2)}) collective-permute-start(f32[16,4096]{1,0:T(8,128)S(1)} %slice.45), channel_id=1, source_target_pairs={{0,8},{4,12},{8,0},{12,4},{16,24},{20,28},{24,16},{28,20},{1,9},{5... | collective-permute-start | bytes 786440 | tf_op jit(solution)/shard_map/ppermute | solution.py:144
  52.8 8.9 %collective-permute-start.8 = (f32[8,4096]{1,0:T(8,128)S(1)}, f32[8,4096]{1,0:T(8,128)S(1)}, u32[]{:S(2)}, u32[]{:S(2)}) collective-permute-start(f32[8,4096]{1,0:T(8,128)S(1)} %slice.47), channel_id=1, source_target_pairs={{0,16},{4,20},{8,24},{12,28},{16,0},{20,4},{24,8},{28,12},{1,17},{... | collective-permute-start | bytes 393224 | tf_op jit(solution)/shard_map/ppermute | solution.py:144

commit v7 on v6

--- a/solution.py
+++ b/solution.py
@@ -136,10 +136,10 @@
     return [(i, i ^ (1 << bit)) for i in range(count)]
 
 
-def _reduce_scatter(x, axis_name):
+def _reduce_scatter(keep, give, axis_name):
     count = lax.axis_size(axis_name)
-    current = x
-    for bit in range(count.bit_length() - 1):
+    current = keep + lax.ppermute(give, axis_name, _pair_perm(count, 0))
+    for bit in range(1, count.bit_length() - 1):
         half = current.shape[0] // 2
         current = current[:half] + lax.ppermute(current[half:], axis_name, _pair_perm(count, bit))
     return current
@@ -227,15 +227,25 @@
         scratch_shapes=[pltpu.VMEM((2 ** (levels + 1) - 2, 2, source_count, rank_width), jnp.bfloat16)],
     )(excitation, leaf_inverse[0], level_right[0], level_left[0])
 
-    field = pl.pallas_call(
-        _far_kernel,
-        out_shape=jax.ShapeDtypeStruct((source_count, 2 * row_count), jnp.float32),
-        in_specs=[_SMEM, _SMEM] + [_VMEM] * 4,
-        out_specs=_VMEM,
-        scratch_shapes=[pltpu.VMEM((2, source_count, rank_width), jnp.bfloat16)],
-        input_output_aliases={2: 0},
-    )(quad_weight[0], rank, near, block_left[0], coupling, all_projected)
-    summed = _reduce_scatter(field, "ang")
+    half = source_count // 2
+    halves = []
+    for h in (1, 0):
+        halves.append(pl.pallas_call(
+            _far_kernel,
+            out_shape=jax.ShapeDtypeStruct((half, 2 * row_count), jnp.float32),
+            grid=(1,),
+            in_specs=[
+                _SMEM,
+                _SMEM,
+                pl.BlockSpec((half, 2 * row_count), lambda i, h=h: (h, 0)),
+                pl.BlockSpec(block_left.shape[1:], lambda i: (0, 0, 0)),
+                pl.BlockSpec(coupling.shape, lambda i: (0, 0, 0)),
+                pl.BlockSpec((row_blocks, 2, half, rank_width), lambda i, h=h: (0, 0, h, 0)),
+            ],
+            out_specs=pl.BlockSpec((half, 2 * row_count), lambda i: (0, 0)),
+            scratch_shapes=[pltpu.VMEM((2, half, rank_width), jnp.bfloat16)],
+        )(quad_weight[0], rank, near, block_left[0], coupling, all_projected))
+    summed = _reduce_scatter(halves[1], halves[0], "ang")
     return summed.reshape(summed.shape[0], 2, row_count)
 
 

time: 62.9 us -> 62.6 us (level)
  Pallas kernels: 12.1 us -> 14.1 us
  waiting for transfers between devices: 24.5 us -> 23.4 us
  local copies, waits for them, and re-layouts: 5.16 us -> 4.09 us
    pallas_call x1 -> x2, Pallas kernels: 2.97 us -> 4.96 us  [shards(): pl.pallas_call(_far_kernel, out_shape=jax.ShapeDtypeStruct((half, 2 * row...]
    add x0 -> x1, other arithmetic: none -> 1.13 us  [_reduce_scatter(): current = keep + lax.ppermute(give, axis_name, _pair_perm(count, 0))]
    add x3 -> x2, other arithmetic: 1.17 us -> 0.04 us  [_reduce_scatter(): current[:half]]
    ppermute x3 -> x2, waiting for transfers between devices: 14.6 us -> 13.5 us  [_reduce_scatter(): lax.ppermute(current[half:], axis_name, _pair_perm(count, bit))]
    slice x3 -> x2, local copies, waits for them, and re-layouts: 1.1 us -> 0.03 us  [_reduce_scatter(): current[half:]]
    ppermute x3 -> x2, starting transfers between devices: 4.74 us -> 4.69 us  [_reduce_scatter(): lax.ppermute(current[half:], axis_name, _pair_perm(count, bit))]
  transfers between devices with their start and end apart: 9 -> 9, of which waited for: 5 -> 4; matrix products, arithmetic and copies ran while one was open for 10% -> 10% of each run, Pallas kernels for 10% -> 14%
where the time goes in v7:
time: 62.6 us; the launch traced here: 62.3 us
  waiting for transfers between devices  23.4 us (37%)
  Pallas kernels  14.1 us (23%)
  starting transfers between devices  13.1 us (21%)
  other arithmetic  6.76 us (11%)
  local copies, waits for them, and re-layouts  4.09 us (7%)
  between operations  0.76 us (1%)
    ppermute x2, waiting for transfers between devices, _reduce_scatter(): lax.ppermute(current[half:], axis_name, _pair_perm(count, bit))  13.5 us
    ppermute x3, waiting for transfers between devices, _all_gather(): other = lax.ppermute(current, axis_name, _pair_perm(count, bit))  9.92 us
    pallas_call x1, Pallas kernels, shards(): pl.pallas_call(_near_kernel, out_shape=jax.ShapeDtypeStruct((source_count...  6.25 us
    pallas_call x2, Pallas kernels, shards(): pl.pallas_call(_far_kernel, out_shape=jax.ShapeDtypeStruct((half, 2 * row...  4.96 us
    ppermute x3, starting transfers between devices, _all_gather(): other = lax.ppermute(current, axis_name, _pair_perm(count, bit))  4.96 us
    ppermute x2, starting transfers between devices, _reduce_scatter(): lax.ppermute(current[half:], axis_name, _pair_perm(count, bit))  4.69 us
    ppermute x3, starting transfers between devices, _exchange(): lax.ppermute(x, axis_name, [(i, i ^ p) for i in range(count)])  3.49 us
    pallas_call x1, Pallas kernels, shards(): pl.pallas_call(_excite_kernel, out_shape=(jax.ShapeDtypeStruct((2, source...  2.92 us
  transfers between devices with their start and end apart: 9, of which 4 were waited for; matrix products, arithmetic and copies ran while one was open for 10% of the time, Pallas kernels for 14%

profile of v7, /device:TPU:0, one launch (start us, length us, event | category | flops | bytes accessed | tf_op | source)
XLA Modules:
  0.0 62.3 jit_solution(12199334026959373732)
XLA Ops:
  0.0 0.0 copy-start
  0.0 1.0 %reshape_squeeze.6 = bf16[32,8,256]{2,1,0:T(8,128)(2,1)S(1)} reshape(bf16[1,32,8,2,128]{4,3,2,1,0:T(2,128)(2,1)} %param.12) | data formatting | bytes 262144 | tf_op jit(solution)/shard_map/reshape;squeeze | solution.py:196
  1.0 4.1 %collective-permute-start = (bf16[32,8,256]{2,1,0:T(8,128)(2,1)S(1)}, bf16[32,8,256]{2,1,0:T(8,128)(2,1)S(1)}, u32[]{:S(2)}, u32[]{:S(2)}) collective-permute-start(bf16[32,8,256]{2,1,0:T(8,128)(2,1)S(1)} %reshape_squeeze.6), channel_id=1, source_target_pairs={{0,16},{4,20},{8,24},{12,28},{16,0},{20,4},{24,8},{28,12},{1,17},{... | collective-permute-start | bytes 393224 | tf_op jit(solution)/shard_map/ppermute | solution.py:152
  5.1 0.0 copy-done
  5.1 0.1 constant_dynamic-slice_fusion
  5.2 6.2 %collective-permute-done = bf16[32,8,256]{2,1,0:T(8,128)(2,1)S(1)} collective-permute-done((bf16[32,8,256]{2,1,0:T(8,128)(2,1)S(1)}, bf16[32,8,256]{2,1,0:T(8,128)(2,1)S(1)}, u32[]{:S(2)}, u32[]{:S(2)}) %collective-permute-start) | collective-permute-done | bytes 131104 | tf_op jit(solution)/shard_map/ppermute | solution.py:152
  11.4 0.8 %collective-permute-start.1 = (bf16[32,16,256]{2,1,0:T(8,128)(2,1)S(1)}, bf16[32,16,256]{2,1,0:T(8,128)(2,1)S(1)}, u32[]{:S(2)}, u32[]{:S(2)}) collective-permute-start(bf16[32,16,256]{2,1,0:T(8,128)(2,1)S(1)} %pad_maximum_fusion.2), channel_id=1, source_target_pairs={{0,8},{4,12},{8,0},{12,4},{16,24},{20,28},{24,16},{28,20},{1,9},{5... | collective-permute-start | bytes 786440 | tf_op jit(solution)/shard_map/ppermute | solution.py:152
  12.9 0.1 broadcast_in_dim.14
  13.0 0.1 broadcast_in_dim.15
  13.1 0.8 %reshape_squeeze.7 = bf16[2,32,4,32]{3,2,1,0:T(4,128)(2,1)S(1)} reshape(bf16[1,1,2,32,128]{4,3,2,1,0:T(8,128)(2,1)} %param.21) | data formatting | bytes 32768 | tf_op jit(solution)/shard_map/reshape;squeeze | solution.py:219
  13.9 0.6 gather_fusion
  14.5 0.1 copy.17
  14.5 0.1 gather.7
  14.6 0.7 %convert_bitcast_fusion = f32[32,2]{0,1:T(2,128)S(1)} fusion(s32[1,32,2]{1,2,0:T(2,128)} %param.14), kind=kLoop, calls=%fused_computation.12 | loop fusion | flops 64 | bytes 512 | tf_op jit(solution)/shard_map/convert_element_type | solution.py:190
  15.3 3.7 %collective-permute-done.1 = bf16[32,16,256]{2,1,0:T(8,128)(2,1)S(1)} collective-permute-done((bf16[32,16,256]{2,1,0:T(8,128)(2,1)S(1)}, bf16[32,16,256]{2,1,0:T(8,128)(2,1)S(1)}, u32[]{:S(2)}, u32[]{:S(2)}) %collective-permute-start.1) | collective-permute-done | bytes 262176 | tf_op jit(solution)/shard_map/ppermute | solution.py:152
  19.0 0.1 pad_maximum_fusion.1
  19.1 0.1 collective-permute-start.2
  19.1 0.5 fusion.1
  19.7 1.9 %reduce-precision_bitcast_fusion = (f32[32]{0:T(128)}, f32[32,1]{0,1:T(1,128)S(1)}) fusion(f32[32,2]{0,1:T(2,128)S(1)} %convert_bitcast_fusion, f32[]{:T(128)} %bitcast.5, f32[]{:T(128)} %bitcast.3), kind=kLoop, calls=%fused_computation.14 | loop fusion | flops 128 | bytes 520 | tf_op jit(solution)/shard_map/reduce_precision | solution.py:194
  21.5 0.6 reduce-precision_bitcast_fusion.1.cos_ref
  22.1 0.0 collective-permute-done.2
  22.1 1.1 %pad_maximum_fusion.g_ref = bf16[32,64,256]{2,1,0:T(8,128)(2,1)} fusion(bf16[32,32,256]{2,1,0:T(8,128)(2,1)S(1)} %collective-permute-done.2, bf16[32,16,256]{2,1,0:T(8,128)(2,1)S(1)} %collective-permute-done.1, bf16[32,8,256]{2,1,0:T(8,128)(2,1)S(1)} %collective-permute-done, bf16[32,8,256]{2,1,0:T(8,128)(2,1)S(1)} %reshape_squeeze.6), kind=kLoop, calls=%fused_computation.1 | loop fusion | flops 4194304 | bytes 2097152 | tf_op jit(solution)/shard_map/concatenate | solution.py:153
  23.2 2.9 %shard_map.118 = (bf16[2,64,2048]{2,1,0:T(8,128)(2,1)}, bf16[2,64,32]{2,1,0:T(8,128)(2,1)}) custom-call(s32[32]{0:T(128)} %bitcast.43, f32[32]{0:T(128)} %reduce-precision_bitcast_fusion.1.cos_ref, f32[32]{0:T(128)} %get-tuple-element.9.sin_ref, s32[1]{0:T(128)} %bitcast.26.rank_ref, bf16[32,64,256]{2,1,0:T(8,128)(2,1)} %pad_maximum_fusion.g_ref, ...), custom_call_target="tpu_custom_call" | custom-call | tf_op jit(solution)/shard_map/pallas_call | solution.py:201
  26.1 2.2 %collective-permute-start.5 = (bf16[2,64,32]{2,1,0:T(8,128)(2,1)}, bf16[2,64,32]{2,1,0:T(8,128)(2,1)S(1)}, u32[]{:S(2)}, u32[]{:S(2)}) collective-permute-start(bf16[2,64,32]{2,1,0:T(8,128)(2,1)} %get-tuple-element.8), channel_id=1, source_target_pairs={{0,3},{1,2},{2,1},{3,0},{4,7},{5,6},{6,5},{7,4},{8,11},{9,10},{10,... | collective-permute-start | bytes 24584 | tf_op jit(solution)/shard_map/ppermute | solution.py:161
  28.3 0.5 collective-permute-start.4
  28.8 0.8 %collective-permute-start.3 = (bf16[2,64,32]{2,1,0:T(8,128)(2,1)}, bf16[2,64,32]{2,1,0:T(8,128)(2,1)S(1)}, u32[]{:S(2)}, u32[]{:S(2)}) collective-permute-start(bf16[2,64,32]{2,1,0:T(8,128)(2,1)} %get-tuple-element.8), channel_id=1, source_target_pairs={{0,1},{1,0},{2,3},{3,2},{4,5},{5,4},{6,7},{7,6},{8,9},{9,8},{10,11... | collective-permute-start | bytes 24584 | tf_op jit(solution)/shard_map/ppermute | solution.py:161
  29.6 0.6 broadcast_select_fusion.cp_ref
  30.2 0.0 copy-start.1
  30.2 6.2 %shard_map.119.near_ref = f32[64,4096]{1,0:T(8,128)} custom-call(bf16[2,64,2048]{2,1,0:T(8,128)(2,1)} %get-tuple-element.7.e_ref, bf16[2,2048,256]{2,1,0:T(8,128)(2,1)} %bitcast.29, bf16[3,2,32,2048]{3,2,1,0:T(8,128)(2,1)} %bitcast.32, bf16[3,2,32,2048]{3,2,1,0:T(8,128)(2,1)} %bitcast.33), custom_call_target="tpu_custom_call" | custom-call | tf_op jit(solution)/shard_map/pallas_call | solution.py:222
  36.4 0.0 collective-permute-done.5
  36.4 0.0 collective-permute-done.4
  36.4 0.0 collective-permute-done.3
  36.4 0.0 copy-done.1
  36.5 0.7 %pad_maximum_fusion.3.bpa_ref = bf16[4,2,64,32]{3,2,1,0:T(8,128)(2,1)} fusion(bf16[1,2,64,32]{3,2,1,0:T(8,128)(2,1)S(1)} %bitcast.38, bf16[1,2,64,32]{3,2,1,0:T(8,128)(2,1)S(1)} %bitcast.39, bf16[1,2,64,32]{3,2,1,0:T(8,128)(2,1)S(1)} %bitcast.40, bf16[1,2,64,32]{3,2,1,0:T(8,128)(2,1)S(1)} %bitcast.37), kind=kLoop, calls=%fused_computation.6 | loop fusion | flops 49152 | bytes 65536 | tf_op jit(solution)/shard_map/stack | solution.py:162
  37.2 2.5 %shard_map.121 = f32[32,4096]{1,0:T(8,128)} custom-call(f32[2]{0:T(128)} %bitcast.41, s32[1]{0:T(128)} %bitcast.28.rank_ref, f32[64,4096]{1,0:T(8,128)} %shard_map.119.near_ref, bf16[2,32,2048]{2,1,0:T(8,128)(2,1)} %bitcast.30, bf16[2,32,128]{2,1,0:T(8,128)(2,1)} %broadcast_select_fusion.cp_ref, bf16[4,2,64,32]{3,2,1,0:T(8,128)(2,1)} %pad_maximum_fusion.3.bpa_ref), custom_call_target="tpu_custom_call" | custom-call | tf_op jit(solution)/shard_map/pallas_call | solution.py:233
  39.6 0.0 collective-permute-start.6
  39.6 2.5 %shard_map.120 = f32[32,4096]{1,0:T(8,128)} custom-call(f32[2]{0:T(128)} %bitcast.42, s32[1]{0:T(128)} %bitcast.27.rank_ref, f32[64,4096]{1,0:T(8,128)} %shard_map.119.near_ref, bf16[2,32,2048]{2,1,0:T(8,128)(2,1)} %bitcast.31, bf16[2,32,128]{2,1,0:T(8,128)(2,1)} %broadcast_select_fusion.cp_ref, bf16[4,2,64,32]{3,2,1,0:T(8,128)(2,1)} %pad_maximum_fusion.3.bpa_ref), custom_call_target="tpu_custom_call" | custom-call | tf_op jit(solution)/shard_map/pallas_call | solution.py:233
  42.1 0.0 collective-permute-done.6
  42.1 1.1 %add.35 = f32[32,4096]{1,0:T(8,128)S(1)} add(f32[32,4096]{1,0:T(8,128)} %shard_map.120, f32[32,4096]{1,0:T(8,128)S(1)} %collective-permute-done.6) | non-fusion elementwise | flops 131072 | bytes 1572864 | tf_op jit(solution)/shard_map/add | solution.py:141
  43.3 1.5 %collective-permute-start.7 = (f32[16,4096]{1,0:T(8,128)S(1)}, f32[16,4096]{1,0:T(8,128)S(1)}, u32[]{:S(2)}, u32[]{:S(2)}) collective-permute-start(f32[16,4096]{1,0:T(8,128)S(1)} %slice.35), channel_id=1, source_target_pairs={{0,8},{4,12},{8,0},{12,4},{16,24},{20,28},{24,16},{28,20},{1,9},{5... | collective-permute-start | bytes 786440 | tf_op jit(solution)/shard_map/ppermute | solution.py:144
  44.8 7.3 %collective-permute-done.7 = f32[16,4096]{1,0:T(8,128)S(1)} collective-permute-done((f32[16,4096]{1,0:T(8,128)S(1)}, f32[16,4096]{1,0:T(8,128)S(1)}, u32[]{:S(2)}, u32[]{:S(2)}) %collective-permute-start.7) | collective-permute-done | bytes 262176 | tf_op jit(solution)/shard_map/ppermute | solution.py:144
  52.1 3.2 %collective-permute-start.8 = (f32[8,4096]{1,0:T(8,128)S(1)}, f32[8,4096]{1,0:T(8,128)S(1)}, u32[]{:S(2)}, u32[]{:S(2)}) collective-permute-start(f32[8,4096]{1,0:T(8,128)S(1)} %slice.37), channel_id=1, source_target_pairs={{0,16},{4,20},{8,24},{12,28},{16,0},{20,4},{24,8},{28,12},{1,17},{... | collective-permute-start | bytes 393224 | tf_op jit(solution)/shard_map/ppermute | solution.py:144
  55.3 6.2 %collective-permute-done.8 = f32[8,4096]{1,0:T(8,128)S(1)} collective-permute-done((f32[8,4096]{1,0:T(8,128)S(1)}, f32[8,4096]{1,0:T(8,128)S(1)}, u32[]{:S(2)}, u32[]{:S(2)}) %collective-permute-start.8) | collective-permute-done | bytes 131104 | tf_op jit(solution)/shard_map/ppermute | solution.py:144
  61.5 0.8 %copy.18 = f32[8,2,2048]{2,1,0:T(2,128)} copy(f32[8,2,2048]{2,0,1:T(8,128)S(1)} %bitcast.34) | data formatting | bytes 262144 | tf_op jit(solution)/shard_map/reshape | solution.py:249
  (9 shorter events, 0.1 us)
Async XLA Ops:
  0.0 5.1 %copy-start = (f32[8,2]{0,1:T(2,128)S(1)}, f32[8,2]{0,1:T(2,128)}, u32[]{:S(2)}) copy-start(f32[8,2]{0,1:T(2,128)} %param.15) | copy-start | bytes 196
  1.0 10.4 %collective-permute-start = (bf16[32,8,256]{2,1,0:T(8,128)(2,1)S(1)}, bf16[32,8,256]{2,1,0:T(8,128)(2,1)S(1)}, u32[]{:S(2)}, u32[]{:S(2)}) collective-permute-start(bf16[32,8,256]{2,1,0:T(8,128)(2,1)S(1)} %reshape_squeeze.6), channel_id=1, source_target_pairs={{0,16},{4,20},{8,24},{12,28},{16,0},{20,4},{24,8},{28,12},{1,17},{... | collective-permute-start | bytes 393224 | tf_op jit(solution)/shard_map/ppermute | solution.py:152
  11.4 7.6 %collective-permute-start.1 = (bf16[32,16,256]{2,1,0:T(8,128)(2,1)S(1)}, bf16[32,16,256]{2,1,0:T(8,128)(2,1)S(1)}, u32[]{:S(2)}, u32[]{:S(2)}) collective-permute-start(bf16[32,16,256]{2,1,0:T(8,128)(2,1)S(1)} %pad_maximum_fusion.2), channel_id=1, source_target_pairs={{0,8},{4,12},{8,0},{12,4},{16,24},{20,28},{24,16},{28,20},{1,9},{5... | collective-permute-start | bytes 786440 | tf_op jit(solution)/shard_map/ppermute | solution.py:152
  19.1 3.0 %collective-permute-start.2 = (bf16[32,32,256]{2,1,0:T(8,128)(2,1)S(1)}, bf16[32,32,256]{2,1,0:T(8,128)(2,1)S(1)}, u32[]{:S(2)}, u32[]{:S(2)}) collective-permute-start(bf16[32,32,256]{2,1,0:T(8,128)(2,1)S(1)} %pad_maximum_fusion.1), channel_id=1, source_target_pairs={{0,4},{4,0},{8,12},{12,8},{16,20},{20,16},{24,28},{28,24},{1,5},{5... | collective-permute-start | bytes 1572872 | tf_op jit(solution)/shard_map/ppermute | solution.py:152
  26.1 10.4 %collective-permute-start.5 = (bf16[2,64,32]{2,1,0:T(8,128)(2,1)}, bf16[2,64,32]{2,1,0:T(8,128)(2,1)S(1)}, u32[]{:S(2)}, u32[]{:S(2)}) collective-permute-start(bf16[2,64,32]{2,1,0:T(8,128)(2,1)} %get-tuple-element.8), channel_id=1, source_target_pairs={{0,3},{1,2},{2,1},{3,0},{4,7},{5,6},{6,5},{7,4},{8,11},{9,10},{10,... | collective-permute-start | bytes 24584 | tf_op jit(solution)/shard_map/ppermute | solution.py:161
  28.3 8.2 %collective-permute-start.4 = (bf16[2,64,32]{2,1,0:T(8,128)(2,1)}, bf16[2,64,32]{2,1,0:T(8,128)(2,1)S(1)}, u32[]{:S(2)}, u32[]{:S(2)}) collective-permute-start(bf16[2,64,32]{2,1,0:T(8,128)(2,1)} %get-tuple-element.8), channel_id=1, source_target_pairs={{0,2},{1,3},{2,0},{3,1},{4,6},{5,7},{6,4},{7,5},{8,10},{9,11},{10,... | collective-permute-start | bytes 24584 | tf_op jit(solution)/shard_map/ppermute | solution.py:161
  28.8 7.7 %collective-permute-start.3 = (bf16[2,64,32]{2,1,0:T(8,128)(2,1)}, bf16[2,64,32]{2,1,0:T(8,128)(2,1)S(1)}, u32[]{:S(2)}, u32[]{:S(2)}) collective-permute-start(bf16[2,64,32]{2,1,0:T(8,128)(2,1)} %get-tuple-element.8), channel_id=1, source_target_pairs={{0,1},{1,0},{2,3},{3,2},{4,5},{5,4},{6,7},{7,6},{8,9},{9,8},{10,11... | collective-permute-start | bytes 24584 | tf_op jit(solution)/shard_map/ppermute | solution.py:161
  30.2 6.3 %copy-start.1 = (bf16[2,64,32]{2,1,0:T(8,128)(2,1)S(1)}, bf16[2,64,32]{2,1,0:T(8,128)(2,1)}, u32[]{:S(2)}) copy-start(bf16[2,64,32]{2,1,0:T(8,128)(2,1)} %get-tuple-element.8) | copy-start | bytes 24580
  39.6 2.5 %collective-permute-start.6 = (f32[32,4096]{1,0:T(8,128)}, f32[32,4096]{1,0:T(8,128)S(1)}, u32[]{:S(2)}, u32[]{:S(2)}) collective-permute-start(f32[32,4096]{1,0:T(8,128)} %shard_map.121), channel_id=1, source_target_pairs={{0,4},{4,0},{8,12},{12,8},{16,20},{20,16},{24,28},{28,24},{1,5},{5... | collective-permute-start | bytes 1572872 | tf_op jit(solution)/shard_map/ppermute | solution.py:141
  43.3 8.8 %collective-permute-start.7 = (f32[16,4096]{1,0:T(8,128)S(1)}, f32[16,4096]{1,0:T(8,128)S(1)}, u32[]{:S(2)}, u32[]{:S(2)}) collective-permute-start(f32[16,4096]{1,0:T(8,128)S(1)} %slice.35), channel_id=1, source_target_pairs={{0,8},{4,12},{8,0},{12,4},{16,24},{20,28},{24,16},{28,20},{1,9},{5... | collective-permute-start | bytes 786440 | tf_op jit(solution)/shard_map/ppermute | solution.py:144
  52.1 9.4 %collective-permute-start.8 = (f32[8,4096]{1,0:T(8,128)S(1)}, f32[8,4096]{1,0:T(8,128)S(1)}, u32[]{:S(2)}, u32[]{:S(2)}) collective-permute-start(f32[8,4096]{1,0:T(8,128)S(1)} %slice.37), channel_id=1, source_target_pairs={{0,16},{4,20},{8,24},{12,28},{16,0},{20,4},{24,8},{28,12},{1,17},{... | collective-permute-start | bytes 393224 | tf_op jit(solution)/shard_map/ppermute | solution.py:144

commit v8 on v7

--- a/solution.py
+++ b/solution.py
@@ -23,8 +23,8 @@
     return lax.broadcasted_iota(jnp.int32, shape, 0) < rank_ref[0]
 
 
-def _excite_kernel(slot_ref, cos_ref, sin_ref, rank_ref, g_ref, br_ref, e_ref, bp_ref, acc_re, acc_im):
-    panel_count, _, width2 = g_ref.shape
+def _excite_kernel(slot_ref, cos_ref, sin_ref, rank_ref, ga_ref, gb_ref, br_ref, e_ref, bp_ref, acc_re, acc_im):
+    panel_count, part, width2 = ga_ref.shape
     width = width2 // 2
     slots = acc_re.shape[0]
     acc_re[...] = jnp.zeros(acc_re.shape, jnp.float32)
@@ -34,10 +34,11 @@
         k = slot_ref[q]
         c = cos_ref[q]
         s = sin_ref[q]
-        p_re = g_ref[q, :, :width].astype(jnp.float32)
-        p_im = g_ref[q, :, width:].astype(jnp.float32)
-        acc_re[k] = acc_re[k] + (c * p_re + s * p_im)
-        acc_im[k] = acc_im[k] + (c * p_im - s * p_re)
+        for rows, g_ref in ((slice(0, part), ga_ref), (slice(part, 2 * part), gb_ref)):
+            p_re = g_ref[q, :, :width].astype(jnp.float32)
+            p_im = g_ref[q, :, width:].astype(jnp.float32)
+            acc_re[k, rows] = acc_re[k, rows] + (c * p_re + s * p_im)
+            acc_im[k, rows] = acc_im[k, rows] + (c * p_im - s * p_re)
         return carry
 
     lax.fori_loop(0, panel_count, body, 0)
@@ -136,28 +137,35 @@
     return [(i, i ^ (1 << bit)) for i in range(count)]
 
 
-def _reduce_scatter(keep, give, axis_name):
+def _reduce_scatter(keep, give, axis_name, shape):
     count = lax.axis_size(axis_name)
-    current = keep + lax.ppermute(give, axis_name, _pair_perm(count, 0))
-    for bit in range(1, count.bit_length() - 1):
+    bits = count.bit_length() - 1
+    got = lax.ppermute(give, axis_name, _pair_perm(count, 0))
+    for bit in range(1, bits):
+        current = keep + got
         half = current.shape[0] // 2
-        current = current[:half] + lax.ppermute(current[half:], axis_name, _pair_perm(count, bit))
-    return current
-
-
-def _all_gather(x, axis_name, axis, bits):
+        keep = current[:half]
+        got = lax.ppermute(current[half:], axis_name, _pair_perm(count, bit))
+    return keep.reshape(shape) + got.reshape(shape)
+
+
+def _all_gather(x, axis_name, axis, bits, companions=()):
     count = lax.axis_size(axis_name)
     current = x
-    for bit in bits:
+    for step, bit in enumerate(bits):
+        if step == 1 and companions:
+            current, companions = lax.optimization_barrier((current, companions))
         other = lax.ppermute(current, axis_name, _pair_perm(count, bit))
+        if step == len(bits) - 1:
+            return current, other, companions
         current = jnp.concatenate([current, other], axis=axis)
-    return current
 
 
 def _exchange(x, axis_name):
     count = lax.axis_size(axis_name)
     if count > 4:
-        return _all_gather(x[None], axis_name, 0, list(range(count.bit_length() - 1)))
+        current, other, _ = _all_gather(x[None], axis_name, 0, list(range(count.bit_length() - 1)))
+        return jnp.concatenate([current, other], axis=0)
     parts = [x] + [lax.ppermute(x, axis_name, [(i, i ^ p) for i in range(count)]) for p in range(1, count)]
     return jnp.stack(parts, axis=0)
 
@@ -195,7 +203,8 @@
 
     local_panels = panels[0].reshape(panel_count, local_sources, 2 * panel_width)
     ang_bits = lax.axis_size("ang").bit_length() - 1
-    gathered = _all_gather(local_panels, "ang", 1, list(range(ang_bits))[::-1])
+    first, second, (own_cos, own_sin) = _all_gather(
+        local_panels, "ang", 1, list(range(ang_bits))[::-1], (own_cos, own_sin))
     rank = rank_count[0].reshape(1)
 
     excitation, projected = pl.pallas_call(
@@ -204,13 +213,13 @@
             jax.ShapeDtypeStruct((2, source_count, row_count), jnp.bfloat16),
             jax.ShapeDtypeStruct((2, source_count, rank_width), jnp.bfloat16),
         ),
-        in_specs=[_SMEM, _SMEM, _SMEM, _SMEM, _VMEM, _VMEM],
+        in_specs=[_SMEM, _SMEM, _SMEM, _SMEM, _VMEM, _VMEM, _VMEM],
         out_specs=(_VMEM, _VMEM),
         scratch_shapes=[
             pltpu.VMEM((slot_count, source_count, panel_width), jnp.float32),
             pltpu.VMEM((slot_count, source_count, panel_width), jnp.float32),
         ],
-    )(panel_slot[0], own_cos, own_sin, rank, gathered, block_right[0])
+    )(panel_slot[0], own_cos, own_sin, rank, first, second, block_right[0])
 
     row_blocks = lax.axis_size("row")
     all_projected = _exchange(projected, "row")
@@ -245,8 +254,7 @@
             out_specs=pl.BlockSpec((half, 2 * row_count), lambda i: (0, 0)),
             scratch_shapes=[pltpu.VMEM((2, half, rank_width), jnp.bfloat16)],
         )(quad_weight[0], rank, near, block_left[0], coupling, all_projected))
-    summed = _reduce_scatter(halves[1], halves[0], "ang")
-    return summed.reshape(summed.shape[0], 2, row_count)
+    return _reduce_scatter(halves[1], halves[0], "ang", (local_sources, 2, row_count))
 
 
 def solution(mesh):

time: 62.6 us -> 61.9 us (0.989)
  other arithmetic: 6.76 us -> 5.65 us
  local copies, waits for them, and re-layouts: 4.09 us -> 4.97 us
  waiting for transfers between devices: 23.4 us -> 22.7 us
    concatenate x3 -> x1, other arithmetic: 1.16 us -> 0.02 us  [_all_gather(): current = jnp.concatenate([current, other], axis=axis)]
    unnamed x4 -> x9, local copies, waits for them, and re-layouts: 0.01 us -> 0.81 us
    add x0 -> x1, local copies, waits for them, and re-layouts: none -> 0.76 us  [_reduce_scatter(): return keep.reshape(shape) + got.reshape(shape)]
    reshape x1 -> x0, local copies, waits for them, and re-layouts: 0.76 us -> none  [shards(): return summed.reshape(summed.shape[0], 2, row_count)]
    ppermute x3, waiting for transfers between devices: 9.92 us -> 9.25 us  [_all_gather(): other = lax.ppermute(current, axis_name, _pair_perm(count, bit))]
where the time goes in v8:
time: 61.9 us; the launch traced here: 61.5 us
  waiting for transfers between devices  22.7 us (37%)
  Pallas kernels  14.1 us (23%)
  starting transfers between devices  13.2 us (21%)
  other arithmetic  5.65 us (9%)
  local copies, waits for them, and re-layouts  4.97 us (8%)
  between operations  0.84 us (1%)
    ppermute x2, waiting for transfers between devices, _reduce_scatter(): got = lax.ppermute(current[half:], axis_name, _pair_perm(count, bit))  13.5 us
    ppermute x3, waiting for transfers between devices, _all_gather(): other = lax.ppermute(current, axis_name, _pair_perm(count, bit))  9.25 us
    pallas_call x1, Pallas kernels, shards(): pl.pallas_call(_near_kernel, out_shape=jax.ShapeDtypeStruct((source_count...  6.19 us
    pallas_call x2, Pallas kernels, shards(): pl.pallas_call(_far_kernel, out_shape=jax.ShapeDtypeStruct((half, 2 * row...  4.98 us
    ppermute x3, starting transfers between devices, _all_gather(): other = lax.ppermute(current, axis_name, _pair_perm(count, bit))  4.96 us
    ppermute x2, starting transfers between devices, _reduce_scatter(): got = lax.ppermute(current[half:], axis_name, _pair_perm(count, bit))  4.77 us
    ppermute x3, starting transfers between devices, _exchange(): lax.ppermute(x, axis_name, [(i, i ^ p) for i in range(count)])  3.49 us
    pallas_call x1, Pallas kernels, shards(): pl.pallas_call(_excite_kernel, out_shape=(jax.ShapeDtypeStruct((2, source...  2.92 us
  transfers between devices with their start and end apart: 9, of which 4 were waited for; matrix products, arithmetic and copies ran while one was open for 10% of the time, Pallas kernels for 14%

profile of v8, /device:TPU:0, one launch (start us, length us, event | category | flops | bytes accessed | tf_op | source)
XLA Modules:
  0.0 61.5 jit_solution(12893759286906958689)
XLA Ops:
  0.0 0.0 copy-start
  0.0 1.0 %reshape_squeeze.6 = bf16[32,8,256]{2,1,0:T(8,128)(2,1)S(1)} reshape(bf16[1,32,8,2,128]{4,3,2,1,0:T(2,128)(2,1)} %param.12) | data formatting | bytes 262144 | tf_op jit(solution)/shard_map/reshape;squeeze | solution.py:204
  1.0 4.1 %collective-permute-start = (bf16[32,8,256]{2,1,0:T(8,128)(2,1)S(1)}, bf16[32,8,256]{2,1,0:T(8,128)(2,1)S(1)}, u32[]{:S(2)}, u32[]{:S(2)}) collective-permute-start(bf16[32,8,256]{2,1,0:T(8,128)(2,1)S(1)} %reshape_squeeze.6), channel_id=1, source_target_pairs={{0,16},{4,20},{8,24},{12,28},{16,0},{20,4},{24,8},{28,12},{1,17},{... | collective-permute-start | bytes 393224 | tf_op jit(solution)/shard_map/ppermute | solution.py:158
  5.1 0.0 copy-done
  5.1 0.1 constant_dynamic-slice_fusion
  5.2 0.6 fusion.1
  5.8 0.7 %convert_bitcast_fusion = f32[32,2]{0,1:T(2,128)S(1)} fusion(s32[1,32,2]{1,2,0:T(2,128)} %param.14), kind=kLoop, calls=%fused_computation.12 | loop fusion | flops 64 | bytes 512 | tf_op jit(solution)/shard_map/convert_element_type | solution.py:198
  6.5 1.8 %reduce-precision_bitcast_fusion = (f32[32]{0:T(128)}, f32[32,1]{0,1:T(1,128)S(1)}) fusion(f32[32,2]{0,1:T(2,128)S(1)} %convert_bitcast_fusion, f32[]{:T(128)} %bitcast.5, f32[]{:T(128)} %bitcast.3), kind=kLoop, calls=%fused_computation.14 | loop fusion | flops 128 | bytes 520 | tf_op jit(solution)/shard_map/reduce_precision | solution.py:202
  8.3 0.6 %reduce-precision_bitcast_fusion.1.cos_ref = f32[32]{0:T(128)} fusion(f32[32,1]{0,1:T(1,128)S(1)} %get-tuple-element.16), kind=kLoop, calls=%fused_computation.15 | loop fusion | flops 32 | bytes 256 | tf_op jit(solution)/shard_map/reduce_precision | solution.py:201
  8.9 2.5 %collective-permute-done = bf16[32,8,256]{2,1,0:T(8,128)(2,1)S(1)} collective-permute-done((bf16[32,8,256]{2,1,0:T(8,128)(2,1)S(1)}, bf16[32,8,256]{2,1,0:T(8,128)(2,1)S(1)}, u32[]{:S(2)}, u32[]{:S(2)}) %collective-permute-start) | collective-permute-done | bytes 131104 | tf_op jit(solution)/shard_map/ppermute | solution.py:158
  11.4 0.8 %collective-permute-start.1 = (bf16[32,16,256]{2,1,0:T(8,128)(2,1)S(1)}, bf16[32,16,256]{2,1,0:T(8,128)(2,1)S(1)}, u32[]{:S(2)}, u32[]{:S(2)}) collective-permute-start(bf16[32,16,256]{2,1,0:T(8,128)(2,1)S(1)} %pad_maximum_fusion), channel_id=1, source_target_pairs={{0,8},{4,12},{8,0},{12,4},{16,24},{20,28},{24,16},{28,20},{1,9},{5... | collective-permute-start | bytes 786440 | tf_op jit(solution)/shard_map/ppermute | solution.py:158
  12.3 6.7 %collective-permute-done.1 = bf16[32,16,256]{2,1,0:T(8,128)(2,1)S(1)} collective-permute-done((bf16[32,16,256]{2,1,0:T(8,128)(2,1)S(1)}, bf16[32,16,256]{2,1,0:T(8,128)(2,1)S(1)}, u32[]{:S(2)}, u32[]{:S(2)}) %collective-permute-start.1) | collective-permute-done | bytes 262176 | tf_op jit(solution)/shard_map/ppermute | solution.py:158
  19.0 0.0 copy-start.1
  19.0 0.1 collective-permute-start.2
  19.8 0.1 broadcast_in_dim.14
  19.9 0.1 broadcast_in_dim.15
  20.0 0.8 %reshape_squeeze.7 = bf16[2,32,4,32]{3,2,1,0:T(4,128)(2,1)S(1)} reshape(bf16[1,1,2,32,128]{4,3,2,1,0:T(8,128)(2,1)} %param.21) | data formatting | bytes 32768 | tf_op jit(solution)/shard_map/reshape;squeeze | solution.py:228
  20.8 0.6 gather_fusion
  21.4 0.1 copy.17
  21.5 0.1 gather.7
  21.6 0.0 collective-permute-done.2.gb_ref
  21.6 0.0 copy-start.2
  21.6 0.0 copy-done.1
  21.6 0.8 %copy-done.2 = bf16[32,32,256]{2,1,0:T(8,128)(2,1)} copy-done((bf16[32,32,256]{2,1,0:T(8,128)(2,1)}, bf16[32,32,256]{2,1,0:T(8,128)(2,1)S(1)}, u32[]{:S(2)}) %copy-start.2) | copy-done | bytes 524312
  22.4 2.9 %shard_map.118 = (bf16[2,64,2048]{2,1,0:T(8,128)(2,1)}, bf16[2,64,32]{2,1,0:T(8,128)(2,1)}) custom-call(s32[32]{0:T(128)} %bitcast.43, f32[32]{0:T(128)} %reduce-precision_bitcast_fusion.1.cos_ref, f32[32]{0:T(128)} %get-tuple-element.11.sin_ref, s32[1]{0:T(128)} %bitcast.26.rank_ref, bf16[32,32,256]{2,1,0:T(8,128)(2,1)} %copy-done.1, ...), custom_call_target="tpu_custom_call" | custom-call | tf_op jit(solution)/shard_map/pallas_call | solution.py:210
  25.3 2.2 %collective-permute-start.5 = (bf16[2,64,32]{2,1,0:T(8,128)(2,1)}, bf16[2,64,32]{2,1,0:T(8,128)(2,1)S(1)}, u32[]{:S(2)}, u32[]{:S(2)}) collective-permute-start(bf16[2,64,32]{2,1,0:T(8,128)(2,1)} %get-tuple-element.14), channel_id=1, source_target_pairs={{0,3},{1,2},{2,1},{3,0},{4,7},{5,6},{6,5},{7,4},{8,11},{9,10},{10,... | collective-permute-start | bytes 24584 | tf_op jit(solution)/shard_map/ppermute | solution.py:169
  27.5 0.5 collective-permute-start.4
  28.0 0.8 %collective-permute-start.3 = (bf16[2,64,32]{2,1,0:T(8,128)(2,1)}, bf16[2,64,32]{2,1,0:T(8,128)(2,1)S(1)}, u32[]{:S(2)}, u32[]{:S(2)}) collective-permute-start(bf16[2,64,32]{2,1,0:T(8,128)(2,1)} %get-tuple-element.14), channel_id=1, source_target_pairs={{0,1},{1,0},{2,3},{3,2},{4,5},{5,4},{6,7},{7,6},{8,9},{9,8},{10,11... | collective-permute-start | bytes 24584 | tf_op jit(solution)/shard_map/ppermute | solution.py:169
  28.8 0.6 broadcast_select_fusion.cp_ref
  29.4 0.0 copy-start.3
  29.4 6.2 %shard_map.119.near_ref = f32[64,4096]{1,0:T(8,128)} custom-call(bf16[2,64,2048]{2,1,0:T(8,128)(2,1)} %get-tuple-element.13.e_ref, bf16[2,2048,256]{2,1,0:T(8,128)(2,1)} %bitcast.29, bf16[3,2,32,2048]{3,2,1,0:T(8,128)(2,1)} %bitcast.32, bf16[3,2,32,2048]{3,2,1,0:T(8,128)(2,1)} %bitcast.33), custom_call_target="tpu_custom_call" | custom-call | tf_op jit(solution)/shard_map/pallas_call | solution.py:231
  35.6 0.0 collective-permute-done.5
  35.6 0.0 collective-permute-done.4
  35.6 0.0 collective-permute-done.3
  35.6 0.0 copy-done.3
  35.6 0.7 %pad_maximum_fusion.1.bpa_ref = bf16[4,2,64,32]{3,2,1,0:T(8,128)(2,1)} fusion(bf16[1,2,64,32]{3,2,1,0:T(8,128)(2,1)S(1)} %bitcast.38, bf16[1,2,64,32]{3,2,1,0:T(8,128)(2,1)S(1)} %bitcast.39, bf16[1,2,64,32]{3,2,1,0:T(8,128)(2,1)S(1)} %bitcast.40, bf16[1,2,64,32]{3,2,1,0:T(8,128)(2,1)S(1)} %bitcast.37), kind=kLoop, calls=%fused_computation.4 | loop fusion | flops 49152 | bytes 65536 | tf_op jit(solution)/shard_map/stack | solution.py:170
  36.3 2.5 %shard_map.121 = f32[32,4096]{1,0:T(8,128)} custom-call(f32[2]{0:T(128)} %bitcast.41, s32[1]{0:T(128)} %bitcast.28.rank_ref, f32[64,4096]{1,0:T(8,128)} %shard_map.119.near_ref, bf16[2,32,2048]{2,1,0:T(8,128)(2,1)} %bitcast.30, bf16[2,32,128]{2,1,0:T(8,128)(2,1)} %broadcast_select_fusion.cp_ref, bf16[4,2,64,32]{3,2,1,0:T(8,128)(2,1)} %pad_maximum_fusion.1.bpa_ref), custom_call_target="tpu_custom_call" | custom-call | tf_op jit(solution)/shard_map/pallas_call | solution.py:242
  38.8 0.0 collective-permute-start.6
  38.8 2.5 %shard_map.120 = f32[32,4096]{1,0:T(8,128)} custom-call(f32[2]{0:T(128)} %bitcast.42, s32[1]{0:T(128)} %bitcast.27.rank_ref, f32[64,4096]{1,0:T(8,128)} %shard_map.119.near_ref, bf16[2,32,2048]{2,1,0:T(8,128)(2,1)} %bitcast.31, bf16[2,32,128]{2,1,0:T(8,128)(2,1)} %broadcast_select_fusion.cp_ref, bf16[4,2,64,32]{3,2,1,0:T(8,128)(2,1)} %pad_maximum_fusion.1.bpa_ref), custom_call_target="tpu_custom_call" | custom-call | tf_op jit(solution)/shard_map/pallas_call | solution.py:242
  41.3 0.0 collective-permute-done.6
  41.3 1.1 %add.38 = f32[32,4096]{1,0:T(8,128)S(1)} add(f32[32,4096]{1,0:T(8,128)} %shard_map.120, f32[32,4096]{1,0:T(8,128)S(1)} %collective-permute-done.6) | non-fusion elementwise | flops 131072 | bytes 1572864 | tf_op jit(solution)/shard_map/add | solution.py:145
  42.4 1.6 %collective-permute-start.7 = (f32[16,4096]{1,0:T(8,128)S(1)}, f32[16,4096]{1,0:T(8,128)S(1)}, u32[]{:S(2)}, u32[]{:S(2)}) collective-permute-start(f32[16,4096]{1,0:T(8,128)S(1)} %slice.35), channel_id=1, source_target_pairs={{0,8},{4,12},{8,0},{12,4},{16,24},{20,28},{24,16},{28,20},{1,9},{5... | collective-permute-start | bytes 786440 | tf_op jit(solution)/shard_map/ppermute | solution.py:148
  44.0 7.2 %collective-permute-done.7 = f32[16,4096]{1,0:T(8,128)S(1)} collective-permute-done((f32[16,4096]{1,0:T(8,128)S(1)}, f32[16,4096]{1,0:T(8,128)S(1)}, u32[]{:S(2)}, u32[]{:S(2)}) %collective-permute-start.7) | collective-permute-done | bytes 262176 | tf_op jit(solution)/shard_map/ppermute | solution.py:148
  51.3 3.2 %collective-permute-start.8 = (f32[8,4096]{1,0:T(8,128)S(1)}, f32[8,4096]{1,0:T(8,128)S(1)}, u32[]{:S(2)}, u32[]{:S(2)}) collective-permute-start(f32[8,4096]{1,0:T(8,128)S(1)} %slice.37), channel_id=1, source_target_pairs={{0,16},{4,20},{8,24},{12,28},{16,0},{20,4},{24,8},{28,12},{1,17},{... | collective-permute-start | bytes 393224 | tf_op jit(solution)/shard_map/ppermute | solution.py:148
  54.5 6.3 %collective-permute-done.8 = f32[8,4096]{1,0:T(8,128)S(1)} collective-permute-done((f32[8,4096]{1,0:T(8,128)S(1)}, f32[8,4096]{1,0:T(8,128)S(1)}, u32[]{:S(2)}, u32[]{:S(2)}) %collective-permute-start.8) | collective-permute-done | bytes 131104 | tf_op jit(solution)/shard_map/ppermute | solution.py:148
  60.8 0.8 %copy.18 = f32[8,2,2048]{2,1,0:T(2,128)} copy(f32[8,2,2048]{2,0,1:T(8,128)S(1)} %bitcast.34) | data formatting | bytes 262144 | tf_op jit(solution)/shard_map/add | solution.py:149
  (11 shorter events, 0.2 us)
Async XLA Ops:
  0.0 5.1 %copy-start = (f32[8,2]{0,1:T(2,128)S(1)}, f32[8,2]{0,1:T(2,128)}, u32[]{:S(2)}) copy-start(f32[8,2]{0,1:T(2,128)} %param.15) | copy-start | bytes 196
  1.0 10.4 %collective-permute-start = (bf16[32,8,256]{2,1,0:T(8,128)(2,1)S(1)}, bf16[32,8,256]{2,1,0:T(8,128)(2,1)S(1)}, u32[]{:S(2)}, u32[]{:S(2)}) collective-permute-start(bf16[32,8,256]{2,1,0:T(8,128)(2,1)S(1)} %reshape_squeeze.6), channel_id=1, source_target_pairs={{0,16},{4,20},{8,24},{12,28},{16,0},{20,4},{24,8},{28,12},{1,17},{... | collective-permute-start | bytes 393224 | tf_op jit(solution)/shard_map/ppermute | solution.py:158
  11.4 7.6 %collective-permute-start.1 = (bf16[32,16,256]{2,1,0:T(8,128)(2,1)S(1)}, bf16[32,16,256]{2,1,0:T(8,128)(2,1)S(1)}, u32[]{:S(2)}, u32[]{:S(2)}) collective-permute-start(bf16[32,16,256]{2,1,0:T(8,128)(2,1)S(1)} %pad_maximum_fusion), channel_id=1, source_target_pairs={{0,8},{4,12},{8,0},{12,4},{16,24},{20,28},{24,16},{28,20},{1,9},{5... | collective-permute-start | bytes 786440 | tf_op jit(solution)/shard_map/ppermute | solution.py:158
  19.0 2.6 %copy-start.1 = (bf16[32,32,256]{2,1,0:T(8,128)(2,1)}, bf16[32,32,256]{2,1,0:T(8,128)(2,1)S(1)}, u32[]{:S(2)}) copy-start(bf16[32,32,256]{2,1,0:T(8,128)(2,1)S(1)} %constant_dynamic-update-slice_fusion.ga_ref) | copy-start | bytes 1572868
  19.0 2.5 %collective-permute-start.2 = (bf16[32,32,256]{2,1,0:T(8,128)(2,1)S(1)}, bf16[32,32,256]{2,1,0:T(8,128)(2,1)S(1)}, u32[]{:S(2)}, u32[]{:S(2)}) collective-permute-start(bf16[32,32,256]{2,1,0:T(8,128)(2,1)S(1)} %constant_dynamic-update-slice_fusion.ga_ref), channel_id=1, source_target_pairs={{0,4},{4,0},{8,12},{12,8},{16,20},{20,16},{24,28},{28,24},{1,5},{5... | collective-permute-start | bytes 1572872 | tf_op jit(solution)/shard_map/ppermute | solution.py:158
  21.6 0.8 %copy-start.2 = (bf16[32,32,256]{2,1,0:T(8,128)(2,1)}, bf16[32,32,256]{2,1,0:T(8,128)(2,1)S(1)}, u32[]{:S(2)}) copy-start(bf16[32,32,256]{2,1,0:T(8,128)(2,1)S(1)} %collective-permute-done.2.gb_ref) | copy-start | bytes 1572868
  25.3 10.3 %collective-permute-start.5 = (bf16[2,64,32]{2,1,0:T(8,128)(2,1)}, bf16[2,64,32]{2,1,0:T(8,128)(2,1)S(1)}, u32[]{:S(2)}, u32[]{:S(2)}) collective-permute-start(bf16[2,64,32]{2,1,0:T(8,128)(2,1)} %get-tuple-element.14), channel_id=1, source_target_pairs={{0,3},{1,2},{2,1},{3,0},{4,7},{5,6},{6,5},{7,4},{8,11},{9,10},{10,... | collective-permute-start | bytes 24584 | tf_op jit(solution)/shard_map/ppermute | solution.py:169
  27.5 8.1 %collective-permute-start.4 = (bf16[2,64,32]{2,1,0:T(8,128)(2,1)}, bf16[2,64,32]{2,1,0:T(8,128)(2,1)S(1)}, u32[]{:S(2)}, u32[]{:S(2)}) collective-permute-start(bf16[2,64,32]{2,1,0:T(8,128)(2,1)} %get-tuple-element.14), channel_id=1, source_target_pairs={{0,2},{1,3},{2,0},{3,1},{4,6},{5,7},{6,4},{7,5},{8,10},{9,11},{10,... | collective-permute-start | bytes 24584 | tf_op jit(solution)/shard_map/ppermute | solution.py:169
  28.0 7.6 %collective-permute-start.3 = (bf16[2,64,32]{2,1,0:T(8,128)(2,1)}, bf16[2,64,32]{2,1,0:T(8,128)(2,1)S(1)}, u32[]{:S(2)}, u32[]{:S(2)}) collective-permute-start(bf16[2,64,32]{2,1,0:T(8,128)(2,1)} %get-tuple-element.14), channel_id=1, source_target_pairs={{0,1},{1,0},{2,3},{3,2},{4,5},{5,4},{6,7},{7,6},{8,9},{9,8},{10,11... | collective-permute-start | bytes 24584 | tf_op jit(solution)/shard_map/ppermute | solution.py:169
  29.4 6.2 %copy-start.3 = (bf16[2,64,32]{2,1,0:T(8,128)(2,1)S(1)}, bf16[2,64,32]{2,1,0:T(8,128)(2,1)}, u32[]{:S(2)}) copy-start(bf16[2,64,32]{2,1,0:T(8,128)(2,1)} %get-tuple-element.14) | copy-start | bytes 24580
  38.8 2.5 %collective-permute-start.6 = (f32[32,4096]{1,0:T(8,128)}, f32[32,4096]{1,0:T(8,128)S(1)}, u32[]{:S(2)}, u32[]{:S(2)}) collective-permute-start(f32[32,4096]{1,0:T(8,128)} %shard_map.121), channel_id=1, source_target_pairs={{0,4},{4,0},{8,12},{12,8},{16,20},{20,16},{24,28},{28,24},{1,5},{5... | collective-permute-start | bytes 1572872 | tf_op jit(solution)/shard_map/ppermute | solution.py:143
  42.4 8.8 %collective-permute-start.7 = (f32[16,4096]{1,0:T(8,128)S(1)}, f32[16,4096]{1,0:T(8,128)S(1)}, u32[]{:S(2)}, u32[]{:S(2)}) collective-permute-start(f32[16,4096]{1,0:T(8,128)S(1)} %slice.35), channel_id=1, source_target_pairs={{0,8},{4,12},{8,0},{12,4},{16,24},{20,28},{24,16},{28,20},{1,9},{5... | collective-permute-start | bytes 786440 | tf_op jit(solution)/shard_map/ppermute | solution.py:148
  51.3 9.5 %collective-permute-start.8 = (f32[8,4096]{1,0:T(8,128)S(1)}, f32[8,4096]{1,0:T(8,128)S(1)}, u32[]{:S(2)}, u32[]{:S(2)}) collective-permute-start(f32[8,4096]{1,0:T(8,128)S(1)} %slice.37), channel_id=1, source_target_pairs={{0,16},{4,20},{8,24},{12,28},{16,0},{20,4},{24,8},{28,12},{1,17},{... | collective-permute-start | bytes 393224 | tf_op jit(solution)/shard_map/ppermute | solution.py:148

commit v9 on v8

--- a/solution.py
+++ b/solution.py
@@ -133,39 +133,70 @@
         out_ref[:, imag_cols] = w_re * f_im + w_im * f_re
 
 
-def _pair_perm(count, bit):
-    return [(i, i ^ (1 << bit)) for i in range(count)]
+def _bit_groups(count):
+    bits = count.bit_length() - 1
+    groups = [[b, b - 1] for b in range(bits - 1, 1, -2)]
+    rest = [b for b in range(bits) if all(b not in g for g in groups)]
+    return groups + [[b] for b in rest[::-1]]
+
+
+def _offset(value, group):
+    return sum(1 << b for k, b in enumerate(group) if (value >> k) & 1)
+
+
+def _permute(x, axis_name, count, offset):
+    return lax.ppermute(x, axis_name, [(i, i ^ offset) for i in range(count)])
+
+
+def _all_gather(x, axis_name, axis, companions=()):
+    count = lax.axis_size(axis_name)
+    groups = _bit_groups(count)
+    current = x
+    for step, group in enumerate(groups):
+        if step == 1 and companions:
+            current, companions = lax.optimization_barrier((current, companions))
+        parts = [current] + [_permute(current, axis_name, count, _offset(j, group)) for j in range(1, 2 ** len(group))]
+        if step == len(groups) - 1:
+            return parts, companions
+        current = jnp.concatenate(parts, axis=axis)
 
 
 def _reduce_scatter(keep, give, axis_name, shape):
     count = lax.axis_size(axis_name)
-    bits = count.bit_length() - 1
-    got = lax.ppermute(give, axis_name, _pair_perm(count, 0))
-    for bit in range(1, bits):
-        current = keep + got
-        half = current.shape[0] // 2
-        keep = current[:half]
-        got = lax.ppermute(current[half:], axis_name, _pair_perm(count, bit))
-    return keep.reshape(shape) + got.reshape(shape)
-
-
-def _all_gather(x, axis_name, axis, bits, companions=()):
-    count = lax.axis_size(axis_name)
-    current = x
-    for step, bit in enumerate(bits):
-        if step == 1 and companions:
-            current, companions = lax.optimization_barrier((current, companions))
-        other = lax.ppermute(current, axis_name, _pair_perm(count, bit))
-        if step == len(bits) - 1:
-            return current, other, companions
-        current = jnp.concatenate([current, other], axis=axis)
+    groups = _bit_groups(count)
+    flat = sum(groups, [])
+
+    def offset_of(position):
+        return sum(1 << flat[k] for k in range(len(flat)) if (position >> k) & 1)
+
+    chunks = 2 * keep.shape[0] // shape[0]
+    current = keep + _permute(give, axis_name, count, offset_of(chunks // 2))
+    chunks //= 2
+    for group in groups[::-1][1:]:
+        size = 2 ** len(group)
+        block = chunks // size
+        rows = block * shape[0]
+        total = current[:rows]
+        for t in range(1, size):
+            part = current[t * rows:(t + 1) * rows]
+            total = total + _permute(part, axis_name, count, offset_of(t * block))
+        current = total
+        chunks = block
+    return current.reshape(shape)
+
+
+def _position_offsets(count):
+    if count <= 4:
+        return list(range(count))
+    flat = sum(_bit_groups(count), [])
+    return [sum(1 << flat[k] for k in range(len(flat)) if (p >> k) & 1) for p in range(count)]
 
 
 def _exchange(x, axis_name):
     count = lax.axis_size(axis_name)
     if count > 4:
-        current, other, _ = _all_gather(x[None], axis_name, 0, list(range(count.bit_length() - 1)))
-        return jnp.concatenate([current, other], axis=0)
+        parts, _ = _all_gather(x[None], axis_name, 0)
+        return jnp.concatenate(parts, axis=0)
     parts = [x] + [lax.ppermute(x, axis_name, [(i, i ^ p) for i in range(count)]) for p in range(1, count)]
     return jnp.stack(parts, axis=0)
 
@@ -202,9 +233,7 @@
     own_sin = lax.reduce_precision(jnp.sin(theta), exponent_bits=8, mantissa_bits=7)
 
     local_panels = panels[0].reshape(panel_count, local_sources, 2 * panel_width)
-    ang_bits = lax.axis_size("ang").bit_length() - 1
-    first, second, (own_cos, own_sin) = _all_gather(
-        local_panels, "ang", 1, list(range(ang_bits))[::-1], (own_cos, own_sin))
+    (first, second), (own_cos, own_sin) = _all_gather(local_panels, "ang", 1, (own_cos, own_sin))
     rank = rank_count[0].reshape(1)
 
     excitation, projected = pl.pallas_call(
@@ -226,7 +255,8 @@
     me = lax.axis_index("row")
     coupling = block_coupling[0, 0]
     coupling = coupling.reshape(2, rank_width, row_blocks, coupling.shape[2] // row_blocks)
-    coupling = jnp.take(coupling, me ^ jnp.arange(row_blocks), axis=2).reshape(block_coupling.shape[2:])
+    offsets = jnp.array(_position_offsets(row_blocks), jnp.int32)
+    coupling = jnp.take(coupling, me ^ offsets, axis=2).reshape(block_coupling.shape[2:])
 
     near = pl.pallas_call(
         _near_kernel,

time: 61.9 us -> 55.7 us (0.90)
  waiting for transfers between devices: 22.7 us -> 16.7 us
    ppermute x6 -> x8, waiting for transfers between devices: 22.7 us -> 16.7 us  [_permute(): return lax.ppermute(x, axis_name, [(i, i ^ offset) for i in range(count)])]
    add x1 -> x0, local copies, waits for them, and re-layouts: 0.76 us -> none  [_reduce_scatter(): return keep.reshape(shape) + got.reshape(shape)]
    reshape x0 -> x1, local copies, waits for them, and re-layouts: none -> 0.76 us  [_reduce_scatter(): return current.reshape(shape)]
    ppermute x6 -> x8, starting transfers between devices: 9.73 us -> 9.38 us  [_permute(): return lax.ppermute(x, axis_name, [(i, i ^ offset) for i in range(count)])]
  transfers between devices with their start and end apart: 9 -> 11, of which waited for: 4 -> 4; matrix products, arithmetic and copies ran while one was open for 10% -> 11% of each run, Pallas kernels for 14% -> 16%
where the time goes in v9:
time: 55.7 us; the launch traced here: 55.3 us
  waiting for transfers between devices  16.7 us (30%)
  Pallas kernels  14.1 us (25%)
  starting transfers between devices  12.9 us (23%)
  other arithmetic  5.79 us (10%)
  local copies, waits for them, and re-layouts  4.95 us (9%)
  between operations  0.82 us (1%)
    ppermute x8, waiting for transfers between devices, _permute(): return lax.ppermute(x, axis_name, [(i, i ^ offset) for i in range(count)])  16.7 us
    ppermute x8, starting transfers between devices, _permute(): return lax.ppermute(x, axis_name, [(i, i ^ offset) for i in range(count)])  9.38 us
    pallas_call x1, Pallas kernels, shards(): pl.pallas_call(_near_kernel, out_shape=jax.ShapeDtypeStruct((source_count...  6.26 us
    pallas_call x2, Pallas kernels, shards(): pl.pallas_call(_far_kernel, out_shape=jax.ShapeDtypeStruct((half, 2 * row...  4.97 us
    ppermute x3, starting transfers between devices, _exchange(): lax.ppermute(x, axis_name, [(i, i ^ p) for i in range(count)])  3.49 us
    pallas_call x1, Pallas kernels, shards(): pl.pallas_call(_excite_kernel, out_shape=(jax.ShapeDtypeStruct((2, source...  2.92 us
    reduce_precision x1, other arithmetic, shards(): lax.reduce_precision(jnp.sin(theta), exponent_bits=8, mantissa_bits=7)  1.94 us
    add x1, other arithmetic, _reduce_scatter(): current = keep + _permute(give, axis_name, count, offset_of(chunks // 2))  1.13 us
  transfers between devices with their start and end apart: 11, of which 4 were waited for; matrix products, arithmetic and copies ran while one was open for 11% of the time, Pallas kernels for 16%

profile of v9, /device:TPU:0, one launch (start us, length us, event | category | flops | bytes accessed | tf_op | source)
XLA Modules:
  0.0 55.3 jit_solution(3276084458584644990)
XLA Ops:
  0.0 0.0 copy-start
  0.0 1.0 %reshape_squeeze.6 = bf16[32,8,256]{2,1,0:T(8,128)(2,1)S(1)} reshape(bf16[1,32,8,2,128]{4,3,2,1,0:T(2,128)(2,1)} %param.13) | data formatting | bytes 262144 | tf_op jit(solution)/shard_map/reshape;squeeze | solution.py:235
  1.0 5.1 %collective-permute-start.2 = (bf16[32,8,256]{2,1,0:T(8,128)(2,1)S(1)}, bf16[32,8,256]{2,1,0:T(8,128)(2,1)S(1)}, u32[]{:S(2)}, u32[]{:S(2)}) collective-permute-start(bf16[32,8,256]{2,1,0:T(8,128)(2,1)S(1)} %reshape_squeeze.6), channel_id=1, source_target_pairs={{0,24},{4,28},{8,16},{12,20},{16,8},{20,12},{24,0},{28,4},{1,25},{... | collective-permute-start | bytes 393224 | tf_op jit(solution)/shard_map/ppermute | solution.py:148
  6.1 0.0 collective-permute-start.1
  6.1 0.6 %collective-permute-start = (bf16[32,8,256]{2,1,0:T(8,128)(2,1)S(1)}, bf16[32,8,256]{2,1,0:T(8,128)(2,1)S(1)}, u32[]{:S(2)}, u32[]{:S(2)}) collective-permute-start(bf16[32,8,256]{2,1,0:T(8,128)(2,1)S(1)} %reshape_squeeze.6), channel_id=1, source_target_pairs={{0,16},{4,20},{8,24},{12,28},{16,0},{20,4},{24,8},{28,12},{1,17},{... | collective-permute-start | bytes 393224 | tf_op jit(solution)/shard_map/ppermute | solution.py:148
  6.8 0.0 copy-done
  6.8 0.1 constant_dynamic-slice_fusion
  6.8 0.6 %fusion.3 = (f32[1,1]{0,1:T(1,128)}, f32[1,1]{0,1:T(1,128)}) fusion(f32[1,2]{0,1:T(2,128)S(1)} %constant_dynamic-slice_fusion), kind=kLoop, calls=%fused_computation.16 | loop fusion | bytes 16 | tf_op jit(solution)/shard_map/slice | solution.py:231
  7.4 0.7 %convert_bitcast_fusion = f32[32,2]{0,1:T(2,128)S(1)} fusion(s32[1,32,2]{1,2,0:T(2,128)} %param.15), kind=kLoop, calls=%fused_computation.10 | loop fusion | flops 64 | bytes 512 | tf_op jit(solution)/shard_map/convert_element_type | solution.py:229
  8.1 1.9 %reduce-precision_bitcast_fusion = (f32[32]{0:T(128)}, f32[32,1]{0,1:T(1,128)S(1)}) fusion(f32[32,2]{0,1:T(2,128)S(1)} %convert_bitcast_fusion, f32[]{:T(128)} %bitcast.5, f32[]{:T(128)} %bitcast.3), kind=kLoop, calls=%fused_computation.11 | loop fusion | flops 128 | bytes 520 | tf_op jit(solution)/shard_map/reduce_precision | solution.py:233
  10.1 0.6 %reduce-precision_bitcast_fusion.1.cos_ref = f32[32]{0:T(128)} fusion(f32[32,1]{0,1:T(1,128)S(1)} %get-tuple-element.16), kind=kLoop, calls=%fused_computation.12 | loop fusion | flops 32 | bytes 256 | tf_op jit(solution)/shard_map/reduce_precision | solution.py:232
  10.7 0.0 collective-permute-done.2
  10.7 2.8 %collective-permute-done.1 = bf16[32,8,256]{2,1,0:T(8,128)(2,1)S(1)} collective-permute-done((bf16[32,8,256]{2,1,0:T(8,128)(2,1)S(1)}, bf16[32,8,256]{2,1,0:T(8,128)(2,1)S(1)}, u32[]{:S(2)}, u32[]{:S(2)}) %collective-permute-start.1) | collective-permute-done | bytes 131104 | tf_op jit(solution)/shard_map/ppermute | solution.py:148
  13.5 3.7 %collective-permute-done = bf16[32,8,256]{2,1,0:T(8,128)(2,1)S(1)} collective-permute-done((bf16[32,8,256]{2,1,0:T(8,128)(2,1)S(1)}, bf16[32,8,256]{2,1,0:T(8,128)(2,1)S(1)}, u32[]{:S(2)}, u32[]{:S(2)}) %collective-permute-start) | collective-permute-done | bytes 131104 | tf_op jit(solution)/shard_map/ppermute | solution.py:148
  17.2 0.1 pad_maximum_fusion.ga_ref
  17.3 0.0 copy-start.1
  17.3 0.1 collective-permute-start.3
  18.1 0.1 broadcast_in_dim.16
  18.1 0.1 broadcast_in_dim.17
  18.2 0.8 %reshape_squeeze.7 = bf16[2,32,4,32]{3,2,1,0:T(4,128)(2,1)S(1)} reshape(bf16[1,1,2,32,128]{4,3,2,1,0:T(8,128)(2,1)} %param.22) | data formatting | bytes 32768 | tf_op jit(solution)/shard_map/reshape;squeeze | solution.py:257
  19.1 0.6 %gather_fusion = bf16[4,2,32,32]{3,2,1,0:T(8,128)(2,1)S(1)} fusion(bf16[2,32,4,32]{3,1,2,0:T(8,128)(2,1)S(1)} %copy.17, s32[1024]{0:T(1024)S(1)} %pad_clamp_fusion), kind=kCustom, calls=%fused_computation | custom fusion | bytes 32784 | tf_op jit(solution)/shard_map/jit(_take)/gather | solution.py:259
  19.6 0.1 copy.18
  19.7 0.1 gather.7
  19.8 0.0 collective-permute-done.3.gb_ref
  19.8 0.8 %copy-done.2 = bf16[32,32,256]{2,1,0:T(8,128)(2,1)} copy-done((bf16[32,32,256]{2,1,0:T(8,128)(2,1)}, bf16[32,32,256]{2,1,0:T(8,128)(2,1)S(1)}, u32[]{:S(2)}) %copy-start.2) | copy-done | bytes 524312
  20.6 2.9 %shard_map.127 = (bf16[2,64,2048]{2,1,0:T(8,128)(2,1)}, bf16[2,64,32]{2,1,0:T(8,128)(2,1)}) custom-call(s32[32]{0:T(128)} %bitcast.41, f32[32]{0:T(128)} %reduce-precision_bitcast_fusion.1.cos_ref, f32[32]{0:T(128)} %get-tuple-element.11.sin_ref, s32[1]{0:T(128)} %bitcast.24.rank_ref, bf16[32,32,256]{2,1,0:T(8,128)(2,1)} %copy-done.1, ...), custom_call_target="tpu_custom_call" | custom-call | tf_op jit(solution)/shard_map/pallas_call | solution.py:239
  23.5 2.4 %collective-permute-start.6 = (bf16[2,64,32]{2,1,0:T(8,128)(2,1)}, bf16[2,64,32]{2,1,0:T(8,128)(2,1)S(1)}, u32[]{:S(2)}, u32[]{:S(2)}) collective-permute-start(bf16[2,64,32]{2,1,0:T(8,128)(2,1)} %get-tuple-element.14), channel_id=1, source_target_pairs={{0,3},{1,2},{2,1},{3,0},{4,7},{5,6},{6,5},{7,4},{8,11},{9,10},{10,... | collective-permute-start | bytes 24584 | tf_op jit(solution)/shard_map/ppermute | solution.py:200
  26.0 0.5 collective-permute-start.5
  26.5 0.5 collective-permute-start.4
  27.0 0.6 %broadcast_select_fusion.cp_ref = bf16[2,32,128]{2,1,0:T(8,128)(2,1)} fusion(bf16[2,32,128]{2,1,0:T(8,128)(2,1)S(1)} %gather.7, pred[128]{0:T(512)(128)(4,1)S(1)} %broadcast_in_dim.17), kind=kLoop, calls=%fused_computation.6 | loop fusion | flops 8192 | bytes 32896 | tf_op jit(solution)/shard_map/jit(_take)/select_n | solution.py:259
  27.6 6.3 %shard_map.128.near_ref = f32[64,4096]{1,0:T(8,128)} custom-call(bf16[2,64,2048]{2,1,0:T(8,128)(2,1)} %get-tuple-element.13.e_ref, bf16[2,2048,256]{2,1,0:T(8,128)(2,1)} %bitcast.27, bf16[3,2,32,2048]{3,2,1,0:T(8,128)(2,1)} %bitcast.30, bf16[3,2,32,2048]{3,2,1,0:T(8,128)(2,1)} %bitcast.31), custom_call_target="tpu_custom_call" | custom-call | tf_op jit(solution)/shard_map/pallas_call | solution.py:261
  33.9 0.0 collective-permute-done.6
  33.9 0.0 collective-permute-done.5
  33.9 0.0 collective-permute-done.4
  33.9 0.0 copy-done.3
  33.9 0.7 %pad_maximum_fusion.1.bpa_ref = bf16[4,2,64,32]{3,2,1,0:T(8,128)(2,1)} fusion(bf16[1,2,64,32]{3,2,1,0:T(8,128)(2,1)S(1)} %bitcast.36, bf16[1,2,64,32]{3,2,1,0:T(8,128)(2,1)S(1)} %bitcast.37, bf16[1,2,64,32]{3,2,1,0:T(8,128)(2,1)S(1)} %bitcast.38, bf16[1,2,64,32]{3,2,1,0:T(8,128)(2,1)S(1)} %bitcast.35), kind=kLoop, calls=%fused_computation.5 | loop fusion | flops 49152 | bytes 65536 | tf_op jit(solution)/shard_map/stack | solution.py:201
  34.6 2.5 %shard_map.130 = f32[32,4096]{1,0:T(8,128)} custom-call(f32[2]{0:T(128)} %bitcast.39, s32[1]{0:T(128)} %bitcast.26.rank_ref, f32[64,4096]{1,0:T(8,128)} %shard_map.128.near_ref, bf16[2,32,2048]{2,1,0:T(8,128)(2,1)} %bitcast.28, bf16[2,32,128]{2,1,0:T(8,128)(2,1)} %broadcast_select_fusion.cp_ref, bf16[4,2,64,32]{3,2,1,0:T(8,128)(2,1)} %pad_maximum_fusion.1.bpa_ref), custom_call_target="tpu_custom_call" | custom-call | tf_op jit(solution)/shard_map/pallas_call | solution.py:272
  37.1 0.0 collective-permute-start.7
  37.1 2.5 %shard_map.129 = f32[32,4096]{1,0:T(8,128)} custom-call(f32[2]{0:T(128)} %bitcast.40, s32[1]{0:T(128)} %bitcast.25.rank_ref, f32[64,4096]{1,0:T(8,128)} %shard_map.128.near_ref, bf16[2,32,2048]{2,1,0:T(8,128)(2,1)} %bitcast.29, bf16[2,32,128]{2,1,0:T(8,128)(2,1)} %broadcast_select_fusion.cp_ref, bf16[4,2,64,32]{3,2,1,0:T(8,128)(2,1)} %pad_maximum_fusion.1.bpa_ref), custom_call_target="tpu_custom_call" | custom-call | tf_op jit(solution)/shard_map/pallas_call | solution.py:272
  39.6 0.0 collective-permute-done.7
  39.6 1.1 %add.26 = f32[32,4096]{1,0:T(8,128)S(1)} add(f32[32,4096]{1,0:T(8,128)} %shard_map.129, f32[32,4096]{1,0:T(8,128)S(1)} %collective-permute-done.7) | non-fusion elementwise | flops 131072 | bytes 1572864 | tf_op jit(solution)/shard_map/add | solution.py:173
  40.8 0.9 %collective-permute-start.8 = (f32[8,4096]{1,0:T(8,128)S(1)}, f32[8,4096]{1,0:T(8,128)S(1)}, u32[]{:S(2)}, u32[]{:S(2)}) collective-permute-start(f32[8,4096]{1,0:T(8,128)S(1)} %get-tuple-element.17), channel_id=1, source_target_pairs={{0,16},{4,20},{8,24},{12,28},{16,0},{20,4},{24,8},{28,12},{1,17},{... | collective-permute-start | bytes 393224 | tf_op jit(solution)/shard_map/ppermute | solution.py:148
  41.6 1.7 %collective-permute-start.10 = (f32[8,4096]{1,0:T(8,128)S(1)}, f32[8,4096]{1,0:T(8,128)S(1)}, u32[]{:S(2)}, u32[]{:S(2)}) collective-permute-start(f32[8,4096]{1,0:T(8,128)S(1)} %get-tuple-element.18), channel_id=1, source_target_pairs={{0,24},{4,28},{8,16},{12,20},{16,8},{20,12},{24,0},{28,4},{1,25},{... | collective-permute-start | bytes 393224 | tf_op jit(solution)/shard_map/ppermute | solution.py:148
  43.4 0.9 %collective-permute-start.9 = (f32[8,4096]{1,0:T(8,128)S(1)}, f32[8,4096]{1,0:T(8,128)S(1)}, u32[]{:S(2)}, u32[]{:S(2)}) collective-permute-start(f32[8,4096]{1,0:T(8,128)S(1)} %get-tuple-element.19), channel_id=1, source_target_pairs={{0,8},{4,12},{8,0},{12,4},{16,24},{20,28},{24,16},{28,20},{1,9},{5... | collective-permute-start | bytes 393224 | tf_op jit(solution)/shard_map/ppermute | solution.py:148
  44.3 8.9 %collective-permute-done.8 = f32[8,4096]{1,0:T(8,128)S(1)} collective-permute-done((f32[8,4096]{1,0:T(8,128)S(1)}, f32[8,4096]{1,0:T(8,128)S(1)}, u32[]{:S(2)}, u32[]{:S(2)}) %collective-permute-start.8) | collective-permute-done | bytes 131104 | tf_op jit(solution)/shard_map/ppermute | solution.py:148
  53.2 0.0 collective-permute-done.10
  53.2 1.3 %collective-permute-done.9 = f32[8,4096]{1,0:T(8,128)S(1)} collective-permute-done((f32[8,4096]{1,0:T(8,128)S(1)}, f32[8,4096]{1,0:T(8,128)S(1)}, u32[]{:S(2)}, u32[]{:S(2)}) %collective-permute-start.9) | collective-permute-done | bytes 131104 | tf_op jit(solution)/shard_map/ppermute | solution.py:148
  54.5 0.8 %copy.19 = f32[8,2,2048]{2,1,0:T(2,128)} copy(f32[8,2,2048]{2,0,1:T(8,128)S(1)} %bitcast.32) | data formatting | bytes 262144 | tf_op jit(solution)/shard_map/reshape | solution.py:185
  (9 shorter events, 0.1 us)
Async XLA Ops:
  0.0 6.8 %copy-start = (f32[8,2]{0,1:T(2,128)S(1)}, f32[8,2]{0,1:T(2,128)}, u32[]{:S(2)}) copy-start(f32[8,2]{0,1:T(2,128)} %param.16) | copy-start | bytes 196
  1.0 9.7 %collective-permute-start.2 = (bf16[32,8,256]{2,1,0:T(8,128)(2,1)S(1)}, bf16[32,8,256]{2,1,0:T(8,128)(2,1)S(1)}, u32[]{:S(2)}, u32[]{:S(2)}) collective-permute-start(bf16[32,8,256]{2,1,0:T(8,128)(2,1)S(1)} %reshape_squeeze.6), channel_id=1, source_target_pairs={{0,24},{4,28},{8,16},{12,20},{16,8},{20,12},{24,0},{28,4},{1,25},{... | collective-permute-start | bytes 393224 | tf_op jit(solution)/shard_map/ppermute | solution.py:148
  6.1 7.4 %collective-permute-start.1 = (bf16[32,8,256]{2,1,0:T(8,128)(2,1)S(1)}, bf16[32,8,256]{2,1,0:T(8,128)(2,1)S(1)}, u32[]{:S(2)}, u32[]{:S(2)}) collective-permute-start(bf16[32,8,256]{2,1,0:T(8,128)(2,1)S(1)} %reshape_squeeze.6), channel_id=1, source_target_pairs={{0,8},{4,12},{8,0},{12,4},{16,24},{20,28},{24,16},{28,20},{1,9},{5... | collective-permute-start | bytes 393224 | tf_op jit(solution)/shard_map/ppermute | solution.py:148
  6.1 11.1 %collective-permute-start = (bf16[32,8,256]{2,1,0:T(8,128)(2,1)S(1)}, bf16[32,8,256]{2,1,0:T(8,128)(2,1)S(1)}, u32[]{:S(2)}, u32[]{:S(2)}) collective-permute-start(bf16[32,8,256]{2,1,0:T(8,128)(2,1)S(1)} %reshape_squeeze.6), channel_id=1, source_target_pairs={{0,16},{4,20},{8,24},{12,28},{16,0},{20,4},{24,8},{28,12},{1,17},{... | collective-permute-start | bytes 393224 | tf_op jit(solution)/shard_map/ppermute | solution.py:148
  17.3 2.6 %copy-start.1 = (bf16[32,32,256]{2,1,0:T(8,128)(2,1)}, bf16[32,32,256]{2,1,0:T(8,128)(2,1)S(1)}, u32[]{:S(2)}) copy-start(bf16[32,32,256]{2,1,0:T(8,128)(2,1)S(1)} %pad_maximum_fusion.ga_ref) | copy-start | bytes 1572868
  17.3 2.5 %collective-permute-start.3 = (bf16[32,32,256]{2,1,0:T(8,128)(2,1)S(1)}, bf16[32,32,256]{2,1,0:T(8,128)(2,1)S(1)}, u32[]{:S(2)}, u32[]{:S(2)}) collective-permute-start(bf16[32,32,256]{2,1,0:T(8,128)(2,1)S(1)} %pad_maximum_fusion.ga_ref), channel_id=1, source_target_pairs={{0,4},{4,0},{8,12},{12,8},{16,20},{20,16},{24,28},{28,24},{1,5},{5... | collective-permute-start | bytes 1572872 | tf_op jit(solution)/shard_map/ppermute | solution.py:148
  19.8 0.8 %copy-start.2 = (bf16[32,32,256]{2,1,0:T(8,128)(2,1)}, bf16[32,32,256]{2,1,0:T(8,128)(2,1)S(1)}, u32[]{:S(2)}) copy-start(bf16[32,32,256]{2,1,0:T(8,128)(2,1)S(1)} %collective-permute-done.3.gb_ref) | copy-start | bytes 1572868
  23.5 10.4 %collective-permute-start.6 = (bf16[2,64,32]{2,1,0:T(8,128)(2,1)}, bf16[2,64,32]{2,1,0:T(8,128)(2,1)S(1)}, u32[]{:S(2)}, u32[]{:S(2)}) collective-permute-start(bf16[2,64,32]{2,1,0:T(8,128)(2,1)} %get-tuple-element.14), channel_id=1, source_target_pairs={{0,3},{1,2},{2,1},{3,0},{4,7},{5,6},{6,5},{7,4},{8,11},{9,10},{10,... | collective-permute-start | bytes 24584 | tf_op jit(solution)/shard_map/ppermute | solution.py:200
  26.0 7.9 %collective-permute-start.5 = (bf16[2,64,32]{2,1,0:T(8,128)(2,1)}, bf16[2,64,32]{2,1,0:T(8,128)(2,1)S(1)}, u32[]{:S(2)}, u32[]{:S(2)}) collective-permute-start(bf16[2,64,32]{2,1,0:T(8,128)(2,1)} %get-tuple-element.14), channel_id=1, source_target_pairs={{0,2},{1,3},{2,0},{3,1},{4,6},{5,7},{6,4},{7,5},{8,10},{9,11},{10,... | collective-permute-start | bytes 24584 | tf_op jit(solution)/shard_map/ppermute | solution.py:200
  26.5 7.4 %collective-permute-start.4 = (bf16[2,64,32]{2,1,0:T(8,128)(2,1)}, bf16[2,64,32]{2,1,0:T(8,128)(2,1)S(1)}, u32[]{:S(2)}, u32[]{:S(2)}) collective-permute-start(bf16[2,64,32]{2,1,0:T(8,128)(2,1)} %get-tuple-element.14), channel_id=1, source_target_pairs={{0,1},{1,0},{2,3},{3,2},{4,5},{5,4},{6,7},{7,6},{8,9},{9,8},{10,11... | collective-permute-start | bytes 24584 | tf_op jit(solution)/shard_map/ppermute | solution.py:200
  27.6 6.3 %copy-start.3 = (bf16[2,64,32]{2,1,0:T(8,128)(2,1)S(1)}, bf16[2,64,32]{2,1,0:T(8,128)(2,1)}, u32[]{:S(2)}) copy-start(bf16[2,64,32]{2,1,0:T(8,128)(2,1)} %get-tuple-element.14) | copy-start | bytes 24580
  37.1 2.5 %collective-permute-start.7 = (f32[32,4096]{1,0:T(8,128)}, f32[32,4096]{1,0:T(8,128)S(1)}, u32[]{:S(2)}, u32[]{:S(2)}) collective-permute-start(f32[32,4096]{1,0:T(8,128)} %shard_map.130), channel_id=1, source_target_pairs={{0,4},{4,0},{8,12},{12,8},{16,20},{20,16},{24,28},{28,24},{1,5},{5... | collective-permute-start | bytes 1572872 | tf_op jit(solution)/shard_map/ppermute | solution.py:148
  40.8 12.4 %collective-permute-start.8 = (f32[8,4096]{1,0:T(8,128)S(1)}, f32[8,4096]{1,0:T(8,128)S(1)}, u32[]{:S(2)}, u32[]{:S(2)}) collective-permute-start(f32[8,4096]{1,0:T(8,128)S(1)} %get-tuple-element.17), channel_id=1, source_target_pairs={{0,16},{4,20},{8,24},{12,28},{16,0},{20,4},{24,8},{28,12},{1,17},{... | collective-permute-start | bytes 393224 | tf_op jit(solution)/shard_map/ppermute | solution.py:148
  41.6 11.5 %collective-permute-start.10 = (f32[8,4096]{1,0:T(8,128)S(1)}, f32[8,4096]{1,0:T(8,128)S(1)}, u32[]{:S(2)}, u32[]{:S(2)}) collective-permute-start(f32[8,4096]{1,0:T(8,128)S(1)} %get-tuple-element.18), channel_id=1, source_target_pairs={{0,24},{4,28},{8,16},{12,20},{16,8},{20,12},{24,0},{28,4},{1,25},{... | collective-permute-start | bytes 393224 | tf_op jit(solution)/shard_map/ppermute | solution.py:148
  43.4 11.1 %collective-permute-start.9 = (f32[8,4096]{1,0:T(8,128)S(1)}, f32[8,4096]{1,0:T(8,128)S(1)}, u32[]{:S(2)}, u32[]{:S(2)}) collective-permute-start(f32[8,4096]{1,0:T(8,128)S(1)} %get-tuple-element.19), channel_id=1, source_target_pairs={{0,8},{4,12},{8,0},{12,4},{16,24},{20,28},{24,16},{28,20},{1,9},{5... | collective-permute-start | bytes 393224 | tf_op jit(solution)/shard_map/ppermute | solution.py:148

commit v10 on v9

--- a/solution.py
+++ b/solution.py
@@ -97,18 +97,20 @@
         out_ref[:, row_count + l * LEAF:row_count + (l + 1) * LEAF] = f_im
 
 
-def _far_kernel(qw_ref, rank_ref, near_ref, bl_ref, cp_ref, bpa_ref, out_ref, cu_ref):
+def _far_kernel(qw_ref, rank_ref, near_ref, bl_ref, cp_ref, *refs):
+    part_refs = refs[:-2]
+    out_ref, cu_ref = refs[-2:]
     source_count = near_ref.shape[0]
     row_count = bl_ref.shape[2]
     rank_width = bl_ref.shape[1]
-    blocks = bpa_ref.shape[0]
-    coupling_rank = bpa_ref.shape[3]
+    blocks = len(part_refs) + 1
+    coupling_rank = part_refs[0].shape[2]
 
     c_re = jnp.zeros((source_count, rank_width), jnp.float32)
     c_im = jnp.zeros((source_count, rank_width), jnp.float32)
     for u in range(1, blocks):
-        b_re = bpa_ref[u, 0]
-        b_im = bpa_ref[u, 1]
+        b_re = part_refs[u - 1][0]
+        b_im = part_refs[u - 1][1]
         k_re = cp_ref[0, :, u * coupling_rank:(u + 1) * coupling_rank]
         k_im = cp_ref[1, :, u * coupling_rank:(u + 1) * coupling_rank]
         c_re = c_re + (_nt(b_re, k_re) - _nt(b_im, k_im))
@@ -196,9 +198,8 @@
     count = lax.axis_size(axis_name)
     if count > 4:
         parts, _ = _all_gather(x[None], axis_name, 0)
-        return jnp.concatenate(parts, axis=0)
-    parts = [x] + [lax.ppermute(x, axis_name, [(i, i ^ p) for i in range(count)]) for p in range(1, count)]
-    return jnp.stack(parts, axis=0)
+        return list(jnp.concatenate(parts, axis=0)[1:])
+    return [lax.ppermute(x, axis_name, [(i, i ^ p) for i in range(count)]) for p in range(1, count)]
 
 
 def shards(
@@ -233,7 +234,13 @@
     own_sin = lax.reduce_precision(jnp.sin(theta), exponent_bits=8, mantissa_bits=7)
 
     local_panels = panels[0].reshape(panel_count, local_sources, 2 * panel_width)
-    (first, second), (own_cos, own_sin) = _all_gather(local_panels, "ang", 1, (own_cos, own_sin))
+    row_blocks = lax.axis_size("row")
+    me = lax.axis_index("row")
+    coupling = block_coupling[0, 0]
+    coupling = coupling.reshape(2, rank_width, row_blocks, coupling.shape[2] // row_blocks)
+    offsets = jnp.array(_position_offsets(row_blocks), jnp.int32)
+    coupling = jnp.take(coupling, me ^ offsets, axis=2).reshape(block_coupling.shape[2:])
+    (first, second), (own_cos, own_sin, coupling) = _all_gather(local_panels, "ang", 1, (own_cos, own_sin, coupling))
     rank = rank_count[0].reshape(1)
 
     excitation, projected = pl.pallas_call(
@@ -249,14 +256,7 @@
             pltpu.VMEM((slot_count, source_count, panel_width), jnp.float32),
         ],
     )(panel_slot[0], own_cos, own_sin, rank, first, second, block_right[0])
-
-    row_blocks = lax.axis_size("row")
     all_projected = _exchange(projected, "row")
-    me = lax.axis_index("row")
-    coupling = block_coupling[0, 0]
-    coupling = coupling.reshape(2, rank_width, row_blocks, coupling.shape[2] // row_blocks)
-    offsets = jnp.array(_position_offsets(row_blocks), jnp.int32)
-    coupling = jnp.take(coupling, me ^ offsets, axis=2).reshape(block_coupling.shape[2:])
 
     near = pl.pallas_call(
         _near_kernel,
@@ -279,11 +279,10 @@
                 pl.BlockSpec((half, 2 * row_count), lambda i, h=h: (h, 0)),
                 pl.BlockSpec(block_left.shape[1:], lambda i: (0, 0, 0)),
                 pl.BlockSpec(coupling.shape, lambda i: (0, 0, 0)),
-                pl.BlockSpec((row_blocks, 2, half, rank_width), lambda i, h=h: (0, 0, h, 0)),
-            ],
+            ] + [pl.BlockSpec((2, half, rank_width), lambda i, h=h: (0, h, 0))] * (row_blocks - 1),
             out_specs=pl.BlockSpec((half, 2 * row_count), lambda i: (0, 0)),
             scratch_shapes=[pltpu.VMEM((2, half, rank_width), jnp.bfloat16)],
-        )(quad_weight[0], rank, near, block_left[0], coupling, all_projected))
+        )(quad_weight[0], rank, near, block_left[0], coupling, *all_projected))
     return _reduce_scatter(halves[1], halves[0], "ang", (local_sources, 2, row_count))
 
 

time: 55.7 us -> 54.4 us (0.977)
  other arithmetic: 5.79 us -> 4.86 us
  waiting for transfers between devices: 16.7 us -> 15.9 us
    ppermute x8, waiting for transfers between devices: 16.7 us -> 15.9 us  [_permute(): return lax.ppermute(x, axis_name, [(i, i ^ offset) for i in range(count)])]
    another operation x1 -> x0, other arithmetic: 0.69 us -> none  [_exchange(): return jnp.stack(parts, axis=0)]
    unnamed x8 -> x12, local copies, waits for them, and re-layouts: 0.8 us -> 1.41 us
  transfers between devices with their start and end apart: 11 -> 11, of which waited for: 4 -> 5; matrix products, arithmetic and copies ran while one was open for 11% -> 11% of each run, Pallas kernels for 16% -> 16%
where the time goes in v10:
time: 54.4 us; the launch traced here: 54.1 us
  waiting for transfers between devices  15.9 us (29%)
  Pallas kernels  14.2 us (26%)
  starting transfers between devices  12.9 us (24%)
  local copies, waits for them, and re-layouts  5.49 us (10%)
  other arithmetic  4.86 us (9%)
  between operations  0.81 us (1%)
    ppermute x8, waiting for transfers between devices, _permute(): return lax.ppermute(x, axis_name, [(i, i ^ offset) for i in range(count)])  15.9 us
    ppermute x8, starting transfers between devices, _permute(): return lax.ppermute(x, axis_name, [(i, i ^ offset) for i in range(count)])  9.38 us
    pallas_call x1, Pallas kernels, shards(): pl.pallas_call(_near_kernel, out_shape=jax.ShapeDtypeStruct((source_count...  6.26 us
    pallas_call x2, Pallas kernels, shards(): pl.pallas_call(_far_kernel, out_shape=jax.ShapeDtypeStruct((half, 2 * row...  4.98 us
    ppermute x3, starting transfers between devices, _exchange(): lax.ppermute(x, axis_name, [(i, i ^ p) for i in range(count)])  3.49 us
    pallas_call x1, Pallas kernels, shards(): pl.pallas_call(_excite_kernel, out_shape=(jax.ShapeDtypeStruct((2, source...  2.92 us
    reduce_precision x1, other arithmetic, shards(): lax.reduce_precision(jnp.sin(theta), exponent_bits=8, mantissa_bits=7)  1.78 us
    unnamed x12, local copies, waits for them, and re-layouts  1.41 us
  transfers between devices with their start and end apart: 11, of which 5 were waited for; matrix products, arithmetic and copies ran while one was open for 11% of the time, Pallas kernels for 16%

profile of v10, /device:TPU:0, one launch (start us, length us, event | category | flops | bytes accessed | tf_op | source)
XLA Modules:
  0.0 54.1 jit_solution(12204075581017704870)
XLA Ops:
  0.0 0.0 copy-start
  0.0 1.0 %reshape_squeeze.6 = bf16[32,8,256]{2,1,0:T(8,128)(2,1)S(1)} reshape(bf16[1,32,8,2,128]{4,3,2,1,0:T(2,128)(2,1)} %param.13) | data formatting | bytes 262144 | tf_op jit(solution)/shard_map/reshape;squeeze | solution.py:236
  1.0 5.1 %collective-permute-start.2 = (bf16[32,8,256]{2,1,0:T(8,128)(2,1)S(1)}, bf16[32,8,256]{2,1,0:T(8,128)(2,1)S(1)}, u32[]{:S(2)}, u32[]{:S(2)}) collective-permute-start(bf16[32,8,256]{2,1,0:T(8,128)(2,1)S(1)} %reshape_squeeze.6), channel_id=1, source_target_pairs={{0,24},{4,28},{8,16},{12,20},{16,8},{20,12},{24,0},{28,4},{1,25},{... | collective-permute-start | bytes 393224 | tf_op jit(solution)/shard_map/ppermute | solution.py:150
  6.1 0.0 collective-permute-start.1
  6.1 0.6 %collective-permute-start = (bf16[32,8,256]{2,1,0:T(8,128)(2,1)S(1)}, bf16[32,8,256]{2,1,0:T(8,128)(2,1)S(1)}, u32[]{:S(2)}, u32[]{:S(2)}) collective-permute-start(bf16[32,8,256]{2,1,0:T(8,128)(2,1)S(1)} %reshape_squeeze.6), channel_id=1, source_target_pairs={{0,16},{4,20},{8,24},{12,28},{16,0},{20,4},{24,8},{28,12},{1,17},{... | collective-permute-start | bytes 393224 | tf_op jit(solution)/shard_map/ppermute | solution.py:150
  6.8 0.1 constant_dynamic-slice_fusion
  6.9 0.5 fusion.3
  7.4 0.1 broadcast_in_dim.16
  7.5 0.1 broadcast_in_dim.17
  7.6 0.7 %convert_bitcast_fusion = f32[32,2]{0,1:T(2,128)S(1)} fusion(s32[1,32,2]{1,2,0:T(2,128)} %param.15), kind=kLoop, calls=%fused_computation.9 | loop fusion | flops 64 | bytes 512 | tf_op jit(solution)/shard_map/convert_element_type | solution.py:230
  8.2 0.8 %reshape_squeeze.7 = bf16[2,32,4,32]{3,2,1,0:T(4,128)(2,1)S(1)} reshape(bf16[1,1,2,32,128]{4,3,2,1,0:T(8,128)(2,1)} %param.22) | data formatting | bytes 32768 | tf_op jit(solution)/shard_map/reshape;squeeze | solution.py:240
  9.1 0.6 %gather_fusion = bf16[4,2,32,32]{3,2,1,0:T(8,128)(2,1)S(1)} fusion(bf16[2,32,4,32]{3,1,2,0:T(8,128)(2,1)S(1)} %copy.17, s32[1024]{0:T(1024)S(1)} %pad_clamp_fusion), kind=kCustom, calls=%fused_computation | custom fusion | bytes 32784 | tf_op jit(solution)/shard_map/jit(_take)/gather | solution.py:242
  9.6 0.1 copy.18
  9.7 0.1 gather.7
  9.8 0.6 %broadcast_select_fusion.cp_ref = bf16[2,32,128]{2,1,0:T(8,128)(2,1)} fusion(bf16[2,32,128]{2,1,0:T(8,128)(2,1)S(1)} %gather.7, pred[128]{0:T(512)(128)(4,1)S(1)} %broadcast_in_dim.17), kind=kLoop, calls=%fused_computation.5 | loop fusion | flops 8192 | bytes 32896 | tf_op jit(solution)/shard_map/jit(_take)/select_n | solution.py:242
  10.4 1.8 %reduce-precision_bitcast_fusion = (f32[32]{0:T(128)}, f32[32,1]{0,1:T(1,128)S(1)}) fusion(f32[32,2]{0,1:T(2,128)S(1)} %convert_bitcast_fusion, f32[]{:T(128)} %bitcast.5, f32[]{:T(128)} %bitcast.3), kind=kLoop, calls=%fused_computation.10 | loop fusion | flops 128 | bytes 520 | tf_op jit(solution)/shard_map/reduce_precision | solution.py:234
  12.2 0.6 %reduce-precision_bitcast_fusion.1.cos_ref = f32[32]{0:T(128)} fusion(f32[32,1]{0,1:T(1,128)S(1)} %get-tuple-element.18), kind=kLoop, calls=%fused_computation.11 | loop fusion | flops 32 | bytes 256 | tf_op jit(solution)/shard_map/reduce_precision | solution.py:233
  12.8 0.0 collective-permute-done.2
  12.8 0.8 %collective-permute-done.1 = bf16[32,8,256]{2,1,0:T(8,128)(2,1)S(1)} collective-permute-done((bf16[32,8,256]{2,1,0:T(8,128)(2,1)S(1)}, bf16[32,8,256]{2,1,0:T(8,128)(2,1)S(1)}, u32[]{:S(2)}, u32[]{:S(2)}) %collective-permute-start.1) | collective-permute-done | bytes 131104 | tf_op jit(solution)/shard_map/ppermute | solution.py:150
  13.5 3.7 %collective-permute-done = bf16[32,8,256]{2,1,0:T(8,128)(2,1)S(1)} collective-permute-done((bf16[32,8,256]{2,1,0:T(8,128)(2,1)S(1)}, bf16[32,8,256]{2,1,0:T(8,128)(2,1)S(1)}, u32[]{:S(2)}, u32[]{:S(2)}) %collective-permute-start) | collective-permute-done | bytes 131104 | tf_op jit(solution)/shard_map/ppermute | solution.py:150
  17.2 0.1 pad_maximum_fusion.ga_ref
  17.3 0.1 collective-permute-start.3
  18.0 1.2 %collective-permute-done.3.gb_ref = bf16[32,32,256]{2,1,0:T(8,128)(2,1)S(1)} collective-permute-done((bf16[32,32,256]{2,1,0:T(8,128)(2,1)S(1)}, bf16[32,32,256]{2,1,0:T(8,128)(2,1)S(1)}, u32[]{:S(2)}, u32[]{:S(2)}) %collective-permute-start.3) | collective-permute-done | bytes 524320 | tf_op jit(solution)/shard_map/ppermute | solution.py:150
  19.3 0.8 %copy-done.2 = bf16[32,32,256]{2,1,0:T(8,128)(2,1)} copy-done((bf16[32,32,256]{2,1,0:T(8,128)(2,1)}, bf16[32,32,256]{2,1,0:T(8,128)(2,1)S(1)}, u32[]{:S(2)}) %copy-start.2) | copy-done | bytes 524312
  20.0 2.9 %shard_map.127 = (bf16[2,64,2048]{2,1,0:T(8,128)(2,1)}, bf16[2,64,32]{2,1,0:T(8,128)(2,1)}) custom-call(s32[32]{0:T(128)} %bitcast.33, f32[32]{0:T(128)} %reduce-precision_bitcast_fusion.1.cos_ref, f32[32]{0:T(128)} %get-tuple-element.12.sin_ref, s32[1]{0:T(128)} %bitcast.20.rank_ref, bf16[32,32,256]{2,1,0:T(8,128)(2,1)} %copy-done.1, ...), custom_call_target="tpu_custom_call" | custom-call | tf_op jit(solution)/shard_map/pallas_call | solution.py:246
  23.0 2.4 %collective-permute-start.6 = (bf16[2,64,32]{2,1,0:T(8,128)(2,1)}, bf16[2,64,32]{2,1,0:T(8,128)(2,1)S(1)}, u32[]{:S(2)}, u32[]{:S(2)}) collective-permute-start(bf16[2,64,32]{2,1,0:T(8,128)(2,1)} %get-tuple-element.16), channel_id=1, source_target_pairs={{0,3},{1,2},{2,1},{3,0},{4,7},{5,6},{6,5},{7,4},{8,11},{9,10},{10,... | collective-permute-start | bytes 24584 | tf_op jit(solution)/shard_map/ppermute | solution.py:202
  25.4 0.5 collective-permute-start.5
  25.9 0.5 collective-permute-start.4
  26.5 6.3 %shard_map.128.near_ref = f32[64,4096]{1,0:T(8,128)} custom-call(bf16[2,64,2048]{2,1,0:T(8,128)(2,1)} %get-tuple-element.14.e_ref, bf16[2,2048,256]{2,1,0:T(8,128)(2,1)} %bitcast.23, bf16[3,2,32,2048]{3,2,1,0:T(8,128)(2,1)} %bitcast.26, bf16[3,2,32,2048]{3,2,1,0:T(8,128)(2,1)} %bitcast.27), custom_call_target="tpu_custom_call" | custom-call | tf_op jit(solution)/shard_map/pallas_call | solution.py:261
  32.7 0.0 collective-permute-done.6.refs_2_
  32.7 0.0 collective-permute-done.5.refs_1_
  32.7 0.0 collective-permute-done.4.refs_0_
  32.7 0.0 copy-start.5
  32.8 0.6 %copy-done.3 = bf16[2,64,32]{2,1,0:T(8,128)(2,1)} copy-done((bf16[2,64,32]{2,1,0:T(8,128)(2,1)}, bf16[2,64,32]{2,1,0:T(8,128)(2,1)S(1)}, u32[]{:S(2)}) %copy-start.3) | copy-done | bytes 8216
  33.3 0.0 copy-done.4
  33.4 0.0 copy-done.5
  33.4 2.5 %shard_map.130 = f32[32,4096]{1,0:T(8,128)} custom-call(f32[2]{0:T(128)} %bitcast.31, s32[1]{0:T(128)} %bitcast.22.rank_ref, f32[64,4096]{1,0:T(8,128)} %shard_map.128.near_ref, bf16[2,32,2048]{2,1,0:T(8,128)(2,1)} %bitcast.24, bf16[2,32,128]{2,1,0:T(8,128)(2,1)} %broadcast_select_fusion.cp_ref, bf16[2,64,32]{2,1,0:T(8,128)(2,1)} %copy-done.5, ...), custom_call_target="tpu_custom_call" | custom-call | tf_op jit(solution)/shard_map/pallas_call | solution.py:272
  35.9 0.0 collective-permute-start.7
  35.9 2.5 %shard_map.129 = f32[32,4096]{1,0:T(8,128)} custom-call(f32[2]{0:T(128)} %bitcast.32, s32[1]{0:T(128)} %bitcast.21.rank_ref, f32[64,4096]{1,0:T(8,128)} %shard_map.128.near_ref, bf16[2,32,2048]{2,1,0:T(8,128)(2,1)} %bitcast.25, bf16[2,32,128]{2,1,0:T(8,128)(2,1)} %broadcast_select_fusion.cp_ref, bf16[2,64,32]{2,1,0:T(8,128)(2,1)} %copy-done.5, ...), custom_call_target="tpu_custom_call" | custom-call | tf_op jit(solution)/shard_map/pallas_call | solution.py:272
  38.4 0.0 collective-permute-done.7
  38.4 1.1 %add.26 = f32[32,4096]{1,0:T(8,128)S(1)} add(f32[32,4096]{1,0:T(8,128)} %shard_map.129, f32[32,4096]{1,0:T(8,128)S(1)} %collective-permute-done.7) | non-fusion elementwise | flops 131072 | bytes 1572864 | tf_op jit(solution)/shard_map/add | solution.py:175
  39.5 0.9 %collective-permute-start.8 = (f32[8,4096]{1,0:T(8,128)S(1)}, f32[8,4096]{1,0:T(8,128)S(1)}, u32[]{:S(2)}, u32[]{:S(2)}) collective-permute-start(f32[8,4096]{1,0:T(8,128)S(1)} %get-tuple-element.19), channel_id=1, source_target_pairs={{0,16},{4,20},{8,24},{12,28},{16,0},{20,4},{24,8},{28,12},{1,17},{... | collective-permute-start | bytes 393224 | tf_op jit(solution)/shard_map/ppermute | solution.py:150
  40.4 1.7 %collective-permute-start.10 = (f32[8,4096]{1,0:T(8,128)S(1)}, f32[8,4096]{1,0:T(8,128)S(1)}, u32[]{:S(2)}, u32[]{:S(2)}) collective-permute-start(f32[8,4096]{1,0:T(8,128)S(1)} %get-tuple-element.20), channel_id=1, source_target_pairs={{0,24},{4,28},{8,16},{12,20},{16,8},{20,12},{24,0},{28,4},{1,25},{... | collective-permute-start | bytes 393224 | tf_op jit(solution)/shard_map/ppermute | solution.py:150
  42.1 0.9 %collective-permute-start.9 = (f32[8,4096]{1,0:T(8,128)S(1)}, f32[8,4096]{1,0:T(8,128)S(1)}, u32[]{:S(2)}, u32[]{:S(2)}) collective-permute-start(f32[8,4096]{1,0:T(8,128)S(1)} %get-tuple-element.21), channel_id=1, source_target_pairs={{0,8},{4,12},{8,0},{12,4},{16,24},{20,28},{24,16},{28,20},{1,9},{5... | collective-permute-start | bytes 393224 | tf_op jit(solution)/shard_map/ppermute | solution.py:150
  43.1 8.9 %collective-permute-done.8 = f32[8,4096]{1,0:T(8,128)S(1)} collective-permute-done((f32[8,4096]{1,0:T(8,128)S(1)}, f32[8,4096]{1,0:T(8,128)S(1)}, u32[]{:S(2)}, u32[]{:S(2)}) %collective-permute-start.8) | collective-permute-done | bytes 131104 | tf_op jit(solution)/shard_map/ppermute | solution.py:150
  52.0 0.0 collective-permute-done.10
  52.0 1.3 %collective-permute-done.9 = f32[8,4096]{1,0:T(8,128)S(1)} collective-permute-done((f32[8,4096]{1,0:T(8,128)S(1)}, f32[8,4096]{1,0:T(8,128)S(1)}, u32[]{:S(2)}, u32[]{:S(2)}) %collective-permute-start.9) | collective-permute-done | bytes 131104 | tf_op jit(solution)/shard_map/ppermute | solution.py:150
  53.3 0.8 %copy.19 = f32[8,2,2048]{2,1,0:T(2,128)} copy(f32[8,2,2048]{2,0,1:T(8,128)S(1)} %bitcast.28) | data formatting | bytes 262144 | tf_op jit(solution)/shard_map/reshape | solution.py:187
  (12 shorter events, 0.1 us)
Async XLA Ops:
  0.0 6.8 %copy-start = (f32[8,2]{0,1:T(2,128)S(1)}, f32[8,2]{0,1:T(2,128)}, u32[]{:S(2)}) copy-start(f32[8,2]{0,1:T(2,128)} %param.16) | copy-start | bytes 196
  1.0 11.8 %collective-permute-start.2 = (bf16[32,8,256]{2,1,0:T(8,128)(2,1)S(1)}, bf16[32,8,256]{2,1,0:T(8,128)(2,1)S(1)}, u32[]{:S(2)}, u32[]{:S(2)}) collective-permute-start(bf16[32,8,256]{2,1,0:T(8,128)(2,1)S(1)} %reshape_squeeze.6), channel_id=1, source_target_pairs={{0,24},{4,28},{8,16},{12,20},{16,8},{20,12},{24,0},{28,4},{1,25},{... | collective-permute-start | bytes 393224 | tf_op jit(solution)/shard_map/ppermute | solution.py:150
  6.1 7.4 %collective-permute-start.1 = (bf16[32,8,256]{2,1,0:T(8,128)(2,1)S(1)}, bf16[32,8,256]{2,1,0:T(8,128)(2,1)S(1)}, u32[]{:S(2)}, u32[]{:S(2)}) collective-permute-start(bf16[32,8,256]{2,1,0:T(8,128)(2,1)S(1)} %reshape_squeeze.6), channel_id=1, source_target_pairs={{0,8},{4,12},{8,0},{12,4},{16,24},{20,28},{24,16},{28,20},{1,9},{5... | collective-permute-start | bytes 393224 | tf_op jit(solution)/shard_map/ppermute | solution.py:150
  6.1 11.1 %collective-permute-start = (bf16[32,8,256]{2,1,0:T(8,128)(2,1)S(1)}, bf16[32,8,256]{2,1,0:T(8,128)(2,1)S(1)}, u32[]{:S(2)}, u32[]{:S(2)}) collective-permute-start(bf16[32,8,256]{2,1,0:T(8,128)(2,1)S(1)} %reshape_squeeze.6), channel_id=1, source_target_pairs={{0,16},{4,20},{8,24},{12,28},{16,0},{20,4},{24,8},{28,12},{1,17},{... | collective-permute-start | bytes 393224 | tf_op jit(solution)/shard_map/ppermute | solution.py:150
  17.3 2.0 %copy-start.1 = (bf16[32,32,256]{2,1,0:T(8,128)(2,1)}, bf16[32,32,256]{2,1,0:T(8,128)(2,1)S(1)}, u32[]{:S(2)}) copy-start(bf16[32,32,256]{2,1,0:T(8,128)(2,1)S(1)} %pad_maximum_fusion.ga_ref) | copy-start | bytes 1572868
  17.3 2.0 %collective-permute-start.3 = (bf16[32,32,256]{2,1,0:T(8,128)(2,1)S(1)}, bf16[32,32,256]{2,1,0:T(8,128)(2,1)S(1)}, u32[]{:S(2)}, u32[]{:S(2)}) collective-permute-start(bf16[32,32,256]{2,1,0:T(8,128)(2,1)S(1)} %pad_maximum_fusion.ga_ref), channel_id=1, source_target_pairs={{0,4},{4,0},{8,12},{12,8},{16,20},{20,16},{24,28},{28,24},{1,5},{5... | collective-permute-start | bytes 1572872 | tf_op jit(solution)/shard_map/ppermute | solution.py:150
  19.2 0.8 %copy-start.2 = (bf16[32,32,256]{2,1,0:T(8,128)(2,1)}, bf16[32,32,256]{2,1,0:T(8,128)(2,1)S(1)}, u32[]{:S(2)}) copy-start(bf16[32,32,256]{2,1,0:T(8,128)(2,1)S(1)} %collective-permute-done.3.gb_ref) | copy-start | bytes 1572868
  23.0 9.8 %collective-permute-start.6 = (bf16[2,64,32]{2,1,0:T(8,128)(2,1)}, bf16[2,64,32]{2,1,0:T(8,128)(2,1)S(1)}, u32[]{:S(2)}, u32[]{:S(2)}) collective-permute-start(bf16[2,64,32]{2,1,0:T(8,128)(2,1)} %get-tuple-element.16), channel_id=1, source_target_pairs={{0,3},{1,2},{2,1},{3,0},{4,7},{5,6},{6,5},{7,4},{8,11},{9,10},{10,... | collective-permute-start | bytes 24584 | tf_op jit(solution)/shard_map/ppermute | solution.py:202
  25.4 7.3 %collective-permute-start.5 = (bf16[2,64,32]{2,1,0:T(8,128)(2,1)}, bf16[2,64,32]{2,1,0:T(8,128)(2,1)S(1)}, u32[]{:S(2)}, u32[]{:S(2)}) collective-permute-start(bf16[2,64,32]{2,1,0:T(8,128)(2,1)} %get-tuple-element.16), channel_id=1, source_target_pairs={{0,2},{1,3},{2,0},{3,1},{4,6},{5,7},{6,4},{7,5},{8,10},{9,11},{10,... | collective-permute-start | bytes 24584 | tf_op jit(solution)/shard_map/ppermute | solution.py:202
  25.9 6.8 %collective-permute-start.4 = (bf16[2,64,32]{2,1,0:T(8,128)(2,1)}, bf16[2,64,32]{2,1,0:T(8,128)(2,1)S(1)}, u32[]{:S(2)}, u32[]{:S(2)}) collective-permute-start(bf16[2,64,32]{2,1,0:T(8,128)(2,1)} %get-tuple-element.16), channel_id=1, source_target_pairs={{0,1},{1,0},{2,3},{3,2},{4,5},{5,4},{6,7},{7,6},{8,9},{9,8},{10,11... | collective-permute-start | bytes 24584 | tf_op jit(solution)/shard_map/ppermute | solution.py:202
  32.7 0.6 %copy-start.3 = (bf16[2,64,32]{2,1,0:T(8,128)(2,1)}, bf16[2,64,32]{2,1,0:T(8,128)(2,1)S(1)}, u32[]{:S(2)}) copy-start(bf16[2,64,32]{2,1,0:T(8,128)(2,1)S(1)} %collective-permute-done.6.refs_2_) | copy-start | bytes 24580
  32.7 0.6 %copy-start.4 = (bf16[2,64,32]{2,1,0:T(8,128)(2,1)}, bf16[2,64,32]{2,1,0:T(8,128)(2,1)S(1)}, u32[]{:S(2)}) copy-start(bf16[2,64,32]{2,1,0:T(8,128)(2,1)S(1)} %collective-permute-done.5.refs_1_) | copy-start | bytes 24580
  32.7 0.6 %copy-start.5 = (bf16[2,64,32]{2,1,0:T(8,128)(2,1)}, bf16[2,64,32]{2,1,0:T(8,128)(2,1)S(1)}, u32[]{:S(2)}) copy-start(bf16[2,64,32]{2,1,0:T(8,128)(2,1)S(1)} %collective-permute-done.4.refs_0_) | copy-start | bytes 24580
  35.9 2.5 %collective-permute-start.7 = (f32[32,4096]{1,0:T(8,128)}, f32[32,4096]{1,0:T(8,128)S(1)}, u32[]{:S(2)}, u32[]{:S(2)}) collective-permute-start(f32[32,4096]{1,0:T(8,128)} %shard_map.130), channel_id=1, source_target_pairs={{0,4},{4,0},{8,12},{12,8},{16,20},{20,16},{24,28},{28,24},{1,5},{5... | collective-permute-start | bytes 1572872 | tf_op jit(solution)/shard_map/ppermute | solution.py:150
  39.5 12.4 %collective-permute-start.8 = (f32[8,4096]{1,0:T(8,128)S(1)}, f32[8,4096]{1,0:T(8,128)S(1)}, u32[]{:S(2)}, u32[]{:S(2)}) collective-permute-start(f32[8,4096]{1,0:T(8,128)S(1)} %get-tuple-element.19), channel_id=1, source_target_pairs={{0,16},{4,20},{8,24},{12,28},{16,0},{20,4},{24,8},{28,12},{1,17},{... | collective-permute-start | bytes 393224 | tf_op jit(solution)/shard_map/ppermute | solution.py:150
  40.4 11.5 %collective-permute-start.10 = (f32[8,4096]{1,0:T(8,128)S(1)}, f32[8,4096]{1,0:T(8,128)S(1)}, u32[]{:S(2)}, u32[]{:S(2)}) collective-permute-start(f32[8,4096]{1,0:T(8,128)S(1)} %get-tuple-element.20), channel_id=1, source_target_pairs={{0,24},{4,28},{8,16},{12,20},{16,8},{20,12},{24,0},{28,4},{1,25},{... | collective-permute-start | bytes 393224 | tf_op jit(solution)/shard_map/ppermute | solution.py:150
  42.1 11.1 %collective-permute-start.9 = (f32[8,4096]{1,0:T(8,128)S(1)}, f32[8,4096]{1,0:T(8,128)S(1)}, u32[]{:S(2)}, u32[]{:S(2)}) collective-permute-start(f32[8,4096]{1,0:T(8,128)S(1)} %get-tuple-element.21), channel_id=1, source_target_pairs={{0,8},{4,12},{8,0},{12,4},{16,24},{20,28},{24,16},{28,20},{1,9},{5... | collective-permute-start | bytes 393224 | tf_op jit(solution)/shard_map/ppermute | solution.py:150

commit v11 on v10

--- a/solution.py
+++ b/solution.py
@@ -55,52 +55,57 @@
     bp_ref[1] = (_nt(e_re, r_im) + _nt(e_im, r_re)).astype(jnp.bfloat16)
 
 
-def _near_kernel(e_ref, leaf_ref, lr_ref, ll_ref, out_ref, pj_ref):
+def _near_kernel(e_ref, leaf_ref, lr_ref, ll_ref, out_re, out_im, pj_ref):
     _, source_count, row_count = e_ref.shape
     levels = lr_ref.shape[0]
-    e_re = e_ref[0]
-    e_im = e_ref[1]
-
-    first_group = []
+    width = leaf_ref.shape[1]
+    l = pl.program_id(0)
+
+    group_starts = []
     slot = 0
     for j in range(levels):
-        node = row_count // 2 ** (j + 1)
-        first_group.append(slot)
-        for g in range(2 ** (j + 1)):
-            cols = slice(g * node, (g + 1) * node)
-            a = e_re[:, cols]
-            b = e_im[:, cols]
-            r_re = lr_ref[j, 0, :, cols]
-            r_im = lr_ref[j, 1, :, cols]
-            pj_ref[slot, 0] = (_nt(a, r_re) - _nt(b, r_im)).astype(jnp.bfloat16)
-            pj_ref[slot, 1] = (_nt(a, r_im) + _nt(b, r_re)).astype(jnp.bfloat16)
-            slot += 1
-
-    for l in range(row_count // LEAF):
-        cols = slice(l * LEAF, (l + 1) * LEAF)
-        a = e_re[:, cols]
-        b = e_im[:, cols]
-        lf_re = leaf_ref[0, cols, :]
-        lf_im = leaf_ref[1, cols, :]
-        f_re = _nt(a, lf_re) - _nt(b, lf_im)
-        f_im = _nt(a, lf_im) + _nt(b, lf_re)
+        group_starts.append(slot)
+        slot += 2 ** (j + 1)
+
+    @pl.when(l == 0)
+    def _():
+        e_re = e_ref[0]
+        e_im = e_ref[1]
         for j in range(levels):
             node = row_count // 2 ** (j + 1)
-            g = (l * LEAF) // node
-            p_re = pj_ref[first_group[j] + (g ^ 1), 0]
-            p_im = pj_ref[first_group[j] + (g ^ 1), 1]
-            m_re = ll_ref[j, 0, :, cols]
-            m_im = ll_ref[j, 1, :, cols]
-            f_re = f_re + (_nn(p_re, m_re) - _nn(p_im, m_im))
-            f_im = f_im + (_nn(p_re, m_im) + _nn(p_im, m_re))
-        out_ref[:, cols] = f_re
-        out_ref[:, row_count + l * LEAF:row_count + (l + 1) * LEAF] = f_im
-
-
-def _far_kernel(qw_ref, rank_ref, near_ref, bl_ref, cp_ref, *refs):
+            for g in range(2 ** (j + 1)):
+                cols = slice(g * node, (g + 1) * node)
+                a = e_re[:, cols]
+                b = e_im[:, cols]
+                r_re = lr_ref[j, 0, :, cols]
+                r_im = lr_ref[j, 1, :, cols]
+                pj_ref[group_starts[j] + g, 0] = (_nt(a, r_re) - _nt(b, r_im)).astype(jnp.bfloat16)
+                pj_ref[group_starts[j] + g, 1] = (_nt(a, r_im) + _nt(b, r_re)).astype(jnp.bfloat16)
+
+    start = pl.multiple_of(l * width, width)
+    a = e_ref[0, :, pl.ds(start, width)]
+    b = e_ref[1, :, pl.ds(start, width)]
+    lf_re = leaf_ref[0]
+    lf_im = leaf_ref[1]
+    f_re = _nt(a, lf_re) - _nt(b, lf_im)
+    f_im = _nt(a, lf_im) + _nt(b, lf_re)
+    for j in range(levels):
+        node = row_count // 2 ** (j + 1)
+        sibling = group_starts[j] + ((l * width) // node ^ 1)
+        p_re = pj_ref[sibling, 0]
+        p_im = pj_ref[sibling, 1]
+        m_re = ll_ref[j, 0]
+        m_im = ll_ref[j, 1]
+        f_re = f_re + (_nn(p_re, m_re) - _nn(p_im, m_im))
+        f_im = f_im + (_nn(p_re, m_im) + _nn(p_im, m_re))
+    out_re[...] = f_re
+    out_im[...] = f_im
+
+
+def _far_kernel(qw_ref, rank_ref, near_re, near_im, bl_ref, cp_ref, *refs):
     part_refs = refs[:-2]
     out_ref, cu_ref = refs[-2:]
-    source_count = near_ref.shape[0]
+    source_count = near_re.shape[0]
     row_count = bl_ref.shape[2]
     rank_width = bl_ref.shape[1]
     blocks = len(part_refs) + 1
@@ -129,8 +134,8 @@
         zero = jnp.zeros((rank_width, LEAF), jnp.bfloat16)
         q_re = jnp.where(keep, bl_ref[0, :, cols], zero)
         q_im = jnp.where(keep, bl_ref[1, :, cols], zero)
-        f_re = near_ref[:, cols] + (_nn(coupled_re, q_re) - _nn(coupled_im, q_im))
-        f_im = near_ref[:, imag_cols] + (_nn(coupled_re, q_im) + _nn(coupled_im, q_re))
+        f_re = near_re[:, cols] + (_nn(coupled_re, q_re) - _nn(coupled_im, q_im))
+        f_im = near_im[:, cols] + (_nn(coupled_re, q_im) + _nn(coupled_im, q_re))
         out_ref[:, cols] = w_re * f_re - w_im * f_im
         out_ref[:, imag_cols] = w_re * f_im + w_im * f_re
 
@@ -258,11 +263,24 @@
     )(panel_slot[0], own_cos, own_sin, rank, first, second, block_right[0])
     all_projected = _exchange(projected, "row")
 
-    near = pl.pallas_call(
+    leaf_width = leaf_inverse.shape[3]
+    near_re, near_im = pl.pallas_call(
         _near_kernel,
-        out_shape=jax.ShapeDtypeStruct((source_count, 2 * row_count), jnp.float32),
-        in_specs=[_VMEM] * 4,
-        out_specs=_VMEM,
+        out_shape=(
+            jax.ShapeDtypeStruct((source_count, row_count), jnp.float32),
+            jax.ShapeDtypeStruct((source_count, row_count), jnp.float32),
+        ),
+        grid=(row_count // leaf_width,),
+        in_specs=[
+            pl.BlockSpec((2, source_count, row_count), lambda l: (0, 0, 0)),
+            pl.BlockSpec((2, leaf_width, leaf_width), lambda l: (0, l, 0)),
+            pl.BlockSpec(level_right.shape[1:], lambda l: (0, 0, 0, 0)),
+            pl.BlockSpec((levels, 2, rank_width, leaf_width), lambda l: (0, 0, 0, l)),
+        ],
+        out_specs=(
+            pl.BlockSpec((source_count, leaf_width), lambda l: (0, l)),
+            pl.BlockSpec((source_count, leaf_width), lambda l: (0, l)),
+        ),
         scratch_shapes=[pltpu.VMEM((2 ** (levels + 1) - 2, 2, source_count, rank_width), jnp.bfloat16)],
     )(excitation, leaf_inverse[0], level_right[0], level_left[0])
 
@@ -276,13 +294,14 @@
             in_specs=[
                 _SMEM,
                 _SMEM,
-                pl.BlockSpec((half, 2 * row_count), lambda i, h=h: (h, 0)),
+                pl.BlockSpec((half, row_count), lambda i, h=h: (h, 0)),
+                pl.BlockSpec((half, row_count), lambda i, h=h: (h, 0)),
                 pl.BlockSpec(block_left.shape[1:], lambda i: (0, 0, 0)),
                 pl.BlockSpec(coupling.shape, lambda i: (0, 0, 0)),
             ] + [pl.BlockSpec((2, half, rank_width), lambda i, h=h: (0, h, 0))] * (row_blocks - 1),
             out_specs=pl.BlockSpec((half, 2 * row_count), lambda i: (0, 0)),
             scratch_shapes=[pltpu.VMEM((2, half, rank_width), jnp.bfloat16)],
-        )(quad_weight[0], rank, near, block_left[0], coupling, *all_projected))
+        )(quad_weight[0], rank, near_re, near_im, block_left[0], coupling, *all_projected))
     return _reduce_scatter(halves[1], halves[0], "ang", (local_sources, 2, row_count))
 
 

time: 54.4 us -> 56.7 us (1.042)
  Pallas kernels: 14.2 us -> 16.3 us
    pallas_call x1, Pallas kernels: 6.26 us -> 8.45 us  [shards(): pl.pallas_call(_near_kernel, out_shape=(jax.ShapeDtypeStruct((source_coun...]
  transfers between devices with their start and end apart: 11 -> 11, of which waited for: 5 -> 5; matrix products, arithmetic and copies ran while one was open for 11% -> 11% of each run, Pallas kernels for 16% -> 19%
where the time goes in v11:
time: 56.7 us; the launch traced here: 56.2 us
  Pallas kernels  16.3 us (29%)
  waiting for transfers between devices  15.7 us (28%)
  starting transfers between devices  12.9 us (23%)
  local copies, waits for them, and re-layouts  5.55 us (10%)
  other arithmetic  4.99 us (9%)
  between operations  0.83 us (1%)
    ppermute x8, waiting for transfers between devices, _permute(): return lax.ppermute(x, axis_name, [(i, i ^ offset) for i in range(count)])  15.7 us
    ppermute x8, starting transfers between devices, _permute(): return lax.ppermute(x, axis_name, [(i, i ^ offset) for i in range(count)])  9.38 us
    pallas_call x1, Pallas kernels, shards(): pl.pallas_call(_near_kernel, out_shape=(jax.ShapeDtypeStruct((source_coun...  8.45 us
    pallas_call x2, Pallas kernels, shards(): pl.pallas_call(_far_kernel, out_shape=jax.ShapeDtypeStruct((half, 2 * row...  4.93 us
    ppermute x3, starting transfers between devices, _exchange(): lax.ppermute(x, axis_name, [(i, i ^ p) for i in range(count)])  3.49 us
    pallas_call x1, Pallas kernels, shards(): pl.pallas_call(_excite_kernel, out_shape=(jax.ShapeDtypeStruct((2, source...  2.92 us
    reduce_precision x1, other arithmetic, shards(): lax.reduce_precision(jnp.sin(theta), exponent_bits=8, mantissa_bits=7)  1.85 us
    unnamed x12, local copies, waits for them, and re-layouts  1.41 us
  transfers between devices with their start and end apart: 11, of which 5 were waited for; matrix products, arithmetic and copies ran while one was open for 11% of the time, Pallas kernels for 19%

profile of v11, /device:TPU:0, one launch (start us, length us, event | category | flops | bytes accessed | tf_op | source)
XLA Modules:
  0.0 56.2 jit_solution(44956576743092138)
XLA Ops:
  0.0 0.0 copy-start
  0.0 1.0 %reshape_squeeze.6 = bf16[32,8,256]{2,1,0:T(8,128)(2,1)S(1)} reshape(bf16[1,32,8,2,128]{4,3,2,1,0:T(2,128)(2,1)} %param.13) | data formatting | bytes 262144 | tf_op jit(solution)/shard_map/reshape;squeeze | solution.py:241
  1.0 5.1 %collective-permute-start.2 = (bf16[32,8,256]{2,1,0:T(8,128)(2,1)S(1)}, bf16[32,8,256]{2,1,0:T(8,128)(2,1)S(1)}, u32[]{:S(2)}, u32[]{:S(2)}) collective-permute-start(bf16[32,8,256]{2,1,0:T(8,128)(2,1)S(1)} %reshape_squeeze.6), channel_id=1, source_target_pairs={{0,24},{4,28},{8,16},{12,20},{16,8},{20,12},{24,0},{28,4},{1,25},{... | collective-permute-start | bytes 393224 | tf_op jit(solution)/shard_map/ppermute | solution.py:155
  6.1 0.0 collective-permute-start.1
  6.1 0.6 %collective-permute-start = (bf16[32,8,256]{2,1,0:T(8,128)(2,1)S(1)}, bf16[32,8,256]{2,1,0:T(8,128)(2,1)S(1)}, u32[]{:S(2)}, u32[]{:S(2)}) collective-permute-start(bf16[32,8,256]{2,1,0:T(8,128)(2,1)S(1)} %reshape_squeeze.6), channel_id=1, source_target_pairs={{0,16},{4,20},{8,24},{12,28},{16,0},{20,4},{24,8},{28,12},{1,17},{... | collective-permute-start | bytes 393224 | tf_op jit(solution)/shard_map/ppermute | solution.py:155
  6.8 0.1 constant_dynamic-slice_fusion
  6.9 0.6 %fusion.3 = (f32[1,1]{0,1:T(1,128)}, f32[1,1]{0,1:T(1,128)}) fusion(f32[1,2]{0,1:T(2,128)S(1)} %constant_dynamic-slice_fusion), kind=kLoop, calls=%fused_computation.15 | loop fusion | bytes 16 | tf_op jit(solution)/shard_map/slice | solution.py:237
  7.5 0.1 broadcast_in_dim.16
  7.5 0.1 broadcast_in_dim.17
  7.6 0.7 %convert_bitcast_fusion = f32[32,2]{0,1:T(2,128)S(1)} fusion(s32[1,32,2]{1,2,0:T(2,128)} %param.15), kind=kLoop, calls=%fused_computation.9 | loop fusion | flops 64 | bytes 512 | tf_op jit(solution)/shard_map/convert_element_type | solution.py:235
  8.3 0.8 %reshape_squeeze.7 = bf16[2,32,4,32]{3,2,1,0:T(4,128)(2,1)S(1)} reshape(bf16[1,1,2,32,128]{4,3,2,1,0:T(8,128)(2,1)} %param.22) | data formatting | bytes 32768 | tf_op jit(solution)/shard_map/reshape;squeeze | solution.py:245
  9.1 0.6 %gather_fusion = bf16[4,2,32,32]{3,2,1,0:T(8,128)(2,1)S(1)} fusion(bf16[2,32,4,32]{3,1,2,0:T(8,128)(2,1)S(1)} %copy.17, s32[1024]{0:T(1024)S(1)} %pad_clamp_fusion), kind=kCustom, calls=%fused_computation | custom fusion | bytes 32784 | tf_op jit(solution)/shard_map/jit(_take)/gather | solution.py:247
  9.7 0.1 copy.18
  9.8 0.1 gather.7
  9.9 0.6 %broadcast_select_fusion.cp_ref = bf16[2,32,128]{2,1,0:T(8,128)(2,1)} fusion(bf16[2,32,128]{2,1,0:T(8,128)(2,1)S(1)} %gather.7, pred[128]{0:T(512)(128)(4,1)S(1)} %broadcast_in_dim.17), kind=kLoop, calls=%fused_computation.5 | loop fusion | flops 8192 | bytes 32896 | tf_op jit(solution)/shard_map/jit(_take)/select_n | solution.py:247
  10.5 1.8 %reduce-precision_bitcast_fusion = (f32[32]{0:T(128)}, f32[32,1]{0,1:T(1,128)S(1)}) fusion(f32[32,2]{0,1:T(2,128)S(1)} %convert_bitcast_fusion, f32[]{:T(128)} %bitcast.5, f32[]{:T(128)} %bitcast.3), kind=kLoop, calls=%fused_computation.10 | loop fusion | flops 128 | bytes 520 | tf_op jit(solution)/shard_map/reduce_precision | solution.py:239
  12.3 0.6 %reduce-precision_bitcast_fusion.1.cos_ref = f32[32]{0:T(128)} fusion(f32[32,1]{0,1:T(1,128)S(1)} %get-tuple-element.22), kind=kLoop, calls=%fused_computation.11 | loop fusion | flops 32 | bytes 256 | tf_op jit(solution)/shard_map/reduce_precision | solution.py:238
  13.0 0.0 collective-permute-done.2
  13.0 0.6 %collective-permute-done.1 = bf16[32,8,256]{2,1,0:T(8,128)(2,1)S(1)} collective-permute-done((bf16[32,8,256]{2,1,0:T(8,128)(2,1)S(1)}, bf16[32,8,256]{2,1,0:T(8,128)(2,1)S(1)}, u32[]{:S(2)}, u32[]{:S(2)}) %collective-permute-start.1) | collective-permute-done | bytes 131104 | tf_op jit(solution)/shard_map/ppermute | solution.py:155
  13.5 3.7 %collective-permute-done = bf16[32,8,256]{2,1,0:T(8,128)(2,1)S(1)} collective-permute-done((bf16[32,8,256]{2,1,0:T(8,128)(2,1)S(1)}, bf16[32,8,256]{2,1,0:T(8,128)(2,1)S(1)}, u32[]{:S(2)}, u32[]{:S(2)}) %collective-permute-start) | collective-permute-done | bytes 131104 | tf_op jit(solution)/shard_map/ppermute | solution.py:155
  17.2 0.1 pad_maximum_fusion.ga_ref
  17.3 0.1 collective-permute-start.3
  18.0 1.2 %collective-permute-done.3.gb_ref = bf16[32,32,256]{2,1,0:T(8,128)(2,1)S(1)} collective-permute-done((bf16[32,32,256]{2,1,0:T(8,128)(2,1)S(1)}, bf16[32,32,256]{2,1,0:T(8,128)(2,1)S(1)}, u32[]{:S(2)}, u32[]{:S(2)}) %collective-permute-start.3) | collective-permute-done | bytes 524320 | tf_op jit(solution)/shard_map/ppermute | solution.py:155
  19.3 0.8 %copy-done.2 = bf16[32,32,256]{2,1,0:T(8,128)(2,1)} copy-done((bf16[32,32,256]{2,1,0:T(8,128)(2,1)}, bf16[32,32,256]{2,1,0:T(8,128)(2,1)S(1)}, u32[]{:S(2)}) %copy-start.2) | copy-done | bytes 524312
  20.0 2.9 %shard_map.127 = (bf16[2,64,2048]{2,1,0:T(8,128)(2,1)}, bf16[2,64,32]{2,1,0:T(8,128)(2,1)}) custom-call(s32[32]{0:T(128)} %bitcast.33, f32[32]{0:T(128)} %reduce-precision_bitcast_fusion.1.cos_ref, f32[32]{0:T(128)} %get-tuple-element.14.sin_ref, s32[1]{0:T(128)} %bitcast.20.rank_ref, bf16[32,32,256]{2,1,0:T(8,128)(2,1)} %copy-done.1, ...), custom_call_target="tpu_custom_call" | custom-call | tf_op jit(solution)/shard_map/pallas_call | solution.py:251
  23.0 2.4 %collective-permute-start.6 = (bf16[2,64,32]{2,1,0:T(8,128)(2,1)}, bf16[2,64,32]{2,1,0:T(8,128)(2,1)S(1)}, u32[]{:S(2)}, u32[]{:S(2)}) collective-permute-start(bf16[2,64,32]{2,1,0:T(8,128)(2,1)} %get-tuple-element.20), channel_id=1, source_target_pairs={{0,3},{1,2},{2,1},{3,0},{4,7},{5,6},{6,5},{7,4},{8,11},{9,10},{10,... | collective-permute-start | bytes 24584 | tf_op jit(solution)/shard_map/ppermute | solution.py:207
  25.4 0.5 collective-permute-start.5
  25.9 0.5 collective-permute-start.4
  26.4 8.4 %shard_map.128 = (f32[64,2048]{1,0:T(8,128)}, f32[64,2048]{1,0:T(8,128)}) custom-call(bf16[2,64,2048]{2,1,0:T(8,128)(2,1)} %get-tuple-element.16.e_ref, bf16[2,2048,256]{2,1,0:T(8,128)(2,1)} %bitcast.23, bf16[3,2,32,2048]{3,2,1,0:T(8,128)(2,1)} %bitcast.26, bf16[3,2,32,2048]{3,2,1,0:T(8,128)(2,1)} %bitcast.27), custom_call_target="tpu_custom_call" | custom-call | tf_op jit(solution)/shard_map/pallas_call | solution.py:267
  34.9 0.0 collective-permute-done.6.refs_2_
  34.9 0.0 collective-permute-done.5.refs_1_
  34.9 0.0 collective-permute-done.4.refs_0_
  34.9 0.0 copy-start.5
  35.0 0.5 copy-done.3
  35.5 0.0 copy-done.4
  35.5 0.0 copy-done.5
  35.6 2.5 %shard_map.130 = f32[32,4096]{1,0:T(8,128)} custom-call(f32[2]{0:T(128)} %bitcast.31, s32[1]{0:T(128)} %bitcast.22.rank_ref, f32[64,2048]{1,0:T(8,128)} %get-tuple-element.17.near_re, f32[64,2048]{1,0:T(8,128)} %get-tuple-element.18.near_im, bf16[2,32,2048]{2,1,0:T(8,128)(2,1)} %bitcast.24, bf16[2,32,128]{2,1,0:T(8,128)(2,1)} %broadcast_select_fusion.cp_ref, ...), custom_call_target="tpu_custom_call" | custom-call | tf_op jit(solution)/shard_map/pallas_call | solution.py:290
  38.0 0.0 collective-permute-start.7
  38.0 2.5 %shard_map.129 = f32[32,4096]{1,0:T(8,128)} custom-call(f32[2]{0:T(128)} %bitcast.32, s32[1]{0:T(128)} %bitcast.21.rank_ref, f32[64,2048]{1,0:T(8,128)} %get-tuple-element.17.near_re, f32[64,2048]{1,0:T(8,128)} %get-tuple-element.18.near_im, bf16[2,32,2048]{2,1,0:T(8,128)(2,1)} %bitcast.25, bf16[2,32,128]{2,1,0:T(8,128)(2,1)} %broadcast_select_fusion.cp_ref, ...), custom_call_target="tpu_custom_call" | custom-call | tf_op jit(solution)/shard_map/pallas_call | solution.py:290
  40.5 0.0 collective-permute-done.7
  40.5 1.1 %add.26 = f32[32,4096]{1,0:T(8,128)S(1)} add(f32[32,4096]{1,0:T(8,128)} %shard_map.129, f32[32,4096]{1,0:T(8,128)S(1)} %collective-permute-done.7) | non-fusion elementwise | flops 131072 | bytes 1572864 | tf_op jit(solution)/shard_map/add | solution.py:180
  41.7 0.9 %collective-permute-start.8 = (f32[8,4096]{1,0:T(8,128)S(1)}, f32[8,4096]{1,0:T(8,128)S(1)}, u32[]{:S(2)}, u32[]{:S(2)}) collective-permute-start(f32[8,4096]{1,0:T(8,128)S(1)} %get-tuple-element.23), channel_id=1, source_target_pairs={{0,16},{4,20},{8,24},{12,28},{16,0},{20,4},{24,8},{28,12},{1,17},{... | collective-permute-start | bytes 393224 | tf_op jit(solution)/shard_map/ppermute | solution.py:155
  42.6 1.7 %collective-permute-start.10 = (f32[8,4096]{1,0:T(8,128)S(1)}, f32[8,4096]{1,0:T(8,128)S(1)}, u32[]{:S(2)}, u32[]{:S(2)}) collective-permute-start(f32[8,4096]{1,0:T(8,128)S(1)} %get-tuple-element.24), channel_id=1, source_target_pairs={{0,24},{4,28},{8,16},{12,20},{16,8},{20,12},{24,0},{28,4},{1,25},{... | collective-permute-start | bytes 393224 | tf_op jit(solution)/shard_map/ppermute | solution.py:155
  44.3 0.9 %collective-permute-start.9 = (f32[8,4096]{1,0:T(8,128)S(1)}, f32[8,4096]{1,0:T(8,128)S(1)}, u32[]{:S(2)}, u32[]{:S(2)}) collective-permute-start(f32[8,4096]{1,0:T(8,128)S(1)} %get-tuple-element.25), channel_id=1, source_target_pairs={{0,8},{4,12},{8,0},{12,4},{16,24},{20,28},{24,16},{28,20},{1,9},{5... | collective-permute-start | bytes 393224 | tf_op jit(solution)/shard_map/ppermute | solution.py:155
  45.2 8.9 %collective-permute-done.8 = f32[8,4096]{1,0:T(8,128)S(1)} collective-permute-done((f32[8,4096]{1,0:T(8,128)S(1)}, f32[8,4096]{1,0:T(8,128)S(1)}, u32[]{:S(2)}, u32[]{:S(2)}) %collective-permute-start.8) | collective-permute-done | bytes 131104 | tf_op jit(solution)/shard_map/ppermute | solution.py:155
  54.1 0.0 collective-permute-done.10
  54.1 1.3 %collective-permute-done.9 = f32[8,4096]{1,0:T(8,128)S(1)} collective-permute-done((f32[8,4096]{1,0:T(8,128)S(1)}, f32[8,4096]{1,0:T(8,128)S(1)}, u32[]{:S(2)}, u32[]{:S(2)}) %collective-permute-start.9) | collective-permute-done | bytes 131104 | tf_op jit(solution)/shard_map/ppermute | solution.py:155
  55.5 0.8 %copy.19 = f32[8,2,2048]{2,1,0:T(2,128)} copy(f32[8,2,2048]{2,0,1:T(8,128)S(1)} %bitcast.28) | data formatting | bytes 262144 | tf_op jit(solution)/shard_map/reshape | solution.py:192
  (12 shorter events, 0.1 us)
Async XLA Ops:
  0.0 6.8 %copy-start = (f32[8,2]{0,1:T(2,128)S(1)}, f32[8,2]{0,1:T(2,128)}, u32[]{:S(2)}) copy-start(f32[8,2]{0,1:T(2,128)} %param.16) | copy-start | bytes 196
  1.0 11.9 %collective-permute-start.2 = (bf16[32,8,256]{2,1,0:T(8,128)(2,1)S(1)}, bf16[32,8,256]{2,1,0:T(8,128)(2,1)S(1)}, u32[]{:S(2)}, u32[]{:S(2)}) collective-permute-start(bf16[32,8,256]{2,1,0:T(8,128)(2,1)S(1)} %reshape_squeeze.6), channel_id=1, source_target_pairs={{0,24},{4,28},{8,16},{12,20},{16,8},{20,12},{24,0},{28,4},{1,25},{... | collective-permute-start | bytes 393224 | tf_op jit(solution)/shard_map/ppermute | solution.py:155
  6.1 7.4 %collective-permute-start.1 = (bf16[32,8,256]{2,1,0:T(8,128)(2,1)S(1)}, bf16[32,8,256]{2,1,0:T(8,128)(2,1)S(1)}, u32[]{:S(2)}, u32[]{:S(2)}) collective-permute-start(bf16[32,8,256]{2,1,0:T(8,128)(2,1)S(1)} %reshape_squeeze.6), channel_id=1, source_target_pairs={{0,8},{4,12},{8,0},{12,4},{16,24},{20,28},{24,16},{28,20},{1,9},{5... | collective-permute-start | bytes 393224 | tf_op jit(solution)/shard_map/ppermute | solution.py:155
  6.1 11.1 %collective-permute-start = (bf16[32,8,256]{2,1,0:T(8,128)(2,1)S(1)}, bf16[32,8,256]{2,1,0:T(8,128)(2,1)S(1)}, u32[]{:S(2)}, u32[]{:S(2)}) collective-permute-start(bf16[32,8,256]{2,1,0:T(8,128)(2,1)S(1)} %reshape_squeeze.6), channel_id=1, source_target_pairs={{0,16},{4,20},{8,24},{12,28},{16,0},{20,4},{24,8},{28,12},{1,17},{... | collective-permute-start | bytes 393224 | tf_op jit(solution)/shard_map/ppermute | solution.py:155
  17.3 2.0 %copy-start.1 = (bf16[32,32,256]{2,1,0:T(8,128)(2,1)}, bf16[32,32,256]{2,1,0:T(8,128)(2,1)S(1)}, u32[]{:S(2)}) copy-start(bf16[32,32,256]{2,1,0:T(8,128)(2,1)S(1)} %pad_maximum_fusion.ga_ref) | copy-start | bytes 1572868
  17.3 2.0 %collective-permute-start.3 = (bf16[32,32,256]{2,1,0:T(8,128)(2,1)S(1)}, bf16[32,32,256]{2,1,0:T(8,128)(2,1)S(1)}, u32[]{:S(2)}, u32[]{:S(2)}) collective-permute-start(bf16[32,32,256]{2,1,0:T(8,128)(2,1)S(1)} %pad_maximum_fusion.ga_ref), channel_id=1, source_target_pairs={{0,4},{4,0},{8,12},{12,8},{16,20},{20,16},{24,28},{28,24},{1,5},{5... | collective-permute-start | bytes 1572872 | tf_op jit(solution)/shard_map/ppermute | solution.py:155
  19.2 0.8 %copy-start.2 = (bf16[32,32,256]{2,1,0:T(8,128)(2,1)}, bf16[32,32,256]{2,1,0:T(8,128)(2,1)S(1)}, u32[]{:S(2)}) copy-start(bf16[32,32,256]{2,1,0:T(8,128)(2,1)S(1)} %collective-permute-done.3.gb_ref) | copy-start | bytes 1572868
  23.0 11.9 %collective-permute-start.6 = (bf16[2,64,32]{2,1,0:T(8,128)(2,1)}, bf16[2,64,32]{2,1,0:T(8,128)(2,1)S(1)}, u32[]{:S(2)}, u32[]{:S(2)}) collective-permute-start(bf16[2,64,32]{2,1,0:T(8,128)(2,1)} %get-tuple-element.20), channel_id=1, source_target_pairs={{0,3},{1,2},{2,1},{3,0},{4,7},{5,6},{6,5},{7,4},{8,11},{9,10},{10,... | collective-permute-start | bytes 24584 | tf_op jit(solution)/shard_map/ppermute | solution.py:207
  25.4 9.5 %collective-permute-start.5 = (bf16[2,64,32]{2,1,0:T(8,128)(2,1)}, bf16[2,64,32]{2,1,0:T(8,128)(2,1)S(1)}, u32[]{:S(2)}, u32[]{:S(2)}) collective-permute-start(bf16[2,64,32]{2,1,0:T(8,128)(2,1)} %get-tuple-element.20), channel_id=1, source_target_pairs={{0,2},{1,3},{2,0},{3,1},{4,6},{5,7},{6,4},{7,5},{8,10},{9,11},{10,... | collective-permute-start | bytes 24584 | tf_op jit(solution)/shard_map/ppermute | solution.py:207
  25.9 9.0 %collective-permute-start.4 = (bf16[2,64,32]{2,1,0:T(8,128)(2,1)}, bf16[2,64,32]{2,1,0:T(8,128)(2,1)S(1)}, u32[]{:S(2)}, u32[]{:S(2)}) collective-permute-start(bf16[2,64,32]{2,1,0:T(8,128)(2,1)} %get-tuple-element.20), channel_id=1, source_target_pairs={{0,1},{1,0},{2,3},{3,2},{4,5},{5,4},{6,7},{7,6},{8,9},{9,8},{10,11... | collective-permute-start | bytes 24584 | tf_op jit(solution)/shard_map/ppermute | solution.py:207
  34.9 0.6 %copy-start.3 = (bf16[2,64,32]{2,1,0:T(8,128)(2,1)}, bf16[2,64,32]{2,1,0:T(8,128)(2,1)S(1)}, u32[]{:S(2)}) copy-start(bf16[2,64,32]{2,1,0:T(8,128)(2,1)S(1)} %collective-permute-done.6.refs_2_) | copy-start | bytes 24580
  34.9 0.6 %copy-start.4 = (bf16[2,64,32]{2,1,0:T(8,128)(2,1)}, bf16[2,64,32]{2,1,0:T(8,128)(2,1)S(1)}, u32[]{:S(2)}) copy-start(bf16[2,64,32]{2,1,0:T(8,128)(2,1)S(1)} %collective-permute-done.5.refs_1_) | copy-start | bytes 24580
  34.9 0.6 %copy-start.5 = (bf16[2,64,32]{2,1,0:T(8,128)(2,1)}, bf16[2,64,32]{2,1,0:T(8,128)(2,1)S(1)}, u32[]{:S(2)}) copy-start(bf16[2,64,32]{2,1,0:T(8,128)(2,1)S(1)} %collective-permute-done.4.refs_0_) | copy-start | bytes 24580
  38.0 2.5 %collective-permute-start.7 = (f32[32,4096]{1,0:T(8,128)}, f32[32,4096]{1,0:T(8,128)S(1)}, u32[]{:S(2)}, u32[]{:S(2)}) collective-permute-start(f32[32,4096]{1,0:T(8,128)} %shard_map.130), channel_id=1, source_target_pairs={{0,4},{4,0},{8,12},{12,8},{16,20},{20,16},{24,28},{28,24},{1,5},{5... | collective-permute-start | bytes 1572872 | tf_op jit(solution)/shard_map/ppermute | solution.py:155
  41.7 12.4 %collective-permute-start.8 = (f32[8,4096]{1,0:T(8,128)S(1)}, f32[8,4096]{1,0:T(8,128)S(1)}, u32[]{:S(2)}, u32[]{:S(2)}) collective-permute-start(f32[8,4096]{1,0:T(8,128)S(1)} %get-tuple-element.23), channel_id=1, source_target_pairs={{0,16},{4,20},{8,24},{12,28},{16,0},{20,4},{24,8},{28,12},{1,17},{... | collective-permute-start | bytes 393224 | tf_op jit(solution)/shard_map/ppermute | solution.py:155
  42.6 11.5 %collective-permute-start.10 = (f32[8,4096]{1,0:T(8,128)S(1)}, f32[8,4096]{1,0:T(8,128)S(1)}, u32[]{:S(2)}, u32[]{:S(2)}) collective-permute-start(f32[8,4096]{1,0:T(8,128)S(1)} %get-tuple-element.24), channel_id=1, source_target_pairs={{0,24},{4,28},{8,16},{12,20},{16,8},{20,12},{24,0},{28,4},{1,25},{... | collective-permute-start | bytes 393224 | tf_op jit(solution)/shard_map/ppermute | solution.py:155
  44.3 11.1 %collective-permute-start.9 = (f32[8,4096]{1,0:T(8,128)S(1)}, f32[8,4096]{1,0:T(8,128)S(1)}, u32[]{:S(2)}, u32[]{:S(2)}) collective-permute-start(f32[8,4096]{1,0:T(8,128)S(1)} %get-tuple-element.25), channel_id=1, source_target_pairs={{0,8},{4,12},{8,0},{12,4},{16,24},{20,28},{24,16},{28,20},{1,9},{5... | collective-permute-start | bytes 393224 | tf_op jit(solution)/shard_map/ppermute | solution.py:155

commit v12 on v10

--- a/solution.py
+++ b/solution.py
@@ -45,21 +45,21 @@
     for k in range(slots):
         e_ref[0, :, k * width:(k + 1) * width] = acc_re[k].astype(jnp.bfloat16)
         e_ref[1, :, k * width:(k + 1) * width] = acc_im[k].astype(jnp.bfloat16)
-    e_re = e_ref[0]
-    e_im = e_ref[1]
+    sources = e_ref.shape[1]
+    stacked = e_ref[...].reshape(2 * sources, e_ref.shape[2])
     keep = _rank_mask(rank_ref, br_ref.shape[1:])
     zero = jnp.zeros(br_ref.shape[1:], jnp.bfloat16)
-    r_re = jnp.where(keep, br_ref[0], zero)
-    r_im = jnp.where(keep, br_ref[1], zero)
-    bp_ref[0] = (_nt(e_re, r_re) - _nt(e_im, r_im)).astype(jnp.bfloat16)
-    bp_ref[1] = (_nt(e_re, r_im) + _nt(e_im, r_re)).astype(jnp.bfloat16)
+    t_re = _nt(stacked, jnp.where(keep, br_ref[0], zero))
+    t_im = _nt(stacked, jnp.where(keep, br_ref[1], zero))
+    bp_ref[0] = (t_re[:sources] - t_im[sources:]).astype(jnp.bfloat16)
+    bp_ref[1] = (t_im[:sources] + t_re[sources:]).astype(jnp.bfloat16)
 
 
 def _near_kernel(e_ref, leaf_ref, lr_ref, ll_ref, out_ref, pj_ref):
     _, source_count, row_count = e_ref.shape
     levels = lr_ref.shape[0]
-    e_re = e_ref[0]
-    e_im = e_ref[1]
+    sc = source_count
+    stacked = e_ref[...].reshape(2 * sc, row_count)
 
     first_group = []
     slot = 0
@@ -68,31 +68,28 @@
         first_group.append(slot)
         for g in range(2 ** (j + 1)):
             cols = slice(g * node, (g + 1) * node)
-            a = e_re[:, cols]
-            b = e_im[:, cols]
-            r_re = lr_ref[j, 0, :, cols]
-            r_im = lr_ref[j, 1, :, cols]
-            pj_ref[slot, 0] = (_nt(a, r_re) - _nt(b, r_im)).astype(jnp.bfloat16)
-            pj_ref[slot, 1] = (_nt(a, r_im) + _nt(b, r_re)).astype(jnp.bfloat16)
+            ab = stacked[:, cols]
+            t_re = _nt(ab, lr_ref[j, 0, :, cols])
+            t_im = _nt(ab, lr_ref[j, 1, :, cols])
+            pj_ref[slot, 0] = (t_re[:sc] - t_im[sc:]).astype(jnp.bfloat16)
+            pj_ref[slot, 1] = (t_im[:sc] + t_re[sc:]).astype(jnp.bfloat16)
             slot += 1
 
     for l in range(row_count // LEAF):
         cols = slice(l * LEAF, (l + 1) * LEAF)
-        a = e_re[:, cols]
-        b = e_im[:, cols]
-        lf_re = leaf_ref[0, cols, :]
-        lf_im = leaf_ref[1, cols, :]
-        f_re = _nt(a, lf_re) - _nt(b, lf_im)
-        f_im = _nt(a, lf_im) + _nt(b, lf_re)
+        ab = stacked[:, cols]
+        t_re = _nt(ab, leaf_ref[0, cols, :])
+        t_im = _nt(ab, leaf_ref[1, cols, :])
+        f_re = t_re[:sc] - t_im[sc:]
+        f_im = t_im[:sc] + t_re[sc:]
         for j in range(levels):
             node = row_count // 2 ** (j + 1)
             g = (l * LEAF) // node
-            p_re = pj_ref[first_group[j] + (g ^ 1), 0]
-            p_im = pj_ref[first_group[j] + (g ^ 1), 1]
-            m_re = ll_ref[j, 0, :, cols]
-            m_im = ll_ref[j, 1, :, cols]
-            f_re = f_re + (_nn(p_re, m_re) - _nn(p_im, m_im))
-            f_im = f_im + (_nn(p_re, m_im) + _nn(p_im, m_re))
+            pp = pj_ref[first_group[j] + (g ^ 1)].reshape(2 * sc, pj_ref.shape[3])
+            v_re = _nn(pp, ll_ref[j, 0, :, cols])
+            v_im = _nn(pp, ll_ref[j, 1, :, cols])
+            f_re = f_re + (v_re[:sc] - v_im[sc:])
+            f_im = f_im + (v_im[:sc] + v_re[sc:])
         out_ref[:, cols] = f_re
         out_ref[:, row_count + l * LEAF:row_count + (l + 1) * LEAF] = f_im
 
@@ -108,17 +105,16 @@
 
     c_re = jnp.zeros((source_count, rank_width), jnp.float32)
     c_im = jnp.zeros((source_count, rank_width), jnp.float32)
+    sc = source_count
     for u in range(1, blocks):
-        b_re = part_refs[u - 1][0]
-        b_im = part_refs[u - 1][1]
-        k_re = cp_ref[0, :, u * coupling_rank:(u + 1) * coupling_rank]
-        k_im = cp_ref[1, :, u * coupling_rank:(u + 1) * coupling_rank]
-        c_re = c_re + (_nt(b_re, k_re) - _nt(b_im, k_im))
-        c_im = c_im + (_nt(b_re, k_im) + _nt(b_im, k_re))
+        bb = part_refs[u - 1][...].reshape(2 * sc, coupling_rank)
+        t_re = _nt(bb, cp_ref[0, :, u * coupling_rank:(u + 1) * coupling_rank])
+        t_im = _nt(bb, cp_ref[1, :, u * coupling_rank:(u + 1) * coupling_rank])
+        c_re = c_re + (t_re[:sc] - t_im[sc:])
+        c_im = c_im + (t_im[:sc] + t_re[sc:])
     cu_ref[0] = c_re.astype(jnp.bfloat16)
     cu_ref[1] = c_im.astype(jnp.bfloat16)
-    coupled_re = cu_ref[0]
-    coupled_im = cu_ref[1]
+    coupled = cu_ref[...].reshape(2 * sc, rank_width)
 
     w_re = qw_ref[0]
     w_im = qw_ref[1]
@@ -129,8 +125,10 @@
         zero = jnp.zeros((rank_width, LEAF), jnp.bfloat16)
         q_re = jnp.where(keep, bl_ref[0, :, cols], zero)
         q_im = jnp.where(keep, bl_ref[1, :, cols], zero)
-        f_re = near_ref[:, cols] + (_nn(coupled_re, q_re) - _nn(coupled_im, q_im))
-        f_im = near_ref[:, imag_cols] + (_nn(coupled_re, q_im) + _nn(coupled_im, q_re))
+        v_re = _nn(coupled, q_re)
+        v_im = _nn(coupled, q_im)
+        f_re = near_ref[:, cols] + (v_re[:sc] - v_im[sc:])
+        f_im = near_ref[:, imag_cols] + (v_im[:sc] + v_re[sc:])
         out_ref[:, cols] = w_re * f_re - w_im * f_im
         out_ref[:, imag_cols] = w_re * f_im + w_im * f_re
 

time: 54.4 us -> 53.8 us (0.989)
  Pallas kernels: 14.2 us -> 13.6 us
    pallas_call x1, Pallas kernels: 6.26 us -> 5.62 us  [shards(): pl.pallas_call(_near_kernel, out_shape=jax.ShapeDtypeStruct((source_count...]
  transfers between devices with their start and end apart: 11 -> 11, of which waited for: 5 -> 5; matrix products, arithmetic and copies ran while one was open for 11% -> 11% of each run, Pallas kernels for 16% -> 15%
where the time goes in v12:
time: 53.8 us; the launch traced here: 53.5 us
  waiting for transfers between devices  15.9 us (30%)
  Pallas kernels  13.6 us (25%)
  starting transfers between devices  12.9 us (24%)
  local copies, waits for them, and re-layouts  5.49 us (10%)
  other arithmetic  4.86 us (9%)
  between operations  0.81 us (2%)
    ppermute x8, waiting for transfers between devices, _permute(): return lax.ppermute(x, axis_name, [(i, i ^ offset) for i in range(count)])  15.9 us
    ppermute x8, starting transfers between devices, _permute(): return lax.ppermute(x, axis_name, [(i, i ^ offset) for i in range(count)])  9.38 us
    pallas_call x1, Pallas kernels, shards(): pl.pallas_call(_near_kernel, out_shape=jax.ShapeDtypeStruct((source_count...  5.62 us
    pallas_call x2, Pallas kernels, shards(): pl.pallas_call(_far_kernel, out_shape=jax.ShapeDtypeStruct((half, 2 * row...  5.03 us
    ppermute x3, starting transfers between devices, _exchange(): lax.ppermute(x, axis_name, [(i, i ^ p) for i in range(count)])  3.49 us
    pallas_call x1, Pallas kernels, shards(): pl.pallas_call(_excite_kernel, out_shape=(jax.ShapeDtypeStruct((2, source...  2.91 us
    reduce_precision x1, other arithmetic, shards(): lax.reduce_precision(jnp.sin(theta), exponent_bits=8, mantissa_bits=7)  1.78 us
    unnamed x12, local copies, waits for them, and re-layouts  1.41 us
  transfers between devices with their start and end apart: 11, of which 5 were waited for; matrix products, arithmetic and copies ran while one was open for 11% of the time, Pallas kernels for 15%

profile of v12, /device:TPU:0, one launch (start us, length us, event | category | flops | bytes accessed | tf_op | source)
XLA Modules:
  0.0 53.5 jit_solution(5064826406791116903)
XLA Ops:
  0.0 1.0 %reshape_squeeze.6 = bf16[32,8,256]{2,1,0:T(8,128)(2,1)S(1)} reshape(bf16[1,32,8,2,128]{4,3,2,1,0:T(2,128)(2,1)} %param.13) | data formatting | bytes 262144 | tf_op jit(solution)/shard_map/reshape;squeeze | solution.py:234
  1.0 5.1 %collective-permute-start.2 = (bf16[32,8,256]{2,1,0:T(8,128)(2,1)S(1)}, bf16[32,8,256]{2,1,0:T(8,128)(2,1)S(1)}, u32[]{:S(2)}, u32[]{:S(2)}) collective-permute-start(bf16[32,8,256]{2,1,0:T(8,128)(2,1)S(1)} %reshape_squeeze.6), channel_id=1, source_target_pairs={{0,24},{4,28},{8,16},{12,20},{16,8},{20,12},{24,0},{28,4},{1,25},{... | collective-permute-start | bytes 393224 | tf_op jit(solution)/shard_map/ppermute | solution.py:148
  6.1 0.0 collective-permute-start.1
  6.1 0.6 %collective-permute-start = (bf16[32,8,256]{2,1,0:T(8,128)(2,1)S(1)}, bf16[32,8,256]{2,1,0:T(8,128)(2,1)S(1)}, u32[]{:S(2)}, u32[]{:S(2)}) collective-permute-start(bf16[32,8,256]{2,1,0:T(8,128)(2,1)S(1)} %reshape_squeeze.6), channel_id=1, source_target_pairs={{0,16},{4,20},{8,24},{12,28},{16,0},{20,4},{24,8},{28,12},{1,17},{... | collective-permute-start | bytes 393224 | tf_op jit(solution)/shard_map/ppermute | solution.py:148
  6.8 0.1 constant_dynamic-slice_fusion
  6.9 0.5 fusion.3
  7.4 0.1 broadcast_in_dim.16
  7.5 0.1 broadcast_in_dim.17
  7.6 0.7 %convert_bitcast_fusion = f32[32,2]{0,1:T(2,128)S(1)} fusion(s32[1,32,2]{1,2,0:T(2,128)} %param.15), kind=kLoop, calls=%fused_computation.9 | loop fusion | flops 64 | bytes 512 | tf_op jit(solution)/shard_map/convert_element_type | solution.py:228
  8.2 0.8 %reshape_squeeze.7 = bf16[2,32,4,32]{3,2,1,0:T(4,128)(2,1)S(1)} reshape(bf16[1,1,2,32,128]{4,3,2,1,0:T(8,128)(2,1)} %param.22) | data formatting | bytes 32768 | tf_op jit(solution)/shard_map/reshape;squeeze | solution.py:238
  9.1 0.6 %gather_fusion = bf16[4,2,32,32]{3,2,1,0:T(8,128)(2,1)S(1)} fusion(bf16[2,32,4,32]{3,1,2,0:T(8,128)(2,1)S(1)} %copy.17, s32[1024]{0:T(1024)S(1)} %pad_clamp_fusion), kind=kCustom, calls=%fused_computation | custom fusion | bytes 32784 | tf_op jit(solution)/shard_map/jit(_take)/gather | solution.py:240
  9.6 0.1 copy.18
  9.7 0.1 gather.7
  9.8 0.6 %broadcast_select_fusion.cp_ref = bf16[2,32,128]{2,1,0:T(8,128)(2,1)} fusion(bf16[2,32,128]{2,1,0:T(8,128)(2,1)S(1)} %gather.7, pred[128]{0:T(512)(128)(4,1)S(1)} %broadcast_in_dim.17), kind=kLoop, calls=%fused_computation.5 | loop fusion | flops 8192 | bytes 32896 | tf_op jit(solution)/shard_map/jit(_take)/select_n | solution.py:240
  10.4 1.8 %reduce-precision_bitcast_fusion = (f32[32]{0:T(128)}, f32[32,1]{0,1:T(1,128)S(1)}) fusion(f32[32,2]{0,1:T(2,128)S(1)} %convert_bitcast_fusion, f32[]{:T(128)} %bitcast.5, f32[]{:T(128)} %bitcast.3), kind=kLoop, calls=%fused_computation.10 | loop fusion | flops 128 | bytes 520 | tf_op jit(solution)/shard_map/reduce_precision | solution.py:232
  12.2 0.6 %reduce-precision_bitcast_fusion.1.cos_ref = f32[32]{0:T(128)} fusion(f32[32,1]{0,1:T(1,128)S(1)} %get-tuple-element.18), kind=kLoop, calls=%fused_computation.11 | loop fusion | flops 32 | bytes 256 | tf_op jit(solution)/shard_map/reduce_precision | solution.py:231
  12.8 0.0 collective-permute-done.2
  12.8 0.8 %collective-permute-done.1 = bf16[32,8,256]{2,1,0:T(8,128)(2,1)S(1)} collective-permute-done((bf16[32,8,256]{2,1,0:T(8,128)(2,1)S(1)}, bf16[32,8,256]{2,1,0:T(8,128)(2,1)S(1)}, u32[]{:S(2)}, u32[]{:S(2)}) %collective-permute-start.1) | collective-permute-done | bytes 131104 | tf_op jit(solution)/shard_map/ppermute | solution.py:148
  13.5 3.7 %collective-permute-done = bf16[32,8,256]{2,1,0:T(8,128)(2,1)S(1)} collective-permute-done((bf16[32,8,256]{2,1,0:T(8,128)(2,1)S(1)}, bf16[32,8,256]{2,1,0:T(8,128)(2,1)S(1)}, u32[]{:S(2)}, u32[]{:S(2)}) %collective-permute-start) | collective-permute-done | bytes 131104 | tf_op jit(solution)/shard_map/ppermute | solution.py:148
  17.2 0.1 pad_maximum_fusion.ga_ref
  17.3 0.1 collective-permute-start.3
  18.0 1.2 %collective-permute-done.3.gb_ref = bf16[32,32,256]{2,1,0:T(8,128)(2,1)S(1)} collective-permute-done((bf16[32,32,256]{2,1,0:T(8,128)(2,1)S(1)}, bf16[32,32,256]{2,1,0:T(8,128)(2,1)S(1)}, u32[]{:S(2)}, u32[]{:S(2)}) %collective-permute-start.3) | collective-permute-done | bytes 524320 | tf_op jit(solution)/shard_map/ppermute | solution.py:148
  19.3 0.8 %copy-done.2 = bf16[32,32,256]{2,1,0:T(8,128)(2,1)} copy-done((bf16[32,32,256]{2,1,0:T(8,128)(2,1)}, bf16[32,32,256]{2,1,0:T(8,128)(2,1)S(1)}, u32[]{:S(2)}) %copy-start.2) | copy-done | bytes 524312
  20.0 2.9 %shard_map.127 = (bf16[2,64,2048]{2,1,0:T(8,128)(2,1)}, bf16[2,64,32]{2,1,0:T(8,128)(2,1)}) custom-call(s32[32]{0:T(128)} %bitcast.33, f32[32]{0:T(128)} %reduce-precision_bitcast_fusion.1.cos_ref, f32[32]{0:T(128)} %get-tuple-element.12.sin_ref, s32[1]{0:T(128)} %bitcast.20.rank_ref, bf16[32,32,256]{2,1,0:T(8,128)(2,1)} %copy-done.1, ...), custom_call_target="tpu_custom_call" | custom-call | tf_op jit(solution)/shard_map/pallas_call | solution.py:244
  23.0 2.4 %collective-permute-start.6 = (bf16[2,64,32]{2,1,0:T(8,128)(2,1)}, bf16[2,64,32]{2,1,0:T(8,128)(2,1)S(1)}, u32[]{:S(2)}, u32[]{:S(2)}) collective-permute-start(bf16[2,64,32]{2,1,0:T(8,128)(2,1)} %get-tuple-element.16), channel_id=1, source_target_pairs={{0,3},{1,2},{2,1},{3,0},{4,7},{5,6},{6,5},{7,4},{8,11},{9,10},{10,... | collective-permute-start | bytes 24584 | tf_op jit(solution)/shard_map/ppermute | solution.py:200
  25.4 0.5 collective-permute-start.5
  25.9 0.5 %collective-permute-start.4 = (bf16[2,64,32]{2,1,0:T(8,128)(2,1)}, bf16[2,64,32]{2,1,0:T(8,128)(2,1)S(1)}, u32[]{:S(2)}, u32[]{:S(2)}) collective-permute-start(bf16[2,64,32]{2,1,0:T(8,128)(2,1)} %get-tuple-element.16), channel_id=1, source_target_pairs={{0,1},{1,0},{2,3},{3,2},{4,5},{5,4},{6,7},{7,6},{8,9},{9,8},{10,11... | collective-permute-start | bytes 24584 | tf_op jit(solution)/shard_map/ppermute | solution.py:200
  26.4 5.6 %shard_map.128.near_ref = f32[64,4096]{1,0:T(8,128)} custom-call(bf16[2,64,2048]{2,1,0:T(8,128)(2,1)} %get-tuple-element.14.e_ref, bf16[2,2048,256]{2,1,0:T(8,128)(2,1)} %bitcast.23, bf16[3,2,32,2048]{3,2,1,0:T(8,128)(2,1)} %bitcast.26, bf16[3,2,32,2048]{3,2,1,0:T(8,128)(2,1)} %bitcast.27), custom_call_target="tpu_custom_call" | custom-call | tf_op jit(solution)/shard_map/pallas_call | solution.py:259
  32.1 0.0 collective-permute-done.6.refs_2_
  32.1 0.0 collective-permute-done.5.refs_1_
  32.1 0.0 copy-start.4
  32.1 0.0 collective-permute-done.4.refs_0_
  32.1 0.0 copy-start.5
  32.1 0.6 %copy-done.3 = bf16[2,64,32]{2,1,0:T(8,128)(2,1)} copy-done((bf16[2,64,32]{2,1,0:T(8,128)(2,1)}, bf16[2,64,32]{2,1,0:T(8,128)(2,1)S(1)}, u32[]{:S(2)}) %copy-start.3) | copy-done | bytes 8216
  32.7 0.0 copy-done.4
  32.7 0.0 copy-done.5
  32.7 2.5 %shard_map.130 = f32[32,4096]{1,0:T(8,128)} custom-call(f32[2]{0:T(128)} %bitcast.31, s32[1]{0:T(128)} %bitcast.22.rank_ref, f32[64,4096]{1,0:T(8,128)} %shard_map.128.near_ref, bf16[2,32,2048]{2,1,0:T(8,128)(2,1)} %bitcast.24, bf16[2,32,128]{2,1,0:T(8,128)(2,1)} %broadcast_select_fusion.cp_ref, bf16[2,64,32]{2,1,0:T(8,128)(2,1)} %copy-done.5, ...), custom_call_target="tpu_custom_call" | custom-call | tf_op jit(solution)/shard_map/pallas_call | solution.py:270
  35.2 0.0 collective-permute-start.7
  35.2 2.5 %shard_map.129 = f32[32,4096]{1,0:T(8,128)} custom-call(f32[2]{0:T(128)} %bitcast.32, s32[1]{0:T(128)} %bitcast.21.rank_ref, f32[64,4096]{1,0:T(8,128)} %shard_map.128.near_ref, bf16[2,32,2048]{2,1,0:T(8,128)(2,1)} %bitcast.25, bf16[2,32,128]{2,1,0:T(8,128)(2,1)} %broadcast_select_fusion.cp_ref, bf16[2,64,32]{2,1,0:T(8,128)(2,1)} %copy-done.5, ...), custom_call_target="tpu_custom_call" | custom-call | tf_op jit(solution)/shard_map/pallas_call | solution.py:270
  37.7 0.0 collective-permute-done.7
  37.7 1.1 %add.26 = f32[32,4096]{1,0:T(8,128)S(1)} add(f32[32,4096]{1,0:T(8,128)} %shard_map.129, f32[32,4096]{1,0:T(8,128)S(1)} %collective-permute-done.7) | non-fusion elementwise | flops 131072 | bytes 1572864 | tf_op jit(solution)/shard_map/add | solution.py:173
  38.9 0.9 %collective-permute-start.8 = (f32[8,4096]{1,0:T(8,128)S(1)}, f32[8,4096]{1,0:T(8,128)S(1)}, u32[]{:S(2)}, u32[]{:S(2)}) collective-permute-start(f32[8,4096]{1,0:T(8,128)S(1)} %get-tuple-element.19), channel_id=1, source_target_pairs={{0,16},{4,20},{8,24},{12,28},{16,0},{20,4},{24,8},{28,12},{1,17},{... | collective-permute-start | bytes 393224 | tf_op jit(solution)/shard_map/ppermute | solution.py:148
  39.8 1.7 %collective-permute-start.10 = (f32[8,4096]{1,0:T(8,128)S(1)}, f32[8,4096]{1,0:T(8,128)S(1)}, u32[]{:S(2)}, u32[]{:S(2)}) collective-permute-start(f32[8,4096]{1,0:T(8,128)S(1)} %get-tuple-element.20), channel_id=1, source_target_pairs={{0,24},{4,28},{8,16},{12,20},{16,8},{20,12},{24,0},{28,4},{1,25},{... | collective-permute-start | bytes 393224 | tf_op jit(solution)/shard_map/ppermute | solution.py:148
  41.5 0.9 %collective-permute-start.9 = (f32[8,4096]{1,0:T(8,128)S(1)}, f32[8,4096]{1,0:T(8,128)S(1)}, u32[]{:S(2)}, u32[]{:S(2)}) collective-permute-start(f32[8,4096]{1,0:T(8,128)S(1)} %get-tuple-element.21), channel_id=1, source_target_pairs={{0,8},{4,12},{8,0},{12,4},{16,24},{20,28},{24,16},{28,20},{1,9},{5... | collective-permute-start | bytes 393224 | tf_op jit(solution)/shard_map/ppermute | solution.py:148
  42.5 8.9 %collective-permute-done.8 = f32[8,4096]{1,0:T(8,128)S(1)} collective-permute-done((f32[8,4096]{1,0:T(8,128)S(1)}, f32[8,4096]{1,0:T(8,128)S(1)}, u32[]{:S(2)}, u32[]{:S(2)}) %collective-permute-start.8) | collective-permute-done | bytes 131104 | tf_op jit(solution)/shard_map/ppermute | solution.py:148
  51.3 0.0 collective-permute-done.10
  51.3 1.3 %collective-permute-done.9 = f32[8,4096]{1,0:T(8,128)S(1)} collective-permute-done((f32[8,4096]{1,0:T(8,128)S(1)}, f32[8,4096]{1,0:T(8,128)S(1)}, u32[]{:S(2)}, u32[]{:S(2)}) %collective-permute-start.9) | collective-permute-done | bytes 131104 | tf_op jit(solution)/shard_map/ppermute | solution.py:148
  52.7 0.8 %copy.19 = f32[8,2,2048]{2,1,0:T(2,128)} copy(f32[8,2,2048]{2,0,1:T(8,128)S(1)} %bitcast.28) | data formatting | bytes 262144 | tf_op jit(solution)/shard_map/reshape | solution.py:185
  (12 shorter events, 0.1 us)
Async XLA Ops:
  0.0 6.8 %copy-start = (f32[8,2]{0,1:T(2,128)S(1)}, f32[8,2]{0,1:T(2,128)}, u32[]{:S(2)}) copy-start(f32[8,2]{0,1:T(2,128)} %param.16) | copy-start | bytes 196
  1.0 11.8 %collective-permute-start.2 = (bf16[32,8,256]{2,1,0:T(8,128)(2,1)S(1)}, bf16[32,8,256]{2,1,0:T(8,128)(2,1)S(1)}, u32[]{:S(2)}, u32[]{:S(2)}) collective-permute-start(bf16[32,8,256]{2,1,0:T(8,128)(2,1)S(1)} %reshape_squeeze.6), channel_id=1, source_target_pairs={{0,24},{4,28},{8,16},{12,20},{16,8},{20,12},{24,0},{28,4},{1,25},{... | collective-permute-start | bytes 393224 | tf_op jit(solution)/shard_map/ppermute | solution.py:148
  6.1 7.4 %collective-permute-start.1 = (bf16[32,8,256]{2,1,0:T(8,128)(2,1)S(1)}, bf16[32,8,256]{2,1,0:T(8,128)(2,1)S(1)}, u32[]{:S(2)}, u32[]{:S(2)}) collective-permute-start(bf16[32,8,256]{2,1,0:T(8,128)(2,1)S(1)} %reshape_squeeze.6), channel_id=1, source_target_pairs={{0,8},{4,12},{8,0},{12,4},{16,24},{20,28},{24,16},{28,20},{1,9},{5... | collective-permute-start | bytes 393224 | tf_op jit(solution)/shard_map/ppermute | solution.py:148
  6.1 11.1 %collective-permute-start = (bf16[32,8,256]{2,1,0:T(8,128)(2,1)S(1)}, bf16[32,8,256]{2,1,0:T(8,128)(2,1)S(1)}, u32[]{:S(2)}, u32[]{:S(2)}) collective-permute-start(bf16[32,8,256]{2,1,0:T(8,128)(2,1)S(1)} %reshape_squeeze.6), channel_id=1, source_target_pairs={{0,16},{4,20},{8,24},{12,28},{16,0},{20,4},{24,8},{28,12},{1,17},{... | collective-permute-start | bytes 393224 | tf_op jit(solution)/shard_map/ppermute | solution.py:148
  17.3 2.0 %copy-start.1 = (bf16[32,32,256]{2,1,0:T(8,128)(2,1)}, bf16[32,32,256]{2,1,0:T(8,128)(2,1)S(1)}, u32[]{:S(2)}) copy-start(bf16[32,32,256]{2,1,0:T(8,128)(2,1)S(1)} %pad_maximum_fusion.ga_ref) | copy-start | bytes 1572868
  17.3 2.0 %collective-permute-start.3 = (bf16[32,32,256]{2,1,0:T(8,128)(2,1)S(1)}, bf16[32,32,256]{2,1,0:T(8,128)(2,1)S(1)}, u32[]{:S(2)}, u32[]{:S(2)}) collective-permute-start(bf16[32,32,256]{2,1,0:T(8,128)(2,1)S(1)} %pad_maximum_fusion.ga_ref), channel_id=1, source_target_pairs={{0,4},{4,0},{8,12},{12,8},{16,20},{20,16},{24,28},{28,24},{1,5},{5... | collective-permute-start | bytes 1572872 | tf_op jit(solution)/shard_map/ppermute | solution.py:148
  19.2 0.8 %copy-start.2 = (bf16[32,32,256]{2,1,0:T(8,128)(2,1)}, bf16[32,32,256]{2,1,0:T(8,128)(2,1)S(1)}, u32[]{:S(2)}) copy-start(bf16[32,32,256]{2,1,0:T(8,128)(2,1)S(1)} %collective-permute-done.3.gb_ref) | copy-start | bytes 1572868
  23.0 9.1 %collective-permute-start.6 = (bf16[2,64,32]{2,1,0:T(8,128)(2,1)}, bf16[2,64,32]{2,1,0:T(8,128)(2,1)S(1)}, u32[]{:S(2)}, u32[]{:S(2)}) collective-permute-start(bf16[2,64,32]{2,1,0:T(8,128)(2,1)} %get-tuple-element.16), channel_id=1, source_target_pairs={{0,3},{1,2},{2,1},{3,0},{4,7},{5,6},{6,5},{7,4},{8,11},{9,10},{10,... | collective-permute-start | bytes 24584 | tf_op jit(solution)/shard_map/ppermute | solution.py:200
  25.4 6.7 %collective-permute-start.5 = (bf16[2,64,32]{2,1,0:T(8,128)(2,1)}, bf16[2,64,32]{2,1,0:T(8,128)(2,1)S(1)}, u32[]{:S(2)}, u32[]{:S(2)}) collective-permute-start(bf16[2,64,32]{2,1,0:T(8,128)(2,1)} %get-tuple-element.16), channel_id=1, source_target_pairs={{0,2},{1,3},{2,0},{3,1},{4,6},{5,7},{6,4},{7,5},{8,10},{9,11},{10,... | collective-permute-start | bytes 24584 | tf_op jit(solution)/shard_map/ppermute | solution.py:200
  25.9 6.2 %collective-permute-start.4 = (bf16[2,64,32]{2,1,0:T(8,128)(2,1)}, bf16[2,64,32]{2,1,0:T(8,128)(2,1)S(1)}, u32[]{:S(2)}, u32[]{:S(2)}) collective-permute-start(bf16[2,64,32]{2,1,0:T(8,128)(2,1)} %get-tuple-element.16), channel_id=1, source_target_pairs={{0,1},{1,0},{2,3},{3,2},{4,5},{5,4},{6,7},{7,6},{8,9},{9,8},{10,11... | collective-permute-start | bytes 24584 | tf_op jit(solution)/shard_map/ppermute | solution.py:200
  32.1 0.6 %copy-start.3 = (bf16[2,64,32]{2,1,0:T(8,128)(2,1)}, bf16[2,64,32]{2,1,0:T(8,128)(2,1)S(1)}, u32[]{:S(2)}) copy-start(bf16[2,64,32]{2,1,0:T(8,128)(2,1)S(1)} %collective-permute-done.6.refs_2_) | copy-start | bytes 24580
  32.1 0.6 %copy-start.4 = (bf16[2,64,32]{2,1,0:T(8,128)(2,1)}, bf16[2,64,32]{2,1,0:T(8,128)(2,1)S(1)}, u32[]{:S(2)}) copy-start(bf16[2,64,32]{2,1,0:T(8,128)(2,1)S(1)} %collective-permute-done.5.refs_1_) | copy-start | bytes 24580
  32.1 0.6 %copy-start.5 = (bf16[2,64,32]{2,1,0:T(8,128)(2,1)}, bf16[2,64,32]{2,1,0:T(8,128)(2,1)S(1)}, u32[]{:S(2)}) copy-start(bf16[2,64,32]{2,1,0:T(8,128)(2,1)S(1)} %collective-permute-done.4.refs_0_) | copy-start | bytes 24580
  35.2 2.5 %collective-permute-start.7 = (f32[32,4096]{1,0:T(8,128)}, f32[32,4096]{1,0:T(8,128)S(1)}, u32[]{:S(2)}, u32[]{:S(2)}) collective-permute-start(f32[32,4096]{1,0:T(8,128)} %shard_map.130), channel_id=1, source_target_pairs={{0,4},{4,0},{8,12},{12,8},{16,20},{20,16},{24,28},{28,24},{1,5},{5... | collective-permute-start | bytes 1572872 | tf_op jit(solution)/shard_map/ppermute | solution.py:148
  38.9 12.4 %collective-permute-start.8 = (f32[8,4096]{1,0:T(8,128)S(1)}, f32[8,4096]{1,0:T(8,128)S(1)}, u32[]{:S(2)}, u32[]{:S(2)}) collective-permute-start(f32[8,4096]{1,0:T(8,128)S(1)} %get-tuple-element.19), channel_id=1, source_target_pairs={{0,16},{4,20},{8,24},{12,28},{16,0},{20,4},{24,8},{28,12},{1,17},{... | collective-permute-start | bytes 393224 | tf_op jit(solution)/shard_map/ppermute | solution.py:148
  39.8 11.5 %collective-permute-start.10 = (f32[8,4096]{1,0:T(8,128)S(1)}, f32[8,4096]{1,0:T(8,128)S(1)}, u32[]{:S(2)}, u32[]{:S(2)}) collective-permute-start(f32[8,4096]{1,0:T(8,128)S(1)} %get-tuple-element.20), channel_id=1, source_target_pairs={{0,24},{4,28},{8,16},{12,20},{16,8},{20,12},{24,0},{28,4},{1,25},{... | collective-permute-start | bytes 393224 | tf_op jit(solution)/shard_map/ppermute | solution.py:148
  41.5 11.1 %collective-permute-start.9 = (f32[8,4096]{1,0:T(8,128)S(1)}, f32[8,4096]{1,0:T(8,128)S(1)}, u32[]{:S(2)}, u32[]{:S(2)}) collective-permute-start(f32[8,4096]{1,0:T(8,128)S(1)} %get-tuple-element.21), channel_id=1, source_target_pairs={{0,8},{4,12},{8,0},{12,4},{16,24},{20,28},{24,16},{28,20},{1,9},{5... | collective-permute-start | bytes 393224 | tf_op jit(solution)/shard_map/ppermute | solution.py:148

commit v13 on v12

--- a/solution.py
+++ b/solution.py
@@ -23,10 +23,9 @@
     return lax.broadcasted_iota(jnp.int32, shape, 0) < rank_ref[0]
 
 
-def _excite_kernel(slot_ref, cos_ref, sin_ref, rank_ref, ga_ref, gb_ref, br_ref, e_ref, bp_ref, acc_re, acc_im):
-    panel_count, part, width2 = ga_ref.shape
+def _accumulate(slot_ref, cos_ref, sin_ref, g_ref, acc_re, acc_im):
+    panel_count, _, width2 = g_ref.shape
     width = width2 // 2
-    slots = acc_re.shape[0]
     acc_re[...] = jnp.zeros(acc_re.shape, jnp.float32)
     acc_im[...] = jnp.zeros(acc_im.shape, jnp.float32)
 
@@ -34,25 +33,41 @@
         k = slot_ref[q]
         c = cos_ref[q]
         s = sin_ref[q]
-        for rows, g_ref in ((slice(0, part), ga_ref), (slice(part, 2 * part), gb_ref)):
-            p_re = g_ref[q, :, :width].astype(jnp.float32)
-            p_im = g_ref[q, :, width:].astype(jnp.float32)
-            acc_re[k, rows] = acc_re[k, rows] + (c * p_re + s * p_im)
-            acc_im[k, rows] = acc_im[k, rows] + (c * p_im - s * p_re)
+        p_re = g_ref[q, :, :width].astype(jnp.float32)
+        p_im = g_ref[q, :, width:].astype(jnp.float32)
+        acc_re[k] = acc_re[k] + (c * p_re + s * p_im)
+        acc_im[k] = acc_im[k] + (c * p_im - s * p_re)
         return carry
 
     lax.fori_loop(0, panel_count, body, 0)
-    for k in range(slots):
+
+
+def _store_excitation(acc_re, acc_im, e_ref):
+    width = acc_re.shape[2]
+    for k in range(acc_re.shape[0]):
         e_ref[0, :, k * width:(k + 1) * width] = acc_re[k].astype(jnp.bfloat16)
         e_ref[1, :, k * width:(k + 1) * width] = acc_im[k].astype(jnp.bfloat16)
-    sources = e_ref.shape[1]
-    stacked = e_ref[...].reshape(2 * sources, e_ref.shape[2])
+
+
+def _excite_first_kernel(slot_ref, cos_ref, sin_ref, g_ref, e_ref, acc_re, acc_im):
+    _accumulate(slot_ref, cos_ref, sin_ref, g_ref, acc_re, acc_im)
+    _store_excitation(acc_re, acc_im, e_ref)
+
+
+def _excite_second_kernel(slot_ref, cos_ref, sin_ref, rank_ref, g_ref, br_ref, e_in, e_ref, bp_ref, acc_re, acc_im):
+    _accumulate(slot_ref, cos_ref, sin_ref, g_ref, acc_re, acc_im)
+    _store_excitation(acc_re, acc_im, e_ref)
+    part = e_ref.shape[1]
     keep = _rank_mask(rank_ref, br_ref.shape[1:])
     zero = jnp.zeros(br_ref.shape[1:], jnp.bfloat16)
-    t_re = _nt(stacked, jnp.where(keep, br_ref[0], zero))
-    t_im = _nt(stacked, jnp.where(keep, br_ref[1], zero))
-    bp_ref[0] = (t_re[:sources] - t_im[sources:]).astype(jnp.bfloat16)
-    bp_ref[1] = (t_im[:sources] + t_re[sources:]).astype(jnp.bfloat16)
+    r_re = jnp.where(keep, br_ref[0], zero)
+    r_im = jnp.where(keep, br_ref[1], zero)
+    for rows, values in ((slice(0, part), e_in[:, :part, :]), (slice(part, 2 * part), e_ref[...])):
+        stacked = values.reshape(2 * part, values.shape[2])
+        t_re = _nt(stacked, r_re)
+        t_im = _nt(stacked, r_im)
+        bp_ref[0, rows, :] = (t_re[:part] - t_im[part:]).astype(jnp.bfloat16)
+        bp_ref[1, rows, :] = (t_im[:part] + t_re[part:]).astype(jnp.bfloat16)
 
 
 def _near_kernel(e_ref, leaf_ref, lr_ref, ll_ref, out_ref, pj_ref):
@@ -241,19 +256,37 @@
     (first, second), (own_cos, own_sin, coupling) = _all_gather(local_panels, "ang", 1, (own_cos, own_sin, coupling))
     rank = rank_count[0].reshape(1)
 
+    part = source_count // 2
+    acc = [pltpu.VMEM((slot_count, part, panel_width), jnp.float32)] * 2
+    whole_e = jax.ShapeDtypeStruct((2, source_count, row_count), jnp.bfloat16)
+    first_e = pl.pallas_call(
+        _excite_first_kernel,
+        out_shape=whole_e,
+        grid=(1,),
+        in_specs=[_SMEM, _SMEM, _SMEM, pl.BlockSpec(first.shape, lambda i: (0, 0, 0))],
+        out_specs=pl.BlockSpec((2, part, row_count), lambda i: (0, 0, 0)),
+        scratch_shapes=acc,
+    )(panel_slot[0], own_cos, own_sin, first)
     excitation, projected = pl.pallas_call(
-        _excite_kernel,
-        out_shape=(
-            jax.ShapeDtypeStruct((2, source_count, row_count), jnp.bfloat16),
-            jax.ShapeDtypeStruct((2, source_count, rank_width), jnp.bfloat16),
+        _excite_second_kernel,
+        out_shape=(whole_e, jax.ShapeDtypeStruct((2, source_count, rank_width), jnp.bfloat16)),
+        grid=(1,),
+        in_specs=[
+            _SMEM,
+            _SMEM,
+            _SMEM,
+            _SMEM,
+            pl.BlockSpec(second.shape, lambda i: (0, 0, 0)),
+            pl.BlockSpec(block_right.shape[1:], lambda i: (0, 0, 0)),
+            pl.BlockSpec((2, source_count, row_count), lambda i: (0, 0, 0)),
+        ],
+        out_specs=(
+            pl.BlockSpec((2, part, row_count), lambda i: (0, 1, 0)),
+            pl.BlockSpec((2, source_count, rank_width), lambda i: (0, 0, 0)),
         ),
-        in_specs=[_SMEM, _SMEM, _SMEM, _SMEM, _VMEM, _VMEM, _VMEM],
-        out_specs=(_VMEM, _VMEM),
-        scratch_shapes=[
-            pltpu.VMEM((slot_count, source_count, panel_width), jnp.float32),
-            pltpu.VMEM((slot_count, source_count, panel_width), jnp.float32),
-        ],
-    )(panel_slot[0], own_cos, own_sin, rank, first, second, block_right[0])
+        scratch_shapes=acc,
+        input_output_aliases={6: 0},
+    )(panel_slot[0], own_cos, own_sin, rank, second, block_right[0], first_e)
     all_projected = _exchange(projected, "row")
 
     near = pl.pallas_call(

time: 53.8 us -> 54.8 us (1.019)
  Pallas kernels: 13.6 us -> 15.7 us
  waiting for transfers between devices: 15.9 us -> 14.6 us
    pallas_call x1 -> x2, Pallas kernels: 2.91 us -> 5.04 us  [the longest x1 2.84 us: shards(): pl.pallas_call(_excite_second_kernel, out_shape=(whole_e, jax.ShapeDtypeS...]
    ppermute x8, waiting for transfers between devices: 15.9 us -> 14.6 us  [_permute(): return lax.ppermute(x, axis_name, [(i, i ^ offset) for i in range(count)])]
  transfers between devices with their start and end apart: 11 -> 11, of which waited for: 5 -> 4; matrix products, arithmetic and copies ran while one was open for 11% -> 11% of each run, Pallas kernels for 15% -> 19%
where the time goes in v13:
time: 54.8 us; the launch traced here: 54.4 us
  Pallas kernels  15.7 us (29%)
  waiting for transfers between devices  14.6 us (27%)
  starting transfers between devices  12.9 us (24%)
  local copies, waits for them, and re-layouts  5.51 us (10%)
  other arithmetic  4.88 us (9%)
  between operations  0.81 us (1%)
    ppermute x8, waiting for transfers between devices, _permute(): return lax.ppermute(x, axis_name, [(i, i ^ offset) for i in range(count)])  14.6 us
    ppermute x8, starting transfers between devices, _permute(): return lax.ppermute(x, axis_name, [(i, i ^ offset) for i in range(count)])  9.38 us
    pallas_call x1, Pallas kernels, shards(): pl.pallas_call(_near_kernel, out_shape=jax.ShapeDtypeStruct((source_count...  5.62 us
    pallas_call x2, Pallas kernels, shards(): pl.pallas_call(_far_kernel, out_shape=jax.ShapeDtypeStruct((half, 2 * row...  5.03 us
    ppermute x3, starting transfers between devices, _exchange(): lax.ppermute(x, axis_name, [(i, i ^ p) for i in range(count)])  3.49 us
    pallas_call x1, Pallas kernels, shards(): pl.pallas_call(_excite_second_kernel, out_shape=(whole_e, jax.ShapeDtypeS...  2.84 us
    pallas_call x1, Pallas kernels, shards(): pl.pallas_call(_excite_first_kernel, out_shape=whole_e, grid=(1,), in_spe...  2.2 us
    reduce_precision x1, other arithmetic, shards(): lax.reduce_precision(jnp.sin(theta), exponent_bits=8, mantissa_bits=7)  1.82 us
  transfers between devices with their start and end apart: 11, of which 4 were waited for; matrix products, arithmetic and copies ran while one was open for 11% of the time, Pallas kernels for 19%

profile of v13, /device:TPU:0, one launch (start us, length us, event | category | flops | bytes accessed | tf_op | source)
XLA Modules:
  0.0 54.4 jit_solution(100848069760140843)
XLA Ops:
  0.0 1.0 %reshape_squeeze.6 = bf16[32,8,256]{2,1,0:T(8,128)(2,1)S(1)} reshape(bf16[1,32,8,2,128]{4,3,2,1,0:T(2,128)(2,1)} %param.13) | data formatting | bytes 262144 | tf_op jit(solution)/shard_map/reshape;squeeze | solution.py:249
  1.0 5.1 %collective-permute-start.2 = (bf16[32,8,256]{2,1,0:T(8,128)(2,1)S(1)}, bf16[32,8,256]{2,1,0:T(8,128)(2,1)S(1)}, u32[]{:S(2)}, u32[]{:S(2)}) collective-permute-start(bf16[32,8,256]{2,1,0:T(8,128)(2,1)S(1)} %reshape_squeeze.6), channel_id=1, source_target_pairs={{0,24},{4,28},{8,16},{12,20},{16,8},{20,12},{24,0},{28,4},{1,25},{... | collective-permute-start | bytes 393224 | tf_op jit(solution)/shard_map/ppermute | solution.py:163
  6.1 0.0 collective-permute-start.1
  6.1 0.6 %collective-permute-start = (bf16[32,8,256]{2,1,0:T(8,128)(2,1)S(1)}, bf16[32,8,256]{2,1,0:T(8,128)(2,1)S(1)}, u32[]{:S(2)}, u32[]{:S(2)}) collective-permute-start(bf16[32,8,256]{2,1,0:T(8,128)(2,1)S(1)} %reshape_squeeze.6), channel_id=1, source_target_pairs={{0,16},{4,20},{8,24},{12,28},{16,0},{20,4},{24,8},{28,12},{1,17},{... | collective-permute-start | bytes 393224 | tf_op jit(solution)/shard_map/ppermute | solution.py:163
  6.8 0.1 constant_dynamic-slice_fusion
  6.9 0.5 fusion.3
  7.4 0.1 broadcast_in_dim.16
  7.5 0.1 broadcast_in_dim.17
  7.6 0.7 %convert_bitcast_fusion = f32[32,2]{0,1:T(2,128)S(1)} fusion(s32[1,32,2]{1,2,0:T(2,128)} %param.15), kind=kLoop, calls=%fused_computation.9 | loop fusion | flops 64 | bytes 512 | tf_op jit(solution)/shard_map/convert_element_type | solution.py:243
  8.2 0.8 %reshape_squeeze.7 = bf16[2,32,4,32]{3,2,1,0:T(4,128)(2,1)S(1)} reshape(bf16[1,1,2,32,128]{4,3,2,1,0:T(8,128)(2,1)} %param.22) | data formatting | bytes 32768 | tf_op jit(solution)/shard_map/reshape;squeeze | solution.py:253
  9.1 0.6 %gather_fusion = bf16[4,2,32,32]{3,2,1,0:T(8,128)(2,1)S(1)} fusion(bf16[2,32,4,32]{3,1,2,0:T(8,128)(2,1)S(1)} %copy.18, s32[1024]{0:T(1024)S(1)} %pad_clamp_fusion), kind=kCustom, calls=%fused_computation | custom fusion | bytes 32784 | tf_op jit(solution)/shard_map/jit(_take)/gather | solution.py:255
  9.6 0.1 copy.19
  9.7 0.1 gather.7
  9.8 0.6 %broadcast_select_fusion.cp_ref = bf16[2,32,128]{2,1,0:T(8,128)(2,1)} fusion(bf16[2,32,128]{2,1,0:T(8,128)(2,1)S(1)} %gather.7, pred[128]{0:T(512)(128)(4,1)S(1)} %broadcast_in_dim.17), kind=kLoop, calls=%fused_computation.5 | loop fusion | flops 8192 | bytes 32896 | tf_op jit(solution)/shard_map/jit(_take)/select_n | solution.py:255
  10.4 1.8 %reduce-precision_bitcast_fusion = (f32[32]{0:T(128)}, f32[32,1]{0,1:T(1,128)S(1)}) fusion(f32[32,2]{0,1:T(2,128)S(1)} %convert_bitcast_fusion, f32[]{:T(128)} %bitcast.5, f32[]{:T(128)} %bitcast.3), kind=kLoop, calls=%fused_computation.10 | loop fusion | flops 128 | bytes 520 | tf_op jit(solution)/shard_map/reduce_precision | solution.py:247
  12.2 0.5 %reduce-precision_bitcast_fusion.1.cos_ref = f32[32]{0:T(128)} fusion(f32[32,1]{0,1:T(1,128)S(1)} %get-tuple-element.18), kind=kLoop, calls=%fused_computation.11 | loop fusion | flops 32 | bytes 256 | tf_op jit(solution)/shard_map/reduce_precision | solution.py:246
  12.8 0.0 collective-permute-done.2
  12.8 0.7 %collective-permute-done.1 = bf16[32,8,256]{2,1,0:T(8,128)(2,1)S(1)} collective-permute-done((bf16[32,8,256]{2,1,0:T(8,128)(2,1)S(1)}, bf16[32,8,256]{2,1,0:T(8,128)(2,1)S(1)}, u32[]{:S(2)}, u32[]{:S(2)}) %collective-permute-start.1) | collective-permute-done | bytes 131104 | tf_op jit(solution)/shard_map/ppermute | solution.py:163
  13.5 3.7 %collective-permute-done = bf16[32,8,256]{2,1,0:T(8,128)(2,1)S(1)} collective-permute-done((bf16[32,8,256]{2,1,0:T(8,128)(2,1)S(1)}, bf16[32,8,256]{2,1,0:T(8,128)(2,1)S(1)}, u32[]{:S(2)}, u32[]{:S(2)}) %collective-permute-start) | collective-permute-done | bytes 131104 | tf_op jit(solution)/shard_map/ppermute | solution.py:163
  17.2 0.1 pad_maximum_fusion.g_ref
  17.3 0.1 collective-permute-start.3
  18.0 0.0 copy-done.1
  18.1 2.2 %shard_map.127.e_in = bf16[2,64,2048]{2,1,0:T(8,128)(2,1)} custom-call(s32[32]{0:T(128)} %bitcast.31, f32[32]{0:T(128)} %reduce-precision_bitcast_fusion.1.cos_ref, f32[32]{0:T(128)} %get-tuple-element.12.sin_ref, bf16[32,32,256]{2,1,0:T(8,128)(2,1)} %copy-done.1), custom_call_target="tpu_custom_call" | custom-call | tf_op jit(solution)/shard_map/pallas_call | solution.py:262
  20.3 0.0 collective-permute-done.3.g_ref
  20.3 0.8 %copy-done.2 = bf16[32,32,256]{2,1,0:T(8,128)(2,1)} copy-done((bf16[32,32,256]{2,1,0:T(8,128)(2,1)}, bf16[32,32,256]{2,1,0:T(8,128)(2,1)S(1)}, u32[]{:S(2)}) %copy-start.2) | copy-done | bytes 524312
  21.1 2.8 %shard_map.128 = (bf16[2,64,2048]{2,1,0:T(8,128)(2,1)}, bf16[2,64,32]{2,1,0:T(8,128)(2,1)}) custom-call(s32[32]{0:T(128)} %bitcast.32, f32[32]{0:T(128)} %reduce-precision_bitcast_fusion.1.cos_ref, f32[32]{0:T(128)} %get-tuple-element.12.sin_ref, s32[1]{0:T(128)} %bitcast.20.rank_ref, ...), custom_call_target="tpu_custom_call", output_to_operand_aliasing={{0}: (6, {})} | custom-call | tf_op jit(solution)/shard_map/pallas_call | solution.py:270
  23.9 2.4 %collective-permute-start.6 = (bf16[2,64,32]{2,1,0:T(8,128)(2,1)}, bf16[2,64,32]{2,1,0:T(8,128)(2,1)S(1)}, u32[]{:S(2)}, u32[]{:S(2)}) collective-permute-start(bf16[2,64,32]{2,1,0:T(8,128)(2,1)} %get-tuple-element.16), channel_id=1, source_target_pairs={{0,3},{1,2},{2,1},{3,0},{4,7},{5,6},{6,5},{7,4},{8,11},{9,10},{10,... | collective-permute-start | bytes 24584 | tf_op jit(solution)/shard_map/ppermute | solution.py:215
  26.3 0.5 collective-permute-start.5
  26.8 0.5 collective-permute-start.4
  27.4 5.6 %shard_map.129.near_ref = f32[64,4096]{1,0:T(8,128)} custom-call(bf16[2,64,2048]{2,1,0:T(8,128)(2,1)} %get-tuple-element.14.e_ref, bf16[2,2048,256]{2,1,0:T(8,128)(2,1)} %bitcast.23, bf16[3,2,32,2048]{3,2,1,0:T(8,128)(2,1)} %bitcast.26, bf16[3,2,32,2048]{3,2,1,0:T(8,128)(2,1)} %bitcast.27), custom_call_target="tpu_custom_call" | custom-call | tf_op jit(solution)/shard_map/pallas_call | solution.py:292
  33.0 0.0 collective-permute-done.6.refs_2_
  33.0 0.0 collective-permute-done.4.refs_0_
  33.0 0.0 copy-start.5
  33.0 0.6 %copy-done.3 = bf16[2,64,32]{2,1,0:T(8,128)(2,1)} copy-done((bf16[2,64,32]{2,1,0:T(8,128)(2,1)}, bf16[2,64,32]{2,1,0:T(8,128)(2,1)S(1)}, u32[]{:S(2)}) %copy-start.3) | copy-done | bytes 8216
  33.6 0.0 copy-done.4
  33.6 0.0 copy-done.5
  33.7 2.5 %shard_map.131 = f32[32,4096]{1,0:T(8,128)} custom-call(f32[2]{0:T(128)} %bitcast.33, s32[1]{0:T(128)} %bitcast.22.rank_ref, f32[64,4096]{1,0:T(8,128)} %shard_map.129.near_ref, bf16[2,32,2048]{2,1,0:T(8,128)(2,1)} %bitcast.24, bf16[2,32,128]{2,1,0:T(8,128)(2,1)} %broadcast_select_fusion.cp_ref, bf16[2,64,32]{2,1,0:T(8,128)(2,1)} %copy-done.5, ...), custom_call_target="tpu_custom_call" | custom-call | tf_op jit(solution)/shard_map/pallas_call | solution.py:303
  36.2 0.0 collective-permute-start.7
  36.2 2.5 %shard_map.130 = f32[32,4096]{1,0:T(8,128)} custom-call(f32[2]{0:T(128)} %bitcast.34, s32[1]{0:T(128)} %bitcast.21.rank_ref, f32[64,4096]{1,0:T(8,128)} %shard_map.129.near_ref, bf16[2,32,2048]{2,1,0:T(8,128)(2,1)} %bitcast.25, bf16[2,32,128]{2,1,0:T(8,128)(2,1)} %broadcast_select_fusion.cp_ref, bf16[2,64,32]{2,1,0:T(8,128)(2,1)} %copy-done.5, ...), custom_call_target="tpu_custom_call" | custom-call | tf_op jit(solution)/shard_map/pallas_call | solution.py:303
  38.7 0.0 collective-permute-done.7
  38.7 1.1 %add.26 = f32[32,4096]{1,0:T(8,128)S(1)} add(f32[32,4096]{1,0:T(8,128)} %shard_map.130, f32[32,4096]{1,0:T(8,128)S(1)} %collective-permute-done.7) | non-fusion elementwise | flops 131072 | bytes 1572864 | tf_op jit(solution)/shard_map/add | solution.py:188
  39.9 0.9 %collective-permute-start.8 = (f32[8,4096]{1,0:T(8,128)S(1)}, f32[8,4096]{1,0:T(8,128)S(1)}, u32[]{:S(2)}, u32[]{:S(2)}) collective-permute-start(f32[8,4096]{1,0:T(8,128)S(1)} %get-tuple-element.19), channel_id=1, source_target_pairs={{0,16},{4,20},{8,24},{12,28},{16,0},{20,4},{24,8},{28,12},{1,17},{... | collective-permute-start | bytes 393224 | tf_op jit(solution)/shard_map/ppermute | solution.py:163
  40.7 1.7 %collective-permute-start.10 = (f32[8,4096]{1,0:T(8,128)S(1)}, f32[8,4096]{1,0:T(8,128)S(1)}, u32[]{:S(2)}, u32[]{:S(2)}) collective-permute-start(f32[8,4096]{1,0:T(8,128)S(1)} %get-tuple-element.20), channel_id=1, source_target_pairs={{0,24},{4,28},{8,16},{12,20},{16,8},{20,12},{24,0},{28,4},{1,25},{... | collective-permute-start | bytes 393224 | tf_op jit(solution)/shard_map/ppermute | solution.py:163
  42.5 0.9 %collective-permute-start.9 = (f32[8,4096]{1,0:T(8,128)S(1)}, f32[8,4096]{1,0:T(8,128)S(1)}, u32[]{:S(2)}, u32[]{:S(2)}) collective-permute-start(f32[8,4096]{1,0:T(8,128)S(1)} %get-tuple-element.21), channel_id=1, source_target_pairs={{0,8},{4,12},{8,0},{12,4},{16,24},{20,28},{24,16},{28,20},{1,9},{5... | collective-permute-start | bytes 393224 | tf_op jit(solution)/shard_map/ppermute | solution.py:163
  43.4 8.9 %collective-permute-done.8 = f32[8,4096]{1,0:T(8,128)S(1)} collective-permute-done((f32[8,4096]{1,0:T(8,128)S(1)}, f32[8,4096]{1,0:T(8,128)S(1)}, u32[]{:S(2)}, u32[]{:S(2)}) %collective-permute-start.8) | collective-permute-done | bytes 131104 | tf_op jit(solution)/shard_map/ppermute | solution.py:163
  52.3 0.0 collective-permute-done.10
  52.3 1.3 %collective-permute-done.9 = f32[8,4096]{1,0:T(8,128)S(1)} collective-permute-done((f32[8,4096]{1,0:T(8,128)S(1)}, f32[8,4096]{1,0:T(8,128)S(1)}, u32[]{:S(2)}, u32[]{:S(2)}) %collective-permute-start.9) | collective-permute-done | bytes 131104 | tf_op jit(solution)/shard_map/ppermute | solution.py:163
  53.6 0.8 %copy.20 = f32[8,2,2048]{2,1,0:T(2,128)} copy(f32[8,2,2048]{2,0,1:T(8,128)S(1)} %bitcast.28) | data formatting | bytes 262144 | tf_op jit(solution)/shard_map/reshape | solution.py:200
  (13 shorter events, 0.1 us)
Async XLA Ops:
  0.0 6.8 %copy-start = (f32[8,2]{0,1:T(2,128)S(1)}, f32[8,2]{0,1:T(2,128)}, u32[]{:S(2)}) copy-start(f32[8,2]{0,1:T(2,128)} %param.16) | copy-start | bytes 196
  1.0 11.8 %collective-permute-start.2 = (bf16[32,8,256]{2,1,0:T(8,128)(2,1)S(1)}, bf16[32,8,256]{2,1,0:T(8,128)(2,1)S(1)}, u32[]{:S(2)}, u32[]{:S(2)}) collective-permute-start(bf16[32,8,256]{2,1,0:T(8,128)(2,1)S(1)} %reshape_squeeze.6), channel_id=1, source_target_pairs={{0,24},{4,28},{8,16},{12,20},{16,8},{20,12},{24,0},{28,4},{1,25},{... | collective-permute-start | bytes 393224 | tf_op jit(solution)/shard_map/ppermute | solution.py:163
  6.1 7.4 %collective-permute-start.1 = (bf16[32,8,256]{2,1,0:T(8,128)(2,1)S(1)}, bf16[32,8,256]{2,1,0:T(8,128)(2,1)S(1)}, u32[]{:S(2)}, u32[]{:S(2)}) collective-permute-start(bf16[32,8,256]{2,1,0:T(8,128)(2,1)S(1)} %reshape_squeeze.6), channel_id=1, source_target_pairs={{0,8},{4,12},{8,0},{12,4},{16,24},{20,28},{24,16},{28,20},{1,9},{5... | collective-permute-start | bytes 393224 | tf_op jit(solution)/shard_map/ppermute | solution.py:163
  6.1 11.1 %collective-permute-start = (bf16[32,8,256]{2,1,0:T(8,128)(2,1)S(1)}, bf16[32,8,256]{2,1,0:T(8,128)(2,1)S(1)}, u32[]{:S(2)}, u32[]{:S(2)}) collective-permute-start(bf16[32,8,256]{2,1,0:T(8,128)(2,1)S(1)} %reshape_squeeze.6), channel_id=1, source_target_pairs={{0,16},{4,20},{8,24},{12,28},{16,0},{20,4},{24,8},{28,12},{1,17},{... | collective-permute-start | bytes 393224 | tf_op jit(solution)/shard_map/ppermute | solution.py:163
  17.3 0.8 %copy-start.1 = (bf16[32,32,256]{2,1,0:T(8,128)(2,1)}, bf16[32,32,256]{2,1,0:T(8,128)(2,1)S(1)}, u32[]{:S(2)}) copy-start(bf16[32,32,256]{2,1,0:T(8,128)(2,1)S(1)} %pad_maximum_fusion.g_ref) | copy-start | bytes 1572868
  17.3 3.0 %collective-permute-start.3 = (bf16[32,32,256]{2,1,0:T(8,128)(2,1)S(1)}, bf16[32,32,256]{2,1,0:T(8,128)(2,1)S(1)}, u32[]{:S(2)}, u32[]{:S(2)}) collective-permute-start(bf16[32,32,256]{2,1,0:T(8,128)(2,1)S(1)} %pad_maximum_fusion.g_ref), channel_id=1, source_target_pairs={{0,4},{4,0},{8,12},{12,8},{16,20},{20,16},{24,28},{28,24},{1,5},{5... | collective-permute-start | bytes 1572872 | tf_op jit(solution)/shard_map/ppermute | solution.py:163
  20.3 0.8 %copy-start.2 = (bf16[32,32,256]{2,1,0:T(8,128)(2,1)}, bf16[32,32,256]{2,1,0:T(8,128)(2,1)S(1)}, u32[]{:S(2)}) copy-start(bf16[32,32,256]{2,1,0:T(8,128)(2,1)S(1)} %collective-permute-done.3.g_ref) | copy-start | bytes 1572868
  23.9 9.1 %collective-permute-start.6 = (bf16[2,64,32]{2,1,0:T(8,128)(2,1)}, bf16[2,64,32]{2,1,0:T(8,128)(2,1)S(1)}, u32[]{:S(2)}, u32[]{:S(2)}) collective-permute-start(bf16[2,64,32]{2,1,0:T(8,128)(2,1)} %get-tuple-element.16), channel_id=1, source_target_pairs={{0,3},{1,2},{2,1},{3,0},{4,7},{5,6},{6,5},{7,4},{8,11},{9,10},{10,... | collective-permute-start | bytes 24584 | tf_op jit(solution)/shard_map/ppermute | solution.py:215
  26.3 6.7 %collective-permute-start.5 = (bf16[2,64,32]{2,1,0:T(8,128)(2,1)}, bf16[2,64,32]{2,1,0:T(8,128)(2,1)S(1)}, u32[]{:S(2)}, u32[]{:S(2)}) collective-permute-start(bf16[2,64,32]{2,1,0:T(8,128)(2,1)} %get-tuple-element.16), channel_id=1, source_target_pairs={{0,2},{1,3},{2,0},{3,1},{4,6},{5,7},{6,4},{7,5},{8,10},{9,11},{10,... | collective-permute-start | bytes 24584 | tf_op jit(solution)/shard_map/ppermute | solution.py:215
  26.8 6.2 %collective-permute-start.4 = (bf16[2,64,32]{2,1,0:T(8,128)(2,1)}, bf16[2,64,32]{2,1,0:T(8,128)(2,1)S(1)}, u32[]{:S(2)}, u32[]{:S(2)}) collective-permute-start(bf16[2,64,32]{2,1,0:T(8,128)(2,1)} %get-tuple-element.16), channel_id=1, source_target_pairs={{0,1},{1,0},{2,3},{3,2},{4,5},{5,4},{6,7},{7,6},{8,9},{9,8},{10,11... | collective-permute-start | bytes 24584 | tf_op jit(solution)/shard_map/ppermute | solution.py:215
  33.0 0.6 %copy-start.3 = (bf16[2,64,32]{2,1,0:T(8,128)(2,1)}, bf16[2,64,32]{2,1,0:T(8,128)(2,1)S(1)}, u32[]{:S(2)}) copy-start(bf16[2,64,32]{2,1,0:T(8,128)(2,1)S(1)} %collective-permute-done.6.refs_2_) | copy-start | bytes 24580
  33.0 0.6 %copy-start.4 = (bf16[2,64,32]{2,1,0:T(8,128)(2,1)}, bf16[2,64,32]{2,1,0:T(8,128)(2,1)S(1)}, u32[]{:S(2)}) copy-start(bf16[2,64,32]{2,1,0:T(8,128)(2,1)S(1)} %collective-permute-done.5.refs_1_) | copy-start | bytes 24580
  33.0 0.6 %copy-start.5 = (bf16[2,64,32]{2,1,0:T(8,128)(2,1)}, bf16[2,64,32]{2,1,0:T(8,128)(2,1)S(1)}, u32[]{:S(2)}) copy-start(bf16[2,64,32]{2,1,0:T(8,128)(2,1)S(1)} %collective-permute-done.4.refs_0_) | copy-start | bytes 24580
  36.2 2.5 %collective-permute-start.7 = (f32[32,4096]{1,0:T(8,128)}, f32[32,4096]{1,0:T(8,128)S(1)}, u32[]{:S(2)}, u32[]{:S(2)}) collective-permute-start(f32[32,4096]{1,0:T(8,128)} %shard_map.131), channel_id=1, source_target_pairs={{0,4},{4,0},{8,12},{12,8},{16,20},{20,16},{24,28},{28,24},{1,5},{5... | collective-permute-start | bytes 1572872 | tf_op jit(solution)/shard_map/ppermute | solution.py:163
  39.9 12.4 %collective-permute-start.8 = (f32[8,4096]{1,0:T(8,128)S(1)}, f32[8,4096]{1,0:T(8,128)S(1)}, u32[]{:S(2)}, u32[]{:S(2)}) collective-permute-start(f32[8,4096]{1,0:T(8,128)S(1)} %get-tuple-element.19), channel_id=1, source_target_pairs={{0,16},{4,20},{8,24},{12,28},{16,0},{20,4},{24,8},{28,12},{1,17},{... | collective-permute-start | bytes 393224 | tf_op jit(solution)/shard_map/ppermute | solution.py:163
  40.7 11.5 %collective-permute-start.10 = (f32[8,4096]{1,0:T(8,128)S(1)}, f32[8,4096]{1,0:T(8,128)S(1)}, u32[]{:S(2)}, u32[]{:S(2)}) collective-permute-start(f32[8,4096]{1,0:T(8,128)S(1)} %get-tuple-element.20), channel_id=1, source_target_pairs={{0,24},{4,28},{8,16},{12,20},{16,8},{20,12},{24,0},{28,4},{1,25},{... | collective-permute-start | bytes 393224 | tf_op jit(solution)/shard_map/ppermute | solution.py:163
  42.5 11.1 %collective-permute-start.9 = (f32[8,4096]{1,0:T(8,128)S(1)}, f32[8,4096]{1,0:T(8,128)S(1)}, u32[]{:S(2)}, u32[]{:S(2)}) collective-permute-start(f32[8,4096]{1,0:T(8,128)S(1)} %get-tuple-element.21), channel_id=1, source_target_pairs={{0,8},{4,12},{8,0},{12,4},{16,24},{20,28},{24,16},{28,20},{1,9},{5... | collective-permute-start | bytes 393224 | tf_op jit(solution)/shard_map/ppermute | solution.py:163

commit v14 on v12

--- a/solution.py
+++ b/solution.py
@@ -59,7 +59,9 @@
     _, source_count, row_count = e_ref.shape
     levels = lr_ref.shape[0]
     sc = source_count
-    stacked = e_ref[...].reshape(2 * sc, row_count)
+
+    def stacked(cols, width):
+        return e_ref[:, :, cols].reshape(2 * sc, width)
 
     first_group = []
     slot = 0
@@ -68,7 +70,7 @@
         first_group.append(slot)
         for g in range(2 ** (j + 1)):
             cols = slice(g * node, (g + 1) * node)
-            ab = stacked[:, cols]
+            ab = stacked(cols, node)
             t_re = _nt(ab, lr_ref[j, 0, :, cols])
             t_im = _nt(ab, lr_ref[j, 1, :, cols])
             pj_ref[slot, 0] = (t_re[:sc] - t_im[sc:]).astype(jnp.bfloat16)
@@ -77,7 +79,7 @@
 
     for l in range(row_count // LEAF):
         cols = slice(l * LEAF, (l + 1) * LEAF)
-        ab = stacked[:, cols]
+        ab = stacked(cols, LEAF)
         t_re = _nt(ab, leaf_ref[0, cols, :])
         t_im = _nt(ab, leaf_ref[1, cols, :])
         f_re = t_re[:sc] - t_im[sc:]

time: 53.8 us -> 53.8 us (level)
  no operation moved by 1% of the time
where the time goes in v14:
time: 53.8 us; the launch traced here: 53.5 us
  waiting for transfers between devices  15.9 us (30%)
  Pallas kernels  13.6 us (25%)
  starting transfers between devices  12.9 us (24%)
  local copies, waits for them, and re-layouts  5.49 us (10%)
  other arithmetic  4.86 us (9%)
  between operations  0.81 us (2%)
    ppermute x8, waiting for transfers between devices, _permute(): return lax.ppermute(x, axis_name, [(i, i ^ offset) for i in range(count)])  15.9 us
    ppermute x8, starting transfers between devices, _permute(): return lax.ppermute(x, axis_name, [(i, i ^ offset) for i in range(count)])  9.38 us
    pallas_call x1, Pallas kernels, shards(): pl.pallas_call(_near_kernel, out_shape=jax.ShapeDtypeStruct((source_count...  5.63 us
    pallas_call x2, Pallas kernels, shards(): pl.pallas_call(_far_kernel, out_shape=jax.ShapeDtypeStruct((half, 2 * row...  5.03 us
    ppermute x3, starting transfers between devices, _exchange(): lax.ppermute(x, axis_name, [(i, i ^ p) for i in range(count)])  3.49 us
    pallas_call x1, Pallas kernels, shards(): pl.pallas_call(_excite_kernel, out_shape=(jax.ShapeDtypeStruct((2, source...  2.91 us
    reduce_precision x1, other arithmetic, shards(): lax.reduce_precision(jnp.sin(theta), exponent_bits=8, mantissa_bits=7)  1.78 us
    unnamed x12, local copies, waits for them, and re-layouts  1.41 us
  transfers between devices with their start and end apart: 11, of which 5 were waited for; matrix products, arithmetic and copies ran while one was open for 11% of the time, Pallas kernels for 15%

profile of v14, /device:TPU:0, one launch (start us, length us, event | category | flops | bytes accessed | tf_op | source)
XLA Modules:
  0.0 53.5 jit_solution(10498773033145821702)
XLA Ops:
  0.0 0.0 copy-start
  0.0 1.0 %reshape_squeeze.6 = bf16[32,8,256]{2,1,0:T(8,128)(2,1)S(1)} reshape(bf16[1,32,8,2,128]{4,3,2,1,0:T(2,128)(2,1)} %param.13) | data formatting | bytes 262144 | tf_op jit(solution)/shard_map/reshape;squeeze | solution.py:236
  1.0 5.1 %collective-permute-start.2 = (bf16[32,8,256]{2,1,0:T(8,128)(2,1)S(1)}, bf16[32,8,256]{2,1,0:T(8,128)(2,1)S(1)}, u32[]{:S(2)}, u32[]{:S(2)}) collective-permute-start(bf16[32,8,256]{2,1,0:T(8,128)(2,1)S(1)} %reshape_squeeze.6), channel_id=1, source_target_pairs={{0,24},{4,28},{8,16},{12,20},{16,8},{20,12},{24,0},{28,4},{1,25},{... | collective-permute-start | bytes 393224 | tf_op jit(solution)/shard_map/ppermute | solution.py:150
  6.1 0.0 collective-permute-start.1
  6.1 0.6 %collective-permute-start = (bf16[32,8,256]{2,1,0:T(8,128)(2,1)S(1)}, bf16[32,8,256]{2,1,0:T(8,128)(2,1)S(1)}, u32[]{:S(2)}, u32[]{:S(2)}) collective-permute-start(bf16[32,8,256]{2,1,0:T(8,128)(2,1)S(1)} %reshape_squeeze.6), channel_id=1, source_target_pairs={{0,16},{4,20},{8,24},{12,28},{16,0},{20,4},{24,8},{28,12},{1,17},{... | collective-permute-start | bytes 393224 | tf_op jit(solution)/shard_map/ppermute | solution.py:150
  6.8 0.1 constant_dynamic-slice_fusion
  6.9 0.5 fusion.3
  7.4 0.1 broadcast_in_dim.16
  7.5 0.1 broadcast_in_dim.17
  7.6 0.7 %convert_bitcast_fusion = f32[32,2]{0,1:T(2,128)S(1)} fusion(s32[1,32,2]{1,2,0:T(2,128)} %param.15), kind=kLoop, calls=%fused_computation.9 | loop fusion | flops 64 | bytes 512 | tf_op jit(solution)/shard_map/convert_element_type | solution.py:230
  8.2 0.8 %reshape_squeeze.7 = bf16[2,32,4,32]{3,2,1,0:T(4,128)(2,1)S(1)} reshape(bf16[1,1,2,32,128]{4,3,2,1,0:T(8,128)(2,1)} %param.22) | data formatting | bytes 32768 | tf_op jit(solution)/shard_map/reshape;squeeze | solution.py:240
  9.1 0.6 %gather_fusion = bf16[4,2,32,32]{3,2,1,0:T(8,128)(2,1)S(1)} fusion(bf16[2,32,4,32]{3,1,2,0:T(8,128)(2,1)S(1)} %copy.17, s32[1024]{0:T(1024)S(1)} %pad_clamp_fusion), kind=kCustom, calls=%fused_computation | custom fusion | bytes 32784 | tf_op jit(solution)/shard_map/jit(_take)/gather | solution.py:242
  9.6 0.1 copy.18
  9.7 0.1 gather.7
  9.8 0.6 %broadcast_select_fusion.cp_ref = bf16[2,32,128]{2,1,0:T(8,128)(2,1)} fusion(bf16[2,32,128]{2,1,0:T(8,128)(2,1)S(1)} %gather.7, pred[128]{0:T(512)(128)(4,1)S(1)} %broadcast_in_dim.17), kind=kLoop, calls=%fused_computation.5 | loop fusion | flops 8192 | bytes 32896 | tf_op jit(solution)/shard_map/jit(_take)/select_n | solution.py:242
  10.4 1.8 %reduce-precision_bitcast_fusion = (f32[32]{0:T(128)}, f32[32,1]{0,1:T(1,128)S(1)}) fusion(f32[32,2]{0,1:T(2,128)S(1)} %convert_bitcast_fusion, f32[]{:T(128)} %bitcast.5, f32[]{:T(128)} %bitcast.3), kind=kLoop, calls=%fused_computation.10 | loop fusion | flops 128 | bytes 520 | tf_op jit(solution)/shard_map/reduce_precision | solution.py:234
  12.2 0.6 %reduce-precision_bitcast_fusion.1.cos_ref = f32[32]{0:T(128)} fusion(f32[32,1]{0,1:T(1,128)S(1)} %get-tuple-element.18), kind=kLoop, calls=%fused_computation.11 | loop fusion | flops 32 | bytes 256 | tf_op jit(solution)/shard_map/reduce_precision | solution.py:233
  12.8 0.0 collective-permute-done.2
  12.8 0.8 %collective-permute-done.1 = bf16[32,8,256]{2,1,0:T(8,128)(2,1)S(1)} collective-permute-done((bf16[32,8,256]{2,1,0:T(8,128)(2,1)S(1)}, bf16[32,8,256]{2,1,0:T(8,128)(2,1)S(1)}, u32[]{:S(2)}, u32[]{:S(2)}) %collective-permute-start.1) | collective-permute-done | bytes 131104 | tf_op jit(solution)/shard_map/ppermute | solution.py:150
  13.5 3.7 %collective-permute-done = bf16[32,8,256]{2,1,0:T(8,128)(2,1)S(1)} collective-permute-done((bf16[32,8,256]{2,1,0:T(8,128)(2,1)S(1)}, bf16[32,8,256]{2,1,0:T(8,128)(2,1)S(1)}, u32[]{:S(2)}, u32[]{:S(2)}) %collective-permute-start) | collective-permute-done | bytes 131104 | tf_op jit(solution)/shard_map/ppermute | solution.py:150
  17.2 0.1 pad_maximum_fusion.ga_ref
  17.3 0.1 collective-permute-start.3
  18.0 1.2 %collective-permute-done.3.gb_ref = bf16[32,32,256]{2,1,0:T(8,128)(2,1)S(1)} collective-permute-done((bf16[32,32,256]{2,1,0:T(8,128)(2,1)S(1)}, bf16[32,32,256]{2,1,0:T(8,128)(2,1)S(1)}, u32[]{:S(2)}, u32[]{:S(2)}) %collective-permute-start.3) | collective-permute-done | bytes 524320 | tf_op jit(solution)/shard_map/ppermute | solution.py:150
  19.3 0.8 %copy-done.2 = bf16[32,32,256]{2,1,0:T(8,128)(2,1)} copy-done((bf16[32,32,256]{2,1,0:T(8,128)(2,1)}, bf16[32,32,256]{2,1,0:T(8,128)(2,1)S(1)}, u32[]{:S(2)}) %copy-start.2) | copy-done | bytes 524312
  20.0 2.9 %shard_map.127 = (bf16[2,64,2048]{2,1,0:T(8,128)(2,1)}, bf16[2,64,32]{2,1,0:T(8,128)(2,1)}) custom-call(s32[32]{0:T(128)} %bitcast.33, f32[32]{0:T(128)} %reduce-precision_bitcast_fusion.1.cos_ref, f32[32]{0:T(128)} %get-tuple-element.12.sin_ref, s32[1]{0:T(128)} %bitcast.20.rank_ref, bf16[32,32,256]{2,1,0:T(8,128)(2,1)} %copy-done.1, ...), custom_call_target="tpu_custom_call" | custom-call | tf_op jit(solution)/shard_map/pallas_call | solution.py:246
  23.0 2.4 %collective-permute-start.6 = (bf16[2,64,32]{2,1,0:T(8,128)(2,1)}, bf16[2,64,32]{2,1,0:T(8,128)(2,1)S(1)}, u32[]{:S(2)}, u32[]{:S(2)}) collective-permute-start(bf16[2,64,32]{2,1,0:T(8,128)(2,1)} %get-tuple-element.16), channel_id=1, source_target_pairs={{0,3},{1,2},{2,1},{3,0},{4,7},{5,6},{6,5},{7,4},{8,11},{9,10},{10,... | collective-permute-start | bytes 24584 | tf_op jit(solution)/shard_map/ppermute | solution.py:202
  25.4 0.5 collective-permute-start.5
  25.9 0.5 %collective-permute-start.4 = (bf16[2,64,32]{2,1,0:T(8,128)(2,1)}, bf16[2,64,32]{2,1,0:T(8,128)(2,1)S(1)}, u32[]{:S(2)}, u32[]{:S(2)}) collective-permute-start(bf16[2,64,32]{2,1,0:T(8,128)(2,1)} %get-tuple-element.16), channel_id=1, source_target_pairs={{0,1},{1,0},{2,3},{3,2},{4,5},{5,4},{6,7},{7,6},{8,9},{9,8},{10,11... | collective-permute-start | bytes 24584 | tf_op jit(solution)/shard_map/ppermute | solution.py:202
  26.4 5.6 %shard_map.128.near_ref = f32[64,4096]{1,0:T(8,128)} custom-call(bf16[2,64,2048]{2,1,0:T(8,128)(2,1)} %get-tuple-element.14.e_ref, bf16[2,2048,256]{2,1,0:T(8,128)(2,1)} %bitcast.23, bf16[3,2,32,2048]{3,2,1,0:T(8,128)(2,1)} %bitcast.26, bf16[3,2,32,2048]{3,2,1,0:T(8,128)(2,1)} %bitcast.27), custom_call_target="tpu_custom_call" | custom-call | tf_op jit(solution)/shard_map/pallas_call | solution.py:261
  32.1 0.0 collective-permute-done.6.refs_2_
  32.1 0.0 collective-permute-done.5.refs_1_
  32.1 0.0 collective-permute-done.4.refs_0_
  32.1 0.0 copy-start.5
  32.1 0.6 %copy-done.3 = bf16[2,64,32]{2,1,0:T(8,128)(2,1)} copy-done((bf16[2,64,32]{2,1,0:T(8,128)(2,1)}, bf16[2,64,32]{2,1,0:T(8,128)(2,1)S(1)}, u32[]{:S(2)}) %copy-start.3) | copy-done | bytes 8216
  32.7 0.0 copy-done.4
  32.7 0.0 copy-done.5
  32.7 2.5 %shard_map.130 = f32[32,4096]{1,0:T(8,128)} custom-call(f32[2]{0:T(128)} %bitcast.31, s32[1]{0:T(128)} %bitcast.22.rank_ref, f32[64,4096]{1,0:T(8,128)} %shard_map.128.near_ref, bf16[2,32,2048]{2,1,0:T(8,128)(2,1)} %bitcast.24, bf16[2,32,128]{2,1,0:T(8,128)(2,1)} %broadcast_select_fusion.cp_ref, bf16[2,64,32]{2,1,0:T(8,128)(2,1)} %copy-done.5, ...), custom_call_target="tpu_custom_call" | custom-call | tf_op jit(solution)/shard_map/pallas_call | solution.py:272
  35.2 0.0 collective-permute-start.7
  35.2 2.5 %shard_map.129 = f32[32,4096]{1,0:T(8,128)} custom-call(f32[2]{0:T(128)} %bitcast.32, s32[1]{0:T(128)} %bitcast.21.rank_ref, f32[64,4096]{1,0:T(8,128)} %shard_map.128.near_ref, bf16[2,32,2048]{2,1,0:T(8,128)(2,1)} %bitcast.25, bf16[2,32,128]{2,1,0:T(8,128)(2,1)} %broadcast_select_fusion.cp_ref, bf16[2,64,32]{2,1,0:T(8,128)(2,1)} %copy-done.5, ...), custom_call_target="tpu_custom_call" | custom-call | tf_op jit(solution)/shard_map/pallas_call | solution.py:272
  37.8 0.0 collective-permute-done.7
  37.8 1.1 %add.26 = f32[32,4096]{1,0:T(8,128)S(1)} add(f32[32,4096]{1,0:T(8,128)} %shard_map.129, f32[32,4096]{1,0:T(8,128)S(1)} %collective-permute-done.7) | non-fusion elementwise | flops 131072 | bytes 1572864 | tf_op jit(solution)/shard_map/add | solution.py:175
  38.9 0.9 %collective-permute-start.8 = (f32[8,4096]{1,0:T(8,128)S(1)}, f32[8,4096]{1,0:T(8,128)S(1)}, u32[]{:S(2)}, u32[]{:S(2)}) collective-permute-start(f32[8,4096]{1,0:T(8,128)S(1)} %get-tuple-element.19), channel_id=1, source_target_pairs={{0,16},{4,20},{8,24},{12,28},{16,0},{20,4},{24,8},{28,12},{1,17},{... | collective-permute-start | bytes 393224 | tf_op jit(solution)/shard_map/ppermute | solution.py:150
  39.8 1.7 %collective-permute-start.10 = (f32[8,4096]{1,0:T(8,128)S(1)}, f32[8,4096]{1,0:T(8,128)S(1)}, u32[]{:S(2)}, u32[]{:S(2)}) collective-permute-start(f32[8,4096]{1,0:T(8,128)S(1)} %get-tuple-element.20), channel_id=1, source_target_pairs={{0,24},{4,28},{8,16},{12,20},{16,8},{20,12},{24,0},{28,4},{1,25},{... | collective-permute-start | bytes 393224 | tf_op jit(solution)/shard_map/ppermute | solution.py:150
  41.5 0.9 %collective-permute-start.9 = (f32[8,4096]{1,0:T(8,128)S(1)}, f32[8,4096]{1,0:T(8,128)S(1)}, u32[]{:S(2)}, u32[]{:S(2)}) collective-permute-start(f32[8,4096]{1,0:T(8,128)S(1)} %get-tuple-element.21), channel_id=1, source_target_pairs={{0,8},{4,12},{8,0},{12,4},{16,24},{20,28},{24,16},{28,20},{1,9},{5... | collective-permute-start | bytes 393224 | tf_op jit(solution)/shard_map/ppermute | solution.py:150
  42.5 8.9 %collective-permute-done.8 = f32[8,4096]{1,0:T(8,128)S(1)} collective-permute-done((f32[8,4096]{1,0:T(8,128)S(1)}, f32[8,4096]{1,0:T(8,128)S(1)}, u32[]{:S(2)}, u32[]{:S(2)}) %collective-permute-start.8) | collective-permute-done | bytes 131104 | tf_op jit(solution)/shard_map/ppermute | solution.py:150
  51.4 0.0 collective-permute-done.10
  51.4 1.3 %collective-permute-done.9 = f32[8,4096]{1,0:T(8,128)S(1)} collective-permute-done((f32[8,4096]{1,0:T(8,128)S(1)}, f32[8,4096]{1,0:T(8,128)S(1)}, u32[]{:S(2)}, u32[]{:S(2)}) %collective-permute-start.9) | collective-permute-done | bytes 131104 | tf_op jit(solution)/shard_map/ppermute | solution.py:150
  52.7 0.8 %copy.19 = f32[8,2,2048]{2,1,0:T(2,128)} copy(f32[8,2,2048]{2,0,1:T(8,128)S(1)} %bitcast.28) | data formatting | bytes 262144 | tf_op jit(solution)/shard_map/reshape | solution.py:187
  (12 shorter events, 0.1 us)
Async XLA Ops:
  0.0 6.8 %copy-start = (f32[8,2]{0,1:T(2,128)S(1)}, f32[8,2]{0,1:T(2,128)}, u32[]{:S(2)}) copy-start(f32[8,2]{0,1:T(2,128)} %param.16) | copy-start | bytes 196
  1.0 11.8 %collective-permute-start.2 = (bf16[32,8,256]{2,1,0:T(8,128)(2,1)S(1)}, bf16[32,8,256]{2,1,0:T(8,128)(2,1)S(1)}, u32[]{:S(2)}, u32[]{:S(2)}) collective-permute-start(bf16[32,8,256]{2,1,0:T(8,128)(2,1)S(1)} %reshape_squeeze.6), channel_id=1, source_target_pairs={{0,24},{4,28},{8,16},{12,20},{16,8},{20,12},{24,0},{28,4},{1,25},{... | collective-permute-start | bytes 393224 | tf_op jit(solution)/shard_map/ppermute | solution.py:150
  6.1 7.4 %collective-permute-start.1 = (bf16[32,8,256]{2,1,0:T(8,128)(2,1)S(1)}, bf16[32,8,256]{2,1,0:T(8,128)(2,1)S(1)}, u32[]{:S(2)}, u32[]{:S(2)}) collective-permute-start(bf16[32,8,256]{2,1,0:T(8,128)(2,1)S(1)} %reshape_squeeze.6), channel_id=1, source_target_pairs={{0,8},{4,12},{8,0},{12,4},{16,24},{20,28},{24,16},{28,20},{1,9},{5... | collective-permute-start | bytes 393224 | tf_op jit(solution)/shard_map/ppermute | solution.py:150
  6.1 11.1 %collective-permute-start = (bf16[32,8,256]{2,1,0:T(8,128)(2,1)S(1)}, bf16[32,8,256]{2,1,0:T(8,128)(2,1)S(1)}, u32[]{:S(2)}, u32[]{:S(2)}) collective-permute-start(bf16[32,8,256]{2,1,0:T(8,128)(2,1)S(1)} %reshape_squeeze.6), channel_id=1, source_target_pairs={{0,16},{4,20},{8,24},{12,28},{16,0},{20,4},{24,8},{28,12},{1,17},{... | collective-permute-start | bytes 393224 | tf_op jit(solution)/shard_map/ppermute | solution.py:150
  17.3 2.0 %copy-start.1 = (bf16[32,32,256]{2,1,0:T(8,128)(2,1)}, bf16[32,32,256]{2,1,0:T(8,128)(2,1)S(1)}, u32[]{:S(2)}) copy-start(bf16[32,32,256]{2,1,0:T(8,128)(2,1)S(1)} %pad_maximum_fusion.ga_ref) | copy-start | bytes 1572868
  17.3 2.0 %collective-permute-start.3 = (bf16[32,32,256]{2,1,0:T(8,128)(2,1)S(1)}, bf16[32,32,256]{2,1,0:T(8,128)(2,1)S(1)}, u32[]{:S(2)}, u32[]{:S(2)}) collective-permute-start(bf16[32,32,256]{2,1,0:T(8,128)(2,1)S(1)} %pad_maximum_fusion.ga_ref), channel_id=1, source_target_pairs={{0,4},{4,0},{8,12},{12,8},{16,20},{20,16},{24,28},{28,24},{1,5},{5... | collective-permute-start | bytes 1572872 | tf_op jit(solution)/shard_map/ppermute | solution.py:150
  19.2 0.8 %copy-start.2 = (bf16[32,32,256]{2,1,0:T(8,128)(2,1)}, bf16[32,32,256]{2,1,0:T(8,128)(2,1)S(1)}, u32[]{:S(2)}) copy-start(bf16[32,32,256]{2,1,0:T(8,128)(2,1)S(1)} %collective-permute-done.3.gb_ref) | copy-start | bytes 1572868
  23.0 9.1 %collective-permute-start.6 = (bf16[2,64,32]{2,1,0:T(8,128)(2,1)}, bf16[2,64,32]{2,1,0:T(8,128)(2,1)S(1)}, u32[]{:S(2)}, u32[]{:S(2)}) collective-permute-start(bf16[2,64,32]{2,1,0:T(8,128)(2,1)} %get-tuple-element.16), channel_id=1, source_target_pairs={{0,3},{1,2},{2,1},{3,0},{4,7},{5,6},{6,5},{7,4},{8,11},{9,10},{10,... | collective-permute-start | bytes 24584 | tf_op jit(solution)/shard_map/ppermute | solution.py:202
  25.4 6.7 %collective-permute-start.5 = (bf16[2,64,32]{2,1,0:T(8,128)(2,1)}, bf16[2,64,32]{2,1,0:T(8,128)(2,1)S(1)}, u32[]{:S(2)}, u32[]{:S(2)}) collective-permute-start(bf16[2,64,32]{2,1,0:T(8,128)(2,1)} %get-tuple-element.16), channel_id=1, source_target_pairs={{0,2},{1,3},{2,0},{3,1},{4,6},{5,7},{6,4},{7,5},{8,10},{9,11},{10,... | collective-permute-start | bytes 24584 | tf_op jit(solution)/shard_map/ppermute | solution.py:202
  25.9 6.2 %collective-permute-start.4 = (bf16[2,64,32]{2,1,0:T(8,128)(2,1)}, bf16[2,64,32]{2,1,0:T(8,128)(2,1)S(1)}, u32[]{:S(2)}, u32[]{:S(2)}) collective-permute-start(bf16[2,64,32]{2,1,0:T(8,128)(2,1)} %get-tuple-element.16), channel_id=1, source_target_pairs={{0,1},{1,0},{2,3},{3,2},{4,5},{5,4},{6,7},{7,6},{8,9},{9,8},{10,11... | collective-permute-start | bytes 24584 | tf_op jit(solution)/shard_map/ppermute | solution.py:202
  32.1 0.6 %copy-start.3 = (bf16[2,64,32]{2,1,0:T(8,128)(2,1)}, bf16[2,64,32]{2,1,0:T(8,128)(2,1)S(1)}, u32[]{:S(2)}) copy-start(bf16[2,64,32]{2,1,0:T(8,128)(2,1)S(1)} %collective-permute-done.6.refs_2_) | copy-start | bytes 24580
  32.1 0.6 %copy-start.4 = (bf16[2,64,32]{2,1,0:T(8,128)(2,1)}, bf16[2,64,32]{2,1,0:T(8,128)(2,1)S(1)}, u32[]{:S(2)}) copy-start(bf16[2,64,32]{2,1,0:T(8,128)(2,1)S(1)} %collective-permute-done.5.refs_1_) | copy-start | bytes 24580
  32.1 0.6 %copy-start.5 = (bf16[2,64,32]{2,1,0:T(8,128)(2,1)}, bf16[2,64,32]{2,1,0:T(8,128)(2,1)S(1)}, u32[]{:S(2)}) copy-start(bf16[2,64,32]{2,1,0:T(8,128)(2,1)S(1)} %collective-permute-done.4.refs_0_) | copy-start | bytes 24580
  35.2 2.5 %collective-permute-start.7 = (f32[32,4096]{1,0:T(8,128)}, f32[32,4096]{1,0:T(8,128)S(1)}, u32[]{:S(2)}, u32[]{:S(2)}) collective-permute-start(f32[32,4096]{1,0:T(8,128)} %shard_map.130), channel_id=1, source_target_pairs={{0,4},{4,0},{8,12},{12,8},{16,20},{20,16},{24,28},{28,24},{1,5},{5... | collective-permute-start | bytes 1572872 | tf_op jit(solution)/shard_map/ppermute | solution.py:150
  38.9 12.4 %collective-permute-start.8 = (f32[8,4096]{1,0:T(8,128)S(1)}, f32[8,4096]{1,0:T(8,128)S(1)}, u32[]{:S(2)}, u32[]{:S(2)}) collective-permute-start(f32[8,4096]{1,0:T(8,128)S(1)} %get-tuple-element.19), channel_id=1, source_target_pairs={{0,16},{4,20},{8,24},{12,28},{16,0},{20,4},{24,8},{28,12},{1,17},{... | collective-permute-start | bytes 393224 | tf_op jit(solution)/shard_map/ppermute | solution.py:150
  39.8 11.6 %collective-permute-start.10 = (f32[8,4096]{1,0:T(8,128)S(1)}, f32[8,4096]{1,0:T(8,128)S(1)}, u32[]{:S(2)}, u32[]{:S(2)}) collective-permute-start(f32[8,4096]{1,0:T(8,128)S(1)} %get-tuple-element.20), channel_id=1, source_target_pairs={{0,24},{4,28},{8,16},{12,20},{16,8},{20,12},{24,0},{28,4},{1,25},{... | collective-permute-start | bytes 393224 | tf_op jit(solution)/shard_map/ppermute | solution.py:150
  41.5 11.1 %collective-permute-start.9 = (f32[8,4096]{1,0:T(8,128)S(1)}, f32[8,4096]{1,0:T(8,128)S(1)}, u32[]{:S(2)}, u32[]{:S(2)}) collective-permute-start(f32[8,4096]{1,0:T(8,128)S(1)} %get-tuple-element.21), channel_id=1, source_target_pairs={{0,8},{4,12},{8,0},{12,4},{16,24},{20,28},{24,16},{28,20},{1,9},{5... | collective-permute-start | bytes 393224 | tf_op jit(solution)/shard_map/ppermute | solution.py:150

commit v15 on v12

--- a/solution.py
+++ b/solution.py
@@ -41,7 +41,7 @@
             acc_im[k, rows] = acc_im[k, rows] + (c * p_im - s * p_re)
         return carry
 
-    lax.fori_loop(0, panel_count, body, 0)
+    lax.fori_loop(0, panel_count, body, 0, unroll=8)
     for k in range(slots):
         e_ref[0, :, k * width:(k + 1) * width] = acc_re[k].astype(jnp.bfloat16)
         e_ref[1, :, k * width:(k + 1) * width] = acc_im[k].astype(jnp.bfloat16)

time: 53.8 us -> 53.7 us (level)
  no operation moved by 1% of the time
where the time goes in v15:
time: 53.7 us; the launch traced here: 53.3 us
  waiting for transfers between devices  15.9 us (30%)
  Pallas kernels  13.4 us (25%)
  starting transfers between devices  12.9 us (24%)
  local copies, waits for them, and re-layouts  5.49 us (10%)
  other arithmetic  4.86 us (9%)
  between operations  0.81 us (2%)
    ppermute x8, waiting for transfers between devices, _permute(): return lax.ppermute(x, axis_name, [(i, i ^ offset) for i in range(count)])  15.9 us
    ppermute x8, starting transfers between devices, _permute(): return lax.ppermute(x, axis_name, [(i, i ^ offset) for i in range(count)])  9.38 us
    pallas_call x1, Pallas kernels, shards(): pl.pallas_call(_near_kernel, out_shape=jax.ShapeDtypeStruct((source_count...  5.62 us
    pallas_call x2, Pallas kernels, shards(): pl.pallas_call(_far_kernel, out_shape=jax.ShapeDtypeStruct((half, 2 * row...  5.03 us
    ppermute x3, starting transfers between devices, _exchange(): lax.ppermute(x, axis_name, [(i, i ^ p) for i in range(count)])  3.49 us
    pallas_call x1, Pallas kernels, shards(): pl.pallas_call(_excite_kernel, out_shape=(jax.ShapeDtypeStruct((2, source...  2.75 us
    reduce_precision x1, other arithmetic, shards(): lax.reduce_precision(jnp.sin(theta), exponent_bits=8, mantissa_bits=7)  1.78 us
    unnamed x12, local copies, waits for them, and re-layouts  1.41 us
  transfers between devices with their start and end apart: 11, of which 5 were waited for; matrix products, arithmetic and copies ran while one was open for 11% of the time, Pallas kernels for 15%

profile of v15, /device:TPU:0, one launch (start us, length us, event | category | flops | bytes accessed | tf_op | source)
XLA Modules:
  0.0 53.3 jit_solution(8470553525696147660)
XLA Ops:
  0.0 0.0 copy-start
  0.0 1.0 %reshape_squeeze.6 = bf16[32,8,256]{2,1,0:T(8,128)(2,1)S(1)} reshape(bf16[1,32,8,2,128]{4,3,2,1,0:T(2,128)(2,1)} %param.13) | data formatting | bytes 262144 | tf_op jit(solution)/shard_map/reshape;squeeze | solution.py:234
  1.0 5.1 %collective-permute-start.2 = (bf16[32,8,256]{2,1,0:T(8,128)(2,1)S(1)}, bf16[32,8,256]{2,1,0:T(8,128)(2,1)S(1)}, u32[]{:S(2)}, u32[]{:S(2)}) collective-permute-start(bf16[32,8,256]{2,1,0:T(8,128)(2,1)S(1)} %reshape_squeeze.6), channel_id=1, source_target_pairs={{0,24},{4,28},{8,16},{12,20},{16,8},{20,12},{24,0},{28,4},{1,25},{... | collective-permute-start | bytes 393224 | tf_op jit(solution)/shard_map/ppermute | solution.py:148
  6.1 0.0 collective-permute-start.1
  6.1 0.6 %collective-permute-start = (bf16[32,8,256]{2,1,0:T(8,128)(2,1)S(1)}, bf16[32,8,256]{2,1,0:T(8,128)(2,1)S(1)}, u32[]{:S(2)}, u32[]{:S(2)}) collective-permute-start(bf16[32,8,256]{2,1,0:T(8,128)(2,1)S(1)} %reshape_squeeze.6), channel_id=1, source_target_pairs={{0,16},{4,20},{8,24},{12,28},{16,0},{20,4},{24,8},{28,12},{1,17},{... | collective-permute-start | bytes 393224 | tf_op jit(solution)/shard_map/ppermute | solution.py:148
  6.8 0.1 constant_dynamic-slice_fusion
  6.9 0.5 fusion.3
  7.4 0.1 broadcast_in_dim.16
  7.5 0.1 broadcast_in_dim.17
  7.6 0.7 %convert_bitcast_fusion = f32[32,2]{0,1:T(2,128)S(1)} fusion(s32[1,32,2]{1,2,0:T(2,128)} %param.15), kind=kLoop, calls=%fused_computation.9 | loop fusion | flops 64 | bytes 512 | tf_op jit(solution)/shard_map/convert_element_type | solution.py:228
  8.2 0.8 %reshape_squeeze.7 = bf16[2,32,4,32]{3,2,1,0:T(4,128)(2,1)S(1)} reshape(bf16[1,1,2,32,128]{4,3,2,1,0:T(8,128)(2,1)} %param.22) | data formatting | bytes 32768 | tf_op jit(solution)/shard_map/reshape;squeeze | solution.py:238
  9.1 0.6 %gather_fusion = bf16[4,2,32,32]{3,2,1,0:T(8,128)(2,1)S(1)} fusion(bf16[2,32,4,32]{3,1,2,0:T(8,128)(2,1)S(1)} %copy.17, s32[1024]{0:T(1024)S(1)} %pad_clamp_fusion), kind=kCustom, calls=%fused_computation | custom fusion | bytes 32784 | tf_op jit(solution)/shard_map/jit(_take)/gather | solution.py:240
  9.6 0.1 copy.18
  9.7 0.1 gather.7
  9.8 0.6 %broadcast_select_fusion.cp_ref = bf16[2,32,128]{2,1,0:T(8,128)(2,1)} fusion(bf16[2,32,128]{2,1,0:T(8,128)(2,1)S(1)} %gather.7, pred[128]{0:T(512)(128)(4,1)S(1)} %broadcast_in_dim.17), kind=kLoop, calls=%fused_computation.5 | loop fusion | flops 8192 | bytes 32896 | tf_op jit(solution)/shard_map/jit(_take)/select_n | solution.py:240
  10.4 1.8 %reduce-precision_bitcast_fusion = (f32[32]{0:T(128)}, f32[32,1]{0,1:T(1,128)S(1)}) fusion(f32[32,2]{0,1:T(2,128)S(1)} %convert_bitcast_fusion, f32[]{:T(128)} %bitcast.5, f32[]{:T(128)} %bitcast.3), kind=kLoop, calls=%fused_computation.10 | loop fusion | flops 128 | bytes 520 | tf_op jit(solution)/shard_map/reduce_precision | solution.py:232
  12.2 0.6 %reduce-precision_bitcast_fusion.1.cos_ref = f32[32]{0:T(128)} fusion(f32[32,1]{0,1:T(1,128)S(1)} %get-tuple-element.18), kind=kLoop, calls=%fused_computation.11 | loop fusion | flops 32 | bytes 256 | tf_op jit(solution)/shard_map/reduce_precision | solution.py:231
  12.8 0.0 collective-permute-done.2
  12.8 0.8 %collective-permute-done.1 = bf16[32,8,256]{2,1,0:T(8,128)(2,1)S(1)} collective-permute-done((bf16[32,8,256]{2,1,0:T(8,128)(2,1)S(1)}, bf16[32,8,256]{2,1,0:T(8,128)(2,1)S(1)}, u32[]{:S(2)}, u32[]{:S(2)}) %collective-permute-start.1) | collective-permute-done | bytes 131104 | tf_op jit(solution)/shard_map/ppermute | solution.py:148
  13.5 3.7 %collective-permute-done = bf16[32,8,256]{2,1,0:T(8,128)(2,1)S(1)} collective-permute-done((bf16[32,8,256]{2,1,0:T(8,128)(2,1)S(1)}, bf16[32,8,256]{2,1,0:T(8,128)(2,1)S(1)}, u32[]{:S(2)}, u32[]{:S(2)}) %collective-permute-start) | collective-permute-done | bytes 131104 | tf_op jit(solution)/shard_map/ppermute | solution.py:148
  17.2 0.1 pad_maximum_fusion.ga_ref
  17.3 0.1 collective-permute-start.3
  18.0 1.2 %collective-permute-done.3.gb_ref = bf16[32,32,256]{2,1,0:T(8,128)(2,1)S(1)} collective-permute-done((bf16[32,32,256]{2,1,0:T(8,128)(2,1)S(1)}, bf16[32,32,256]{2,1,0:T(8,128)(2,1)S(1)}, u32[]{:S(2)}, u32[]{:S(2)}) %collective-permute-start.3) | collective-permute-done | bytes 524320 | tf_op jit(solution)/shard_map/ppermute | solution.py:148
  19.3 0.8 %copy-done.2 = bf16[32,32,256]{2,1,0:T(8,128)(2,1)} copy-done((bf16[32,32,256]{2,1,0:T(8,128)(2,1)}, bf16[32,32,256]{2,1,0:T(8,128)(2,1)S(1)}, u32[]{:S(2)}) %copy-start.2) | copy-done | bytes 524312
  20.0 2.7 %shard_map.127 = (bf16[2,64,2048]{2,1,0:T(8,128)(2,1)}, bf16[2,64,32]{2,1,0:T(8,128)(2,1)}) custom-call(s32[32]{0:T(128)} %bitcast.33, f32[32]{0:T(128)} %reduce-precision_bitcast_fusion.1.cos_ref, f32[32]{0:T(128)} %get-tuple-element.12.sin_ref, s32[1]{0:T(128)} %bitcast.20.rank_ref, bf16[32,32,256]{2,1,0:T(8,128)(2,1)} %copy-done.1, ...), custom_call_target="tpu_custom_call" | custom-call | tf_op jit(solution)/shard_map/pallas_call | solution.py:244
  22.8 2.4 %collective-permute-start.6 = (bf16[2,64,32]{2,1,0:T(8,128)(2,1)}, bf16[2,64,32]{2,1,0:T(8,128)(2,1)S(1)}, u32[]{:S(2)}, u32[]{:S(2)}) collective-permute-start(bf16[2,64,32]{2,1,0:T(8,128)(2,1)} %get-tuple-element.16), channel_id=1, source_target_pairs={{0,3},{1,2},{2,1},{3,0},{4,7},{5,6},{6,5},{7,4},{8,11},{9,10},{10,... | collective-permute-start | bytes 24584 | tf_op jit(solution)/shard_map/ppermute | solution.py:200
  25.2 0.5 collective-permute-start.5
  25.7 0.5 %collective-permute-start.4 = (bf16[2,64,32]{2,1,0:T(8,128)(2,1)}, bf16[2,64,32]{2,1,0:T(8,128)(2,1)S(1)}, u32[]{:S(2)}, u32[]{:S(2)}) collective-permute-start(bf16[2,64,32]{2,1,0:T(8,128)(2,1)} %get-tuple-element.16), channel_id=1, source_target_pairs={{0,1},{1,0},{2,3},{3,2},{4,5},{5,4},{6,7},{7,6},{8,9},{9,8},{10,11... | collective-permute-start | bytes 24584 | tf_op jit(solution)/shard_map/ppermute | solution.py:200
  26.3 5.6 %shard_map.128.near_ref = f32[64,4096]{1,0:T(8,128)} custom-call(bf16[2,64,2048]{2,1,0:T(8,128)(2,1)} %get-tuple-element.14.e_ref, bf16[2,2048,256]{2,1,0:T(8,128)(2,1)} %bitcast.23, bf16[3,2,32,2048]{3,2,1,0:T(8,128)(2,1)} %bitcast.26, bf16[3,2,32,2048]{3,2,1,0:T(8,128)(2,1)} %bitcast.27), custom_call_target="tpu_custom_call" | custom-call | tf_op jit(solution)/shard_map/pallas_call | solution.py:259
  31.9 0.0 collective-permute-done.6.refs_2_
  31.9 0.0 collective-permute-done.5.refs_1_
  31.9 0.0 collective-permute-done.4.refs_0_
  31.9 0.0 copy-start.5
  32.0 0.6 %copy-done.3 = bf16[2,64,32]{2,1,0:T(8,128)(2,1)} copy-done((bf16[2,64,32]{2,1,0:T(8,128)(2,1)}, bf16[2,64,32]{2,1,0:T(8,128)(2,1)S(1)}, u32[]{:S(2)}) %copy-start.3) | copy-done | bytes 8216
  32.5 0.0 copy-done.4
  32.5 0.0 copy-done.5
  32.6 2.5 %shard_map.130 = f32[32,4096]{1,0:T(8,128)} custom-call(f32[2]{0:T(128)} %bitcast.31, s32[1]{0:T(128)} %bitcast.22.rank_ref, f32[64,4096]{1,0:T(8,128)} %shard_map.128.near_ref, bf16[2,32,2048]{2,1,0:T(8,128)(2,1)} %bitcast.24, bf16[2,32,128]{2,1,0:T(8,128)(2,1)} %broadcast_select_fusion.cp_ref, bf16[2,64,32]{2,1,0:T(8,128)(2,1)} %copy-done.5, ...), custom_call_target="tpu_custom_call" | custom-call | tf_op jit(solution)/shard_map/pallas_call | solution.py:270
  35.1 0.0 collective-permute-start.7
  35.1 2.5 %shard_map.129 = f32[32,4096]{1,0:T(8,128)} custom-call(f32[2]{0:T(128)} %bitcast.32, s32[1]{0:T(128)} %bitcast.21.rank_ref, f32[64,4096]{1,0:T(8,128)} %shard_map.128.near_ref, bf16[2,32,2048]{2,1,0:T(8,128)(2,1)} %bitcast.25, bf16[2,32,128]{2,1,0:T(8,128)(2,1)} %broadcast_select_fusion.cp_ref, bf16[2,64,32]{2,1,0:T(8,128)(2,1)} %copy-done.5, ...), custom_call_target="tpu_custom_call" | custom-call | tf_op jit(solution)/shard_map/pallas_call | solution.py:270
  37.6 0.0 collective-permute-done.7
  37.6 1.1 %add.26 = f32[32,4096]{1,0:T(8,128)S(1)} add(f32[32,4096]{1,0:T(8,128)} %shard_map.129, f32[32,4096]{1,0:T(8,128)S(1)} %collective-permute-done.7) | non-fusion elementwise | flops 131072 | bytes 1572864 | tf_op jit(solution)/shard_map/add | solution.py:173
  38.8 0.9 %collective-permute-start.8 = (f32[8,4096]{1,0:T(8,128)S(1)}, f32[8,4096]{1,0:T(8,128)S(1)}, u32[]{:S(2)}, u32[]{:S(2)}) collective-permute-start(f32[8,4096]{1,0:T(8,128)S(1)} %get-tuple-element.19), channel_id=1, source_target_pairs={{0,16},{4,20},{8,24},{12,28},{16,0},{20,4},{24,8},{28,12},{1,17},{... | collective-permute-start | bytes 393224 | tf_op jit(solution)/shard_map/ppermute | solution.py:148
  39.6 1.7 %collective-permute-start.10 = (f32[8,4096]{1,0:T(8,128)S(1)}, f32[8,4096]{1,0:T(8,128)S(1)}, u32[]{:S(2)}, u32[]{:S(2)}) collective-permute-start(f32[8,4096]{1,0:T(8,128)S(1)} %get-tuple-element.20), channel_id=1, source_target_pairs={{0,24},{4,28},{8,16},{12,20},{16,8},{20,12},{24,0},{28,4},{1,25},{... | collective-permute-start | bytes 393224 | tf_op jit(solution)/shard_map/ppermute | solution.py:148
  41.4 0.9 %collective-permute-start.9 = (f32[8,4096]{1,0:T(8,128)S(1)}, f32[8,4096]{1,0:T(8,128)S(1)}, u32[]{:S(2)}, u32[]{:S(2)}) collective-permute-start(f32[8,4096]{1,0:T(8,128)S(1)} %get-tuple-element.21), channel_id=1, source_target_pairs={{0,8},{4,12},{8,0},{12,4},{16,24},{20,28},{24,16},{28,20},{1,9},{5... | collective-permute-start | bytes 393224 | tf_op jit(solution)/shard_map/ppermute | solution.py:148
  42.3 8.9 %collective-permute-done.8 = f32[8,4096]{1,0:T(8,128)S(1)} collective-permute-done((f32[8,4096]{1,0:T(8,128)S(1)}, f32[8,4096]{1,0:T(8,128)S(1)}, u32[]{:S(2)}, u32[]{:S(2)}) %collective-permute-start.8) | collective-permute-done | bytes 131104 | tf_op jit(solution)/shard_map/ppermute | solution.py:148
  51.2 0.0 collective-permute-done.10
  51.2 1.3 %collective-permute-done.9 = f32[8,4096]{1,0:T(8,128)S(1)} collective-permute-done((f32[8,4096]{1,0:T(8,128)S(1)}, f32[8,4096]{1,0:T(8,128)S(1)}, u32[]{:S(2)}, u32[]{:S(2)}) %collective-permute-start.9) | collective-permute-done | bytes 131104 | tf_op jit(solution)/shard_map/ppermute | solution.py:148
  52.5 0.8 %copy.19 = f32[8,2,2048]{2,1,0:T(2,128)} copy(f32[8,2,2048]{2,0,1:T(8,128)S(1)} %bitcast.28) | data formatting | bytes 262144 | tf_op jit(solution)/shard_map/reshape | solution.py:185
  (12 shorter events, 0.1 us)
Async XLA Ops:
  0.0 6.8 %copy-start = (f32[8,2]{0,1:T(2,128)S(1)}, f32[8,2]{0,1:T(2,128)}, u32[]{:S(2)}) copy-start(f32[8,2]{0,1:T(2,128)} %param.16) | copy-start | bytes 196
  1.0 11.8 %collective-permute-start.2 = (bf16[32,8,256]{2,1,0:T(8,128)(2,1)S(1)}, bf16[32,8,256]{2,1,0:T(8,128)(2,1)S(1)}, u32[]{:S(2)}, u32[]{:S(2)}) collective-permute-start(bf16[32,8,256]{2,1,0:T(8,128)(2,1)S(1)} %reshape_squeeze.6), channel_id=1, source_target_pairs={{0,24},{4,28},{8,16},{12,20},{16,8},{20,12},{24,0},{28,4},{1,25},{... | collective-permute-start | bytes 393224 | tf_op jit(solution)/shard_map/ppermute | solution.py:148
  6.1 7.4 %collective-permute-start.1 = (bf16[32,8,256]{2,1,0:T(8,128)(2,1)S(1)}, bf16[32,8,256]{2,1,0:T(8,128)(2,1)S(1)}, u32[]{:S(2)}, u32[]{:S(2)}) collective-permute-start(bf16[32,8,256]{2,1,0:T(8,128)(2,1)S(1)} %reshape_squeeze.6), channel_id=1, source_target_pairs={{0,8},{4,12},{8,0},{12,4},{16,24},{20,28},{24,16},{28,20},{1,9},{5... | collective-permute-start | bytes 393224 | tf_op jit(solution)/shard_map/ppermute | solution.py:148
  6.1 11.1 %collective-permute-start = (bf16[32,8,256]{2,1,0:T(8,128)(2,1)S(1)}, bf16[32,8,256]{2,1,0:T(8,128)(2,1)S(1)}, u32[]{:S(2)}, u32[]{:S(2)}) collective-permute-start(bf16[32,8,256]{2,1,0:T(8,128)(2,1)S(1)} %reshape_squeeze.6), channel_id=1, source_target_pairs={{0,16},{4,20},{8,24},{12,28},{16,0},{20,4},{24,8},{28,12},{1,17},{... | collective-permute-start | bytes 393224 | tf_op jit(solution)/shard_map/ppermute | solution.py:148
  17.3 2.0 %copy-start.1 = (bf16[32,32,256]{2,1,0:T(8,128)(2,1)}, bf16[32,32,256]{2,1,0:T(8,128)(2,1)S(1)}, u32[]{:S(2)}) copy-start(bf16[32,32,256]{2,1,0:T(8,128)(2,1)S(1)} %pad_maximum_fusion.ga_ref) | copy-start | bytes 1572868
  17.3 2.0 %collective-permute-start.3 = (bf16[32,32,256]{2,1,0:T(8,128)(2,1)S(1)}, bf16[32,32,256]{2,1,0:T(8,128)(2,1)S(1)}, u32[]{:S(2)}, u32[]{:S(2)}) collective-permute-start(bf16[32,32,256]{2,1,0:T(8,128)(2,1)S(1)} %pad_maximum_fusion.ga_ref), channel_id=1, source_target_pairs={{0,4},{4,0},{8,12},{12,8},{16,20},{20,16},{24,28},{28,24},{1,5},{5... | collective-permute-start | bytes 1572872 | tf_op jit(solution)/shard_map/ppermute | solution.py:148
  19.2 0.8 %copy-start.2 = (bf16[32,32,256]{2,1,0:T(8,128)(2,1)}, bf16[32,32,256]{2,1,0:T(8,128)(2,1)S(1)}, u32[]{:S(2)}) copy-start(bf16[32,32,256]{2,1,0:T(8,128)(2,1)S(1)} %collective-permute-done.3.gb_ref) | copy-start | bytes 1572868
  22.8 9.1 %collective-permute-start.6 = (bf16[2,64,32]{2,1,0:T(8,128)(2,1)}, bf16[2,64,32]{2,1,0:T(8,128)(2,1)S(1)}, u32[]{:S(2)}, u32[]{:S(2)}) collective-permute-start(bf16[2,64,32]{2,1,0:T(8,128)(2,1)} %get-tuple-element.16), channel_id=1, source_target_pairs={{0,3},{1,2},{2,1},{3,0},{4,7},{5,6},{6,5},{7,4},{8,11},{9,10},{10,... | collective-permute-start | bytes 24584 | tf_op jit(solution)/shard_map/ppermute | solution.py:200
  25.2 6.7 %collective-permute-start.5 = (bf16[2,64,32]{2,1,0:T(8,128)(2,1)}, bf16[2,64,32]{2,1,0:T(8,128)(2,1)S(1)}, u32[]{:S(2)}, u32[]{:S(2)}) collective-permute-start(bf16[2,64,32]{2,1,0:T(8,128)(2,1)} %get-tuple-element.16), channel_id=1, source_target_pairs={{0,2},{1,3},{2,0},{3,1},{4,6},{5,7},{6,4},{7,5},{8,10},{9,11},{10,... | collective-permute-start | bytes 24584 | tf_op jit(solution)/shard_map/ppermute | solution.py:200
  25.7 6.2 %collective-permute-start.4 = (bf16[2,64,32]{2,1,0:T(8,128)(2,1)}, bf16[2,64,32]{2,1,0:T(8,128)(2,1)S(1)}, u32[]{:S(2)}, u32[]{:S(2)}) collective-permute-start(bf16[2,64,32]{2,1,0:T(8,128)(2,1)} %get-tuple-element.16), channel_id=1, source_target_pairs={{0,1},{1,0},{2,3},{3,2},{4,5},{5,4},{6,7},{7,6},{8,9},{9,8},{10,11... | collective-permute-start | bytes 24584 | tf_op jit(solution)/shard_map/ppermute | solution.py:200
  31.9 0.6 %copy-start.3 = (bf16[2,64,32]{2,1,0:T(8,128)(2,1)}, bf16[2,64,32]{2,1,0:T(8,128)(2,1)S(1)}, u32[]{:S(2)}) copy-start(bf16[2,64,32]{2,1,0:T(8,128)(2,1)S(1)} %collective-permute-done.6.refs_2_) | copy-start | bytes 24580
  31.9 0.6 %copy-start.4 = (bf16[2,64,32]{2,1,0:T(8,128)(2,1)}, bf16[2,64,32]{2,1,0:T(8,128)(2,1)S(1)}, u32[]{:S(2)}) copy-start(bf16[2,64,32]{2,1,0:T(8,128)(2,1)S(1)} %collective-permute-done.5.refs_1_) | copy-start | bytes 24580
  31.9 0.6 %copy-start.5 = (bf16[2,64,32]{2,1,0:T(8,128)(2,1)}, bf16[2,64,32]{2,1,0:T(8,128)(2,1)S(1)}, u32[]{:S(2)}) copy-start(bf16[2,64,32]{2,1,0:T(8,128)(2,1)S(1)} %collective-permute-done.4.refs_0_) | copy-start | bytes 24580
  35.1 2.5 %collective-permute-start.7 = (f32[32,4096]{1,0:T(8,128)}, f32[32,4096]{1,0:T(8,128)S(1)}, u32[]{:S(2)}, u32[]{:S(2)}) collective-permute-start(f32[32,4096]{1,0:T(8,128)} %shard_map.130), channel_id=1, source_target_pairs={{0,4},{4,0},{8,12},{12,8},{16,20},{20,16},{24,28},{28,24},{1,5},{5... | collective-permute-start | bytes 1572872 | tf_op jit(solution)/shard_map/ppermute | solution.py:148
  38.8 12.4 %collective-permute-start.8 = (f32[8,4096]{1,0:T(8,128)S(1)}, f32[8,4096]{1,0:T(8,128)S(1)}, u32[]{:S(2)}, u32[]{:S(2)}) collective-permute-start(f32[8,4096]{1,0:T(8,128)S(1)} %get-tuple-element.19), channel_id=1, source_target_pairs={{0,16},{4,20},{8,24},{12,28},{16,0},{20,4},{24,8},{28,12},{1,17},{... | collective-permute-start | bytes 393224 | tf_op jit(solution)/shard_map/ppermute | solution.py:148
  39.6 11.5 %collective-permute-start.10 = (f32[8,4096]{1,0:T(8,128)S(1)}, f32[8,4096]{1,0:T(8,128)S(1)}, u32[]{:S(2)}, u32[]{:S(2)}) collective-permute-start(f32[8,4096]{1,0:T(8,128)S(1)} %get-tuple-element.20), channel_id=1, source_target_pairs={{0,24},{4,28},{8,16},{12,20},{16,8},{20,12},{24,0},{28,4},{1,25},{... | collective-permute-start | bytes 393224 | tf_op jit(solution)/shard_map/ppermute | solution.py:148
  41.4 11.1 %collective-permute-start.9 = (f32[8,4096]{1,0:T(8,128)S(1)}, f32[8,4096]{1,0:T(8,128)S(1)}, u32[]{:S(2)}, u32[]{:S(2)}) collective-permute-start(f32[8,4096]{1,0:T(8,128)S(1)} %get-tuple-element.21), channel_id=1, source_target_pairs={{0,8},{4,12},{8,0},{12,4},{16,24},{20,28},{24,16},{28,20},{1,9},{5... | collective-permute-start | bytes 393224 | tf_op jit(solution)/shard_map/ppermute | solution.py:148

commit v16 on v15

--- a/solution.py
+++ b/solution.py
@@ -55,7 +55,7 @@
     bp_ref[1] = (t_im[:sources] + t_re[sources:]).astype(jnp.bfloat16)
 
 
-def _near_kernel(e_ref, leaf_ref, lr_ref, ll_ref, out_ref, pj_ref):
+def _near_kernel(e_ref, leaf_ref, lr_ref, ll_ref, out_ref, pj_ref, pc_ref):
     _, source_count, row_count = e_ref.shape
     levels = lr_ref.shape[0]
     sc = source_count
@@ -82,14 +82,16 @@
         t_im = _nt(ab, leaf_ref[1, cols, :])
         f_re = t_re[:sc] - t_im[sc:]
         f_im = t_im[:sc] + t_re[sc:]
+        rank = pj_ref.shape[3]
         for j in range(levels):
             node = row_count // 2 ** (j + 1)
             g = (l * LEAF) // node
-            pp = pj_ref[first_group[j] + (g ^ 1)].reshape(2 * sc, pj_ref.shape[3])
-            v_re = _nn(pp, ll_ref[j, 0, :, cols])
-            v_im = _nn(pp, ll_ref[j, 1, :, cols])
-            f_re = f_re + (v_re[:sc] - v_im[sc:])
-            f_im = f_im + (v_im[:sc] + v_re[sc:])
+            pc_ref[:, j * rank:(j + 1) * rank] = pj_ref[first_group[j] + (g ^ 1)].reshape(2 * sc, rank)
+        pp = pc_ref[...]
+        v_re = _nn(pp, ll_ref[:, 0, :, cols].reshape(levels * rank, LEAF))
+        v_im = _nn(pp, ll_ref[:, 1, :, cols].reshape(levels * rank, LEAF))
+        f_re = f_re + (v_re[:sc] - v_im[sc:])
+        f_im = f_im + (v_im[:sc] + v_re[sc:])
         out_ref[:, cols] = f_re
         out_ref[:, row_count + l * LEAF:row_count + (l + 1) * LEAF] = f_im
 
@@ -261,7 +263,10 @@
         out_shape=jax.ShapeDtypeStruct((source_count, 2 * row_count), jnp.float32),
         in_specs=[_VMEM] * 4,
         out_specs=_VMEM,
-        scratch_shapes=[pltpu.VMEM((2 ** (levels + 1) - 2, 2, source_count, rank_width), jnp.bfloat16)],
+        scratch_shapes=[
+            pltpu.VMEM((2 ** (levels + 1) - 2, 2, source_count, rank_width), jnp.bfloat16),
+            pltpu.VMEM((2 * source_count, levels * rank_width), jnp.bfloat16),
+        ],
     )(excitation, leaf_inverse[0], level_right[0], level_left[0])
 
     half = source_count // 2

time: 53.7 us -> 53.2 us (level)
  no operation moved by 1% of the time
where the time goes in v16:
time: 53.2 us; the launch traced here: 52.9 us
  waiting for transfers between devices  15.9 us (30%)
  Pallas kernels  13 us (24%)
  starting transfers between devices  12.9 us (24%)
  local copies, waits for them, and re-layouts  5.49 us (10%)
  other arithmetic  4.86 us (9%)
  between operations  0.81 us (2%)
    ppermute x8, waiting for transfers between devices, _permute(): return lax.ppermute(x, axis_name, [(i, i ^ offset) for i in range(count)])  15.9 us
    ppermute x8, starting transfers between devices, _permute(): return lax.ppermute(x, axis_name, [(i, i ^ offset) for i in range(count)])  9.38 us
    pallas_call x1, Pallas kernels, shards(): pl.pallas_call(_near_kernel, out_shape=jax.ShapeDtypeStruct((source_count...  5.18 us
    pallas_call x2, Pallas kernels, shards(): pl.pallas_call(_far_kernel, out_shape=jax.ShapeDtypeStruct((half, 2 * row...  5.02 us
    ppermute x3, starting transfers between devices, _exchange(): lax.ppermute(x, axis_name, [(i, i ^ p) for i in range(count)])  3.49 us
    pallas_call x1, Pallas kernels, shards(): pl.pallas_call(_excite_kernel, out_shape=(jax.ShapeDtypeStruct((2, source...  2.75 us
    reduce_precision x1, other arithmetic, shards(): lax.reduce_precision(jnp.sin(theta), exponent_bits=8, mantissa_bits=7)  1.78 us
    unnamed x12, local copies, waits for them, and re-layouts  1.41 us
  transfers between devices with their start and end apart: 11, of which 5 were waited for; matrix products, arithmetic and copies ran while one was open for 11% of the time, Pallas kernels for 15%

profile of v16, /device:TPU:0, one launch (start us, length us, event | category | flops | bytes accessed | tf_op | source)
XLA Modules:
  0.0 52.9 jit_solution(146843053554119421)
XLA Ops:
  0.0 0.0 copy-start
  0.0 1.0 %reshape_squeeze.6 = bf16[32,8,256]{2,1,0:T(8,128)(2,1)S(1)} reshape(bf16[1,32,8,2,128]{4,3,2,1,0:T(2,128)(2,1)} %param.13) | data formatting | bytes 262144 | tf_op jit(solution)/shard_map/reshape;squeeze | solution.py:236
  1.0 5.1 %collective-permute-start.2 = (bf16[32,8,256]{2,1,0:T(8,128)(2,1)S(1)}, bf16[32,8,256]{2,1,0:T(8,128)(2,1)S(1)}, u32[]{:S(2)}, u32[]{:S(2)}) collective-permute-start(bf16[32,8,256]{2,1,0:T(8,128)(2,1)S(1)} %reshape_squeeze.6), channel_id=1, source_target_pairs={{0,24},{4,28},{8,16},{12,20},{16,8},{20,12},{24,0},{28,4},{1,25},{... | collective-permute-start | bytes 393224 | tf_op jit(solution)/shard_map/ppermute | solution.py:150
  6.1 0.0 collective-permute-start.1
  6.1 0.6 %collective-permute-start = (bf16[32,8,256]{2,1,0:T(8,128)(2,1)S(1)}, bf16[32,8,256]{2,1,0:T(8,128)(2,1)S(1)}, u32[]{:S(2)}, u32[]{:S(2)}) collective-permute-start(bf16[32,8,256]{2,1,0:T(8,128)(2,1)S(1)} %reshape_squeeze.6), channel_id=1, source_target_pairs={{0,16},{4,20},{8,24},{12,28},{16,0},{20,4},{24,8},{28,12},{1,17},{... | collective-permute-start | bytes 393224 | tf_op jit(solution)/shard_map/ppermute | solution.py:150
  6.8 0.1 constant_dynamic-slice_fusion
  6.9 0.5 fusion.3
  7.4 0.1 broadcast_in_dim.16
  7.5 0.1 broadcast_in_dim.17
  7.6 0.7 %convert_bitcast_fusion = f32[32,2]{0,1:T(2,128)S(1)} fusion(s32[1,32,2]{1,2,0:T(2,128)} %param.15), kind=kLoop, calls=%fused_computation.9 | loop fusion | flops 64 | bytes 512 | tf_op jit(solution)/shard_map/convert_element_type | solution.py:230
  8.2 0.8 %reshape_squeeze.7 = bf16[2,32,4,32]{3,2,1,0:T(4,128)(2,1)S(1)} reshape(bf16[1,1,2,32,128]{4,3,2,1,0:T(8,128)(2,1)} %param.22) | data formatting | bytes 32768 | tf_op jit(solution)/shard_map/reshape;squeeze | solution.py:240
  9.1 0.6 %gather_fusion = bf16[4,2,32,32]{3,2,1,0:T(8,128)(2,1)S(1)} fusion(bf16[2,32,4,32]{3,1,2,0:T(8,128)(2,1)S(1)} %copy.17, s32[1024]{0:T(1024)S(1)} %pad_clamp_fusion), kind=kCustom, calls=%fused_computation | custom fusion | bytes 32784 | tf_op jit(solution)/shard_map/jit(_take)/gather | solution.py:242
  9.6 0.1 copy.18
  9.7 0.1 gather.7
  9.8 0.6 %broadcast_select_fusion.cp_ref = bf16[2,32,128]{2,1,0:T(8,128)(2,1)} fusion(bf16[2,32,128]{2,1,0:T(8,128)(2,1)S(1)} %gather.7, pred[128]{0:T(512)(128)(4,1)S(1)} %broadcast_in_dim.17), kind=kLoop, calls=%fused_computation.5 | loop fusion | flops 8192 | bytes 32896 | tf_op jit(solution)/shard_map/jit(_take)/select_n | solution.py:242
  10.4 1.8 %reduce-precision_bitcast_fusion = (f32[32]{0:T(128)}, f32[32,1]{0,1:T(1,128)S(1)}) fusion(f32[32,2]{0,1:T(2,128)S(1)} %convert_bitcast_fusion, f32[]{:T(128)} %bitcast.5, f32[]{:T(128)} %bitcast.3), kind=kLoop, calls=%fused_computation.10 | loop fusion | flops 128 | bytes 520 | tf_op jit(solution)/shard_map/reduce_precision | solution.py:234
  12.2 0.6 %reduce-precision_bitcast_fusion.1.cos_ref = f32[32]{0:T(128)} fusion(f32[32,1]{0,1:T(1,128)S(1)} %get-tuple-element.18), kind=kLoop, calls=%fused_computation.11 | loop fusion | flops 32 | bytes 256 | tf_op jit(solution)/shard_map/reduce_precision | solution.py:233
  12.8 0.0 collective-permute-done.2
  12.8 0.8 %collective-permute-done.1 = bf16[32,8,256]{2,1,0:T(8,128)(2,1)S(1)} collective-permute-done((bf16[32,8,256]{2,1,0:T(8,128)(2,1)S(1)}, bf16[32,8,256]{2,1,0:T(8,128)(2,1)S(1)}, u32[]{:S(2)}, u32[]{:S(2)}) %collective-permute-start.1) | collective-permute-done | bytes 131104 | tf_op jit(solution)/shard_map/ppermute | solution.py:150
  13.5 3.7 %collective-permute-done = bf16[32,8,256]{2,1,0:T(8,128)(2,1)S(1)} collective-permute-done((bf16[32,8,256]{2,1,0:T(8,128)(2,1)S(1)}, bf16[32,8,256]{2,1,0:T(8,128)(2,1)S(1)}, u32[]{:S(2)}, u32[]{:S(2)}) %collective-permute-start) | collective-permute-done | bytes 131104 | tf_op jit(solution)/shard_map/ppermute | solution.py:150
  17.2 0.1 pad_maximum_fusion.ga_ref
  17.3 0.1 collective-permute-start.3
  18.0 1.2 %collective-permute-done.3.gb_ref = bf16[32,32,256]{2,1,0:T(8,128)(2,1)S(1)} collective-permute-done((bf16[32,32,256]{2,1,0:T(8,128)(2,1)S(1)}, bf16[32,32,256]{2,1,0:T(8,128)(2,1)S(1)}, u32[]{:S(2)}, u32[]{:S(2)}) %collective-permute-start.3) | collective-permute-done | bytes 524320 | tf_op jit(solution)/shard_map/ppermute | solution.py:150
  19.3 0.8 %copy-done.2 = bf16[32,32,256]{2,1,0:T(8,128)(2,1)} copy-done((bf16[32,32,256]{2,1,0:T(8,128)(2,1)}, bf16[32,32,256]{2,1,0:T(8,128)(2,1)S(1)}, u32[]{:S(2)}) %copy-start.2) | copy-done | bytes 524312
  20.0 2.7 %shard_map.127 = (bf16[2,64,2048]{2,1,0:T(8,128)(2,1)}, bf16[2,64,32]{2,1,0:T(8,128)(2,1)}) custom-call(s32[32]{0:T(128)} %bitcast.33, f32[32]{0:T(128)} %reduce-precision_bitcast_fusion.1.cos_ref, f32[32]{0:T(128)} %get-tuple-element.12.sin_ref, s32[1]{0:T(128)} %bitcast.20.rank_ref, bf16[32,32,256]{2,1,0:T(8,128)(2,1)} %copy-done.1, ...), custom_call_target="tpu_custom_call" | custom-call | tf_op jit(solution)/shard_map/pallas_call | solution.py:246
  22.8 2.4 %collective-permute-start.6 = (bf16[2,64,32]{2,1,0:T(8,128)(2,1)}, bf16[2,64,32]{2,1,0:T(8,128)(2,1)S(1)}, u32[]{:S(2)}, u32[]{:S(2)}) collective-permute-start(bf16[2,64,32]{2,1,0:T(8,128)(2,1)} %get-tuple-element.16), channel_id=1, source_target_pairs={{0,3},{1,2},{2,1},{3,0},{4,7},{5,6},{6,5},{7,4},{8,11},{9,10},{10,... | collective-permute-start | bytes 24584 | tf_op jit(solution)/shard_map/ppermute | solution.py:202
  25.2 0.5 collective-permute-start.5
  25.8 0.5 %collective-permute-start.4 = (bf16[2,64,32]{2,1,0:T(8,128)(2,1)}, bf16[2,64,32]{2,1,0:T(8,128)(2,1)S(1)}, u32[]{:S(2)}, u32[]{:S(2)}) collective-permute-start(bf16[2,64,32]{2,1,0:T(8,128)(2,1)} %get-tuple-element.16), channel_id=1, source_target_pairs={{0,1},{1,0},{2,3},{3,2},{4,5},{5,4},{6,7},{7,6},{8,9},{9,8},{10,11... | collective-permute-start | bytes 24584 | tf_op jit(solution)/shard_map/ppermute | solution.py:202
  26.3 5.2 %shard_map.128.near_ref = f32[64,4096]{1,0:T(8,128)} custom-call(bf16[2,64,2048]{2,1,0:T(8,128)(2,1)} %get-tuple-element.14.e_ref, bf16[2,2048,256]{2,1,0:T(8,128)(2,1)} %bitcast.23, bf16[3,2,32,2048]{3,2,1,0:T(8,128)(2,1)} %bitcast.26, bf16[3,2,32,2048]{3,2,1,0:T(8,128)(2,1)} %bitcast.27), custom_call_target="tpu_custom_call" | custom-call | tf_op jit(solution)/shard_map/pallas_call | solution.py:261
  31.5 0.0 collective-permute-done.6.refs_2_
  31.5 0.0 collective-permute-done.5.refs_1_
  31.5 0.0 collective-permute-done.4.refs_0_
  31.5 0.0 copy-start.5
  31.5 0.6 %copy-done.3 = bf16[2,64,32]{2,1,0:T(8,128)(2,1)} copy-done((bf16[2,64,32]{2,1,0:T(8,128)(2,1)}, bf16[2,64,32]{2,1,0:T(8,128)(2,1)S(1)}, u32[]{:S(2)}) %copy-start.3) | copy-done | bytes 8216
  32.1 0.0 copy-done.4
  32.1 0.0 copy-done.5
  32.1 2.5 %shard_map.130 = f32[32,4096]{1,0:T(8,128)} custom-call(f32[2]{0:T(128)} %bitcast.31, s32[1]{0:T(128)} %bitcast.22.rank_ref, f32[64,4096]{1,0:T(8,128)} %shard_map.128.near_ref, bf16[2,32,2048]{2,1,0:T(8,128)(2,1)} %bitcast.24, bf16[2,32,128]{2,1,0:T(8,128)(2,1)} %broadcast_select_fusion.cp_ref, bf16[2,64,32]{2,1,0:T(8,128)(2,1)} %copy-done.5, ...), custom_call_target="tpu_custom_call" | custom-call | tf_op jit(solution)/shard_map/pallas_call | solution.py:275
  34.6 0.0 collective-permute-start.7
  34.6 2.5 %shard_map.129 = f32[32,4096]{1,0:T(8,128)} custom-call(f32[2]{0:T(128)} %bitcast.32, s32[1]{0:T(128)} %bitcast.21.rank_ref, f32[64,4096]{1,0:T(8,128)} %shard_map.128.near_ref, bf16[2,32,2048]{2,1,0:T(8,128)(2,1)} %bitcast.25, bf16[2,32,128]{2,1,0:T(8,128)(2,1)} %broadcast_select_fusion.cp_ref, bf16[2,64,32]{2,1,0:T(8,128)(2,1)} %copy-done.5, ...), custom_call_target="tpu_custom_call" | custom-call | tf_op jit(solution)/shard_map/pallas_call | solution.py:275
  37.1 0.0 collective-permute-done.7
  37.1 1.1 %add.26 = f32[32,4096]{1,0:T(8,128)S(1)} add(f32[32,4096]{1,0:T(8,128)} %shard_map.129, f32[32,4096]{1,0:T(8,128)S(1)} %collective-permute-done.7) | non-fusion elementwise | flops 131072 | bytes 1572864 | tf_op jit(solution)/shard_map/add | solution.py:175
  38.3 0.9 %collective-permute-start.8 = (f32[8,4096]{1,0:T(8,128)S(1)}, f32[8,4096]{1,0:T(8,128)S(1)}, u32[]{:S(2)}, u32[]{:S(2)}) collective-permute-start(f32[8,4096]{1,0:T(8,128)S(1)} %get-tuple-element.19), channel_id=1, source_target_pairs={{0,16},{4,20},{8,24},{12,28},{16,0},{20,4},{24,8},{28,12},{1,17},{... | collective-permute-start | bytes 393224 | tf_op jit(solution)/shard_map/ppermute | solution.py:150
  39.2 1.7 %collective-permute-start.10 = (f32[8,4096]{1,0:T(8,128)S(1)}, f32[8,4096]{1,0:T(8,128)S(1)}, u32[]{:S(2)}, u32[]{:S(2)}) collective-permute-start(f32[8,4096]{1,0:T(8,128)S(1)} %get-tuple-element.20), channel_id=1, source_target_pairs={{0,24},{4,28},{8,16},{12,20},{16,8},{20,12},{24,0},{28,4},{1,25},{... | collective-permute-start | bytes 393224 | tf_op jit(solution)/shard_map/ppermute | solution.py:150
  40.9 0.9 %collective-permute-start.9 = (f32[8,4096]{1,0:T(8,128)S(1)}, f32[8,4096]{1,0:T(8,128)S(1)}, u32[]{:S(2)}, u32[]{:S(2)}) collective-permute-start(f32[8,4096]{1,0:T(8,128)S(1)} %get-tuple-element.21), channel_id=1, source_target_pairs={{0,8},{4,12},{8,0},{12,4},{16,24},{20,28},{24,16},{28,20},{1,9},{5... | collective-permute-start | bytes 393224 | tf_op jit(solution)/shard_map/ppermute | solution.py:150
  41.9 8.9 %collective-permute-done.8 = f32[8,4096]{1,0:T(8,128)S(1)} collective-permute-done((f32[8,4096]{1,0:T(8,128)S(1)}, f32[8,4096]{1,0:T(8,128)S(1)}, u32[]{:S(2)}, u32[]{:S(2)}) %collective-permute-start.8) | collective-permute-done | bytes 131104 | tf_op jit(solution)/shard_map/ppermute | solution.py:150
  50.7 0.0 collective-permute-done.10
  50.7 1.3 %collective-permute-done.9 = f32[8,4096]{1,0:T(8,128)S(1)} collective-permute-done((f32[8,4096]{1,0:T(8,128)S(1)}, f32[8,4096]{1,0:T(8,128)S(1)}, u32[]{:S(2)}, u32[]{:S(2)}) %collective-permute-start.9) | collective-permute-done | bytes 131104 | tf_op jit(solution)/shard_map/ppermute | solution.py:150
  52.1 0.8 %copy.19 = f32[8,2,2048]{2,1,0:T(2,128)} copy(f32[8,2,2048]{2,0,1:T(8,128)S(1)} %bitcast.28) | data formatting | bytes 262144 | tf_op jit(solution)/shard_map/reshape | solution.py:187
  (12 shorter events, 0.1 us)
Async XLA Ops:
  0.0 6.8 %copy-start = (f32[8,2]{0,1:T(2,128)S(1)}, f32[8,2]{0,1:T(2,128)}, u32[]{:S(2)}) copy-start(f32[8,2]{0,1:T(2,128)} %param.16) | copy-start | bytes 196
  1.0 11.8 %collective-permute-start.2 = (bf16[32,8,256]{2,1,0:T(8,128)(2,1)S(1)}, bf16[32,8,256]{2,1,0:T(8,128)(2,1)S(1)}, u32[]{:S(2)}, u32[]{:S(2)}) collective-permute-start(bf16[32,8,256]{2,1,0:T(8,128)(2,1)S(1)} %reshape_squeeze.6), channel_id=1, source_target_pairs={{0,24},{4,28},{8,16},{12,20},{16,8},{20,12},{24,0},{28,4},{1,25},{... | collective-permute-start | bytes 393224 | tf_op jit(solution)/shard_map/ppermute | solution.py:150
  6.1 7.4 %collective-permute-start.1 = (bf16[32,8,256]{2,1,0:T(8,128)(2,1)S(1)}, bf16[32,8,256]{2,1,0:T(8,128)(2,1)S(1)}, u32[]{:S(2)}, u32[]{:S(2)}) collective-permute-start(bf16[32,8,256]{2,1,0:T(8,128)(2,1)S(1)} %reshape_squeeze.6), channel_id=1, source_target_pairs={{0,8},{4,12},{8,0},{12,4},{16,24},{20,28},{24,16},{28,20},{1,9},{5... | collective-permute-start | bytes 393224 | tf_op jit(solution)/shard_map/ppermute | solution.py:150
  6.1 11.1 %collective-permute-start = (bf16[32,8,256]{2,1,0:T(8,128)(2,1)S(1)}, bf16[32,8,256]{2,1,0:T(8,128)(2,1)S(1)}, u32[]{:S(2)}, u32[]{:S(2)}) collective-permute-start(bf16[32,8,256]{2,1,0:T(8,128)(2,1)S(1)} %reshape_squeeze.6), channel_id=1, source_target_pairs={{0,16},{4,20},{8,24},{12,28},{16,0},{20,4},{24,8},{28,12},{1,17},{... | collective-permute-start | bytes 393224 | tf_op jit(solution)/shard_map/ppermute | solution.py:150
  17.3 2.0 %copy-start.1 = (bf16[32,32,256]{2,1,0:T(8,128)(2,1)}, bf16[32,32,256]{2,1,0:T(8,128)(2,1)S(1)}, u32[]{:S(2)}) copy-start(bf16[32,32,256]{2,1,0:T(8,128)(2,1)S(1)} %pad_maximum_fusion.ga_ref) | copy-start | bytes 1572868
  17.3 2.0 %collective-permute-start.3 = (bf16[32,32,256]{2,1,0:T(8,128)(2,1)S(1)}, bf16[32,32,256]{2,1,0:T(8,128)(2,1)S(1)}, u32[]{:S(2)}, u32[]{:S(2)}) collective-permute-start(bf16[32,32,256]{2,1,0:T(8,128)(2,1)S(1)} %pad_maximum_fusion.ga_ref), channel_id=1, source_target_pairs={{0,4},{4,0},{8,12},{12,8},{16,20},{20,16},{24,28},{28,24},{1,5},{5... | collective-permute-start | bytes 1572872 | tf_op jit(solution)/shard_map/ppermute | solution.py:150
  19.2 0.8 %copy-start.2 = (bf16[32,32,256]{2,1,0:T(8,128)(2,1)}, bf16[32,32,256]{2,1,0:T(8,128)(2,1)S(1)}, u32[]{:S(2)}) copy-start(bf16[32,32,256]{2,1,0:T(8,128)(2,1)S(1)} %collective-permute-done.3.gb_ref) | copy-start | bytes 1572868
  22.8 8.7 %collective-permute-start.6 = (bf16[2,64,32]{2,1,0:T(8,128)(2,1)}, bf16[2,64,32]{2,1,0:T(8,128)(2,1)S(1)}, u32[]{:S(2)}, u32[]{:S(2)}) collective-permute-start(bf16[2,64,32]{2,1,0:T(8,128)(2,1)} %get-tuple-element.16), channel_id=1, source_target_pairs={{0,3},{1,2},{2,1},{3,0},{4,7},{5,6},{6,5},{7,4},{8,11},{9,10},{10,... | collective-permute-start | bytes 24584 | tf_op jit(solution)/shard_map/ppermute | solution.py:202
  25.2 6.2 %collective-permute-start.5 = (bf16[2,64,32]{2,1,0:T(8,128)(2,1)}, bf16[2,64,32]{2,1,0:T(8,128)(2,1)S(1)}, u32[]{:S(2)}, u32[]{:S(2)}) collective-permute-start(bf16[2,64,32]{2,1,0:T(8,128)(2,1)} %get-tuple-element.16), channel_id=1, source_target_pairs={{0,2},{1,3},{2,0},{3,1},{4,6},{5,7},{6,4},{7,5},{8,10},{9,11},{10,... | collective-permute-start | bytes 24584 | tf_op jit(solution)/shard_map/ppermute | solution.py:202
  25.8 5.7 %collective-permute-start.4 = (bf16[2,64,32]{2,1,0:T(8,128)(2,1)}, bf16[2,64,32]{2,1,0:T(8,128)(2,1)S(1)}, u32[]{:S(2)}, u32[]{:S(2)}) collective-permute-start(bf16[2,64,32]{2,1,0:T(8,128)(2,1)} %get-tuple-element.16), channel_id=1, source_target_pairs={{0,1},{1,0},{2,3},{3,2},{4,5},{5,4},{6,7},{7,6},{8,9},{9,8},{10,11... | collective-permute-start | bytes 24584 | tf_op jit(solution)/shard_map/ppermute | solution.py:202
  31.5 0.6 %copy-start.3 = (bf16[2,64,32]{2,1,0:T(8,128)(2,1)}, bf16[2,64,32]{2,1,0:T(8,128)(2,1)S(1)}, u32[]{:S(2)}) copy-start(bf16[2,64,32]{2,1,0:T(8,128)(2,1)S(1)} %collective-permute-done.6.refs_2_) | copy-start | bytes 24580
  31.5 0.6 %copy-start.4 = (bf16[2,64,32]{2,1,0:T(8,128)(2,1)}, bf16[2,64,32]{2,1,0:T(8,128)(2,1)S(1)}, u32[]{:S(2)}) copy-start(bf16[2,64,32]{2,1,0:T(8,128)(2,1)S(1)} %collective-permute-done.5.refs_1_) | copy-start | bytes 24580
  31.5 0.6 %copy-start.5 = (bf16[2,64,32]{2,1,0:T(8,128)(2,1)}, bf16[2,64,32]{2,1,0:T(8,128)(2,1)S(1)}, u32[]{:S(2)}) copy-start(bf16[2,64,32]{2,1,0:T(8,128)(2,1)S(1)} %collective-permute-done.4.refs_0_) | copy-start | bytes 24580
  34.6 2.5 %collective-permute-start.7 = (f32[32,4096]{1,0:T(8,128)}, f32[32,4096]{1,0:T(8,128)S(1)}, u32[]{:S(2)}, u32[]{:S(2)}) collective-permute-start(f32[32,4096]{1,0:T(8,128)} %shard_map.130), channel_id=1, source_target_pairs={{0,4},{4,0},{8,12},{12,8},{16,20},{20,16},{24,28},{28,24},{1,5},{5... | collective-permute-start | bytes 1572872 | tf_op jit(solution)/shard_map/ppermute | solution.py:150
  38.3 12.4 %collective-permute-start.8 = (f32[8,4096]{1,0:T(8,128)S(1)}, f32[8,4096]{1,0:T(8,128)S(1)}, u32[]{:S(2)}, u32[]{:S(2)}) collective-permute-start(f32[8,4096]{1,0:T(8,128)S(1)} %get-tuple-element.19), channel_id=1, source_target_pairs={{0,16},{4,20},{8,24},{12,28},{16,0},{20,4},{24,8},{28,12},{1,17},{... | collective-permute-start | bytes 393224 | tf_op jit(solution)/shard_map/ppermute | solution.py:150
  39.2 11.5 %collective-permute-start.10 = (f32[8,4096]{1,0:T(8,128)S(1)}, f32[8,4096]{1,0:T(8,128)S(1)}, u32[]{:S(2)}, u32[]{:S(2)}) collective-permute-start(f32[8,4096]{1,0:T(8,128)S(1)} %get-tuple-element.20), channel_id=1, source_target_pairs={{0,24},{4,28},{8,16},{12,20},{16,8},{20,12},{24,0},{28,4},{1,25},{... | collective-permute-start | bytes 393224 | tf_op jit(solution)/shard_map/ppermute | solution.py:150
  40.9 11.1 %collective-permute-start.9 = (f32[8,4096]{1,0:T(8,128)S(1)}, f32[8,4096]{1,0:T(8,128)S(1)}, u32[]{:S(2)}, u32[]{:S(2)}) collective-permute-start(f32[8,4096]{1,0:T(8,128)S(1)} %get-tuple-element.21), channel_id=1, source_target_pairs={{0,8},{4,12},{8,0},{12,4},{16,24},{20,28},{24,16},{28,20},{1,9},{5... | collective-permute-start | bytes 393224 | tf_op jit(solution)/shard_map/ppermute | solution.py:150

commit v17 on v16

--- a/solution.py
+++ b/solution.py
@@ -97,34 +97,33 @@
 
 
 def _far_kernel(qw_ref, rank_ref, near_ref, bl_ref, cp_ref, *refs):
-    part_refs = refs[:-2]
-    out_ref, cu_ref = refs[-2:]
+    part_refs = refs[:-3]
+    out_ref, cu_ref, bc_ref = refs[-3:]
     source_count = near_ref.shape[0]
     row_count = bl_ref.shape[2]
     rank_width = bl_ref.shape[1]
     blocks = len(part_refs) + 1
     coupling_rank = part_refs[0].shape[2]
 
-    c_re = jnp.zeros((source_count, rank_width), jnp.float32)
-    c_im = jnp.zeros((source_count, rank_width), jnp.float32)
     sc = source_count
     for u in range(1, blocks):
-        bb = part_refs[u - 1][...].reshape(2 * sc, coupling_rank)
-        t_re = _nt(bb, cp_ref[0, :, u * coupling_rank:(u + 1) * coupling_rank])
-        t_im = _nt(bb, cp_ref[1, :, u * coupling_rank:(u + 1) * coupling_rank])
-        c_re = c_re + (t_re[:sc] - t_im[sc:])
-        c_im = c_im + (t_im[:sc] + t_re[sc:])
+        bc_ref[:, (u - 1) * coupling_rank:u * coupling_rank] = part_refs[u - 1][...].reshape(2 * sc, coupling_rank)
+    bb = bc_ref[...]
+    t_re = _nt(bb, cp_ref[0, :, coupling_rank:])
+    t_im = _nt(bb, cp_ref[1, :, coupling_rank:])
+    c_re = t_re[:sc] - t_im[sc:]
+    c_im = t_im[:sc] + t_re[sc:]
     cu_ref[0] = c_re.astype(jnp.bfloat16)
     cu_ref[1] = c_im.astype(jnp.bfloat16)
     coupled = cu_ref[...].reshape(2 * sc, rank_width)
 
     w_re = qw_ref[0]
     w_im = qw_ref[1]
+    keep = _rank_mask(rank_ref, (rank_width, LEAF))
+    zero = jnp.zeros((rank_width, LEAF), jnp.bfloat16)
     for l in range(row_count // LEAF):
         cols = slice(l * LEAF, (l + 1) * LEAF)
         imag_cols = slice(row_count + l * LEAF, row_count + (l + 1) * LEAF)
-        keep = _rank_mask(rank_ref, (rank_width, LEAF))
-        zero = jnp.zeros((rank_width, LEAF), jnp.bfloat16)
         q_re = jnp.where(keep, bl_ref[0, :, cols], zero)
         q_im = jnp.where(keep, bl_ref[1, :, cols], zero)
         v_re = _nn(coupled, q_re)
@@ -284,7 +283,10 @@
                 pl.BlockSpec(coupling.shape, lambda i: (0, 0, 0)),
             ] + [pl.BlockSpec((2, half, rank_width), lambda i, h=h: (0, h, 0))] * (row_blocks - 1),
             out_specs=pl.BlockSpec((half, 2 * row_count), lambda i: (0, 0)),
-            scratch_shapes=[pltpu.VMEM((2, half, rank_width), jnp.bfloat16)],
+            scratch_shapes=[
+                pltpu.VMEM((2, half, rank_width), jnp.bfloat16),
+                pltpu.VMEM((2 * half, (row_blocks - 1) * rank_width), jnp.bfloat16),
+            ],
         )(quad_weight[0], rank, near, block_left[0], coupling, *all_projected))
     return _reduce_scatter(halves[1], halves[0], "ang", (local_sources, 2, row_count))
 

time: 53.2 us -> 53.1 us (level)
  transfers between devices with their start and end apart: 11 -> 11, of which waited for: 5 -> 5; matrix products, arithmetic and copies ran while one was open for 11% -> 11% of each run, Pallas kernels for 15% -> 14%
where the time goes in v17:
time: 53.1 us; the launch traced here: 52.7 us
  waiting for transfers between devices  15.9 us (30%)
  starting transfers between devices  12.9 us (24%)
  Pallas kernels  12.8 us (24%)
  local copies, waits for them, and re-layouts  5.49 us (10%)
  other arithmetic  4.86 us (9%)
  between operations  0.81 us (2%)
    ppermute x8, waiting for transfers between devices, _permute(): return lax.ppermute(x, axis_name, [(i, i ^ offset) for i in range(count)])  15.9 us
    ppermute x8, starting transfers between devices, _permute(): return lax.ppermute(x, axis_name, [(i, i ^ offset) for i in range(count)])  9.38 us
    pallas_call x1, Pallas kernels, shards(): pl.pallas_call(_near_kernel, out_shape=jax.ShapeDtypeStruct((source_count...  5.18 us
    pallas_call x2, Pallas kernels, shards(): pl.pallas_call(_far_kernel, out_shape=jax.ShapeDtypeStruct((half, 2 * row...  4.92 us
    ppermute x3, starting transfers between devices, _exchange(): lax.ppermute(x, axis_name, [(i, i ^ p) for i in range(count)])  3.49 us
    pallas_call x1, Pallas kernels, shards(): pl.pallas_call(_excite_kernel, out_shape=(jax.ShapeDtypeStruct((2, source...  2.75 us
    reduce_precision x1, other arithmetic, shards(): lax.reduce_precision(jnp.sin(theta), exponent_bits=8, mantissa_bits=7)  1.78 us
    unnamed x12, local copies, waits for them, and re-layouts  1.41 us
  transfers between devices with their start and end apart: 11, of which 5 were waited for; matrix products, arithmetic and copies ran while one was open for 11% of the time, Pallas kernels for 14%

profile of v17, /device:TPU:0, one launch (start us, length us, event | category | flops | bytes accessed | tf_op | source)
XLA Modules:
  0.0 52.7 jit_solution(9246039068923509496)
XLA Ops:
  0.0 0.0 copy-start
  0.0 1.0 %reshape_squeeze.6 = bf16[32,8,256]{2,1,0:T(8,128)(2,1)S(1)} reshape(bf16[1,32,8,2,128]{4,3,2,1,0:T(2,128)(2,1)} %param.13) | data formatting | bytes 262144 | tf_op jit(solution)/shard_map/reshape;squeeze | solution.py:235
  1.0 5.1 %collective-permute-start.2 = (bf16[32,8,256]{2,1,0:T(8,128)(2,1)S(1)}, bf16[32,8,256]{2,1,0:T(8,128)(2,1)S(1)}, u32[]{:S(2)}, u32[]{:S(2)}) collective-permute-start(bf16[32,8,256]{2,1,0:T(8,128)(2,1)S(1)} %reshape_squeeze.6), channel_id=1, source_target_pairs={{0,24},{4,28},{8,16},{12,20},{16,8},{20,12},{24,0},{28,4},{1,25},{... | collective-permute-start | bytes 393224 | tf_op jit(solution)/shard_map/ppermute | solution.py:149
  6.1 0.0 collective-permute-start.1
  6.1 0.6 %collective-permute-start = (bf16[32,8,256]{2,1,0:T(8,128)(2,1)S(1)}, bf16[32,8,256]{2,1,0:T(8,128)(2,1)S(1)}, u32[]{:S(2)}, u32[]{:S(2)}) collective-permute-start(bf16[32,8,256]{2,1,0:T(8,128)(2,1)S(1)} %reshape_squeeze.6), channel_id=1, source_target_pairs={{0,16},{4,20},{8,24},{12,28},{16,0},{20,4},{24,8},{28,12},{1,17},{... | collective-permute-start | bytes 393224 | tf_op jit(solution)/shard_map/ppermute | solution.py:149
  6.8 0.1 constant_dynamic-slice_fusion
  6.9 0.5 fusion.3
  7.4 0.1 broadcast_in_dim.16
  7.5 0.1 broadcast_in_dim.17
  7.6 0.7 %convert_bitcast_fusion = f32[32,2]{0,1:T(2,128)S(1)} fusion(s32[1,32,2]{1,2,0:T(2,128)} %param.15), kind=kLoop, calls=%fused_computation.9 | loop fusion | flops 64 | bytes 512 | tf_op jit(solution)/shard_map/convert_element_type | solution.py:229
  8.2 0.8 %reshape_squeeze.7 = bf16[2,32,4,32]{3,2,1,0:T(4,128)(2,1)S(1)} reshape(bf16[1,1,2,32,128]{4,3,2,1,0:T(8,128)(2,1)} %param.22) | data formatting | bytes 32768 | tf_op jit(solution)/shard_map/reshape;squeeze | solution.py:239
  9.1 0.6 %gather_fusion = bf16[4,2,32,32]{3,2,1,0:T(8,128)(2,1)S(1)} fusion(bf16[2,32,4,32]{3,1,2,0:T(8,128)(2,1)S(1)} %copy.17, s32[1024]{0:T(1024)S(1)} %pad_clamp_fusion), kind=kCustom, calls=%fused_computation | custom fusion | bytes 32784 | tf_op jit(solution)/shard_map/jit(_take)/gather | solution.py:241
  9.6 0.1 copy.18
  9.7 0.1 gather.7
  9.8 0.6 %broadcast_select_fusion.cp_ref = bf16[2,32,128]{2,1,0:T(8,128)(2,1)} fusion(bf16[2,32,128]{2,1,0:T(8,128)(2,1)S(1)} %gather.7, pred[128]{0:T(512)(128)(4,1)S(1)} %broadcast_in_dim.17), kind=kLoop, calls=%fused_computation.5 | loop fusion | flops 8192 | bytes 32896 | tf_op jit(solution)/shard_map/jit(_take)/select_n | solution.py:241
  10.4 1.8 %reduce-precision_bitcast_fusion = (f32[32]{0:T(128)}, f32[32,1]{0,1:T(1,128)S(1)}) fusion(f32[32,2]{0,1:T(2,128)S(1)} %convert_bitcast_fusion, f32[]{:T(128)} %bitcast.5, f32[]{:T(128)} %bitcast.3), kind=kLoop, calls=%fused_computation.10 | loop fusion | flops 128 | bytes 520 | tf_op jit(solution)/shard_map/reduce_precision | solution.py:233
  12.2 0.6 %reduce-precision_bitcast_fusion.1.cos_ref = f32[32]{0:T(128)} fusion(f32[32,1]{0,1:T(1,128)S(1)} %get-tuple-element.18), kind=kLoop, calls=%fused_computation.11 | loop fusion | flops 32 | bytes 256 | tf_op jit(solution)/shard_map/reduce_precision | solution.py:232
  12.8 0.0 collective-permute-done.2
  12.8 0.8 %collective-permute-done.1 = bf16[32,8,256]{2,1,0:T(8,128)(2,1)S(1)} collective-permute-done((bf16[32,8,256]{2,1,0:T(8,128)(2,1)S(1)}, bf16[32,8,256]{2,1,0:T(8,128)(2,1)S(1)}, u32[]{:S(2)}, u32[]{:S(2)}) %collective-permute-start.1) | collective-permute-done | bytes 131104 | tf_op jit(solution)/shard_map/ppermute | solution.py:149
  13.5 3.7 %collective-permute-done = bf16[32,8,256]{2,1,0:T(8,128)(2,1)S(1)} collective-permute-done((bf16[32,8,256]{2,1,0:T(8,128)(2,1)S(1)}, bf16[32,8,256]{2,1,0:T(8,128)(2,1)S(1)}, u32[]{:S(2)}, u32[]{:S(2)}) %collective-permute-start) | collective-permute-done | bytes 131104 | tf_op jit(solution)/shard_map/ppermute | solution.py:149
  17.2 0.1 pad_maximum_fusion.ga_ref
  17.3 0.1 collective-permute-start.3
  18.0 1.2 %collective-permute-done.3.gb_ref = bf16[32,32,256]{2,1,0:T(8,128)(2,1)S(1)} collective-permute-done((bf16[32,32,256]{2,1,0:T(8,128)(2,1)S(1)}, bf16[32,32,256]{2,1,0:T(8,128)(2,1)S(1)}, u32[]{:S(2)}, u32[]{:S(2)}) %collective-permute-start.3) | collective-permute-done | bytes 524320 | tf_op jit(solution)/shard_map/ppermute | solution.py:149
  19.3 0.8 %copy-done.2 = bf16[32,32,256]{2,1,0:T(8,128)(2,1)} copy-done((bf16[32,32,256]{2,1,0:T(8,128)(2,1)}, bf16[32,32,256]{2,1,0:T(8,128)(2,1)S(1)}, u32[]{:S(2)}) %copy-start.2) | copy-done | bytes 524312
  20.0 2.7 %shard_map.127 = (bf16[2,64,2048]{2,1,0:T(8,128)(2,1)}, bf16[2,64,32]{2,1,0:T(8,128)(2,1)}) custom-call(s32[32]{0:T(128)} %bitcast.33, f32[32]{0:T(128)} %reduce-precision_bitcast_fusion.1.cos_ref, f32[32]{0:T(128)} %get-tuple-element.12.sin_ref, s32[1]{0:T(128)} %bitcast.20.rank_ref, bf16[32,32,256]{2,1,0:T(8,128)(2,1)} %copy-done.1, ...), custom_call_target="tpu_custom_call" | custom-call | tf_op jit(solution)/shard_map/pallas_call | solution.py:245
  22.8 2.4 %collective-permute-start.6 = (bf16[2,64,32]{2,1,0:T(8,128)(2,1)}, bf16[2,64,32]{2,1,0:T(8,128)(2,1)S(1)}, u32[]{:S(2)}, u32[]{:S(2)}) collective-permute-start(bf16[2,64,32]{2,1,0:T(8,128)(2,1)} %get-tuple-element.16), channel_id=1, source_target_pairs={{0,3},{1,2},{2,1},{3,0},{4,7},{5,6},{6,5},{7,4},{8,11},{9,10},{10,... | collective-permute-start | bytes 24584 | tf_op jit(solution)/shard_map/ppermute | solution.py:201
  25.2 0.5 collective-permute-start.5
  25.7 0.5 %collective-permute-start.4 = (bf16[2,64,32]{2,1,0:T(8,128)(2,1)}, bf16[2,64,32]{2,1,0:T(8,128)(2,1)S(1)}, u32[]{:S(2)}, u32[]{:S(2)}) collective-permute-start(bf16[2,64,32]{2,1,0:T(8,128)(2,1)} %get-tuple-element.16), channel_id=1, source_target_pairs={{0,1},{1,0},{2,3},{3,2},{4,5},{5,4},{6,7},{7,6},{8,9},{9,8},{10,11... | collective-permute-start | bytes 24584 | tf_op jit(solution)/shard_map/ppermute | solution.py:201
  26.3 5.2 %shard_map.128.near_ref = f32[64,4096]{1,0:T(8,128)} custom-call(bf16[2,64,2048]{2,1,0:T(8,128)(2,1)} %get-tuple-element.14.e_ref, bf16[2,2048,256]{2,1,0:T(8,128)(2,1)} %bitcast.23, bf16[3,2,32,2048]{3,2,1,0:T(8,128)(2,1)} %bitcast.26, bf16[3,2,32,2048]{3,2,1,0:T(8,128)(2,1)} %bitcast.27), custom_call_target="tpu_custom_call" | custom-call | tf_op jit(solution)/shard_map/pallas_call | solution.py:260
  31.5 0.0 collective-permute-done.6.refs_2_
  31.5 0.0 collective-permute-done.5.refs_1_
  31.5 0.0 collective-permute-done.4.refs_0_
  31.5 0.0 copy-start.5
  31.5 0.6 %copy-done.3 = bf16[2,64,32]{2,1,0:T(8,128)(2,1)} copy-done((bf16[2,64,32]{2,1,0:T(8,128)(2,1)}, bf16[2,64,32]{2,1,0:T(8,128)(2,1)S(1)}, u32[]{:S(2)}) %copy-start.3) | copy-done | bytes 8216
  32.1 0.0 copy-done.4
  32.1 0.0 copy-done.5
  32.1 2.5 %shard_map.130 = f32[32,4096]{1,0:T(8,128)} custom-call(f32[2]{0:T(128)} %bitcast.31, s32[1]{0:T(128)} %bitcast.22.rank_ref, f32[64,4096]{1,0:T(8,128)} %shard_map.128.near_ref, bf16[2,32,2048]{2,1,0:T(8,128)(2,1)} %bitcast.24, bf16[2,32,128]{2,1,0:T(8,128)(2,1)} %broadcast_select_fusion.cp_ref, bf16[2,64,32]{2,1,0:T(8,128)(2,1)} %copy-done.5, ...), custom_call_target="tpu_custom_call" | custom-call | tf_op jit(solution)/shard_map/pallas_call | solution.py:274
  34.6 0.0 collective-permute-start.7
  34.6 2.5 %shard_map.129 = f32[32,4096]{1,0:T(8,128)} custom-call(f32[2]{0:T(128)} %bitcast.32, s32[1]{0:T(128)} %bitcast.21.rank_ref, f32[64,4096]{1,0:T(8,128)} %shard_map.128.near_ref, bf16[2,32,2048]{2,1,0:T(8,128)(2,1)} %bitcast.25, bf16[2,32,128]{2,1,0:T(8,128)(2,1)} %broadcast_select_fusion.cp_ref, bf16[2,64,32]{2,1,0:T(8,128)(2,1)} %copy-done.5, ...), custom_call_target="tpu_custom_call" | custom-call | tf_op jit(solution)/shard_map/pallas_call | solution.py:274
  37.0 0.0 collective-permute-done.7
  37.0 1.1 %add.26 = f32[32,4096]{1,0:T(8,128)S(1)} add(f32[32,4096]{1,0:T(8,128)} %shard_map.129, f32[32,4096]{1,0:T(8,128)S(1)} %collective-permute-done.7) | non-fusion elementwise | flops 131072 | bytes 1572864 | tf_op jit(solution)/shard_map/add | solution.py:174
  38.2 0.9 %collective-permute-start.8 = (f32[8,4096]{1,0:T(8,128)S(1)}, f32[8,4096]{1,0:T(8,128)S(1)}, u32[]{:S(2)}, u32[]{:S(2)}) collective-permute-start(f32[8,4096]{1,0:T(8,128)S(1)} %get-tuple-element.19), channel_id=1, source_target_pairs={{0,16},{4,20},{8,24},{12,28},{16,0},{20,4},{24,8},{28,12},{1,17},{... | collective-permute-start | bytes 393224 | tf_op jit(solution)/shard_map/ppermute | solution.py:149
  39.1 1.7 %collective-permute-start.10 = (f32[8,4096]{1,0:T(8,128)S(1)}, f32[8,4096]{1,0:T(8,128)S(1)}, u32[]{:S(2)}, u32[]{:S(2)}) collective-permute-start(f32[8,4096]{1,0:T(8,128)S(1)} %get-tuple-element.20), channel_id=1, source_target_pairs={{0,24},{4,28},{8,16},{12,20},{16,8},{20,12},{24,0},{28,4},{1,25},{... | collective-permute-start | bytes 393224 | tf_op jit(solution)/shard_map/ppermute | solution.py:149
  40.8 1.0 %collective-permute-start.9 = (f32[8,4096]{1,0:T(8,128)S(1)}, f32[8,4096]{1,0:T(8,128)S(1)}, u32[]{:S(2)}, u32[]{:S(2)}) collective-permute-start(f32[8,4096]{1,0:T(8,128)S(1)} %get-tuple-element.21), channel_id=1, source_target_pairs={{0,8},{4,12},{8,0},{12,4},{16,24},{20,28},{24,16},{28,20},{1,9},{5... | collective-permute-start | bytes 393224 | tf_op jit(solution)/shard_map/ppermute | solution.py:149
  41.8 8.9 %collective-permute-done.8 = f32[8,4096]{1,0:T(8,128)S(1)} collective-permute-done((f32[8,4096]{1,0:T(8,128)S(1)}, f32[8,4096]{1,0:T(8,128)S(1)}, u32[]{:S(2)}, u32[]{:S(2)}) %collective-permute-start.8) | collective-permute-done | bytes 131104 | tf_op jit(solution)/shard_map/ppermute | solution.py:149
  50.6 0.0 collective-permute-done.10
  50.6 1.3 %collective-permute-done.9 = f32[8,4096]{1,0:T(8,128)S(1)} collective-permute-done((f32[8,4096]{1,0:T(8,128)S(1)}, f32[8,4096]{1,0:T(8,128)S(1)}, u32[]{:S(2)}, u32[]{:S(2)}) %collective-permute-start.9) | collective-permute-done | bytes 131104 | tf_op jit(solution)/shard_map/ppermute | solution.py:149
  52.0 0.8 %copy.19 = f32[8,2,2048]{2,1,0:T(2,128)} copy(f32[8,2,2048]{2,0,1:T(8,128)S(1)} %bitcast.28) | data formatting | bytes 262144 | tf_op jit(solution)/shard_map/reshape | solution.py:186
  (12 shorter events, 0.1 us)
Async XLA Ops:
  0.0 6.8 %copy-start = (f32[8,2]{0,1:T(2,128)S(1)}, f32[8,2]{0,1:T(2,128)}, u32[]{:S(2)}) copy-start(f32[8,2]{0,1:T(2,128)} %param.16) | copy-start | bytes 196
  1.0 11.8 %collective-permute-start.2 = (bf16[32,8,256]{2,1,0:T(8,128)(2,1)S(1)}, bf16[32,8,256]{2,1,0:T(8,128)(2,1)S(1)}, u32[]{:S(2)}, u32[]{:S(2)}) collective-permute-start(bf16[32,8,256]{2,1,0:T(8,128)(2,1)S(1)} %reshape_squeeze.6), channel_id=1, source_target_pairs={{0,24},{4,28},{8,16},{12,20},{16,8},{20,12},{24,0},{28,4},{1,25},{... | collective-permute-start | bytes 393224 | tf_op jit(solution)/shard_map/ppermute | solution.py:149
  6.1 7.4 %collective-permute-start.1 = (bf16[32,8,256]{2,1,0:T(8,128)(2,1)S(1)}, bf16[32,8,256]{2,1,0:T(8,128)(2,1)S(1)}, u32[]{:S(2)}, u32[]{:S(2)}) collective-permute-start(bf16[32,8,256]{2,1,0:T(8,128)(2,1)S(1)} %reshape_squeeze.6), channel_id=1, source_target_pairs={{0,8},{4,12},{8,0},{12,4},{16,24},{20,28},{24,16},{28,20},{1,9},{5... | collective-permute-start | bytes 393224 | tf_op jit(solution)/shard_map/ppermute | solution.py:149
  6.1 11.1 %collective-permute-start = (bf16[32,8,256]{2,1,0:T(8,128)(2,1)S(1)}, bf16[32,8,256]{2,1,0:T(8,128)(2,1)S(1)}, u32[]{:S(2)}, u32[]{:S(2)}) collective-permute-start(bf16[32,8,256]{2,1,0:T(8,128)(2,1)S(1)} %reshape_squeeze.6), channel_id=1, source_target_pairs={{0,16},{4,20},{8,24},{12,28},{16,0},{20,4},{24,8},{28,12},{1,17},{... | collective-permute-start | bytes 393224 | tf_op jit(solution)/shard_map/ppermute | solution.py:149
  17.3 2.0 %copy-start.1 = (bf16[32,32,256]{2,1,0:T(8,128)(2,1)}, bf16[32,32,256]{2,1,0:T(8,128)(2,1)S(1)}, u32[]{:S(2)}) copy-start(bf16[32,32,256]{2,1,0:T(8,128)(2,1)S(1)} %pad_maximum_fusion.ga_ref) | copy-start | bytes 1572868
  17.3 2.0 %collective-permute-start.3 = (bf16[32,32,256]{2,1,0:T(8,128)(2,1)S(1)}, bf16[32,32,256]{2,1,0:T(8,128)(2,1)S(1)}, u32[]{:S(2)}, u32[]{:S(2)}) collective-permute-start(bf16[32,32,256]{2,1,0:T(8,128)(2,1)S(1)} %pad_maximum_fusion.ga_ref), channel_id=1, source_target_pairs={{0,4},{4,0},{8,12},{12,8},{16,20},{20,16},{24,28},{28,24},{1,5},{5... | collective-permute-start | bytes 1572872 | tf_op jit(solution)/shard_map/ppermute | solution.py:149
  19.2 0.8 %copy-start.2 = (bf16[32,32,256]{2,1,0:T(8,128)(2,1)}, bf16[32,32,256]{2,1,0:T(8,128)(2,1)S(1)}, u32[]{:S(2)}) copy-start(bf16[32,32,256]{2,1,0:T(8,128)(2,1)S(1)} %collective-permute-done.3.gb_ref) | copy-start | bytes 1572868
  22.8 8.7 %collective-permute-start.6 = (bf16[2,64,32]{2,1,0:T(8,128)(2,1)}, bf16[2,64,32]{2,1,0:T(8,128)(2,1)S(1)}, u32[]{:S(2)}, u32[]{:S(2)}) collective-permute-start(bf16[2,64,32]{2,1,0:T(8,128)(2,1)} %get-tuple-element.16), channel_id=1, source_target_pairs={{0,3},{1,2},{2,1},{3,0},{4,7},{5,6},{6,5},{7,4},{8,11},{9,10},{10,... | collective-permute-start | bytes 24584 | tf_op jit(solution)/shard_map/ppermute | solution.py:201
  25.2 6.2 %collective-permute-start.5 = (bf16[2,64,32]{2,1,0:T(8,128)(2,1)}, bf16[2,64,32]{2,1,0:T(8,128)(2,1)S(1)}, u32[]{:S(2)}, u32[]{:S(2)}) collective-permute-start(bf16[2,64,32]{2,1,0:T(8,128)(2,1)} %get-tuple-element.16), channel_id=1, source_target_pairs={{0,2},{1,3},{2,0},{3,1},{4,6},{5,7},{6,4},{7,5},{8,10},{9,11},{10,... | collective-permute-start | bytes 24584 | tf_op jit(solution)/shard_map/ppermute | solution.py:201
  25.7 5.7 %collective-permute-start.4 = (bf16[2,64,32]{2,1,0:T(8,128)(2,1)}, bf16[2,64,32]{2,1,0:T(8,128)(2,1)S(1)}, u32[]{:S(2)}, u32[]{:S(2)}) collective-permute-start(bf16[2,64,32]{2,1,0:T(8,128)(2,1)} %get-tuple-element.16), channel_id=1, source_target_pairs={{0,1},{1,0},{2,3},{3,2},{4,5},{5,4},{6,7},{7,6},{8,9},{9,8},{10,11... | collective-permute-start | bytes 24584 | tf_op jit(solution)/shard_map/ppermute | solution.py:201
  31.5 0.6 %copy-start.3 = (bf16[2,64,32]{2,1,0:T(8,128)(2,1)}, bf16[2,64,32]{2,1,0:T(8,128)(2,1)S(1)}, u32[]{:S(2)}) copy-start(bf16[2,64,32]{2,1,0:T(8,128)(2,1)S(1)} %collective-permute-done.6.refs_2_) | copy-start | bytes 24580
  31.5 0.6 %copy-start.4 = (bf16[2,64,32]{2,1,0:T(8,128)(2,1)}, bf16[2,64,32]{2,1,0:T(8,128)(2,1)S(1)}, u32[]{:S(2)}) copy-start(bf16[2,64,32]{2,1,0:T(8,128)(2,1)S(1)} %collective-permute-done.5.refs_1_) | copy-start | bytes 24580
  31.5 0.6 %copy-start.5 = (bf16[2,64,32]{2,1,0:T(8,128)(2,1)}, bf16[2,64,32]{2,1,0:T(8,128)(2,1)S(1)}, u32[]{:S(2)}) copy-start(bf16[2,64,32]{2,1,0:T(8,128)(2,1)S(1)} %collective-permute-done.4.refs_0_) | copy-start | bytes 24580
  34.6 2.5 %collective-permute-start.7 = (f32[32,4096]{1,0:T(8,128)}, f32[32,4096]{1,0:T(8,128)S(1)}, u32[]{:S(2)}, u32[]{:S(2)}) collective-permute-start(f32[32,4096]{1,0:T(8,128)} %shard_map.130), channel_id=1, source_target_pairs={{0,4},{4,0},{8,12},{12,8},{16,20},{20,16},{24,28},{28,24},{1,5},{5... | collective-permute-start | bytes 1572872 | tf_op jit(solution)/shard_map/ppermute | solution.py:149
  38.2 12.4 %collective-permute-start.8 = (f32[8,4096]{1,0:T(8,128)S(1)}, f32[8,4096]{1,0:T(8,128)S(1)}, u32[]{:S(2)}, u32[]{:S(2)}) collective-permute-start(f32[8,4096]{1,0:T(8,128)S(1)} %get-tuple-element.19), channel_id=1, source_target_pairs={{0,16},{4,20},{8,24},{12,28},{16,0},{20,4},{24,8},{28,12},{1,17},{... | collective-permute-start | bytes 393224 | tf_op jit(solution)/shard_map/ppermute | solution.py:149
  39.1 11.6 %collective-permute-start.10 = (f32[8,4096]{1,0:T(8,128)S(1)}, f32[8,4096]{1,0:T(8,128)S(1)}, u32[]{:S(2)}, u32[]{:S(2)}) collective-permute-start(f32[8,4096]{1,0:T(8,128)S(1)} %get-tuple-element.20), channel_id=1, source_target_pairs={{0,24},{4,28},{8,16},{12,20},{16,8},{20,12},{24,0},{28,4},{1,25},{... | collective-permute-start | bytes 393224 | tf_op jit(solution)/shard_map/ppermute | solution.py:149
  40.8 11.2 %collective-permute-start.9 = (f32[8,4096]{1,0:T(8,128)S(1)}, f32[8,4096]{1,0:T(8,128)S(1)}, u32[]{:S(2)}, u32[]{:S(2)}) collective-permute-start(f32[8,4096]{1,0:T(8,128)S(1)} %get-tuple-element.21), channel_id=1, source_target_pairs={{0,8},{4,12},{8,0},{12,4},{16,24},{20,28},{24,16},{28,20},{1,9},{5... | collective-permute-start | bytes 393224 | tf_op jit(solution)/shard_map/ppermute | solution.py:149

commit v18 on v16

--- a/solution.py
+++ b/solution.py
@@ -61,19 +61,25 @@
     sc = source_count
     stacked = e_ref[...].reshape(2 * sc, row_count)
 
+    rank = lr_ref.shape[2]
     first_group = []
     slot = 0
     for j in range(levels):
-        node = row_count // 2 ** (j + 1)
         first_group.append(slot)
-        for g in range(2 ** (j + 1)):
-            cols = slice(g * node, (g + 1) * node)
-            ab = stacked[:, cols]
-            t_re = _nt(ab, lr_ref[j, 0, :, cols])
-            t_im = _nt(ab, lr_ref[j, 1, :, cols])
-            pj_ref[slot, 0] = (t_re[:sc] - t_im[sc:]).astype(jnp.bfloat16)
-            pj_ref[slot, 1] = (t_im[:sc] + t_re[sc:]).astype(jnp.bfloat16)
-            slot += 1
+        slot += 2 ** (j + 1)
+    sums = {}
+    for l in range(row_count // LEAF):
+        cols = slice(l * LEAF, (l + 1) * LEAF)
+        ab = stacked[:, cols]
+        t_re = _nt(ab, lr_ref[:, 0, :, cols].reshape(levels * rank, LEAF))
+        t_im = _nt(ab, lr_ref[:, 1, :, cols].reshape(levels * rank, LEAF))
+        for j in range(levels):
+            key = first_group[j] + (l * LEAF) // (row_count // 2 ** (j + 1))
+            pair = (t_re[:, j * rank:(j + 1) * rank], t_im[:, j * rank:(j + 1) * rank])
+            sums[key] = pair if key not in sums else (sums[key][0] + pair[0], sums[key][1] + pair[1])
+    for key, (u_re, u_im) in sums.items():
+        pj_ref[key, 0] = (u_re[:sc] - u_im[sc:]).astype(jnp.bfloat16)
+        pj_ref[key, 1] = (u_im[:sc] + u_re[sc:]).astype(jnp.bfloat16)
 
     for l in range(row_count // LEAF):
         cols = slice(l * LEAF, (l + 1) * LEAF)
@@ -82,7 +88,6 @@
         t_im = _nt(ab, leaf_ref[1, cols, :])
         f_re = t_re[:sc] - t_im[sc:]
         f_im = t_im[:sc] + t_re[sc:]
-        rank = pj_ref.shape[3]
         for j in range(levels):
             node = row_count // 2 ** (j + 1)
             g = (l * LEAF) // node

time: 53.2 us -> 52.7 us (level)
  Pallas kernels: 13 us -> 12.4 us
  transfers between devices with their start and end apart: 11 -> 11, of which waited for: 5 -> 5; matrix products, arithmetic and copies ran while one was open for 11% -> 11% of each run, Pallas kernels for 15% -> 14%
where the time goes in v18:
time: 52.7 us; the launch traced here: 52.3 us
  waiting for transfers between devices  15.9 us (30%)
  starting transfers between devices  12.9 us (24%)
  Pallas kernels  12.4 us (24%)
  local copies, waits for them, and re-layouts  5.49 us (10%)
  other arithmetic  4.86 us (9%)
  between operations  0.81 us (2%)
    ppermute x8, waiting for transfers between devices, _permute(): return lax.ppermute(x, axis_name, [(i, i ^ offset) for i in range(count)])  15.9 us
    ppermute x8, starting transfers between devices, _permute(): return lax.ppermute(x, axis_name, [(i, i ^ offset) for i in range(count)])  9.38 us
    pallas_call x2, Pallas kernels, shards(): pl.pallas_call(_far_kernel, out_shape=jax.ShapeDtypeStruct((half, 2 * row...  5.02 us
    pallas_call x1, Pallas kernels, shards(): pl.pallas_call(_near_kernel, out_shape=jax.ShapeDtypeStruct((source_count...  4.67 us
    ppermute x3, starting transfers between devices, _exchange(): lax.ppermute(x, axis_name, [(i, i ^ p) for i in range(count)])  3.49 us
    pallas_call x1, Pallas kernels, shards(): pl.pallas_call(_excite_kernel, out_shape=(jax.ShapeDtypeStruct((2, source...  2.75 us
    reduce_precision x1, other arithmetic, shards(): lax.reduce_precision(jnp.sin(theta), exponent_bits=8, mantissa_bits=7)  1.78 us
    unnamed x12, local copies, waits for them, and re-layouts  1.41 us
  transfers between devices with their start and end apart: 11, of which 5 were waited for; matrix products, arithmetic and copies ran while one was open for 11% of the time, Pallas kernels for 14%

profile of v18, /device:TPU:0, one launch (start us, length us, event | category | flops | bytes accessed | tf_op | source)
XLA Modules:
  0.0 52.3 jit_solution(1277299014728266737)
XLA Ops:
  0.0 0.0 copy-start
  0.0 1.0 %reshape_squeeze.6 = bf16[32,8,256]{2,1,0:T(8,128)(2,1)S(1)} reshape(bf16[1,32,8,2,128]{4,3,2,1,0:T(2,128)(2,1)} %param.13) | data formatting | bytes 262144 | tf_op jit(solution)/shard_map/reshape;squeeze | solution.py:241
  1.0 5.1 %collective-permute-start.2 = (bf16[32,8,256]{2,1,0:T(8,128)(2,1)S(1)}, bf16[32,8,256]{2,1,0:T(8,128)(2,1)S(1)}, u32[]{:S(2)}, u32[]{:S(2)}) collective-permute-start(bf16[32,8,256]{2,1,0:T(8,128)(2,1)S(1)} %reshape_squeeze.6), channel_id=1, source_target_pairs={{0,24},{4,28},{8,16},{12,20},{16,8},{20,12},{24,0},{28,4},{1,25},{... | collective-permute-start | bytes 393224 | tf_op jit(solution)/shard_map/ppermute | solution.py:155
  6.1 0.0 collective-permute-start.1
  6.1 0.6 %collective-permute-start = (bf16[32,8,256]{2,1,0:T(8,128)(2,1)S(1)}, bf16[32,8,256]{2,1,0:T(8,128)(2,1)S(1)}, u32[]{:S(2)}, u32[]{:S(2)}) collective-permute-start(bf16[32,8,256]{2,1,0:T(8,128)(2,1)S(1)} %reshape_squeeze.6), channel_id=1, source_target_pairs={{0,16},{4,20},{8,24},{12,28},{16,0},{20,4},{24,8},{28,12},{1,17},{... | collective-permute-start | bytes 393224 | tf_op jit(solution)/shard_map/ppermute | solution.py:155
  6.8 0.1 constant_dynamic-slice_fusion
  6.9 0.5 %fusion.3 = (f32[1,1]{0,1:T(1,128)}, f32[1,1]{0,1:T(1,128)}) fusion(f32[1,2]{0,1:T(2,128)S(1)} %constant_dynamic-slice_fusion), kind=kLoop, calls=%fused_computation.15 | loop fusion | bytes 16 | tf_op jit(solution)/shard_map/slice | solution.py:237
  7.4 0.1 broadcast_in_dim.16
  7.5 0.1 broadcast_in_dim.17
  7.6 0.7 %convert_bitcast_fusion = f32[32,2]{0,1:T(2,128)S(1)} fusion(s32[1,32,2]{1,2,0:T(2,128)} %param.15), kind=kLoop, calls=%fused_computation.9 | loop fusion | flops 64 | bytes 512 | tf_op jit(solution)/shard_map/convert_element_type | solution.py:235
  8.2 0.8 %reshape_squeeze.7 = bf16[2,32,4,32]{3,2,1,0:T(4,128)(2,1)S(1)} reshape(bf16[1,1,2,32,128]{4,3,2,1,0:T(8,128)(2,1)} %param.22) | data formatting | bytes 32768 | tf_op jit(solution)/shard_map/reshape;squeeze | solution.py:245
  9.1 0.6 %gather_fusion = bf16[4,2,32,32]{3,2,1,0:T(8,128)(2,1)S(1)} fusion(bf16[2,32,4,32]{3,1,2,0:T(8,128)(2,1)S(1)} %copy.17, s32[1024]{0:T(1024)S(1)} %pad_clamp_fusion), kind=kCustom, calls=%fused_computation | custom fusion | bytes 32784 | tf_op jit(solution)/shard_map/jit(_take)/gather | solution.py:247
  9.6 0.1 copy.18
  9.7 0.1 gather.7
  9.8 0.6 %broadcast_select_fusion.cp_ref = bf16[2,32,128]{2,1,0:T(8,128)(2,1)} fusion(bf16[2,32,128]{2,1,0:T(8,128)(2,1)S(1)} %gather.7, pred[128]{0:T(512)(128)(4,1)S(1)} %broadcast_in_dim.17), kind=kLoop, calls=%fused_computation.5 | loop fusion | flops 8192 | bytes 32896 | tf_op jit(solution)/shard_map/jit(_take)/select_n | solution.py:247
  10.4 1.8 %reduce-precision_bitcast_fusion = (f32[32]{0:T(128)}, f32[32,1]{0,1:T(1,128)S(1)}) fusion(f32[32,2]{0,1:T(2,128)S(1)} %convert_bitcast_fusion, f32[]{:T(128)} %bitcast.5, f32[]{:T(128)} %bitcast.3), kind=kLoop, calls=%fused_computation.10 | loop fusion | flops 128 | bytes 520 | tf_op jit(solution)/shard_map/reduce_precision | solution.py:239
  12.2 0.6 %reduce-precision_bitcast_fusion.1.cos_ref = f32[32]{0:T(128)} fusion(f32[32,1]{0,1:T(1,128)S(1)} %get-tuple-element.18), kind=kLoop, calls=%fused_computation.11 | loop fusion | flops 32 | bytes 256 | tf_op jit(solution)/shard_map/reduce_precision | solution.py:238
  12.8 0.0 collective-permute-done.2
  12.8 0.8 %collective-permute-done.1 = bf16[32,8,256]{2,1,0:T(8,128)(2,1)S(1)} collective-permute-done((bf16[32,8,256]{2,1,0:T(8,128)(2,1)S(1)}, bf16[32,8,256]{2,1,0:T(8,128)(2,1)S(1)}, u32[]{:S(2)}, u32[]{:S(2)}) %collective-permute-start.1) | collective-permute-done | bytes 131104 | tf_op jit(solution)/shard_map/ppermute | solution.py:155
  13.5 3.7 %collective-permute-done = bf16[32,8,256]{2,1,0:T(8,128)(2,1)S(1)} collective-permute-done((bf16[32,8,256]{2,1,0:T(8,128)(2,1)S(1)}, bf16[32,8,256]{2,1,0:T(8,128)(2,1)S(1)}, u32[]{:S(2)}, u32[]{:S(2)}) %collective-permute-start) | collective-permute-done | bytes 131104 | tf_op jit(solution)/shard_map/ppermute | solution.py:155
  17.2 0.1 pad_maximum_fusion.ga_ref
  17.3 0.1 collective-permute-start.3
  18.0 1.2 %collective-permute-done.3.gb_ref = bf16[32,32,256]{2,1,0:T(8,128)(2,1)S(1)} collective-permute-done((bf16[32,32,256]{2,1,0:T(8,128)(2,1)S(1)}, bf16[32,32,256]{2,1,0:T(8,128)(2,1)S(1)}, u32[]{:S(2)}, u32[]{:S(2)}) %collective-permute-start.3) | collective-permute-done | bytes 524320 | tf_op jit(solution)/shard_map/ppermute | solution.py:155
  19.3 0.8 %copy-done.2 = bf16[32,32,256]{2,1,0:T(8,128)(2,1)} copy-done((bf16[32,32,256]{2,1,0:T(8,128)(2,1)}, bf16[32,32,256]{2,1,0:T(8,128)(2,1)S(1)}, u32[]{:S(2)}) %copy-start.2) | copy-done | bytes 524312
  20.0 2.7 %shard_map.127 = (bf16[2,64,2048]{2,1,0:T(8,128)(2,1)}, bf16[2,64,32]{2,1,0:T(8,128)(2,1)}) custom-call(s32[32]{0:T(128)} %bitcast.33, f32[32]{0:T(128)} %reduce-precision_bitcast_fusion.1.cos_ref, f32[32]{0:T(128)} %get-tuple-element.12.sin_ref, s32[1]{0:T(128)} %bitcast.20.rank_ref, bf16[32,32,256]{2,1,0:T(8,128)(2,1)} %copy-done.1, ...), custom_call_target="tpu_custom_call" | custom-call | tf_op jit(solution)/shard_map/pallas_call | solution.py:251
  22.8 2.4 %collective-permute-start.6 = (bf16[2,64,32]{2,1,0:T(8,128)(2,1)}, bf16[2,64,32]{2,1,0:T(8,128)(2,1)S(1)}, u32[]{:S(2)}, u32[]{:S(2)}) collective-permute-start(bf16[2,64,32]{2,1,0:T(8,128)(2,1)} %get-tuple-element.16), channel_id=1, source_target_pairs={{0,3},{1,2},{2,1},{3,0},{4,7},{5,6},{6,5},{7,4},{8,11},{9,10},{10,... | collective-permute-start | bytes 24584 | tf_op jit(solution)/shard_map/ppermute | solution.py:207
  25.2 0.5 collective-permute-start.5
  25.7 0.5 %collective-permute-start.4 = (bf16[2,64,32]{2,1,0:T(8,128)(2,1)}, bf16[2,64,32]{2,1,0:T(8,128)(2,1)S(1)}, u32[]{:S(2)}, u32[]{:S(2)}) collective-permute-start(bf16[2,64,32]{2,1,0:T(8,128)(2,1)} %get-tuple-element.16), channel_id=1, source_target_pairs={{0,1},{1,0},{2,3},{3,2},{4,5},{5,4},{6,7},{7,6},{8,9},{9,8},{10,11... | collective-permute-start | bytes 24584 | tf_op jit(solution)/shard_map/ppermute | solution.py:207
  26.3 4.7 %shard_map.128.near_ref = f32[64,4096]{1,0:T(8,128)} custom-call(bf16[2,64,2048]{2,1,0:T(8,128)(2,1)} %get-tuple-element.14.e_ref, bf16[2,2048,256]{2,1,0:T(8,128)(2,1)} %bitcast.23, bf16[3,2,32,2048]{3,2,1,0:T(8,128)(2,1)} %bitcast.26, bf16[3,2,32,2048]{3,2,1,0:T(8,128)(2,1)} %bitcast.27), custom_call_target="tpu_custom_call" | custom-call | tf_op jit(solution)/shard_map/pallas_call | solution.py:266
  31.0 0.0 collective-permute-done.6.refs_2_
  31.0 0.0 collective-permute-done.5.refs_1_
  31.0 0.0 collective-permute-done.4.refs_0_
  31.0 0.0 copy-start.5
  31.0 0.6 %copy-done.3 = bf16[2,64,32]{2,1,0:T(8,128)(2,1)} copy-done((bf16[2,64,32]{2,1,0:T(8,128)(2,1)}, bf16[2,64,32]{2,1,0:T(8,128)(2,1)S(1)}, u32[]{:S(2)}) %copy-start.3) | copy-done | bytes 8216
  31.6 0.0 copy-done.4
  31.6 0.0 copy-done.5
  31.6 2.5 %shard_map.130 = f32[32,4096]{1,0:T(8,128)} custom-call(f32[2]{0:T(128)} %bitcast.31, s32[1]{0:T(128)} %bitcast.22.rank_ref, f32[64,4096]{1,0:T(8,128)} %shard_map.128.near_ref, bf16[2,32,2048]{2,1,0:T(8,128)(2,1)} %bitcast.24, bf16[2,32,128]{2,1,0:T(8,128)(2,1)} %broadcast_select_fusion.cp_ref, bf16[2,64,32]{2,1,0:T(8,128)(2,1)} %copy-done.5, ...), custom_call_target="tpu_custom_call" | custom-call | tf_op jit(solution)/shard_map/pallas_call | solution.py:280
  34.1 0.0 collective-permute-start.7
  34.1 2.5 %shard_map.129 = f32[32,4096]{1,0:T(8,128)} custom-call(f32[2]{0:T(128)} %bitcast.32, s32[1]{0:T(128)} %bitcast.21.rank_ref, f32[64,4096]{1,0:T(8,128)} %shard_map.128.near_ref, bf16[2,32,2048]{2,1,0:T(8,128)(2,1)} %bitcast.25, bf16[2,32,128]{2,1,0:T(8,128)(2,1)} %broadcast_select_fusion.cp_ref, bf16[2,64,32]{2,1,0:T(8,128)(2,1)} %copy-done.5, ...), custom_call_target="tpu_custom_call" | custom-call | tf_op jit(solution)/shard_map/pallas_call | solution.py:280
  36.6 0.0 collective-permute-done.7
  36.6 1.1 %add.26 = f32[32,4096]{1,0:T(8,128)S(1)} add(f32[32,4096]{1,0:T(8,128)} %shard_map.129, f32[32,4096]{1,0:T(8,128)S(1)} %collective-permute-done.7) | non-fusion elementwise | flops 131072 | bytes 1572864 | tf_op jit(solution)/shard_map/add | solution.py:180
  37.8 0.9 %collective-permute-start.8 = (f32[8,4096]{1,0:T(8,128)S(1)}, f32[8,4096]{1,0:T(8,128)S(1)}, u32[]{:S(2)}, u32[]{:S(2)}) collective-permute-start(f32[8,4096]{1,0:T(8,128)S(1)} %get-tuple-element.19), channel_id=1, source_target_pairs={{0,16},{4,20},{8,24},{12,28},{16,0},{20,4},{24,8},{28,12},{1,17},{... | collective-permute-start | bytes 393224 | tf_op jit(solution)/shard_map/ppermute | solution.py:155
  38.7 1.7 %collective-permute-start.10 = (f32[8,4096]{1,0:T(8,128)S(1)}, f32[8,4096]{1,0:T(8,128)S(1)}, u32[]{:S(2)}, u32[]{:S(2)}) collective-permute-start(f32[8,4096]{1,0:T(8,128)S(1)} %get-tuple-element.20), channel_id=1, source_target_pairs={{0,24},{4,28},{8,16},{12,20},{16,8},{20,12},{24,0},{28,4},{1,25},{... | collective-permute-start | bytes 393224 | tf_op jit(solution)/shard_map/ppermute | solution.py:155
  40.4 0.9 %collective-permute-start.9 = (f32[8,4096]{1,0:T(8,128)S(1)}, f32[8,4096]{1,0:T(8,128)S(1)}, u32[]{:S(2)}, u32[]{:S(2)}) collective-permute-start(f32[8,4096]{1,0:T(8,128)S(1)} %get-tuple-element.21), channel_id=1, source_target_pairs={{0,8},{4,12},{8,0},{12,4},{16,24},{20,28},{24,16},{28,20},{1,9},{5... | collective-permute-start | bytes 393224 | tf_op jit(solution)/shard_map/ppermute | solution.py:155
  41.4 8.9 %collective-permute-done.8 = f32[8,4096]{1,0:T(8,128)S(1)} collective-permute-done((f32[8,4096]{1,0:T(8,128)S(1)}, f32[8,4096]{1,0:T(8,128)S(1)}, u32[]{:S(2)}, u32[]{:S(2)}) %collective-permute-start.8) | collective-permute-done | bytes 131104 | tf_op jit(solution)/shard_map/ppermute | solution.py:155
  50.2 0.0 collective-permute-done.10
  50.2 1.3 %collective-permute-done.9 = f32[8,4096]{1,0:T(8,128)S(1)} collective-permute-done((f32[8,4096]{1,0:T(8,128)S(1)}, f32[8,4096]{1,0:T(8,128)S(1)}, u32[]{:S(2)}, u32[]{:S(2)}) %collective-permute-start.9) | collective-permute-done | bytes 131104 | tf_op jit(solution)/shard_map/ppermute | solution.py:155
  51.6 0.8 %copy.19 = f32[8,2,2048]{2,1,0:T(2,128)} copy(f32[8,2,2048]{2,0,1:T(8,128)S(1)} %bitcast.28) | data formatting | bytes 262144 | tf_op jit(solution)/shard_map/reshape | solution.py:192
  (12 shorter events, 0.1 us)
Async XLA Ops:
  0.0 6.8 %copy-start = (f32[8,2]{0,1:T(2,128)S(1)}, f32[8,2]{0,1:T(2,128)}, u32[]{:S(2)}) copy-start(f32[8,2]{0,1:T(2,128)} %param.16) | copy-start | bytes 196
  1.0 11.8 %collective-permute-start.2 = (bf16[32,8,256]{2,1,0:T(8,128)(2,1)S(1)}, bf16[32,8,256]{2,1,0:T(8,128)(2,1)S(1)}, u32[]{:S(2)}, u32[]{:S(2)}) collective-permute-start(bf16[32,8,256]{2,1,0:T(8,128)(2,1)S(1)} %reshape_squeeze.6), channel_id=1, source_target_pairs={{0,24},{4,28},{8,16},{12,20},{16,8},{20,12},{24,0},{28,4},{1,25},{... | collective-permute-start | bytes 393224 | tf_op jit(solution)/shard_map/ppermute | solution.py:155
  6.1 7.4 %collective-permute-start.1 = (bf16[32,8,256]{2,1,0:T(8,128)(2,1)S(1)}, bf16[32,8,256]{2,1,0:T(8,128)(2,1)S(1)}, u32[]{:S(2)}, u32[]{:S(2)}) collective-permute-start(bf16[32,8,256]{2,1,0:T(8,128)(2,1)S(1)} %reshape_squeeze.6), channel_id=1, source_target_pairs={{0,8},{4,12},{8,0},{12,4},{16,24},{20,28},{24,16},{28,20},{1,9},{5... | collective-permute-start | bytes 393224 | tf_op jit(solution)/shard_map/ppermute | solution.py:155
  6.1 11.1 %collective-permute-start = (bf16[32,8,256]{2,1,0:T(8,128)(2,1)S(1)}, bf16[32,8,256]{2,1,0:T(8,128)(2,1)S(1)}, u32[]{:S(2)}, u32[]{:S(2)}) collective-permute-start(bf16[32,8,256]{2,1,0:T(8,128)(2,1)S(1)} %reshape_squeeze.6), channel_id=1, source_target_pairs={{0,16},{4,20},{8,24},{12,28},{16,0},{20,4},{24,8},{28,12},{1,17},{... | collective-permute-start | bytes 393224 | tf_op jit(solution)/shard_map/ppermute | solution.py:155
  17.3 2.0 %copy-start.1 = (bf16[32,32,256]{2,1,0:T(8,128)(2,1)}, bf16[32,32,256]{2,1,0:T(8,128)(2,1)S(1)}, u32[]{:S(2)}) copy-start(bf16[32,32,256]{2,1,0:T(8,128)(2,1)S(1)} %pad_maximum_fusion.ga_ref) | copy-start | bytes 1572868
  17.3 2.0 %collective-permute-start.3 = (bf16[32,32,256]{2,1,0:T(8,128)(2,1)S(1)}, bf16[32,32,256]{2,1,0:T(8,128)(2,1)S(1)}, u32[]{:S(2)}, u32[]{:S(2)}) collective-permute-start(bf16[32,32,256]{2,1,0:T(8,128)(2,1)S(1)} %pad_maximum_fusion.ga_ref), channel_id=1, source_target_pairs={{0,4},{4,0},{8,12},{12,8},{16,20},{20,16},{24,28},{28,24},{1,5},{5... | collective-permute-start | bytes 1572872 | tf_op jit(solution)/shard_map/ppermute | solution.py:155
  19.2 0.8 %copy-start.2 = (bf16[32,32,256]{2,1,0:T(8,128)(2,1)}, bf16[32,32,256]{2,1,0:T(8,128)(2,1)S(1)}, u32[]{:S(2)}) copy-start(bf16[32,32,256]{2,1,0:T(8,128)(2,1)S(1)} %collective-permute-done.3.gb_ref) | copy-start | bytes 1572868
  22.8 8.2 %collective-permute-start.6 = (bf16[2,64,32]{2,1,0:T(8,128)(2,1)}, bf16[2,64,32]{2,1,0:T(8,128)(2,1)S(1)}, u32[]{:S(2)}, u32[]{:S(2)}) collective-permute-start(bf16[2,64,32]{2,1,0:T(8,128)(2,1)} %get-tuple-element.16), channel_id=1, source_target_pairs={{0,3},{1,2},{2,1},{3,0},{4,7},{5,6},{6,5},{7,4},{8,11},{9,10},{10,... | collective-permute-start | bytes 24584 | tf_op jit(solution)/shard_map/ppermute | solution.py:207
  25.2 5.7 %collective-permute-start.5 = (bf16[2,64,32]{2,1,0:T(8,128)(2,1)}, bf16[2,64,32]{2,1,0:T(8,128)(2,1)S(1)}, u32[]{:S(2)}, u32[]{:S(2)}) collective-permute-start(bf16[2,64,32]{2,1,0:T(8,128)(2,1)} %get-tuple-element.16), channel_id=1, source_target_pairs={{0,2},{1,3},{2,0},{3,1},{4,6},{5,7},{6,4},{7,5},{8,10},{9,11},{10,... | collective-permute-start | bytes 24584 | tf_op jit(solution)/shard_map/ppermute | solution.py:207
  25.7 5.2 %collective-permute-start.4 = (bf16[2,64,32]{2,1,0:T(8,128)(2,1)}, bf16[2,64,32]{2,1,0:T(8,128)(2,1)S(1)}, u32[]{:S(2)}, u32[]{:S(2)}) collective-permute-start(bf16[2,64,32]{2,1,0:T(8,128)(2,1)} %get-tuple-element.16), channel_id=1, source_target_pairs={{0,1},{1,0},{2,3},{3,2},{4,5},{5,4},{6,7},{7,6},{8,9},{9,8},{10,11... | collective-permute-start | bytes 24584 | tf_op jit(solution)/shard_map/ppermute | solution.py:207
  31.0 0.6 %copy-start.3 = (bf16[2,64,32]{2,1,0:T(8,128)(2,1)}, bf16[2,64,32]{2,1,0:T(8,128)(2,1)S(1)}, u32[]{:S(2)}) copy-start(bf16[2,64,32]{2,1,0:T(8,128)(2,1)S(1)} %collective-permute-done.6.refs_2_) | copy-start | bytes 24580
  31.0 0.6 %copy-start.4 = (bf16[2,64,32]{2,1,0:T(8,128)(2,1)}, bf16[2,64,32]{2,1,0:T(8,128)(2,1)S(1)}, u32[]{:S(2)}) copy-start(bf16[2,64,32]{2,1,0:T(8,128)(2,1)S(1)} %collective-permute-done.5.refs_1_) | copy-start | bytes 24580
  31.0 0.6 %copy-start.5 = (bf16[2,64,32]{2,1,0:T(8,128)(2,1)}, bf16[2,64,32]{2,1,0:T(8,128)(2,1)S(1)}, u32[]{:S(2)}) copy-start(bf16[2,64,32]{2,1,0:T(8,128)(2,1)S(1)} %collective-permute-done.4.refs_0_) | copy-start | bytes 24580
  34.1 2.5 %collective-permute-start.7 = (f32[32,4096]{1,0:T(8,128)}, f32[32,4096]{1,0:T(8,128)S(1)}, u32[]{:S(2)}, u32[]{:S(2)}) collective-permute-start(f32[32,4096]{1,0:T(8,128)} %shard_map.130), channel_id=1, source_target_pairs={{0,4},{4,0},{8,12},{12,8},{16,20},{20,16},{24,28},{28,24},{1,5},{5... | collective-permute-start | bytes 1572872 | tf_op jit(solution)/shard_map/ppermute | solution.py:155
  37.8 12.4 %collective-permute-start.8 = (f32[8,4096]{1,0:T(8,128)S(1)}, f32[8,4096]{1,0:T(8,128)S(1)}, u32[]{:S(2)}, u32[]{:S(2)}) collective-permute-start(f32[8,4096]{1,0:T(8,128)S(1)} %get-tuple-element.19), channel_id=1, source_target_pairs={{0,16},{4,20},{8,24},{12,28},{16,0},{20,4},{24,8},{28,12},{1,17},{... | collective-permute-start | bytes 393224 | tf_op jit(solution)/shard_map/ppermute | solution.py:155
  38.7 11.5 %collective-permute-start.10 = (f32[8,4096]{1,0:T(8,128)S(1)}, f32[8,4096]{1,0:T(8,128)S(1)}, u32[]{:S(2)}, u32[]{:S(2)}) collective-permute-start(f32[8,4096]{1,0:T(8,128)S(1)} %get-tuple-element.20), channel_id=1, source_target_pairs={{0,24},{4,28},{8,16},{12,20},{16,8},{20,12},{24,0},{28,4},{1,25},{... | collective-permute-start | bytes 393224 | tf_op jit(solution)/shard_map/ppermute | solution.py:155
  40.4 11.1 %collective-permute-start.9 = (f32[8,4096]{1,0:T(8,128)S(1)}, f32[8,4096]{1,0:T(8,128)S(1)}, u32[]{:S(2)}, u32[]{:S(2)}) collective-permute-start(f32[8,4096]{1,0:T(8,128)S(1)} %get-tuple-element.21), channel_id=1, source_target_pairs={{0,8},{4,12},{8,0},{12,4},{16,24},{20,28},{24,16},{28,20},{1,9},{5... | collective-permute-start | bytes 393224 | tf_op jit(solution)/shard_map/ppermute | solution.py:155
